TPU v7x, 128 devices: a whole 4x4x4 slice. The times are simulated.
128 devices in a mesh: gx: 8 (over x, z_lo), gy: 4 (over z_hi, core), gz: 4 (over y).
Axes of the slice: x: 4, y: 4, z: 4 (z_hi: 2, z_lo: 2; z = z_hi * 2 + z_lo), core: 2. Of those that a mesh axis runs over, the one named last changes fastest.
Arguments:
- e_forward: float32 [3, 128, 64, 4096], P(None, 'gx', 'gy', 'gz'), may hold values from -6 to 6
- e_adjoint: float32 [3, 128, 64, 4096], P(None, 'gx', 'gy', 'gz'), may hold values from -6 to 6
- h_adjoint: float32 [3, 128, 64, 4096], P(None, 'gx', 'gy', 'gz'), may hold values from -6 to 6
- inv_perm: float32 [128, 64, 4096], P('gx', 'gy', 'gz'), may hold values from 0.08 to 1
- voxel_cell: int32 [8, 4, 4, 1024], P('gx', 'gy', 'gz'), may hold values from 0 to 262143
- voxel_owner: int32 [8, 4, 4, 1024, 1], P('gx', 'gy', 'gz'), may hold values from 0 to 127; in each aligned block of 1024 rows (0 to 1023, 1024 to 2047, ..., all dimensions but the last counted through in order) at most 16 rows name the same one
- voxel_slot: int32 [8, 4, 4, 1024], P('gx', 'gy', 'gz'), may hold values from 0 to 255
Outputs:
- e_adjoint_new: float32 [3, 128, 64, 4096], P(None, 'gx', 'gy', 'gz')
- h_adjoint_new: float32 [3, 128, 64, 4096], P(None, 'gx', 'gy', 'gz')
- gradient: float32 [32768], P(('gx', 'gy', 'gz'))
Inputs may be any that keep to these rules, and one draw needn't show every extreme that they name: `voxel_owner`: among the 1024 design voxels of one device, at most 16 name the same owner.
All inputs are finite; a program needn't handle non-finite values.
Results may differ from a plain program's by a relative error of at most 0.00014.
Values sent between devices are 32-bit elements; how exact they have to be, the bound alone decides.
No kernel may reach another device: no remote copies, remote signals or barrier semaphores. Data moves between devices by JAX's collectives and lax.ppermute only.
A program may use at most 576 MiB of HBM per device.

v0:
```python
import jax
import jax.numpy as jnp
from jax import lax
from jax.sharding import PartitionSpec as P

STEPS = 2
P_DEV = 256


courant = 0.5


def extended(x, sides, width):
    for axis, dim in sides:
        peers, length = (lax.axis_size(axis), x.shape[dim])
        up = [(i, (i + 1) % peers) for i in range(peers - 1)]
        down = [(j, i) for i, j in up]
        last = lax.slice_in_dim(x, length - width, length, axis=dim)
        initial = lax.slice_in_dim(x, 0, width, axis=dim)
        before = lax.ppermute(last, axis, up)
        after = lax.ppermute(initial, axis, down)
        x = jnp.concatenate([before, x, after], axis=dim)
    return x


def inside(position, total, count, first, extent):
    coords = position * extent + first + jnp.arange(count, dtype=jnp.int32)
    return ((coords >= 0) & (coords < extent * total)).astype(jnp.float32)


def region_mask(counts, first, extents):
    along_x = inside(lax.axis_index("gx"), lax.axis_size("gx"), counts[0], first, extents[0])
    along_y = inside(lax.axis_index("gy"), lax.axis_size("gy"), counts[1], first, extents[1])
    along_z = inside(lax.axis_index("gz"), lax.axis_size("gz"), counts[2], first, extents[2])
    return along_x[:, None, None] * along_y[None, :, None] * along_z[None, None, :]


def leapfrog(fields, inv_region, first, extents):
    elec_x, elec_y, elec_z = (fields[0], fields[1], fields[2])
    magn_x, magn_y, magn_z = (fields[3], fields[4], fields[5])
    sizes = fields.shape[1:]
    core = (slice(0, -1), slice(0, -1), slice(0, -1))
    up_x = (slice(1, None), slice(0, -1), slice(0, -1))
    up_y = (slice(0, -1), slice(1, None), slice(0, -1))
    up_z = (slice(0, -1), slice(0, -1), slice(1, None))
    h_mask = region_mask((sizes[0] - 1, sizes[1] - 1, sizes[2] - 1), first, extents)
    new_hx = (
        magn_x[core] - courant * (elec_z[up_y] - elec_z[core] - (elec_y[up_z] - elec_y[core]))
    ) * h_mask
    new_hy = (
        magn_y[core] - courant * (elec_x[up_z] - elec_x[core] - (elec_z[up_x] - elec_z[core]))
    ) * h_mask
    new_hz = (
        magn_z[core] - courant * (elec_y[up_x] - elec_y[core] - (elec_x[up_y] - elec_x[core]))
    ) * h_mask
    here = (slice(1, None), slice(1, None), slice(1, None))
    low_x = (slice(0, -1), slice(1, None), slice(1, None))
    low_y = (slice(1, None), slice(0, -1), slice(1, None))
    low_z = (slice(1, None), slice(1, None), slice(0, -1))
    inner = (slice(1, -1), slice(1, -1), slice(1, -1))
    e_mask = region_mask((sizes[0] - 2, sizes[1] - 2, sizes[2] - 2), first + 1, extents)
    new_ex = (
        elec_x[inner]
        + courant * inv_region * (new_hz[here] - new_hz[low_y] - (new_hy[here] - new_hy[low_z]))
    ) * e_mask
    new_ey = (
        elec_y[inner]
        + courant * inv_region * (new_hx[here] - new_hx[low_z] - (new_hz[here] - new_hz[low_x]))
    ) * e_mask
    new_ez = (
        elec_z[inner]
        + courant * inv_region * (new_hy[here] - new_hy[low_x] - (new_hx[here] - new_hx[low_y]))
    ) * e_mask
    return jnp.stack([new_ex, new_ey, new_ez, new_hx[here], new_hy[here], new_hz[here]])


def body(e_forward, e_adjoint, h_adjoint, inv_perm, voxel_cell, voxel_owner, voxel_slot):
    extents = e_adjoint.shape[1:]
    fields = jnp.concatenate([e_adjoint, h_adjoint], axis=0)
    for repeat in range(STEPS):
        padded = extended(fields, (("gx", 1), ("gy", 2), ("gz", 3)), 1)
        fields = leapfrog(padded, inv_perm, -1, extents)
    intersection = e_forward[0] * fields[0] + e_forward[1] * fields[1] + e_forward[2] * fields[2]
    count = voxel_cell.shape[-1]
    voxel_rows = voxel_cell.reshape(count)
    owners = voxel_owner.reshape(count)
    slot_ids = voxel_slot.reshape(count)
    terms = intersection.reshape(-1)[voxel_rows]
    devices = lax.axis_size("gx") * lax.axis_size("gy") * lax.axis_size("gz")
    params = owners * P_DEV + slot_ids
    dense_terms = jax.ops.segment_sum(terms, params, num_segments=devices * P_DEV)
    gradient = lax.psum_scatter(dense_terms, ("gx", "gy", "gz"), scatter_dimension=0, tiled=True)
    return (fields[:3], fields[3:], gradient)


def solution(mesh):
    return jax.shard_map(
        body,
        mesh=mesh,
        in_specs=(
            P(None, "gx", "gy", "gz"),
            P(None, "gx", "gy", "gz"),
            P(None, "gx", "gy", "gz"),
            P("gx", "gy", "gz"),
            P("gx", "gy", "gz", None),
            P("gx", "gy", "gz", None, None),
            P("gx", "gy", "gz", None),
        ),
        out_specs=(P(None, "gx", "gy", "gz"), P(None, "gx", "gy", "gz"), P(("gx", "gy", "gz"))),
        check_vma=False,
    )
```

profile of v0, /device:TPU:1, one launch (start us, length us, event | category | flops | bytes accessed | tf_op | source)
XLA Modules:
  0.0 354.8 jit_solution(17653637620297011843)
XLA Ops:
  7.2 2.3 constant_dynamic-update-slice_fusion.1
  10.2 2.6 copy-done.2
  12.9 4.4 %collective-permute-start = (f32[6,1,16,1024]{3,2,1,0:T(8,128)S(1)}, f32[6,1,16,1024]{3,2,1,0:T(8,128)S(1)}, u32[]{:S(2)}, u32[]{:S(2)}) collective-permute-start(f32[6,1,16,1024]{3,2,1,0:T(8,128)S(1)} %get-tuple-element.35), channel_id=1, source_target_pairs={{0,16},{16,32},{32,48},{48,64},{64,80},{80,96},{96,112},{1,17},{17... | collective-permute-start | bytes 1179656 | tf_op jit(solution)/shard_map/ppermute | solution.py:20
  18.7 14.8 %collective-permute-done = f32[6,1,16,1024]{3,2,1,0:T(8,128)S(1)} collective-permute-done((f32[6,1,16,1024]{3,2,1,0:T(8,128)S(1)}, f32[6,1,16,1024]{3,2,1,0:T(8,128)S(1)}, u32[]{:S(2)}, u32[]{:S(2)}) %collective-permute-start) | collective-permute-done | bytes 393248 | tf_op jit(solution)/shard_map/ppermute | solution.py:20
  33.5 4.0 %pad_maximum_fusion.9 = (f32[6,18,1,1024]{3,2,1,0:T(1,128)S(1)}, f32[6,18,1,1024]{3,2,1,0:T(1,128)S(1)}) fusion(f32[6,1,16,1024]{3,2,1,0:T(8,128)S(1)} %collective-permute-done.1, f32[6,16,16,1024]{3,2,1,0:T(8,128)} %copy-done.2, f32[6,1,16,1024]{3,2,1,0:T(8,128)S(1)} %collective-permute-done), kind=kLoop, calls=%fused_computation.112 | loop fusion | flops 442368 | bytes 7962624 | tf_op jit(solution)/shard_map/slice | solution.py:18
  37.5 6.6 %collective-permute-start.2 = (f32[6,18,1,1024]{3,2,1,0:T(1,128)S(1)}, f32[6,18,1,1024]{3,2,1,0:T(1,128)S(1)}, u32[]{:S(2)}, u32[]{:S(2)}) collective-permute-start(f32[6,18,1,1024]{3,2,1,0:T(1,128)S(1)} %get-tuple-element.31), channel_id=1, source_target_pairs={{0,4},{4,8},{8,12},{1,5},{5,9},{9,13},{2,6},{6,10},{10,14},{3,7},{... | collective-permute-start | bytes 1327112 | tf_op jit(solution)/shard_map/ppermute | solution.py:20
  46.2 3.2 collective-permute-done.2
  49.3 5.9 %collective-permute-done.3 = f32[6,18,1,1024]{3,2,1,0:T(1,128)S(1)} collective-permute-done((f32[6,18,1,1024]{3,2,1,0:T(1,128)S(1)}, f32[6,18,1,1024]{3,2,1,0:T(1,128)S(1)}, u32[]{:S(2)}, u32[]{:S(2)}) %collective-permute-start.3) | collective-permute-done | bytes 442400 | tf_op jit(solution)/shard_map/ppermute | solution.py:21
  55.2 2.6 pad_maximum_fusion
  57.8 3.9 %copy-done.1 = f32[6,18,18,1024]{3,2,1,0:T(8,128)} copy-done((f32[6,18,18,1024]{3,2,1,0:T(8,128)}, f32[6,18,18,1024]{3,2,1,0:T(8,128)S(1)}, u32[]{:S(2)}) %copy-start.1) | copy-done | bytes 7962648
  63.0 3.2 collective-permute-start.4
  69.2 2.6 collective-permute-done.5
  72.6 14.8 %concatenate.26 = f32[6,18,18,1026]{3,2,1,0:T(8,128)} concatenate(f32[6,18,18,1]{3,2,1,0:T(8,128)S(1)} %copy.29, f32[6,18,18,1024]{3,2,1,0:T(8,128)} %copy-done.1, f32[6,18,18,1]{3,2,1,0:T(8,128)S(1)} %copy.30), dimensions={3} | concatenate | bytes 15956352 | tf_op jit(solution)/shard_map/concatenate | solution.py:22
  87.4 7.2 %slice_bitcast_fusion.6 = (f32[18,18,1026]{2,1,0:T(8,128)}, f32[18,18,1026]{2,1,0:T(8,128)S(1)}, f32[18,18,1026]{2,1,0:T(8,128)}, f32[18,18,1026]{2,1,0:T(8,128)...) fusion(f32[6,18,18,1026]{3,2,1,0:T(8,128)} %concatenate.26), kind=kLoop, calls=%fused_computation.24 | loop fusion | bytes 15956352 | tf_op jit(solution)/shard_map/squeeze | solution.py:40
  94.6 4.3 %multiply_multiply_fusion.3 = (f32[17,17,1025]{2,1,0:T(8,128)S(1)}, f32[17,17,1025]{2,1,0:T(8,128)S(1)}, f32[17,17,1025]{2,1,0:T(8,128)S(1)}) fusion(f32[18,18,1026]{2,1,0:T(8,128)S(1)} %get-tuple-element.22, f32[18,18,1026]{2,1,0:T(8,128)S(1)} %get-tuple-element.20, f32[18,18,1026]{2,1,0:T(8,128)} %get-tuple-element.19, f32[1025]{0:T(1024)S(1)} %fusion.49, ...), kind=kLoop, calls=%fused_computation.7 | loop fusion | flops 5628275 | bytes 17778756 | tf_op jit(solution)/shard_map/mul | solution.py:47
  104.5 3.5 collective-permute-start.6
  109.5 11.6 %collective-permute-done.6 = f32[6,1,16,1024]{3,2,1,0:T(8,128)S(1)} collective-permute-done((f32[6,1,16,1024]{3,2,1,0:T(8,128)S(1)}, f32[6,1,16,1024]{3,2,1,0:T(8,128)S(1)}, u32[]{:S(2)}, u32[]{:S(2)}) %collective-permute-start.6) | collective-permute-done | bytes 393248 | tf_op jit(solution)/shard_map/ppermute | solution.py:20
  124.0 2.4 collective-permute-start.9
  126.5 2.7 collective-permute-done.8
  129.2 5.9 %collective-permute-done.9 = f32[6,18,1,1024]{3,2,1,0:T(1,128)S(1)} collective-permute-done((f32[6,18,1,1024]{3,2,1,0:T(1,128)S(1)}, f32[6,18,1,1024]{3,2,1,0:T(1,128)S(1)}, u32[]{:S(2)}, u32[]{:S(2)}) %collective-permute-start.9) | collective-permute-done | bytes 442400 | tf_op jit(solution)/shard_map/ppermute | solution.py:21
  135.1 2.6 pad_maximum_fusion.1
  137.8 3.9 %copy-done = f32[6,18,18,1024]{3,2,1,0:T(8,128)} copy-done((f32[6,18,18,1024]{3,2,1,0:T(8,128)}, f32[6,18,18,1024]{3,2,1,0:T(8,128)S(1)}, u32[]{:S(2)}) %copy-start) | copy-done | bytes 7962648
  145.7 3.2 collective-permute-start.10
  148.9 2.0 copy.38
  157.7 15.6 %concatenate.29 = f32[6,18,18,1026]{3,2,1,0:T(8,128)} concatenate(f32[6,18,18,1]{3,2,1,0:T(8,128)} %copy.33, f32[6,18,18,1024]{3,2,1,0:T(8,128)} %copy-done, f32[6,18,18,1]{3,2,1,0:T(8,128)} %copy.34), dimensions={3} | concatenate | bytes 15956352 | tf_op jit(solution)/shard_map/concatenate | solution.py:22
  173.3 7.2 %slice_bitcast_fusion = (f32[18,18,1026]{2,1,0:T(8,128)}, f32[18,18,1026]{2,1,0:T(8,128)S(1)}, f32[18,18,1026]{2,1,0:T(8,128)}, f32[18,18,1026]{2,1,0:T(8,128)S(...) fusion(f32[6,18,18,1026]{3,2,1,0:T(8,128)} %concatenate.29), kind=kLoop, calls=%fused_computation.18 | loop fusion | bytes 15956352 | tf_op jit(solution)/shard_map/squeeze | solution.py:40
  180.5 4.2 %multiply_multiply_fusion = (f32[17,17,1025]{2,1,0:T(8,128)S(1)}, f32[17,17,1025]{2,1,0:T(8,128)S(1)}, f32[17,17,1025]{2,1,0:T(8,128)S(1)}) fusion(f32[18,18,1026]{2,1,0:T(8,128)S(1)} %get-tuple-element.16, f32[18,18,1026]{2,1,0:T(8,128)S(1)} %get-tuple-element.14, f32[18,18,1026]{2,1,0:T(8,128)} %get-tuple-element.13, f32[1025]{0:T(1024)S(1)} %fusion.49, ...), kind=kLoop, calls=%fused_computation.4 | loop fusion | flops 5628275 | bytes 17778756 | tf_op jit(solution)/shard_map/mul | solution.py:47
  187.3 5.1 %fusion.42 = (f32[16,16,1024]{2,1,0:T(8,128)S(1)}, f32[16,16,1024]{2,1,0:T(8,128)S(1)}, f32[16,16,1024]{2,1,0:T(8,128)}, f32[16,16,1024]{2,1,0:T(8,128)}, f32[1,16,16,1024]{3,2,1,0:T(8,128)}) fusion(f32[3,16,16,1024]{3,2,1,0:T(8,128)S(1)} %copy-done.9, f32[1024]{0:T(1024)S(1)} %fusion.53, f32[16,16]{1,0:T(8,128)S(1)} %broadcast_multiply_fusion.1, ...), kind=kLoop, calls=%fused_computation.97 | loop fusion | flops 6553600 | bytes 22025216 | tf_op jit(solution)/shard_map/add | solution.py:83
  192.6 6.2 %gather_fusion = f32[1024]{0:T(1024)S(1)} fusion(f32[262144]{0:T(1024)S(1)} %bitcast.75, s32[1024]{0:T(1024)S(1)} %broadcast_clamp_fusion), kind=kCustom, calls=%fused_computation | custom fusion | bytes 12288 | tf_op jit(solution)/shard_map/gather | solution.py:88
  198.8 6.5 %scatter_custom_fusion = f32[32768]{0:T(1024)} fusion(s32[1024]{0:T(1024)S(1)} %bitcast.81, f32[1024]{0:T(1024)S(1)} %gather_fusion, f32[]{:T(128)} %constant.10.clone.1), kind=kCustom, calls=%fused_computation.113 | custom fusion | flops 1024 | bytes 131076 | tf_op jit(solution)/shard_map/scatter-add | solution.py:91
  205.4 3.7 %pad_maximum_fusion.3 = f32[3,16,16,1024]{3,2,1,0:T(8,128)} fusion(f32[1,16,16,1024]{3,2,1,0:T(8,128)} %slice_bitcast_fusion.14, f32[1,16,16,1024]{3,2,1,0:T(8,128)} %slice_bitcast_fusion.13, f32[1,16,16,1024]{3,2,1,0:T(8,128)S(1)} %copy-done.7), kind=kLoop, calls=%fused_computation.17 | loop fusion | flops 1572864 | bytes 6291456 | tf_op jit(solution)/shard_map/stack | solution.py:74
  210.9 135.7 %all-reduce.3.cloned.1.call-done = f32[32768]{0:T(1024)} async-done(((f32[32768]{0:T(1024)}), f32[32768]{0:T(1024)}) %all-reduce.3.cloned.1.call-update) | async-done | bytes 131088
  (69 shorter events, 35.9 us)
Async XLA Ops:
  7.2 2.8 copy-start.8
  7.2 339.5 %all-reduce.3.cloned.1.call-start = ((), (), s32[]{:S(2)}) async-start(), calls=%async_computation | async-start | bytes 262144
  10.2 2.6 copy-start.2
  12.9 20.6 %collective-permute-start = (f32[6,1,16,1024]{3,2,1,0:T(8,128)S(1)}, f32[6,1,16,1024]{3,2,1,0:T(8,128)S(1)}, u32[]{:S(2)}, u32[]{:S(2)}) collective-permute-start(f32[6,1,16,1024]{3,2,1,0:T(8,128)S(1)} %get-tuple-element.35), channel_id=1, source_target_pairs={{0,16},{16,32},{32,48},{48,64},{64,80},{80,96},{96,112},{1,17},{17... | collective-permute-start | bytes 1179656 | tf_op jit(solution)/shard_map/ppermute | solution.py:20
  17.3 16.2 %collective-permute-start.1 = (f32[6,1,16,1024]{3,2,1,0:T(8,128)S(1)}, f32[6,1,16,1024]{3,2,1,0:T(8,128)S(1)}, u32[]{:S(2)}, u32[]{:S(2)}) collective-permute-start(f32[6,1,16,1024]{3,2,1,0:T(8,128)S(1)} %get-tuple-element.36), channel_id=1, source_target_pairs={{16,0},{32,16},{48,32},{64,48},{80,64},{96,80},{112,96},{17,1},{33... | collective-permute-start | bytes 1179656 | tf_op jit(solution)/shard_map/ppermute | solution.py:21
  33.5 21.7 %copy-start.3 = (f32[6,16,16,1024]{3,2,1,0:T(8,128)S(1)}, f32[6,16,16,1024]{3,2,1,0:T(8,128)}, u32[]{:S(2)}) copy-start(f32[6,16,16,1024]{3,2,1,0:T(8,128)} %copy-done.2) | copy-start | bytes 18874372
  37.5 11.9 %collective-permute-start.2 = (f32[6,18,1,1024]{3,2,1,0:T(1,128)S(1)}, f32[6,18,1,1024]{3,2,1,0:T(1,128)S(1)}, u32[]{:S(2)}, u32[]{:S(2)}) collective-permute-start(f32[6,18,1,1024]{3,2,1,0:T(1,128)S(1)} %get-tuple-element.31), channel_id=1, source_target_pairs={{0,4},{4,8},{8,12},{1,5},{5,9},{9,13},{2,6},{6,10},{10,14},{3,7},{... | collective-permute-start | bytes 1327112 | tf_op jit(solution)/shard_map/ppermute | solution.py:20
  44.1 11.1 %collective-permute-start.3 = (f32[6,18,1,1024]{3,2,1,0:T(1,128)S(1)}, f32[6,18,1,1024]{3,2,1,0:T(1,128)S(1)}, u32[]{:S(2)}, u32[]{:S(2)}) collective-permute-start(f32[6,18,1,1024]{3,2,1,0:T(1,128)S(1)} %get-tuple-element.32), channel_id=1, source_target_pairs={{4,0},{8,4},{12,8},{5,1},{9,5},{13,9},{6,2},{10,6},{14,10},{7,3},{... | collective-permute-start | bytes 1327112 | tf_op jit(solution)/shard_map/ppermute | solution.py:21
  57.8 3.9 %copy-start.1 = (f32[6,18,18,1024]{3,2,1,0:T(8,128)}, f32[6,18,18,1024]{3,2,1,0:T(8,128)S(1)}, u32[]{:S(2)}) copy-start(f32[6,18,18,1024]{3,2,1,0:T(8,128)S(1)} %pad_maximum_fusion) | copy-start | bytes 23887876
  63.0 5.4 %collective-permute-start.4 = (f32[6,18,18,1]{2,3,1,0:T(1,128)S(1)}, f32[6,18,18,1]{2,3,1,0:T(1,128)S(1)}, u32[]{:S(2)}, u32[]{:S(2)}) collective-permute-start(f32[6,18,18,1]{2,3,1,0:T(1,128)S(1)} %copy.35), channel_id=1, source_target_pairs={{0,1},{1,2},{2,3},{4,5},{5,6},{6,7},{8,9},{9,10},{10,11},{12,13},{... | collective-permute-start | bytes 23336 | tf_op jit(solution)/shard_map/ppermute | solution.py:20
  66.9 4.9 %collective-permute-start.5 = (f32[6,18,18,1]{2,3,1,0:T(1,128)S(1)}, f32[6,18,18,1]{2,3,1,0:T(1,128)S(1)}, u32[]{:S(2)}, u32[]{:S(2)}) collective-permute-start(f32[6,18,18,1]{2,3,1,0:T(1,128)S(1)} %copy.36), channel_id=1, source_target_pairs={{1,0},{2,1},{3,2},{5,4},{6,5},{7,6},{9,8},{10,9},{11,10},{13,12},{... | collective-permute-start | bytes 23336 | tf_op jit(solution)/shard_map/ppermute | solution.py:21
  94.6 4.3 %copy-start.4 = (f32[16,16,1024]{2,1,0:T(8,128)S(1)}, f32[16,16,1024]{2,1,0:T(8,128)}, u32[]{:S(2)}) copy-start(f32[16,16,1024]{2,1,0:T(8,128)} %param.10) | copy-start | bytes 3145732
  104.5 16.6 %collective-permute-start.6 = (f32[6,1,16,1024]{3,2,1,0:T(8,128)S(1)}, f32[6,1,16,1024]{3,2,1,0:T(8,128)S(1)}, u32[]{:S(2)}, u32[]{:S(2)}) collective-permute-start(f32[6,1,16,1024]{3,2,1,0:T(8,128)S(1)} %get-tuple-element.33), channel_id=1, source_target_pairs={{0,16},{16,32},{32,48},{48,64},{64,80},{80,96},{96,112},{1,17},{17... | collective-permute-start | bytes 1179656 | tf_op jit(solution)/shard_map/ppermute | solution.py:20
  108.0 18.4 %copy-start.12 = (s32[1,1,1,1024]{3,2,1,0:T(1,128)S(1)}, s32[1,1,1,1024]{3,2,1,0:T(1,128)}, u32[]{:S(2)}) copy-start(s32[1,1,1,1024]{3,2,1,0:T(1,128)} %param.11) | copy-start | bytes 12292
  108.0 18.4 %copy-start.10 = (s32[1,1,1,1024]{3,2,1,0:T(1,128)S(1)}, s32[1,1,1,1024]{3,2,1,0:T(1,128)}, u32[]{:S(2)}) copy-start(s32[1,1,1,1024]{3,2,1,0:T(1,128)} %param.13) | copy-start | bytes 12292
  108.0 18.4 %copy-start.11 = (s32[1,1,1,1024,1]{3,4,2,1,0:T(1,128)S(1)}, s32[1,1,1,1024,1]{3,4,2,1,0:T(1,128)}, u32[]{:S(2)}) copy-start(s32[1,1,1,1024,1]{3,4,2,1,0:T(1,128)} %param.12) | copy-start | bytes 12292
  108.1 13.1 %collective-permute-start.7 = (f32[6,1,16,1024]{3,2,1,0:T(8,128)S(1)}, f32[6,1,16,1024]{3,2,1,0:T(8,128)S(1)}, u32[]{:S(2)}, u32[]{:S(2)}) collective-permute-start(f32[6,1,16,1024]{3,2,1,0:T(8,128)S(1)} %get-tuple-element.34), channel_id=1, source_target_pairs={{16,0},{32,16},{48,32},{64,48},{80,64},{96,80},{112,96},{17,1},{33... | collective-permute-start | bytes 1179656 | tf_op jit(solution)/shard_map/ppermute | solution.py:21
  122.1 7.2 %collective-permute-start.8 = (f32[6,18,1,1024]{3,2,1,0:T(1,128)S(1)}, f32[6,18,1,1024]{3,2,1,0:T(1,128)S(1)}, u32[]{:S(2)}, u32[]{:S(2)}) collective-permute-start(f32[6,18,1,1024]{3,2,1,0:T(1,128)S(1)} %get-tuple-element.29), channel_id=1, source_target_pairs={{0,4},{4,8},{8,12},{1,5},{5,9},{9,13},{2,6},{6,10},{10,14},{3,7},{... | collective-permute-start | bytes 1327112 | tf_op jit(solution)/shard_map/ppermute | solution.py:20
  124.0 11.1 %collective-permute-start.9 = (f32[6,18,1,1024]{3,2,1,0:T(1,128)S(1)}, f32[6,18,1,1024]{3,2,1,0:T(1,128)S(1)}, u32[]{:S(2)}, u32[]{:S(2)}) collective-permute-start(f32[6,18,1,1024]{3,2,1,0:T(1,128)S(1)} %get-tuple-element.30), channel_id=1, source_target_pairs={{4,0},{8,4},{12,8},{5,1},{9,5},{13,9},{6,2},{10,6},{14,10},{7,3},{... | collective-permute-start | bytes 1327112 | tf_op jit(solution)/shard_map/ppermute | solution.py:21
  137.8 3.9 %copy-start = (f32[6,18,18,1024]{3,2,1,0:T(8,128)}, f32[6,18,18,1024]{3,2,1,0:T(8,128)S(1)}, u32[]{:S(2)}) copy-start(f32[6,18,18,1024]{3,2,1,0:T(8,128)S(1)} %pad_maximum_fusion.1) | copy-start | bytes 23887876
  145.7 6.8 %collective-permute-start.10 = (f32[6,18,18,1]{2,3,1,0:T(1,128)S(1)}, f32[6,18,18,1]{2,3,1,0:T(1,128)S(1)}, u32[]{:S(2)}, u32[]{:S(2)}) collective-permute-start(f32[6,18,18,1]{2,3,1,0:T(1,128)S(1)} %copy.37), channel_id=1, source_target_pairs={{0,1},{1,2},{2,3},{4,5},{5,6},{6,7},{8,9},{9,10},{10,11},{12,13},{... | collective-permute-start | bytes 23336 | tf_op jit(solution)/shard_map/ppermute | solution.py:20
  151.0 4.9 %collective-permute-start.11 = (f32[6,18,18,1]{2,3,1,0:T(1,128)S(1)}, f32[6,18,18,1]{2,3,1,0:T(1,128)S(1)}, u32[]{:S(2)}, u32[]{:S(2)}) collective-permute-start(f32[6,18,18,1]{2,3,1,0:T(1,128)S(1)} %copy.38), channel_id=1, source_target_pairs={{1,0},{2,1},{3,2},{5,4},{6,5},{7,6},{9,8},{10,9},{11,10},{13,12},{... | collective-permute-start | bytes 23336 | tf_op jit(solution)/shard_map/ppermute | solution.py:21
  184.7 2.6 copy-start.9
  192.6 12.7 %copy-start.7 = (f32[1,16,16,1024]{3,2,1,0:T(8,128)S(1)}, f32[1,16,16,1024]{3,2,1,0:T(8,128)}, u32[]{:S(2)}) copy-start(f32[1,16,16,1024]{3,2,1,0:T(8,128)} %get-tuple-element.43) | copy-start | bytes 3145732
  205.3 3.7 %copy-start.5 = (f32[16,16,1024]{2,1,0:T(8,128)S(1)}, f32[16,16,1024]{2,1,0:T(8,128)}, u32[]{:S(2)}) copy-start(f32[16,16,1024]{2,1,0:T(8,128)} %get-tuple-element.11) | copy-start | bytes 3145732
  205.4 3.7 %copy-start.6 = (f32[16,16,1024]{2,1,0:T(8,128)S(1)}, f32[16,16,1024]{2,1,0:T(8,128)}, u32[]{:S(2)}) copy-start(f32[16,16,1024]{2,1,0:T(8,128)} %get-tuple-element.12) | copy-start | bytes 3145732
Sparse Core Ops, SparseCore 0:
  205.4 141.1 all-reduce.2
where the time goes:
time: 356 us; the launch traced here: 355 us
  waiting for transfers between devices  184 us (52%)
  local copies, waits for them, and re-layouts  83.1 us (23%)
  other arithmetic  40.4 us (11%)
  starting transfers between devices  32.9 us (9%)
  between operations  14.5 us (4%)
    unnamed x2, waiting for transfers between devices  136 us
    ppermute x6, waiting for transfers between devices, extended(): before = lax.ppermute(last, axis, up)  32.4 us
    concatenate x2, local copies, waits for them, and re-layouts, extended(): x = jnp.concatenate([before, x, after], axis=dim)  30.4 us
    ppermute x6, starting transfers between devices, extended(): before = lax.ppermute(last, axis, up)  22.8 us
    unnamed x35, local copies, waits for them, and re-layouts  21.1 us
    ppermute x6, waiting for transfers between devices, extended(): after = lax.ppermute(initial, axis, down)  15.9 us
    squeeze x2, local copies, waits for them, and re-layouts, leapfrog(): magn_x, magn_y, magn_z = (fields[3], fields[4], fields[5])  14.5 us
    ppermute x6, starting transfers between devices, extended(): after = lax.ppermute(initial, axis, down)  10 us
  transfers between devices with their start and end apart: 13, of which 9 were waited for; matrix products, arithmetic and copies ran while one was open for 3% of the time, Pallas kernels for 0%

commit v1 on v0

--- a/solution.py
+++ b/solution.py
@@ -89,7 +89,9 @@
     devices = lax.axis_size("gx") * lax.axis_size("gy") * lax.axis_size("gz")
     params = owners * P_DEV + slot_ids
     dense_terms = jax.ops.segment_sum(terms, params, num_segments=devices * P_DEV)
-    gradient = lax.psum_scatter(dense_terms, ("gx", "gy", "gz"), scatter_dimension=0, tiled=True)
+    per_owner = dense_terms.reshape(devices, P_DEV)
+    received = lax.all_to_all(per_owner, ("gx", "gy", "gz"), 0, 0, tiled=True)
+    gradient = received.sum(axis=0)
     return (fields[:3], fields[3:], gradient)
 
 

time: 356 us -> 219 us (0.62)
  waiting for transfers between devices: 184 us -> 52.9 us
  between operations: 14.5 us -> 1.08 us
  starting transfers between devices: 32.9 us -> 40.3 us
    unnamed x2 -> x0, waiting for transfers between devices: 136 us -> none
    all_to_all x0 -> x1, starting transfers between devices: none -> 7.39 us  [body(): received = lax.all_to_all(per_owner, ('gx', 'gy', 'gz'), 0, 0, tiled=True)]
    all_to_all x0 -> x1, waiting for transfers between devices: none -> 4.62 us  [body(): received = lax.all_to_all(per_owner, ('gx', 'gy', 'gz'), 0, 0, tiled=True)]
    unnamed x35 -> x34, local copies, waits for them, and re-layouts: 21.1 us -> 19.8 us
  transfers between devices with their start and end apart: 13 -> 13, of which waited for: 9 -> 9; matrix products, arithmetic and copies ran while one was open for 3% -> 5% of each run, Pallas kernels for 0% -> 0%
where the time goes in v1:
time: 219 us; the launch traced here: 217 us
  local copies, waits for them, and re-layouts  82 us (37%)
  waiting for transfers between devices  52.9 us (24%)
  other arithmetic  41.1 us (19%)
  starting transfers between devices  40.3 us (18%)
    ppermute x6, waiting for transfers between devices, extended(): before = lax.ppermute(last, axis, up)  32.4 us
    concatenate x2, local copies, waits for them, and re-layouts, extended(): x = jnp.concatenate([before, x, after], axis=dim)  30.4 us
    ppermute x6, starting transfers between devices, extended(): before = lax.ppermute(last, axis, up)  22.8 us
    unnamed x34, local copies, waits for them, and re-layouts  19.8 us
    ppermute x6, waiting for transfers between devices, extended(): after = lax.ppermute(initial, axis, down)  15.9 us
    squeeze x2, local copies, waits for them, and re-layouts, leapfrog(): magn_x, magn_y, magn_z = (fields[3], fields[4], fields[5])  14.5 us
    ppermute x6, starting transfers between devices, extended(): after = lax.ppermute(initial, axis, down)  10 us
    mul x2, other arithmetic, leapfrog(): (magn_x[core] - courant * (elec_z[up_y] - elec_z[core] - (elec_y[up_z] -...  8.43 us
  transfers between devices with their start and end apart: 13, of which 9 were waited for; matrix products, arithmetic and copies ran while one was open for 5% of the time, Pallas kernels for 0%

profile of v1, /device:TPU:1, one launch (start us, length us, event | category | flops | bytes accessed | tf_op | source)
XLA Modules:
  0.0 217.3 jit_solution(2200925393536141898)
XLA Ops:
  0.6 2.3 %constant_dynamic-update-slice_fusion.1 = f32[6,16,16,1024]{3,2,1,0:T(8,128)S(1)} fusion(f32[3,16,16,1024]{3,2,1,0:T(8,128)} %param.8), kind=kLoop, calls=%fused_computation.117 | loop fusion | bytes 6291456
  3.9 2.6 %copy-done.2 = f32[6,16,16,1024]{3,2,1,0:T(8,128)} copy-done((f32[6,16,16,1024]{3,2,1,0:T(8,128)}, f32[6,16,16,1024]{3,2,1,0:T(8,128)S(1)}, u32[]{:S(2)}) %copy-start.2) | copy-done | bytes 6291480
  6.6 4.4 %collective-permute-start = (f32[6,1,16,1024]{3,2,1,0:T(8,128)S(1)}, f32[6,1,16,1024]{3,2,1,0:T(8,128)S(1)}, u32[]{:S(2)}, u32[]{:S(2)}) collective-permute-start(f32[6,1,16,1024]{3,2,1,0:T(8,128)S(1)} %get-tuple-element.35), channel_id=1, source_target_pairs={{0,16},{16,32},{32,48},{48,64},{64,80},{80,96},{96,112},{1,17},{17... | collective-permute-start | bytes 1179656 | tf_op jit(solution)/shard_map/ppermute | solution.py:20
  12.3 14.8 %collective-permute-done = f32[6,1,16,1024]{3,2,1,0:T(8,128)S(1)} collective-permute-done((f32[6,1,16,1024]{3,2,1,0:T(8,128)S(1)}, f32[6,1,16,1024]{3,2,1,0:T(8,128)S(1)}, u32[]{:S(2)}, u32[]{:S(2)}) %collective-permute-start) | collective-permute-done | bytes 393248 | tf_op jit(solution)/shard_map/ppermute | solution.py:20
  27.1 4.0 %pad_maximum_fusion.9 = (f32[6,18,1,1024]{3,2,1,0:T(1,128)S(1)}, f32[6,18,1,1024]{3,2,1,0:T(1,128)S(1)}) fusion(f32[6,1,16,1024]{3,2,1,0:T(8,128)S(1)} %collective-permute-done.1, f32[6,16,16,1024]{3,2,1,0:T(8,128)} %copy-done.2, f32[6,1,16,1024]{3,2,1,0:T(8,128)S(1)} %collective-permute-done), kind=kLoop, calls=%fused_computation.112 | loop fusion | flops 442368 | bytes 7962624 | tf_op jit(solution)/shard_map/slice | solution.py:18
  31.1 6.6 %collective-permute-start.2 = (f32[6,18,1,1024]{3,2,1,0:T(1,128)S(1)}, f32[6,18,1,1024]{3,2,1,0:T(1,128)S(1)}, u32[]{:S(2)}, u32[]{:S(2)}) collective-permute-start(f32[6,18,1,1024]{3,2,1,0:T(1,128)S(1)} %get-tuple-element.31), channel_id=1, source_target_pairs={{0,4},{4,8},{8,12},{1,5},{5,9},{9,13},{2,6},{6,10},{10,14},{3,7},{... | collective-permute-start | bytes 1327112 | tf_op jit(solution)/shard_map/ppermute | solution.py:20
  39.8 3.2 %collective-permute-done.2 = f32[6,18,1,1024]{3,2,1,0:T(1,128)S(1)} collective-permute-done((f32[6,18,1,1024]{3,2,1,0:T(1,128)S(1)}, f32[6,18,1,1024]{3,2,1,0:T(1,128)S(1)}, u32[]{:S(2)}, u32[]{:S(2)}) %collective-permute-start.2) | collective-permute-done | bytes 442400 | tf_op jit(solution)/shard_map/ppermute | solution.py:20
  43.0 5.9 %collective-permute-done.3 = f32[6,18,1,1024]{3,2,1,0:T(1,128)S(1)} collective-permute-done((f32[6,18,1,1024]{3,2,1,0:T(1,128)S(1)}, f32[6,18,1,1024]{3,2,1,0:T(1,128)S(1)}, u32[]{:S(2)}, u32[]{:S(2)}) %collective-permute-start.3) | collective-permute-done | bytes 442400 | tf_op jit(solution)/shard_map/ppermute | solution.py:21
  48.9 2.6 %pad_maximum_fusion = f32[6,18,18,1024]{3,2,1,0:T(8,128)S(1)} fusion(f32[6,18,1,1024]{3,2,1,0:T(1,128)S(1)} %collective-permute-done.3, f32[6,1,16,1024]{3,2,1,0:T(8,128)S(1)} %collective-permute-done.1, f32[6,16,16,1024]{3,2,1,0:T(8,128)S(1)} %copy-done.3, f32[6,1,16,1024]{3,2,1,0:T(8,128)S(1)} %collective-permute-done, ...), kind=kLoop, calls=%fused_computation.2 | loop fusion | flops 7962624 | bytes 15925248 | tf_op jit(solution)/shard_map/concatenate | solution.py:22
  51.5 3.9 %copy-done = f32[6,18,18,1024]{3,2,1,0:T(8,128)} copy-done((f32[6,18,18,1024]{3,2,1,0:T(8,128)}, f32[6,18,18,1024]{3,2,1,0:T(8,128)S(1)}, u32[]{:S(2)}) %copy-start) | copy-done | bytes 7962648
  56.6 3.2 %collective-permute-start.4 = (f32[6,18,18,1]{2,3,1,0:T(1,128)S(1)}, f32[6,18,18,1]{2,3,1,0:T(1,128)S(1)}, u32[]{:S(2)}, u32[]{:S(2)}) collective-permute-start(f32[6,18,18,1]{2,3,1,0:T(1,128)S(1)} %copy.53), channel_id=1, source_target_pairs={{0,1},{1,2},{2,3},{4,5},{5,6},{6,7},{8,9},{9,10},{10,11},{12,13},{... | collective-permute-start | bytes 23336 | tf_op jit(solution)/shard_map/ppermute | solution.py:20
  62.8 2.6 %collective-permute-done.5 = f32[6,18,18,1]{2,3,1,0:T(1,128)S(1)} collective-permute-done((f32[6,18,18,1]{2,3,1,0:T(1,128)S(1)}, f32[6,18,18,1]{2,3,1,0:T(1,128)S(1)}, u32[]{:S(2)}, u32[]{:S(2)}) %collective-permute-start.5) | collective-permute-done | bytes 7808 | tf_op jit(solution)/shard_map/ppermute | solution.py:21
  66.2 14.8 %concatenate.26 = f32[6,18,18,1026]{3,2,1,0:T(8,128)} concatenate(f32[6,18,18,1]{3,2,1,0:T(8,128)S(1)} %copy.45, f32[6,18,18,1024]{3,2,1,0:T(8,128)} %copy-done, f32[6,18,18,1]{3,2,1,0:T(8,128)S(1)} %copy.46), dimensions={3} | concatenate | bytes 15956352 | tf_op jit(solution)/shard_map/concatenate | solution.py:22
  81.0 7.2 %slice_bitcast_fusion.6 = (f32[18,18,1026]{2,1,0:T(8,128)}, f32[18,18,1026]{2,1,0:T(8,128)S(1)}, f32[18,18,1026]{2,1,0:T(8,128)}, f32[18,18,1026]{2,1,0:T(8,128)...) fusion(f32[6,18,18,1026]{3,2,1,0:T(8,128)} %concatenate.26), kind=kLoop, calls=%fused_computation.24 | loop fusion | bytes 15956352 | tf_op jit(solution)/shard_map/squeeze | solution.py:40
  88.3 4.3 %multiply_multiply_fusion.3 = (f32[17,17,1025]{2,1,0:T(8,128)S(1)}, f32[17,17,1025]{2,1,0:T(8,128)S(1)}, f32[17,17,1025]{2,1,0:T(8,128)S(1)}) fusion(f32[18,18,1026]{2,1,0:T(8,128)S(1)} %get-tuple-element.22, f32[18,18,1026]{2,1,0:T(8,128)S(1)} %get-tuple-element.20, f32[18,18,1026]{2,1,0:T(8,128)} %get-tuple-element.19, f32[1025]{0:T(1024)S(1)} %fusion.49, ...), kind=kLoop, calls=%fused_computation.7 | loop fusion | flops 5628275 | bytes 17778756 | tf_op jit(solution)/shard_map/mul | solution.py:47
  98.1 3.5 %collective-permute-start.6 = (f32[6,1,16,1024]{3,2,1,0:T(8,128)S(1)}, f32[6,1,16,1024]{3,2,1,0:T(8,128)S(1)}, u32[]{:S(2)}, u32[]{:S(2)}) collective-permute-start(f32[6,1,16,1024]{3,2,1,0:T(8,128)S(1)} %get-tuple-element.33), channel_id=1, source_target_pairs={{0,16},{16,32},{32,48},{48,64},{64,80},{80,96},{96,112},{1,17},{17... | collective-permute-start | bytes 1179656 | tf_op jit(solution)/shard_map/ppermute | solution.py:20
  103.1 11.6 %collective-permute-done.6 = f32[6,1,16,1024]{3,2,1,0:T(8,128)S(1)} collective-permute-done((f32[6,1,16,1024]{3,2,1,0:T(8,128)S(1)}, f32[6,1,16,1024]{3,2,1,0:T(8,128)S(1)}, u32[]{:S(2)}, u32[]{:S(2)}) %collective-permute-start.6) | collective-permute-done | bytes 393248 | tf_op jit(solution)/shard_map/ppermute | solution.py:20
  117.7 2.4 %collective-permute-start.9 = (f32[6,18,1,1024]{3,2,1,0:T(1,128)S(1)}, f32[6,18,1,1024]{3,2,1,0:T(1,128)S(1)}, u32[]{:S(2)}, u32[]{:S(2)}) collective-permute-start(f32[6,18,1,1024]{3,2,1,0:T(1,128)S(1)} %get-tuple-element.30), channel_id=1, source_target_pairs={{4,0},{8,4},{12,8},{5,1},{9,5},{13,9},{6,2},{10,6},{14,10},{7,3},{... | collective-permute-start | bytes 1327112 | tf_op jit(solution)/shard_map/ppermute | solution.py:21
  120.2 2.7 %collective-permute-done.8 = f32[6,18,1,1024]{3,2,1,0:T(1,128)S(1)} collective-permute-done((f32[6,18,1,1024]{3,2,1,0:T(1,128)S(1)}, f32[6,18,1,1024]{3,2,1,0:T(1,128)S(1)}, u32[]{:S(2)}, u32[]{:S(2)}) %collective-permute-start.8) | collective-permute-done | bytes 442400 | tf_op jit(solution)/shard_map/ppermute | solution.py:20
  122.9 5.9 %collective-permute-done.9 = f32[6,18,1,1024]{3,2,1,0:T(1,128)S(1)} collective-permute-done((f32[6,18,1,1024]{3,2,1,0:T(1,128)S(1)}, f32[6,18,1,1024]{3,2,1,0:T(1,128)S(1)}, u32[]{:S(2)}, u32[]{:S(2)}) %collective-permute-start.9) | collective-permute-done | bytes 442400 | tf_op jit(solution)/shard_map/ppermute | solution.py:21
  128.8 2.6 %pad_maximum_fusion.1 = f32[6,18,18,1024]{3,2,1,0:T(8,128)S(1)} fusion(f32[6,18,1,1024]{3,2,1,0:T(1,128)S(1)} %collective-permute-done.9, f32[6,1,16,1024]{3,2,1,0:T(8,128)S(1)} %collective-permute-done.7, f32[6,16,16,1024]{3,2,1,0:T(8,128)S(1)} %bitcast_dynamic-update-slice_fusion, f32[6,1,16,1024]{3,2,1,0:T(8,128)S(1)} %collective-permute-done.6, ...), kind=kLoop, calls=%fused_computation.3 | loop fusion | flops 7962624 | bytes 15925248 | tf_op jit(solution)/shard_map/concatenate | solution.py:22
  131.4 3.9 %copy-done.1 = f32[6,18,18,1024]{3,2,1,0:T(8,128)} copy-done((f32[6,18,18,1024]{3,2,1,0:T(8,128)}, f32[6,18,18,1024]{3,2,1,0:T(8,128)S(1)}, u32[]{:S(2)}) %copy-start.1) | copy-done | bytes 7962648
  139.4 3.2 %collective-permute-start.10 = (f32[6,18,18,1]{2,3,1,0:T(1,128)S(1)}, f32[6,18,18,1]{2,3,1,0:T(1,128)S(1)}, u32[]{:S(2)}, u32[]{:S(2)}) collective-permute-start(f32[6,18,18,1]{2,3,1,0:T(1,128)S(1)} %copy.55), channel_id=1, source_target_pairs={{0,1},{1,2},{2,3},{4,5},{5,6},{6,7},{8,9},{9,10},{10,11},{12,13},{... | collective-permute-start | bytes 23336 | tf_op jit(solution)/shard_map/ppermute | solution.py:20
  151.3 15.6 %concatenate.29 = f32[6,18,18,1026]{3,2,1,0:T(8,128)} concatenate(f32[6,18,18,1]{3,2,1,0:T(8,128)} %copy.49, f32[6,18,18,1024]{3,2,1,0:T(8,128)} %copy-done.1, f32[6,18,18,1]{3,2,1,0:T(8,128)} %copy.50), dimensions={3} | concatenate | bytes 15956352 | tf_op jit(solution)/shard_map/concatenate | solution.py:22
  166.9 7.2 %slice_bitcast_fusion = (f32[18,18,1026]{2,1,0:T(8,128)}, f32[18,18,1026]{2,1,0:T(8,128)S(1)}, f32[18,18,1026]{2,1,0:T(8,128)}, f32[18,18,1026]{2,1,0:T(8,128)S(...) fusion(f32[6,18,18,1026]{3,2,1,0:T(8,128)} %concatenate.29), kind=kLoop, calls=%fused_computation.18 | loop fusion | bytes 15956352 | tf_op jit(solution)/shard_map/squeeze | solution.py:40
  174.2 4.2 %multiply_multiply_fusion = (f32[17,17,1025]{2,1,0:T(8,128)S(1)}, f32[17,17,1025]{2,1,0:T(8,128)S(1)}, f32[17,17,1025]{2,1,0:T(8,128)S(1)}) fusion(f32[18,18,1026]{2,1,0:T(8,128)S(1)} %get-tuple-element.16, f32[18,18,1026]{2,1,0:T(8,128)S(1)} %get-tuple-element.14, f32[18,18,1026]{2,1,0:T(8,128)} %get-tuple-element.13, f32[1025]{0:T(1024)S(1)} %fusion.49, ...), kind=kLoop, calls=%fused_computation.4 | loop fusion | flops 5628275 | bytes 17778756 | tf_op jit(solution)/shard_map/mul | solution.py:47
  181.0 5.1 %fusion.42 = (f32[16,16,1024]{2,1,0:T(8,128)S(1)}, f32[16,16,1024]{2,1,0:T(8,128)S(1)}, f32[16,16,1024]{2,1,0:T(8,128)}, f32[16,16,1024]{2,1,0:T(8,128)}, f32[1,16,16,1024]{3,2,1,0:T(8,128)}) fusion(f32[3,16,16,1024]{3,2,1,0:T(8,128)S(1)} %copy-done.9, f32[1024]{0:T(1024)S(1)} %fusion.53, f32[16,16]{1,0:T(8,128)S(1)} %broadcast_multiply_fusion.1, ...), kind=kLoop, calls=%fused_computation.97 | loop fusion | flops 6553600 | bytes 22025216 | tf_op jit(solution)/shard_map/add | solution.py:83
  186.3 6.2 %gather_fusion = f32[1024]{0:T(1024)S(1)} fusion(f32[262144]{0:T(1024)S(1)} %bitcast.76, s32[1024]{0:T(1024)S(1)} %broadcast_clamp_fusion), kind=kCustom, calls=%fused_computation | custom fusion | bytes 12288 | tf_op jit(solution)/shard_map/gather | solution.py:88
  192.4 6.5 %scatter_custom_fusion = f32[32768]{0:T(1024)} fusion(s32[1024]{0:T(1024)S(1)} %bitcast.82, f32[1024]{0:T(1024)S(1)} %gather_fusion, f32[]{:T(128)} %constant.9.clone.1), kind=kCustom, calls=%fused_computation.113 | custom fusion | flops 1024 | bytes 131076 | tf_op jit(solution)/shard_map/scatter-add | solution.py:91
  199.0 7.4 %all-to-all-start = ((f32[128,1,256]{2,1,0:T(1,128)}), f32[128,1,256]{2,1,0:T(1,128)S(1)}, u32[]{:S(2)}, u32[]{:S(2)}) async-start(f32[128,1,256]{2,1,0:T(1,128)} %bitcast.32), calls=%async_computation | async-start | bytes 262144 | tf_op jit(solution)/shard_map/all_to_all | solution.py:93
  206.4 3.7 %pad_maximum_fusion.3 = f32[3,16,16,1024]{3,2,1,0:T(8,128)} fusion(f32[1,16,16,1024]{3,2,1,0:T(8,128)} %slice_bitcast_fusion.14, f32[1,16,16,1024]{3,2,1,0:T(8,128)} %slice_bitcast_fusion.13, f32[1,16,16,1024]{3,2,1,0:T(8,128)S(1)} %copy-done.7), kind=kLoop, calls=%fused_computation.17 | loop fusion | flops 1572864 | bytes 6291456 | tf_op jit(solution)/shard_map/stack | solution.py:74
  212.0 4.6 %all-to-all-done = f32[128,1,256]{2,1,0:T(1,128)S(1)} async-done(((f32[128,1,256]{2,1,0:T(1,128)}), f32[128,1,256]{2,1,0:T(1,128)S(1)}, u32[]{:S(2)}, u32[]{:S(2)}) %all-to-all-start) | async-done | bytes 131104 | tf_op jit(solution)/shard_map/all_to_all | solution.py:93
  (68 shorter events, 37.6 us)
Async XLA Ops:
  0.6 2.8 %copy-start.8 = (f32[3,16,16,1024]{3,2,1,0:T(8,128)S(1)}, f32[3,16,16,1024]{3,2,1,0:T(8,128)}, u32[]{:S(2)}) copy-start(f32[3,16,16,1024]{3,2,1,0:T(8,128)} %param.9) | copy-start | bytes 9437188
  3.9 2.6 %copy-start.2 = (f32[6,16,16,1024]{3,2,1,0:T(8,128)}, f32[6,16,16,1024]{3,2,1,0:T(8,128)S(1)}, u32[]{:S(2)}) copy-start(f32[6,16,16,1024]{3,2,1,0:T(8,128)S(1)} %constant_dynamic-update-slice_fusion) | copy-start | bytes 18874372
  6.6 20.6 %collective-permute-start = (f32[6,1,16,1024]{3,2,1,0:T(8,128)S(1)}, f32[6,1,16,1024]{3,2,1,0:T(8,128)S(1)}, u32[]{:S(2)}, u32[]{:S(2)}) collective-permute-start(f32[6,1,16,1024]{3,2,1,0:T(8,128)S(1)} %get-tuple-element.35), channel_id=1, source_target_pairs={{0,16},{16,32},{32,48},{48,64},{64,80},{80,96},{96,112},{1,17},{17... | collective-permute-start | bytes 1179656 | tf_op jit(solution)/shard_map/ppermute | solution.py:20
  11.0 16.2 %collective-permute-start.1 = (f32[6,1,16,1024]{3,2,1,0:T(8,128)S(1)}, f32[6,1,16,1024]{3,2,1,0:T(8,128)S(1)}, u32[]{:S(2)}, u32[]{:S(2)}) collective-permute-start(f32[6,1,16,1024]{3,2,1,0:T(8,128)S(1)} %get-tuple-element.36), channel_id=1, source_target_pairs={{16,0},{32,16},{48,32},{64,48},{80,64},{96,80},{112,96},{17,1},{33... | collective-permute-start | bytes 1179656 | tf_op jit(solution)/shard_map/ppermute | solution.py:21
  27.1 21.7 %copy-start.3 = (f32[6,16,16,1024]{3,2,1,0:T(8,128)S(1)}, f32[6,16,16,1024]{3,2,1,0:T(8,128)}, u32[]{:S(2)}) copy-start(f32[6,16,16,1024]{3,2,1,0:T(8,128)} %copy-done.2) | copy-start | bytes 18874372
  31.1 11.9 %collective-permute-start.2 = (f32[6,18,1,1024]{3,2,1,0:T(1,128)S(1)}, f32[6,18,1,1024]{3,2,1,0:T(1,128)S(1)}, u32[]{:S(2)}, u32[]{:S(2)}) collective-permute-start(f32[6,18,1,1024]{3,2,1,0:T(1,128)S(1)} %get-tuple-element.31), channel_id=1, source_target_pairs={{0,4},{4,8},{8,12},{1,5},{5,9},{9,13},{2,6},{6,10},{10,14},{3,7},{... | collective-permute-start | bytes 1327112 | tf_op jit(solution)/shard_map/ppermute | solution.py:20
  37.8 11.1 %collective-permute-start.3 = (f32[6,18,1,1024]{3,2,1,0:T(1,128)S(1)}, f32[6,18,1,1024]{3,2,1,0:T(1,128)S(1)}, u32[]{:S(2)}, u32[]{:S(2)}) collective-permute-start(f32[6,18,1,1024]{3,2,1,0:T(1,128)S(1)} %get-tuple-element.32), channel_id=1, source_target_pairs={{4,0},{8,4},{12,8},{5,1},{9,5},{13,9},{6,2},{10,6},{14,10},{7,3},{... | collective-permute-start | bytes 1327112 | tf_op jit(solution)/shard_map/ppermute | solution.py:21
  51.4 3.9 %copy-start = (f32[6,18,18,1024]{3,2,1,0:T(8,128)}, f32[6,18,18,1024]{3,2,1,0:T(8,128)S(1)}, u32[]{:S(2)}) copy-start(f32[6,18,18,1024]{3,2,1,0:T(8,128)S(1)} %pad_maximum_fusion) | copy-start | bytes 23887876
  56.6 5.4 %collective-permute-start.4 = (f32[6,18,18,1]{2,3,1,0:T(1,128)S(1)}, f32[6,18,18,1]{2,3,1,0:T(1,128)S(1)}, u32[]{:S(2)}, u32[]{:S(2)}) collective-permute-start(f32[6,18,18,1]{2,3,1,0:T(1,128)S(1)} %copy.53), channel_id=1, source_target_pairs={{0,1},{1,2},{2,3},{4,5},{5,6},{6,7},{8,9},{9,10},{10,11},{12,13},{... | collective-permute-start | bytes 23336 | tf_op jit(solution)/shard_map/ppermute | solution.py:20
  60.6 4.9 %collective-permute-start.5 = (f32[6,18,18,1]{2,3,1,0:T(1,128)S(1)}, f32[6,18,18,1]{2,3,1,0:T(1,128)S(1)}, u32[]{:S(2)}, u32[]{:S(2)}) collective-permute-start(f32[6,18,18,1]{2,3,1,0:T(1,128)S(1)} %copy.54), channel_id=1, source_target_pairs={{1,0},{2,1},{3,2},{5,4},{6,5},{7,6},{9,8},{10,9},{11,10},{13,12},{... | collective-permute-start | bytes 23336 | tf_op jit(solution)/shard_map/ppermute | solution.py:21
  88.3 4.3 %copy-start.4 = (f32[16,16,1024]{2,1,0:T(8,128)S(1)}, f32[16,16,1024]{2,1,0:T(8,128)}, u32[]{:S(2)}) copy-start(f32[16,16,1024]{2,1,0:T(8,128)} %param.10) | copy-start | bytes 3145732
  98.1 16.6 %collective-permute-start.6 = (f32[6,1,16,1024]{3,2,1,0:T(8,128)S(1)}, f32[6,1,16,1024]{3,2,1,0:T(8,128)S(1)}, u32[]{:S(2)}, u32[]{:S(2)}) collective-permute-start(f32[6,1,16,1024]{3,2,1,0:T(8,128)S(1)} %get-tuple-element.33), channel_id=1, source_target_pairs={{0,16},{16,32},{32,48},{48,64},{64,80},{80,96},{96,112},{1,17},{17... | collective-permute-start | bytes 1179656 | tf_op jit(solution)/shard_map/ppermute | solution.py:20
  101.7 18.4 %copy-start.12 = (s32[1,1,1,1024]{3,2,1,0:T(1,128)S(1)}, s32[1,1,1,1024]{3,2,1,0:T(1,128)}, u32[]{:S(2)}) copy-start(s32[1,1,1,1024]{3,2,1,0:T(1,128)} %param.11) | copy-start | bytes 12292
  101.7 18.4 %copy-start.10 = (s32[1,1,1,1024]{3,2,1,0:T(1,128)S(1)}, s32[1,1,1,1024]{3,2,1,0:T(1,128)}, u32[]{:S(2)}) copy-start(s32[1,1,1,1024]{3,2,1,0:T(1,128)} %param.13) | copy-start | bytes 12292
  101.7 18.4 %copy-start.11 = (s32[1,1,1,1024,1]{3,4,2,1,0:T(1,128)S(1)}, s32[1,1,1,1024,1]{3,4,2,1,0:T(1,128)}, u32[]{:S(2)}) copy-start(s32[1,1,1,1024,1]{3,4,2,1,0:T(1,128)} %param.12) | copy-start | bytes 12292
  101.7 13.1 %collective-permute-start.7 = (f32[6,1,16,1024]{3,2,1,0:T(8,128)S(1)}, f32[6,1,16,1024]{3,2,1,0:T(8,128)S(1)}, u32[]{:S(2)}, u32[]{:S(2)}) collective-permute-start(f32[6,1,16,1024]{3,2,1,0:T(8,128)S(1)} %get-tuple-element.34), channel_id=1, source_target_pairs={{16,0},{32,16},{48,32},{64,48},{80,64},{96,80},{112,96},{17,1},{33... | collective-permute-start | bytes 1179656 | tf_op jit(solution)/shard_map/ppermute | solution.py:21
  115.7 7.2 %collective-permute-start.8 = (f32[6,18,1,1024]{3,2,1,0:T(1,128)S(1)}, f32[6,18,1,1024]{3,2,1,0:T(1,128)S(1)}, u32[]{:S(2)}, u32[]{:S(2)}) collective-permute-start(f32[6,18,1,1024]{3,2,1,0:T(1,128)S(1)} %get-tuple-element.29), channel_id=1, source_target_pairs={{0,4},{4,8},{8,12},{1,5},{5,9},{9,13},{2,6},{6,10},{10,14},{3,7},{... | collective-permute-start | bytes 1327112 | tf_op jit(solution)/shard_map/ppermute | solution.py:20
  117.7 11.1 %collective-permute-start.9 = (f32[6,18,1,1024]{3,2,1,0:T(1,128)S(1)}, f32[6,18,1,1024]{3,2,1,0:T(1,128)S(1)}, u32[]{:S(2)}, u32[]{:S(2)}) collective-permute-start(f32[6,18,1,1024]{3,2,1,0:T(1,128)S(1)} %get-tuple-element.30), channel_id=1, source_target_pairs={{4,0},{8,4},{12,8},{5,1},{9,5},{13,9},{6,2},{10,6},{14,10},{7,3},{... | collective-permute-start | bytes 1327112 | tf_op jit(solution)/shard_map/ppermute | solution.py:21
  131.4 3.9 %copy-start.1 = (f32[6,18,18,1024]{3,2,1,0:T(8,128)}, f32[6,18,18,1024]{3,2,1,0:T(8,128)S(1)}, u32[]{:S(2)}) copy-start(f32[6,18,18,1024]{3,2,1,0:T(8,128)S(1)} %pad_maximum_fusion.1) | copy-start | bytes 23887876
  139.4 6.8 %collective-permute-start.10 = (f32[6,18,18,1]{2,3,1,0:T(1,128)S(1)}, f32[6,18,18,1]{2,3,1,0:T(1,128)S(1)}, u32[]{:S(2)}, u32[]{:S(2)}) collective-permute-start(f32[6,18,18,1]{2,3,1,0:T(1,128)S(1)} %copy.55), channel_id=1, source_target_pairs={{0,1},{1,2},{2,3},{4,5},{5,6},{6,7},{8,9},{9,10},{10,11},{12,13},{... | collective-permute-start | bytes 23336 | tf_op jit(solution)/shard_map/ppermute | solution.py:20
  144.6 4.9 %collective-permute-start.11 = (f32[6,18,18,1]{2,3,1,0:T(1,128)S(1)}, f32[6,18,18,1]{2,3,1,0:T(1,128)S(1)}, u32[]{:S(2)}, u32[]{:S(2)}) collective-permute-start(f32[6,18,18,1]{2,3,1,0:T(1,128)S(1)} %copy.56), channel_id=1, source_target_pairs={{1,0},{2,1},{3,2},{5,4},{6,5},{7,6},{9,8},{10,9},{11,10},{13,12},{... | collective-permute-start | bytes 23336 | tf_op jit(solution)/shard_map/ppermute | solution.py:21
  178.3 2.7 %copy-start.9 = (f32[3,16,16,1024]{3,2,1,0:T(8,128)S(1)}, f32[3,16,16,1024]{3,2,1,0:T(8,128)}, u32[]{:S(2)}) copy-start(f32[3,16,16,1024]{3,2,1,0:T(8,128)} %param.7) | copy-start | bytes 9437188
  186.3 20.1 %copy-start.7 = (f32[1,16,16,1024]{3,2,1,0:T(8,128)S(1)}, f32[1,16,16,1024]{3,2,1,0:T(8,128)}, u32[]{:S(2)}) copy-start(f32[1,16,16,1024]{3,2,1,0:T(8,128)} %get-tuple-element.43) | copy-start | bytes 3145732
  199.0 17.6 %all-to-all-start = ((f32[128,1,256]{2,1,0:T(1,128)}), f32[128,1,256]{2,1,0:T(1,128)S(1)}, u32[]{:S(2)}, u32[]{:S(2)}) async-start(f32[128,1,256]{2,1,0:T(1,128)} %bitcast.32), calls=%async_computation | async-start | bytes 262144 | tf_op jit(solution)/shard_map/all_to_all | solution.py:93
  206.4 3.7 %copy-start.5 = (f32[16,16,1024]{2,1,0:T(8,128)S(1)}, f32[16,16,1024]{2,1,0:T(8,128)}, u32[]{:S(2)}) copy-start(f32[16,16,1024]{2,1,0:T(8,128)} %get-tuple-element.11) | copy-start | bytes 3145732
  206.4 3.7 %copy-start.6 = (f32[16,16,1024]{2,1,0:T(8,128)S(1)}, f32[16,16,1024]{2,1,0:T(8,128)}, u32[]{:S(2)}) copy-start(f32[16,16,1024]{2,1,0:T(8,128)} %get-tuple-element.12) | copy-start | bytes 3145732

commit v2 on v1

v2 whole, which is shorter than its diff:
```python
import functools

import jax
import jax.numpy as jnp
from jax import lax
from jax.experimental import pallas as pl
from jax.experimental.pallas import tpu as pltpu
from jax.sharding import PartitionSpec as P

STEPS = 2
P_DEV = 256
CHUNK = 4

courant = 0.5


def toward_lower(x, axis):
    peers = lax.axis_size(axis)
    return lax.ppermute(x, axis, [(j, j - 1) for j in range(1, peers)])


def toward_upper(x, axis):
    peers = lax.axis_size(axis)
    return lax.ppermute(x, axis, [(j, j + 1) for j in range(peers - 1)])


def fwd_y(a, row):
    rolled = pltpu.roll(a, a.shape[1] - 1, 1)
    at = lax.broadcasted_iota(jnp.int32, a.shape, 1)
    return jnp.where(at == a.shape[1] - 1, row, rolled)


def fwd_z(a, col):
    rolled = pltpu.roll(a, a.shape[2] - 1, 2)
    at = lax.broadcasted_iota(jnp.int32, a.shape, 2)
    return jnp.where(at == a.shape[2] - 1, col, rolled)


def bwd_y(a, row):
    rolled = pltpu.roll(a, 1, 1)
    at = lax.broadcasted_iota(jnp.int32, a.shape, 1)
    return jnp.where(at == 0, row, rolled)


def bwd_z(a, col):
    rolled = pltpu.roll(a, 1, 2)
    at = lax.broadcasted_iota(jnp.int32, a.shape, 2)
    return jnp.where(at == 0, col, rolled)


def fwd_x(a, nxt):
    if a.shape[0] == 1:
        return nxt
    return jnp.concatenate([a[1:], nxt], axis=0)


def bwd_x(a, prv):
    if a.shape[0] == 1:
        return prv
    return jnp.concatenate([prv, a[:-1]], axis=0)


def h_kernel(e_ref, en_ref, h_ref, hx_ref, hy_ref, hz_ref, out_ref):
    last = pl.program_id(0) == pl.num_programs(0) - 1
    ex, ey, ez = e_ref[0], e_ref[1], e_ref[2]
    nxt_y = jnp.where(last, hx_ref[0], en_ref[1])
    nxt_z = jnp.where(last, hx_ref[1], en_ref[2])
    ez_yp = fwd_y(ez, hy_ref[1])
    ex_yp = fwd_y(ex, hy_ref[0])
    ey_zp = fwd_z(ey, hz_ref[1])
    ex_zp = fwd_z(ex, hz_ref[0])
    ez_xp = fwd_x(ez, nxt_z)
    ey_xp = fwd_x(ey, nxt_y)
    out_ref[0] = h_ref[0] - courant * ((ez_yp - ez) - (ey_zp - ey))
    out_ref[1] = h_ref[1] - courant * ((ex_zp - ex) - (ez_xp - ez))
    out_ref[2] = h_ref[2] - courant * ((ey_xp - ey) - (ex_yp - ex))


def e_update(e_ref, h_ref, hp_ref, inv_ref, hx_ref, hy_ref, hz_ref):
    first = pl.program_id(0) == 0
    hx, hy, hz = h_ref[0], h_ref[1], h_ref[2]
    prv_y = jnp.where(first, hx_ref[0], hp_ref[1])
    prv_z = jnp.where(first, hx_ref[1], hp_ref[2])
    hz_ym = bwd_y(hz, hy_ref[1])
    hx_ym = bwd_y(hx, hy_ref[0])
    hy_zm = bwd_z(hy, hz_ref[1])
    hx_zm = bwd_z(hx, hz_ref[0])
    hz_xm = bwd_x(hz, prv_z)
    hy_xm = bwd_x(hy, prv_y)
    scale = courant * inv_ref[...]
    new_x = e_ref[0] + scale * ((hz - hz_ym) - (hy - hy_zm))
    new_y = e_ref[1] + scale * ((hx - hx_zm) - (hz - hz_xm))
    new_z = e_ref[2] + scale * ((hy - hy_xm) - (hx - hx_ym))
    return new_x, new_y, new_z


def e_kernel(e_ref, h_ref, hp_ref, inv_ref, hx_ref, hy_ref, hz_ref, out_ref):
    new_x, new_y, new_z = e_update(e_ref, h_ref, hp_ref, inv_ref, hx_ref, hy_ref, hz_ref)
    out_ref[0] = new_x
    out_ref[1] = new_y
    out_ref[2] = new_z


def e_last_kernel(e_ref, h_ref, hp_ref, inv_ref, hx_ref, hy_ref, hz_ref, ef_ref, out_ref, inter_ref):
    new_x, new_y, new_z = e_update(e_ref, h_ref, hp_ref, inv_ref, hx_ref, hy_ref, hz_ref)
    out_ref[0] = new_x
    out_ref[1] = new_y
    out_ref[2] = new_z
    inter_ref[...] = ef_ref[0] * new_x + ef_ref[1] * new_y + ef_ref[2] * new_z


def field_spec(nx, ny, nz, chunk):
    return pl.BlockSpec((3, chunk, ny, nz), lambda i: (0, i, 0, 0))


def h_step(e, h):
    _, nx, ny, nz = e.shape
    chunk = CHUNK
    faces_x = toward_lower(e[1:3, 0], "gx")
    faces_y = toward_lower(e[0::2, :, 0:1, :], "gy")
    faces_z = toward_lower(e[0:2, :, :, 0:1], "gz")
    return pl.pallas_call(
        h_kernel,
        grid=(nx // chunk,),
        in_specs=[
            field_spec(nx, ny, nz, chunk),
            pl.BlockSpec((3, 1, ny, nz), lambda i: (0, jnp.minimum((i + 1) * chunk, nx - 1), 0, 0)),
            field_spec(nx, ny, nz, chunk),
            pl.BlockSpec((2, 1, ny, nz), lambda i: (0, 0, 0, 0)),
            pl.BlockSpec((2, chunk, 1, nz), lambda i: (0, i, 0, 0)),
            pl.BlockSpec((2, chunk, ny, 1), lambda i: (0, i, 0, 0)),
        ],
        out_specs=field_spec(nx, ny, nz, chunk),
        out_shape=jax.ShapeDtypeStruct(h.shape, h.dtype),
    )(e, e, h, faces_x[:, None], faces_y, faces_z)


def e_step(e, h, inv, ef=None):
    _, nx, ny, nz = e.shape
    chunk = CHUNK
    faces_x = toward_upper(h[1:3, nx - 1], "gx")
    faces_y = toward_upper(h[0::2, :, ny - 1:ny, :], "gy")
    faces_z = toward_upper(h[0:2, :, :, nz - 1:nz], "gz")
    in_specs = [
        field_spec(nx, ny, nz, chunk),
        field_spec(nx, ny, nz, chunk),
        pl.BlockSpec((3, 1, ny, nz), lambda i: (0, jnp.maximum(i * chunk - 1, 0), 0, 0)),
        pl.BlockSpec((chunk, ny, nz), lambda i: (i, 0, 0)),
        pl.BlockSpec((2, 1, ny, nz), lambda i: (0, 0, 0, 0)),
        pl.BlockSpec((2, chunk, 1, nz), lambda i: (0, i, 0, 0)),
        pl.BlockSpec((2, chunk, ny, 1), lambda i: (0, i, 0, 0)),
    ]
    args = [e, h, h, inv, faces_x[:, None], faces_y, faces_z]
    if ef is None:
        return pl.pallas_call(
            e_kernel,
            grid=(nx // chunk,),
            in_specs=in_specs,
            out_specs=field_spec(nx, ny, nz, chunk),
            out_shape=jax.ShapeDtypeStruct(e.shape, e.dtype),
        )(*args)
    return pl.pallas_call(
        e_last_kernel,
        grid=(nx // chunk,),
        in_specs=in_specs + [field_spec(nx, ny, nz, chunk)],
        out_specs=[field_spec(nx, ny, nz, chunk), pl.BlockSpec((chunk, ny, nz), lambda i: (i, 0, 0))],
        out_shape=[jax.ShapeDtypeStruct(e.shape, e.dtype), jax.ShapeDtypeStruct(e.shape[1:], e.dtype)],
    )(*args, ef)


def body(e_forward, e_adjoint, h_adjoint, inv_perm, voxel_cell, voxel_owner, voxel_slot):
    e, h = e_adjoint, h_adjoint
    intersection = None
    for repeat in range(STEPS):
        h = h_step(e, h)
        if repeat == STEPS - 1:
            e, intersection = e_step(e, h, inv_perm, e_forward)
        else:
            e = e_step(e, h, inv_perm)
    count = voxel_cell.shape[-1]
    voxel_rows = voxel_cell.reshape(count)
    owners = voxel_owner.reshape(count)
    slot_ids = voxel_slot.reshape(count)
    terms = intersection.reshape(-1)[voxel_rows]
    devices = lax.axis_size("gx") * lax.axis_size("gy") * lax.axis_size("gz")
    params = owners * P_DEV + slot_ids
    dense_terms = jax.ops.segment_sum(terms, params, num_segments=devices * P_DEV)
    per_owner = dense_terms.reshape(devices, P_DEV)
    received = lax.all_to_all(per_owner, ("gx", "gy", "gz"), 0, 0, tiled=True)
    gradient = received.sum(axis=0)
    return (e, h, gradient)


def solution(mesh):
    return jax.shard_map(
        body,
        mesh=mesh,
        in_specs=(
            P(None, "gx", "gy", "gz"),
            P(None, "gx", "gy", "gz"),
            P(None, "gx", "gy", "gz"),
            P("gx", "gy", "gz"),
            P("gx", "gy", "gz", None),
            P("gx", "gy", "gz", None, None),
            P("gx", "gy", "gz", None),
        ),
        out_specs=(P(None, "gx", "gy", "gz"), P(None, "gx", "gy", "gz"), P(("gx", "gy", "gz"))),
        check_vma=False,
    )
```

time: 219 us -> 132 us (0.60)
  local copies, waits for them, and re-layouts: 82 us -> 23.4 us
  other arithmetic: 41.1 us -> 6.7 us
  waiting for transfers between devices: 52.9 us -> 18.9 us
  Pallas kernels: 0 us -> 24.1 us
  blocking collectives: 0 us -> 19.5 us
  starting transfers between devices: 40.3 us -> 37.5 us
    concatenate x3 -> x0, local copies, waits for them, and re-layouts: 30.8 us -> none  [the longest x2 30.4 us: extended(): x = jnp.concatenate([before, x, after], axis=dim)]
    ppermute x12, waiting for transfers between devices: 48.3 us -> 18.9 us  [the longest x6 15.2 us: toward_lower(): return lax.ppermute(x, axis, [(j, j - 1) for j in range(1, peers)])]
    pallas_call x0 -> x4, Pallas kernels: none -> 24.1 us  [the longest x2 11.1 us: h_step(): pl.pallas_call(h_kernel, grid=(nx // chunk,), in_specs=[field_spec(nx, ny...]
    all_to_all x0 -> x1, blocking collectives: none -> 19.5 us  [body(): received = lax.all_to_all(per_owner, ('gx', 'gy', 'gz'), 0, 0, tiled=True)]
    unnamed x34 -> x31, local copies, waits for them, and re-layouts: 19.8 us -> 4.15 us
    squeeze x2 -> x4, local copies, waits for them, and re-layouts: 14.5 us -> 3.68 us  [the longest x2 1.84 us: e_step(): faces_x = toward_upper(h[1:3, nx - 1], 'gx')]
    mul x4 -> x0, other arithmetic: 8.57 us -> none  [the longest x2 8.43 us: leapfrog(): (magn_x[core] - courant * (elec_z[up_y] - elec_z[core] - (elec_y[up_z] -...]
    all_to_all x1 -> x0, starting transfers between devices: 7.39 us -> none  [body(): received = lax.all_to_all(per_owner, ('gx', 'gy', 'gz'), 0, 0, tiled=True)]
  transfers between devices with their start and end apart: 13 -> 12, of which waited for: 9 -> 6; matrix products, arithmetic and copies ran while one was open for 5% -> 2% of each run, Pallas kernels for 0% -> 0%
where the time goes in v2:
time: 132 us; the launch traced here: 131 us
  starting transfers between devices  37.5 us (28%)
  Pallas kernels  24.1 us (18%)
  local copies, waits for them, and re-layouts  23.4 us (18%)
  blocking collectives  19.5 us (15%)
  waiting for transfers between devices  18.9 us (14%)
  other arithmetic  6.7 us (5%)
    ppermute x6, starting transfers between devices, toward_upper(): return lax.ppermute(x, axis, [(j, j + 1) for j in range(peers - 1)])  27.1 us
    all_to_all x1, blocking collectives, body(): received = lax.all_to_all(per_owner, ('gx', 'gy', 'gz'), 0, 0, tiled=True)  19.5 us
    ppermute x6, waiting for transfers between devices, toward_lower(): return lax.ppermute(x, axis, [(j, j - 1) for j in range(1, peers)])  15.2 us
    pallas_call x2, Pallas kernels, h_step(): pl.pallas_call(h_kernel, grid=(nx // chunk,), in_specs=[field_spec(nx, ny...  11.1 us
    ppermute x6, starting transfers between devices, toward_lower(): return lax.ppermute(x, axis, [(j, j - 1) for j in range(1, peers)])  10.4 us
    pallas_call x1, Pallas kernels, e_step(): pl.pallas_call(e_last_kernel, grid=(nx // chunk,), in_specs=in_specs + [f...  7.14 us
    gather x1, local copies, waits for them, and re-layouts, body(): terms = intersection.reshape(-1)[voxel_rows]  6.15 us
    scatter-add x1, other arithmetic, body(): jax.ops.segment_sum(terms, params, num_segments=devices * P_DEV)  5.96 us
  transfers between devices with their start and end apart: 12, of which 6 were waited for; matrix products, arithmetic and copies ran while one was open for 2% of the time, Pallas kernels for 0%

profile of v2, /device:TPU:1, one launch (start us, length us, event | category | flops | bytes accessed | tf_op | source)
XLA Modules:
  0.0 131.0 jit_solution(6892798939848637824)
XLA Ops:
  1.6 1.3 collective-permute-start
  2.9 1.3 slice.37
  4.2 3.3 %collective-permute-start.1 = (f32[2,16,1,1024]{3,2,1,0:T(1,128)S(1)}, f32[2,16,1,1024]{3,2,1,0:T(1,128)S(1)}, u32[]{:S(2)}, u32[]{:S(2)}) collective-permute-start(f32[2,16,1,1024]{3,2,1,0:T(1,128)S(1)} %slice.37), channel_id=1, source_target_pairs={{4,0},{8,4},{12,8},{5,1},{9,5},{13,9},{6,2},{10,6},{14,10},{7,3},{... | collective-permute-start | bytes 393224 | tf_op jit(solution)/shard_map/ppermute | solution.py:19
  7.5 1.0 slice.38
  8.4 1.3 collective-permute-start.2
  9.7 8.6 %collective-permute-done.2.hz_ref = f32[2,16,16,1]{3,2,1,0:T(8,128)S(1)} collective-permute-done((f32[2,16,16,1]{3,2,1,0:T(8,128)S(1)}, f32[2,16,16,1]{3,2,1,0:T(8,128)S(1)}, u32[]{:S(2)}, u32[]{:S(2)}) %collective-permute-start.2) | collective-permute-done | bytes 2080 | tf_op jit(solution)/shard_map/ppermute | solution.py:19
  19.1 5.6 %shard_map.94.h_ref.hp_ref = f32[3,16,16,1024]{3,2,1,0:T(8,128)} custom-call(f32[3,16,16,1024]{3,2,1,0:T(8,128)} %e_ref.3, f32[3,16,16,1024]{3,2,1,0:T(8,128)} %e_ref.3, f32[3,16,16,1024]{3,2,1,0:T(8,128)} %h_ref.1, f32[2,1,16,1024]{3,2,1,0:T(8,128)} %bitcast.34, f32[2,16,1,1024]{3,2,1,0:T(1,128)} %copy-done.8, f32[2,16,16,1]{3,2,1,0:T(8,128)} %copy-done.3), custom_call_target="tpu_custom_call" | custom-call | tf_op jit(solution)/shard_map/pallas_call | solution.py:122
  24.7 1.1 slice.51
  26.7 1.4 %slice.40 = f32[2,16,1,1024]{3,2,1,0:T(1,128)S(1)} slice(f32[3,16,16,1024]{3,2,1,0:T(8,128)} %shard_map.94.h_ref.hp_ref), slice={[0:3:2], [0:16:1], [15:16:1], [0:1024:1]} | slice | bytes 262144 | tf_op jit(solution)/shard_map/slice | solution.py:142
  28.1 3.3 %collective-permute-start.5 = (f32[2,16,16,1]{3,2,1,0:T(8,128)S(1)}, f32[2,16,16,1]{3,2,1,0:T(8,128)S(1)}, u32[]{:S(2)}, u32[]{:S(2)}) collective-permute-start(f32[2,16,16,1]{3,2,1,0:T(8,128)S(1)} %slice.51), channel_id=1, source_target_pairs={{0,1},{1,2},{2,3},{4,5},{5,6},{6,7},{8,9},{9,10},{10,11},{12,13},{... | collective-permute-start | bytes 6152 | tf_op jit(solution)/shard_map/ppermute | solution.py:24
  31.4 4.3 %collective-permute-start.3 = (f32[2,16,1024]{2,1,0:T(8,128)S(1)}, f32[2,16,1024]{2,1,0:T(8,128)S(1)}, u32[]{:S(2)}, u32[]{:S(2)}) collective-permute-start(f32[2,16,1024]{2,1,0:T(8,128)S(1)} %slice_bitcast_fusion.2), channel_id=1, source_target_pairs={{0,16},{16,32},{32,48},{48,64},{64,80},{80,96},{96,112},{1,17},{17... | collective-permute-start | bytes 393224 | tf_op jit(solution)/shard_map/ppermute | solution.py:24
  35.7 6.7 %collective-permute-start.4 = (f32[2,16,1,1024]{3,2,1,0:T(1,128)S(1)}, f32[2,16,1,1024]{3,2,1,0:T(1,128)S(1)}, u32[]{:S(2)}, u32[]{:S(2)}) collective-permute-start(f32[2,16,1,1024]{3,2,1,0:T(1,128)S(1)} %slice.40), channel_id=1, source_target_pairs={{0,4},{4,8},{8,12},{1,5},{5,9},{9,13},{2,6},{6,10},{10,14},{3,7},{... | collective-permute-start | bytes 393224 | tf_op jit(solution)/shard_map/ppermute | solution.py:24
  42.4 1.8 %collective-permute-done.4.hy_ref = f32[2,16,1,1024]{3,2,1,0:T(1,128)S(1)} collective-permute-done((f32[2,16,1,1024]{3,2,1,0:T(1,128)S(1)}, f32[2,16,1,1024]{3,2,1,0:T(1,128)S(1)}, u32[]{:S(2)}, u32[]{:S(2)}) %collective-permute-start.4) | collective-permute-done | bytes 131104 | tf_op jit(solution)/shard_map/ppermute | solution.py:24
  44.9 5.8 %shard_map.95.e_ref.en_ref = f32[3,16,16,1024]{3,2,1,0:T(8,128)} custom-call(f32[3,16,16,1024]{3,2,1,0:T(8,128)} %e_ref.3, f32[3,16,16,1024]{3,2,1,0:T(8,128)} %shard_map.94.h_ref.hp_ref, f32[3,16,16,1024]{3,2,1,0:T(8,128)} %shard_map.94.h_ref.hp_ref, f32[16,16,1024]{2,1,0:T(8,128)} %inv_ref.3, f32[2,1,16,1024]{3,2,1,0:T(8,128)} %bitcast.37, ...), custom_call_target="tpu_custom_call" | custom-call | tf_op jit(solution)/shard_map/pallas_call | solution.py:155
  52.7 1.3 slice.43
  54.0 1.3 collective-permute-start.8
  55.3 1.3 collective-permute-start.6
  56.6 1.9 %collective-permute-start.7 = (f32[2,16,1,1024]{3,2,1,0:T(1,128)S(1)}, f32[2,16,1,1024]{3,2,1,0:T(1,128)S(1)}, u32[]{:S(2)}, u32[]{:S(2)}) collective-permute-start(f32[2,16,1,1024]{3,2,1,0:T(1,128)S(1)} %slice.43), channel_id=1, source_target_pairs={{4,0},{8,4},{12,8},{5,1},{9,5},{13,9},{6,2},{10,6},{14,10},{7,3},{... | collective-permute-start | bytes 393224 | tf_op jit(solution)/shard_map/ppermute | solution.py:19
  58.5 2.6 %collective-permute-done.8.hz_ref = f32[2,16,16,1]{3,2,1,0:T(8,128)S(1)} collective-permute-done((f32[2,16,16,1]{3,2,1,0:T(8,128)S(1)}, f32[2,16,16,1]{3,2,1,0:T(8,128)S(1)}, u32[]{:S(2)}, u32[]{:S(2)}) %collective-permute-start.8) | collective-permute-done | bytes 2080 | tf_op jit(solution)/shard_map/ppermute | solution.py:19
  61.2 3.9 %collective-permute-done.7.hy_ref = f32[2,16,1,1024]{3,2,1,0:T(1,128)S(1)} collective-permute-done((f32[2,16,1,1024]{3,2,1,0:T(1,128)S(1)}, f32[2,16,1,1024]{3,2,1,0:T(1,128)S(1)}, u32[]{:S(2)}, u32[]{:S(2)}) %collective-permute-start.7) | collective-permute-done | bytes 131104 | tf_op jit(solution)/shard_map/ppermute | solution.py:19
  65.7 5.5 %shard_map.96.h_ref.hp_ref = f32[3,16,16,1024]{3,2,1,0:T(8,128)} custom-call(f32[3,16,16,1024]{3,2,1,0:T(8,128)} %shard_map.95.e_ref.en_ref, f32[3,16,16,1024]{3,2,1,0:T(8,128)} %shard_map.95.e_ref.en_ref, f32[3,16,16,1024]{3,2,1,0:T(8,128)} %shard_map.94.h_ref.hp_ref, f32[2,1,16,1024]{3,2,1,0:T(8,128)} %bitcast.36, f32[2,16,1,1024]{3,2,1,0:T(1,128)} %copy-done.10, ...), custom_call_target="tpu_custom_call" | custom-call | tf_op jit(solution)/shard_map/pallas_call | solution.py:122
  71.3 1.1 slice.55
  73.3 1.4 %slice.46 = f32[2,16,1,1024]{3,2,1,0:T(1,128)S(1)} slice(f32[3,16,16,1024]{3,2,1,0:T(8,128)} %shard_map.96.h_ref.hp_ref), slice={[0:3:2], [0:16:1], [15:16:1], [0:1024:1]} | slice | bytes 262144 | tf_op jit(solution)/shard_map/slice | solution.py:142
  74.6 4.3 %collective-permute-start.11 = (f32[2,16,16,1]{3,2,1,0:T(8,128)S(1)}, f32[2,16,16,1]{3,2,1,0:T(8,128)S(1)}, u32[]{:S(2)}, u32[]{:S(2)}) collective-permute-start(f32[2,16,16,1]{3,2,1,0:T(8,128)S(1)} %slice.55), channel_id=1, source_target_pairs={{0,1},{1,2},{2,3},{4,5},{5,6},{6,7},{8,9},{9,10},{10,11},{12,13},{... | collective-permute-start | bytes 6152 | tf_op jit(solution)/shard_map/ppermute | solution.py:24
  78.9 4.2 %collective-permute-start.9 = (f32[2,16,1024]{2,1,0:T(8,128)S(1)}, f32[2,16,1024]{2,1,0:T(8,128)S(1)}, u32[]{:S(2)}, u32[]{:S(2)}) collective-permute-start(f32[2,16,1024]{2,1,0:T(8,128)S(1)} %slice_bitcast_fusion), channel_id=1, source_target_pairs={{0,16},{16,32},{32,48},{48,64},{64,80},{80,96},{96,112},{1,17},{17... | collective-permute-start | bytes 393224 | tf_op jit(solution)/shard_map/ppermute | solution.py:24
  83.1 4.4 %collective-permute-start.10 = (f32[2,16,1,1024]{3,2,1,0:T(1,128)S(1)}, f32[2,16,1,1024]{3,2,1,0:T(1,128)S(1)}, u32[]{:S(2)}, u32[]{:S(2)}) collective-permute-start(f32[2,16,1,1024]{3,2,1,0:T(1,128)S(1)} %slice.46), channel_id=1, source_target_pairs={{0,4},{4,8},{8,12},{1,5},{5,9},{9,13},{2,6},{6,10},{10,14},{3,7},{... | collective-permute-start | bytes 393224 | tf_op jit(solution)/shard_map/ppermute | solution.py:24
  87.6 1.9 %collective-permute-done.10.hy_ref = f32[2,16,1,1024]{3,2,1,0:T(1,128)S(1)} collective-permute-done((f32[2,16,1,1024]{3,2,1,0:T(1,128)S(1)}, f32[2,16,1,1024]{3,2,1,0:T(1,128)S(1)}, u32[]{:S(2)}, u32[]{:S(2)}) %collective-permute-start.10) | collective-permute-done | bytes 131104 | tf_op jit(solution)/shard_map/ppermute | solution.py:24
  90.1 7.1 %shard_map.97 = (f32[3,16,16,1024]{3,2,1,0:T(8,128)}, f32[16,16,1024]{2,1,0:T(8,128)}) custom-call(f32[3,16,16,1024]{3,2,1,0:T(8,128)} %shard_map.95.e_ref.en_ref, f32[3,16,16,1024]{3,2,1,0:T(8,128)} %shard_map.96.h_ref.hp_ref, f32[3,16,16,1024]{3,2,1,0:T(8,128)} %shard_map.96.h_ref.hp_ref, f32[16,16,1024]{2,1,0:T(8,128)} %inv_ref.3, ...), custom_call_target="tpu_custom_call" | custom-call | tf_op jit(solution)/shard_map/pallas_call | solution.py:162
  97.2 1.4 %copy.32 = f32[32,8,8,128]{3,1,2,0:T(8,128)S(1)} copy(f32[32,8,8,128]{3,2,1,0:T(8,128)} %bitcast.32) | data formatting | bytes 2097152
  98.7 6.2 %gather_fusion = f32[1024]{0:T(1024)S(1)} fusion(f32[262144]{0:T(1024)S(1)} %bitcast.31, s32[1024]{0:T(1024)S(1)} %broadcast_clamp_fusion), kind=kCustom, calls=%fused_computation | custom fusion | bytes 12288 | tf_op jit(solution)/shard_map/gather | solution.py:184
  104.8 6.0 %scatter_custom_fusion = f32[32768]{0:T(1024)S(1)} fusion(s32[1024]{0:T(1024)S(1)} %bitcast.39, f32[1024]{0:T(1024)S(1)} %gather_fusion, f32[]{:T(128)} %constant.4.clone.1), kind=kCustom, calls=%fused_computation.6 | custom fusion | flops 1024 | bytes 131076 | tf_op jit(solution)/shard_map/scatter-add | solution.py:187
  110.8 19.5 %all_to_all.9 = f32[128,1,256]{2,1,0:T(1,128)S(1)} all-to-all(f32[128,1,256]{2,1,0:T(1,128)S(1)} %bitcast.33), channel_id=1, replica_groups=mesh['gx'=8,'gy'=4,'gz'=4] {'gx','gy','gz'}, dimensions={0} | all-to-all | bytes 262144 | tf_op jit(solution)/shard_map/all_to_all | solution.py:189
  (46 shorter events, 8.2 us)
Async XLA Ops:
  1.6 16.8 %collective-permute-start = (f32[2,16,1024]{2,1,0:T(8,128)S(1)}, f32[2,16,1024]{2,1,0:T(8,128)S(1)}, u32[]{:S(2)}, u32[]{:S(2)}) collective-permute-start(f32[2,16,1024]{2,1,0:T(8,128)S(1)} %slice_bitcast_fusion.3), channel_id=1, source_target_pairs={{16,0},{32,16},{48,32},{64,48},{80,64},{96,80},{112,96},{17,1},{33... | collective-permute-start | bytes 393224 | tf_op jit(solution)/shard_map/ppermute | solution.py:19
  4.2 14.2 %collective-permute-start.1 = (f32[2,16,1,1024]{3,2,1,0:T(1,128)S(1)}, f32[2,16,1,1024]{3,2,1,0:T(1,128)S(1)}, u32[]{:S(2)}, u32[]{:S(2)}) collective-permute-start(f32[2,16,1,1024]{3,2,1,0:T(1,128)S(1)} %slice.37), channel_id=1, source_target_pairs={{4,0},{8,4},{12,8},{5,1},{9,5},{13,9},{6,2},{10,6},{14,10},{7,3},{... | collective-permute-start | bytes 393224 | tf_op jit(solution)/shard_map/ppermute | solution.py:19
  8.4 9.9 %collective-permute-start.2 = (f32[2,16,16,1]{3,2,1,0:T(8,128)S(1)}, f32[2,16,16,1]{3,2,1,0:T(8,128)S(1)}, u32[]{:S(2)}, u32[]{:S(2)}) collective-permute-start(f32[2,16,16,1]{3,2,1,0:T(8,128)S(1)} %slice.38), channel_id=1, source_target_pairs={{1,0},{2,1},{3,2},{5,4},{6,5},{7,6},{9,8},{10,9},{11,10},{13,12},{... | collective-permute-start | bytes 6152 | tf_op jit(solution)/shard_map/ppermute | solution.py:19
  18.3 0.7 copy-start.3
  18.3 0.7 copy-start.4
  18.4 0.8 copy-start.8
  19.1 23.2 %copy-start.12 = (s32[1,1,1,1024]{3,2,1,0:T(1,128)S(1)}, s32[1,1,1,1024]{3,2,1,0:T(1,128)}, u32[]{:S(2)}) copy-start(s32[1,1,1,1024]{3,2,1,0:T(1,128)} %param.13) | copy-start | bytes 12292
  19.1 23.2 %copy-start.13 = (s32[1,1,1,1024,1]{3,4,2,1,0:T(1,128)S(1)}, s32[1,1,1,1024,1]{3,4,2,1,0:T(1,128)}, u32[]{:S(2)}) copy-start(s32[1,1,1,1024,1]{3,4,2,1,0:T(1,128)} %param.12) | copy-start | bytes 12292
  28.1 14.3 %collective-permute-start.5 = (f32[2,16,16,1]{3,2,1,0:T(8,128)S(1)}, f32[2,16,16,1]{3,2,1,0:T(8,128)S(1)}, u32[]{:S(2)}, u32[]{:S(2)}) collective-permute-start(f32[2,16,16,1]{3,2,1,0:T(8,128)S(1)} %slice.51), channel_id=1, source_target_pairs={{0,1},{1,2},{2,3},{4,5},{5,6},{6,7},{8,9},{9,10},{10,11},{12,13},{... | collective-permute-start | bytes 6152 | tf_op jit(solution)/shard_map/ppermute | solution.py:24
  31.4 11.0 %collective-permute-start.3 = (f32[2,16,1024]{2,1,0:T(8,128)S(1)}, f32[2,16,1024]{2,1,0:T(8,128)S(1)}, u32[]{:S(2)}, u32[]{:S(2)}) collective-permute-start(f32[2,16,1024]{2,1,0:T(8,128)S(1)} %slice_bitcast_fusion.2), channel_id=1, source_target_pairs={{0,16},{16,32},{32,48},{48,64},{64,80},{80,96},{96,112},{1,17},{17... | collective-permute-start | bytes 393224 | tf_op jit(solution)/shard_map/ppermute | solution.py:24
  35.7 8.6 %collective-permute-start.4 = (f32[2,16,1,1024]{3,2,1,0:T(1,128)S(1)}, f32[2,16,1,1024]{3,2,1,0:T(1,128)S(1)}, u32[]{:S(2)}, u32[]{:S(2)}) collective-permute-start(f32[2,16,1,1024]{3,2,1,0:T(1,128)S(1)} %slice.40), channel_id=1, source_target_pairs={{0,4},{4,8},{8,12},{1,5},{5,9},{9,13},{2,6},{6,10},{10,14},{3,7},{... | collective-permute-start | bytes 393224 | tf_op jit(solution)/shard_map/ppermute | solution.py:24
  42.4 1.9 %copy-start.1 = (f32[2,16,16,1]{3,2,1,0:T(8,128)}, f32[2,16,16,1]{3,2,1,0:T(8,128)S(1)}, u32[]{:S(2)}) copy-start(f32[2,16,16,1]{3,2,1,0:T(8,128)S(1)} %collective-permute-done.5.hz_ref) | copy-start | bytes 6148
  42.4 1.9 %copy-start.9 = (f32[2,16,1024]{2,1,0:T(8,128)}, f32[2,16,1024]{2,1,0:T(8,128)S(1)}, u32[]{:S(2)}) copy-start(f32[2,16,1024]{2,1,0:T(8,128)S(1)} %collective-permute-done.3) | copy-start | bytes 393220
  44.3 0.6 copy-start.11
  44.9 13.6 %copy-start.14 = (s32[1,1,1,1024]{3,2,1,0:T(1,128)S(1)}, s32[1,1,1,1024]{3,2,1,0:T(1,128)}, u32[]{:S(2)}) copy-start(s32[1,1,1,1024]{3,2,1,0:T(1,128)} %param.11) | copy-start | bytes 12292
  54.0 7.1 %collective-permute-start.8 = (f32[2,16,16,1]{3,2,1,0:T(8,128)S(1)}, f32[2,16,16,1]{3,2,1,0:T(8,128)S(1)}, u32[]{:S(2)}, u32[]{:S(2)}) collective-permute-start(f32[2,16,16,1]{3,2,1,0:T(8,128)S(1)} %slice.53), channel_id=1, source_target_pairs={{1,0},{2,1},{3,2},{5,4},{6,5},{7,6},{9,8},{10,9},{11,10},{13,12},{... | collective-permute-start | bytes 6152 | tf_op jit(solution)/shard_map/ppermute | solution.py:19
  55.3 5.9 %collective-permute-start.6 = (f32[2,16,1024]{2,1,0:T(8,128)S(1)}, f32[2,16,1024]{2,1,0:T(8,128)S(1)}, u32[]{:S(2)}, u32[]{:S(2)}) collective-permute-start(f32[2,16,1024]{2,1,0:T(8,128)S(1)} %slice_bitcast_fusion.1), channel_id=1, source_target_pairs={{16,0},{32,16},{48,32},{64,48},{80,64},{96,80},{112,96},{17,1},{33... | collective-permute-start | bytes 393224 | tf_op jit(solution)/shard_map/ppermute | solution.py:19
  56.6 8.5 %collective-permute-start.7 = (f32[2,16,1,1024]{3,2,1,0:T(1,128)S(1)}, f32[2,16,1,1024]{3,2,1,0:T(1,128)S(1)}, u32[]{:S(2)}, u32[]{:S(2)}) collective-permute-start(f32[2,16,1,1024]{3,2,1,0:T(1,128)S(1)} %slice.43), channel_id=1, source_target_pairs={{4,0},{8,4},{12,8},{5,1},{9,5},{13,9},{6,2},{10,6},{14,10},{7,3},{... | collective-permute-start | bytes 393224 | tf_op jit(solution)/shard_map/ppermute | solution.py:19
  61.1 4.0 %copy-start.2 = (f32[2,16,16,1]{3,2,1,0:T(8,128)}, f32[2,16,16,1]{3,2,1,0:T(8,128)S(1)}, u32[]{:S(2)}) copy-start(f32[2,16,16,1]{3,2,1,0:T(8,128)S(1)} %collective-permute-done.8.hz_ref) | copy-start | bytes 6148
  61.2 3.9 %copy-start.6 = (f32[2,16,1024]{2,1,0:T(8,128)}, f32[2,16,1024]{2,1,0:T(8,128)S(1)}, u32[]{:S(2)}) copy-start(f32[2,16,1024]{2,1,0:T(8,128)S(1)} %collective-permute-done.6) | copy-start | bytes 393220
  65.1 0.6 copy-start.10
  74.6 12.9 %collective-permute-start.11 = (f32[2,16,16,1]{3,2,1,0:T(8,128)S(1)}, f32[2,16,16,1]{3,2,1,0:T(8,128)S(1)}, u32[]{:S(2)}, u32[]{:S(2)}) collective-permute-start(f32[2,16,16,1]{3,2,1,0:T(8,128)S(1)} %slice.55), channel_id=1, source_target_pairs={{0,1},{1,2},{2,3},{4,5},{5,6},{6,7},{8,9},{9,10},{10,11},{12,13},{... | collective-permute-start | bytes 6152 | tf_op jit(solution)/shard_map/ppermute | solution.py:24
  78.9 8.6 %collective-permute-start.9 = (f32[2,16,1024]{2,1,0:T(8,128)S(1)}, f32[2,16,1024]{2,1,0:T(8,128)S(1)}, u32[]{:S(2)}, u32[]{:S(2)}) collective-permute-start(f32[2,16,1024]{2,1,0:T(8,128)S(1)} %slice_bitcast_fusion), channel_id=1, source_target_pairs={{0,16},{16,32},{32,48},{48,64},{64,80},{80,96},{96,112},{1,17},{17... | collective-permute-start | bytes 393224 | tf_op jit(solution)/shard_map/ppermute | solution.py:24
  83.1 6.3 %collective-permute-start.10 = (f32[2,16,1,1024]{3,2,1,0:T(1,128)S(1)}, f32[2,16,1,1024]{3,2,1,0:T(1,128)S(1)}, u32[]{:S(2)}, u32[]{:S(2)}) collective-permute-start(f32[2,16,1,1024]{3,2,1,0:T(1,128)S(1)} %slice.46), channel_id=1, source_target_pairs={{0,4},{4,8},{8,12},{1,5},{5,9},{9,13},{2,6},{6,10},{10,14},{3,7},{... | collective-permute-start | bytes 393224 | tf_op jit(solution)/shard_map/ppermute | solution.py:24
  87.5 1.9 %copy-start = (f32[2,16,16,1]{3,2,1,0:T(8,128)}, f32[2,16,16,1]{3,2,1,0:T(8,128)S(1)}, u32[]{:S(2)}) copy-start(f32[2,16,16,1]{3,2,1,0:T(8,128)S(1)} %collective-permute-done.11.hz_ref) | copy-start | bytes 6148
  87.6 1.9 %copy-start.5 = (f32[2,16,1024]{2,1,0:T(8,128)}, f32[2,16,1024]{2,1,0:T(8,128)S(1)}, u32[]{:S(2)}) copy-start(f32[2,16,1024]{2,1,0:T(8,128)S(1)} %collective-permute-done.9) | copy-start | bytes 393220
  89.4 0.7 copy-start.7

commit v3 on v2

--- a/solution.py
+++ b/solution.py
@@ -60,7 +60,7 @@
     return jnp.concatenate([prv, a[:-1]], axis=0)
 
 
-def h_kernel(e_ref, en_ref, h_ref, hx_ref, hy_ref, hz_ref, out_ref):
+def h_kernel(e_ref, en_ref, h_ref, hx_ref, hy_ref, hz_ref, out_ref, fx_ref, fy_ref, fz_ref):
     last = pl.program_id(0) == pl.num_programs(0) - 1
     ex, ey, ez = e_ref[0], e_ref[1], e_ref[2]
     nxt_y = jnp.where(last, hx_ref[0], en_ref[1])
@@ -74,6 +74,17 @@
     out_ref[0] = h_ref[0] - courant * ((ez_yp - ez) - (ey_zp - ey))
     out_ref[1] = h_ref[1] - courant * ((ex_zp - ex) - (ez_xp - ez))
     out_ref[2] = h_ref[2] - courant * ((ey_xp - ey) - (ex_yp - ex))
+    b, ny, nz = ex.shape
+
+    @pl.when(last)
+    def _():
+        fx_ref[0] = out_ref[1, b - 1:b]
+        fx_ref[1] = out_ref[2, b - 1:b]
+
+    fy_ref[0] = out_ref[0, :, ny - 1:ny, :]
+    fy_ref[1] = out_ref[2, :, ny - 1:ny, :]
+    fz_ref[0] = out_ref[0, :, :, nz - 1:nz]
+    fz_ref[1] = out_ref[1, :, :, nz - 1:nz]
 
 
 def e_update(e_ref, h_ref, hp_ref, inv_ref, hx_ref, hy_ref, hz_ref):
@@ -94,11 +105,21 @@
     return new_x, new_y, new_z
 
 
-def e_kernel(e_ref, h_ref, hp_ref, inv_ref, hx_ref, hy_ref, hz_ref, out_ref):
+def e_kernel(e_ref, h_ref, hp_ref, inv_ref, hx_ref, hy_ref, hz_ref, out_ref, fx_ref, fy_ref, fz_ref):
     new_x, new_y, new_z = e_update(e_ref, h_ref, hp_ref, inv_ref, hx_ref, hy_ref, hz_ref)
     out_ref[0] = new_x
     out_ref[1] = new_y
     out_ref[2] = new_z
+
+    @pl.when(pl.program_id(0) == 0)
+    def _():
+        fx_ref[0] = out_ref[1, 0:1]
+        fx_ref[1] = out_ref[2, 0:1]
+
+    fy_ref[0] = out_ref[0, :, 0:1, :]
+    fy_ref[1] = out_ref[2, :, 0:1, :]
+    fz_ref[0] = out_ref[0, :, :, 0:1]
+    fz_ref[1] = out_ref[1, :, :, 0:1]
 
 
 def e_last_kernel(e_ref, h_ref, hp_ref, inv_ref, hx_ref, hy_ref, hz_ref, ef_ref, out_ref, inter_ref):
@@ -113,12 +134,32 @@
     return pl.BlockSpec((3, chunk, ny, nz), lambda i: (0, i, 0, 0))
 
 
-def h_step(e, h):
+def face_specs(nx, ny, nz, chunk):
+    return [
+        pl.BlockSpec((2, 1, ny, nz), lambda i: (0, 0, 0, 0)),
+        pl.BlockSpec((2, chunk, 1, nz), lambda i: (0, i, 0, 0)),
+        pl.BlockSpec((2, chunk, ny, 1), lambda i: (0, i, 0, 0)),
+    ]
+
+
+def face_shapes(nx, ny, nz, dtype):
+    return [
+        jax.ShapeDtypeStruct((2, 1, ny, nz), dtype),
+        jax.ShapeDtypeStruct((2, nx, 1, nz), dtype),
+        jax.ShapeDtypeStruct((2, nx, ny, 1), dtype),
+    ]
+
+
+def lower_faces_of(e):
+    return e[1:3, 0:1], e[0::2, :, 0:1, :], e[0:2, :, :, 0:1]
+
+
+def h_step(e, h, faces):
     _, nx, ny, nz = e.shape
     chunk = CHUNK
-    faces_x = toward_lower(e[1:3, 0], "gx")
-    faces_y = toward_lower(e[0::2, :, 0:1, :], "gy")
-    faces_z = toward_lower(e[0:2, :, :, 0:1], "gz")
+    faces_x = toward_lower(faces[0], "gx")
+    faces_y = toward_lower(faces[1], "gy")
+    faces_z = toward_lower(faces[2], "gz")
     return pl.pallas_call(
         h_kernel,
         grid=(nx // chunk,),
@@ -130,17 +171,17 @@
             pl.BlockSpec((2, chunk, 1, nz), lambda i: (0, i, 0, 0)),
             pl.BlockSpec((2, chunk, ny, 1), lambda i: (0, i, 0, 0)),
         ],
-        out_specs=field_spec(nx, ny, nz, chunk),
-        out_shape=jax.ShapeDtypeStruct(h.shape, h.dtype),
-    )(e, e, h, faces_x[:, None], faces_y, faces_z)
-
-
-def e_step(e, h, inv, ef=None):
+        out_specs=[field_spec(nx, ny, nz, chunk)] + face_specs(nx, ny, nz, chunk),
+        out_shape=[jax.ShapeDtypeStruct(h.shape, h.dtype)] + face_shapes(nx, ny, nz, h.dtype),
+    )(e, e, h, faces_x, faces_y, faces_z)
+
+
+def e_step(e, h, faces, inv, ef=None):
     _, nx, ny, nz = e.shape
     chunk = CHUNK
-    faces_x = toward_upper(h[1:3, nx - 1], "gx")
-    faces_y = toward_upper(h[0::2, :, ny - 1:ny, :], "gy")
-    faces_z = toward_upper(h[0:2, :, :, nz - 1:nz], "gz")
+    faces_x = toward_upper(faces[0], "gx")
+    faces_y = toward_upper(faces[1], "gy")
+    faces_z = toward_upper(faces[2], "gz")
     in_specs = [
         field_spec(nx, ny, nz, chunk),
         field_spec(nx, ny, nz, chunk),
@@ -150,15 +191,16 @@
         pl.BlockSpec((2, chunk, 1, nz), lambda i: (0, i, 0, 0)),
         pl.BlockSpec((2, chunk, ny, 1), lambda i: (0, i, 0, 0)),
     ]
-    args = [e, h, h, inv, faces_x[:, None], faces_y, faces_z]
+    args = [e, h, h, inv, faces_x, faces_y, faces_z]
     if ef is None:
-        return pl.pallas_call(
+        outs = pl.pallas_call(
             e_kernel,
             grid=(nx // chunk,),
             in_specs=in_specs,
-            out_specs=field_spec(nx, ny, nz, chunk),
-            out_shape=jax.ShapeDtypeStruct(e.shape, e.dtype),
+            out_specs=[field_spec(nx, ny, nz, chunk)] + face_specs(nx, ny, nz, chunk),
+            out_shape=[jax.ShapeDtypeStruct(e.shape, e.dtype)] + face_shapes(nx, ny, nz, e.dtype),
         )(*args)
+        return outs[0], outs[1:]
     return pl.pallas_call(
         e_last_kernel,
         grid=(nx // chunk,),
@@ -170,22 +212,26 @@
 
 def body(e_forward, e_adjoint, h_adjoint, inv_perm, voxel_cell, voxel_owner, voxel_slot):
     e, h = e_adjoint, h_adjoint
+    e_faces = lower_faces_of(e)
     intersection = None
     for repeat in range(STEPS):
-        h = h_step(e, h)
+        h, *h_faces = h_step(e, h, e_faces)
         if repeat == STEPS - 1:
-            e, intersection = e_step(e, h, inv_perm, e_forward)
+            e, intersection = e_step(e, h, h_faces, inv_perm, e_forward)
         else:
-            e = e_step(e, h, inv_perm)
+            e, e_faces = e_step(e, h, h_faces, inv_perm)
     count = voxel_cell.shape[-1]
     voxel_rows = voxel_cell.reshape(count)
     owners = voxel_owner.reshape(count)
     slot_ids = voxel_slot.reshape(count)
-    terms = intersection.reshape(-1)[voxel_rows]
+    nx, ny, nz = intersection.shape
+    rows = intersection.reshape(nx * ny, nz)[voxel_rows // nz]
+    lanes = lax.broadcasted_iota(jnp.int32, rows.shape, 1)
+    terms = jnp.sum(jnp.where(lanes == (voxel_rows % nz)[:, None], rows, 0.0), axis=1)
     devices = lax.axis_size("gx") * lax.axis_size("gy") * lax.axis_size("gz")
-    params = owners * P_DEV + slot_ids
-    dense_terms = jax.ops.segment_sum(terms, params, num_segments=devices * P_DEV)
-    per_owner = dense_terms.reshape(devices, P_DEV)
+    owner_hot = (owners[:, None] == lax.broadcasted_iota(jnp.int32, (count, devices), 1)).astype(jnp.float32)
+    slot_hot = jnp.where(slot_ids[:, None] == lax.broadcasted_iota(jnp.int32, (count, P_DEV), 1), terms[:, None], 0.0)
+    per_owner = jnp.dot(owner_hot.T, slot_hot, precision=lax.Precision.HIGHEST, preferred_element_type=jnp.float32)
     received = lax.all_to_all(per_owner, ("gx", "gy", "gz"), 0, 0, tiled=True)
     gradient = received.sum(axis=0)
     return (e, h, gradient)

time: 132 us -> 128 us (0.970)
  local copies, waits for them, and re-layouts: 23.4 us -> 14.6 us
  waiting for transfers between devices: 18.9 us -> 22.1 us
  other arithmetic: 6.7 us -> 3.62 us
  starting transfers between devices: 37.5 us -> 39.9 us
    slice x8 -> x3, local copies, waits for them, and re-layouts: 9.4 us -> 3.19 us  [lower_faces_of(): return (e[1:3, 0:1], e[0::2, :, 0:1, :], e[0:2, :, :, 0:1])]
    scatter-add x1 -> x0, other arithmetic: 5.96 us -> none  [body(): jax.ops.segment_sum(terms, params, num_segments=devices * P_DEV)]
    squeeze x4 -> x0, local copies, waits for them, and re-layouts: 3.68 us -> none  [the longest x2 1.84 us: e_step(): faces_x = toward_upper(h[1:3, nx - 1], 'gx')]
    ppermute x6, waiting for transfers between devices: 3.73 us -> 7.15 us  [toward_upper(): return lax.ppermute(x, axis, [(j, j + 1) for j in range(peers - 1)])]
    reduce_sum x0 -> x1, other arithmetic: none -> 2.86 us  [body(): jnp.sum(jnp.where(lanes == (voxel_rows % nz)[:, None], rows, 0.0), axis=1)]
    ppermute x6, starting transfers between devices: 27.1 us -> 29.5 us  [toward_upper(): return lax.ppermute(x, axis, [(j, j + 1) for j in range(peers - 1)])]
    gather x1, local copies, waits for them, and re-layouts: 6.15 us -> 7.57 us  [body(): rows = intersection.reshape(nx * ny, nz)[voxel_rows // nz]]
    unnamed x31 -> x30, local copies, waits for them, and re-layouts: 4.15 us -> 3.66 us
  transfers between devices with their start and end apart: 12 -> 12, of which waited for: 6 -> 4; matrix products, arithmetic and copies ran while one was open for 2% -> 2% of each run, Pallas kernels for 0% -> 0%
where the time goes in v3:
time: 128 us; the launch traced here: 127 us
  starting transfers between devices  39.9 us (31%)
  Pallas kernels  24.9 us (19%)
  waiting for transfers between devices  22.1 us (17%)
  blocking collectives  19.8 us (15%)
  local copies, waits for them, and re-layouts  14.6 us (11%)
  other arithmetic  3.62 us (3%)
    ppermute x6, starting transfers between devices, toward_upper(): return lax.ppermute(x, axis, [(j, j + 1) for j in range(peers - 1)])  29.5 us
    all_to_all x1, blocking collectives, body(): received = lax.all_to_all(per_owner, ('gx', 'gy', 'gz'), 0, 0, tiled=True)  19.8 us
    ppermute x6, waiting for transfers between devices, toward_lower(): return lax.ppermute(x, axis, [(j, j - 1) for j in range(1, peers)])  15 us
    pallas_call x2, Pallas kernels, h_step(): pl.pallas_call(h_kernel, grid=(nx // chunk,), in_specs=[field_spec(nx, ny...  11.7 us
    ppermute x6, starting transfers between devices, toward_lower(): return lax.ppermute(x, axis, [(j, j - 1) for j in range(1, peers)])  10.4 us
    gather x1, local copies, waits for them, and re-layouts, body(): rows = intersection.reshape(nx * ny, nz)[voxel_rows // nz]  7.57 us
    pallas_call x1, Pallas kernels, e_step(): pl.pallas_call(e_last_kernel, grid=(nx // chunk,), in_specs=in_specs + [f...  7.15 us
    ppermute x6, waiting for transfers between devices, toward_upper(): return lax.ppermute(x, axis, [(j, j + 1) for j in range(peers - 1)])  7.15 us
  transfers between devices with their start and end apart: 12, of which 4 were waited for; matrix products, arithmetic and copies ran while one was open for 2% of the time, Pallas kernels for 0%

profile of v3, /device:TPU:1, one launch (start us, length us, event | category | flops | bytes accessed | tf_op | source)
XLA Modules:
  0.0 126.8 jit_solution(485334335851636906)
XLA Ops:
  0.6 0.9 slice.9
  1.6 1.3 %collective-permute-start = (f32[2,1,16,1024]{3,2,1,0:T(8,128)S(1)}, f32[2,1,16,1024]{3,2,1,0:T(8,128)S(1)}, u32[]{:S(2)}, u32[]{:S(2)}) collective-permute-start(f32[2,1,16,1024]{3,2,1,0:T(8,128)S(1)} %slice.9), channel_id=1, source_target_pairs={{16,0},{32,16},{48,32},{64,48},{80,64},{96,80},{112,96},{17,1},{33... | collective-permute-start | bytes 393224 | tf_op jit(solution)/shard_map/ppermute | solution.py:19
  2.9 1.3 %slice.10 = f32[2,16,1,1024]{3,2,1,0:T(1,128)S(1)} slice(f32[3,16,16,1024]{3,2,1,0:T(8,128)} %e_ref.3), slice={[0:3:2], [0:16:1], [0:1:1], [0:1024:1]} | slice | bytes 262144 | tf_op jit(solution)/shard_map/slice | solution.py:154
  4.2 3.3 %collective-permute-start.1 = (f32[2,16,1,1024]{3,2,1,0:T(1,128)S(1)}, f32[2,16,1,1024]{3,2,1,0:T(1,128)S(1)}, u32[]{:S(2)}, u32[]{:S(2)}) collective-permute-start(f32[2,16,1,1024]{3,2,1,0:T(1,128)S(1)} %slice.10), channel_id=1, source_target_pairs={{4,0},{8,4},{12,8},{5,1},{9,5},{13,9},{6,2},{10,6},{14,10},{7,3},{... | collective-permute-start | bytes 393224 | tf_op jit(solution)/shard_map/ppermute | solution.py:19
  7.5 1.0 slice.11
  8.4 1.3 %collective-permute-start.2 = (f32[2,16,16,1]{3,2,1,0:T(8,128)S(1)}, f32[2,16,16,1]{3,2,1,0:T(8,128)S(1)}, u32[]{:S(2)}, u32[]{:S(2)}) collective-permute-start(f32[2,16,16,1]{3,2,1,0:T(8,128)S(1)} %slice.11), channel_id=1, source_target_pairs={{1,0},{2,1},{3,2},{5,4},{6,5},{7,6},{9,8},{10,9},{11,10},{13,12},{... | collective-permute-start | bytes 6152 | tf_op jit(solution)/shard_map/ppermute | solution.py:19
  9.7 8.6 %collective-permute-done.2.hz_ref = f32[2,16,16,1]{3,2,1,0:T(8,128)S(1)} collective-permute-done((f32[2,16,16,1]{3,2,1,0:T(8,128)S(1)}, f32[2,16,16,1]{3,2,1,0:T(8,128)S(1)}, u32[]{:S(2)}, u32[]{:S(2)}) %collective-permute-start.2) | collective-permute-done | bytes 2080 | tf_op jit(solution)/shard_map/ppermute | solution.py:19
  18.4 0.7 copy-done.3
  19.7 5.9 %shard_map.94 = (f32[3,16,16,1024]{3,2,1,0:T(8,128)}, f32[2,1,16,1024]{3,2,1,0:T(8,128)}, f32[2,16,1,1024]{3,2,1,0:T(1,128)}, f32[2,16,16,1]{3,2,1,0:T(8,128)}) custom-call(f32[3,16,16,1024]{3,2,1,0:T(8,128)} %e_ref.3, f32[3,16,16,1024]{3,2,1,0:T(8,128)} %e_ref.3, f32[3,16,16,1024]{3,2,1,0:T(8,128)} %h_ref.1, f32[2,1,16,1024]{3,2,1,0:T(8,128)} %copy-done.5, ...), custom_call_target="tpu_custom_call" | custom-call | tf_op jit(solution)/shard_map/pallas_call | solution.py:163
  25.6 4.3 %collective-permute-start.3 = (f32[2,1,16,1024]{3,2,1,0:T(8,128)}, f32[2,1,16,1024]{3,2,1,0:T(8,128)S(1)}, u32[]{:S(2)}, u32[]{:S(2)}) collective-permute-start(f32[2,1,16,1024]{3,2,1,0:T(8,128)} %get-tuple-element.18), channel_id=1, source_target_pairs={{0,16},{16,32},{32,48},{48,64},{64,80},{80,96},{96,112},{1,17},{17... | collective-permute-start | bytes 393224 | tf_op jit(solution)/shard_map/ppermute | solution.py:24
  29.9 6.5 %collective-permute-start.4 = (f32[2,16,1,1024]{3,2,1,0:T(1,128)}, f32[2,16,1,1024]{3,2,1,0:T(1,128)S(1)}, u32[]{:S(2)}, u32[]{:S(2)}) collective-permute-start(f32[2,16,1,1024]{3,2,1,0:T(1,128)} %get-tuple-element.19), channel_id=1, source_target_pairs={{0,4},{4,8},{8,12},{1,5},{5,9},{9,13},{2,6},{6,10},{10,14},{3,7},{... | collective-permute-start | bytes 393224 | tf_op jit(solution)/shard_map/ppermute | solution.py:24
  36.4 3.2 %collective-permute-start.5 = (f32[2,16,16,1]{3,2,1,0:T(8,128)}, f32[2,16,16,1]{3,2,1,0:T(8,128)S(1)}, u32[]{:S(2)}, u32[]{:S(2)}) collective-permute-start(f32[2,16,16,1]{3,2,1,0:T(8,128)} %get-tuple-element.20), channel_id=1, source_target_pairs={{0,1},{1,2},{2,3},{4,5},{5,6},{6,7},{8,9},{9,10},{10,11},{12,13},{... | collective-permute-start | bytes 6152 | tf_op jit(solution)/shard_map/ppermute | solution.py:24
  39.6 3.6 %collective-permute-done.5.hz_ref = f32[2,16,16,1]{3,2,1,0:T(8,128)S(1)} collective-permute-done((f32[2,16,16,1]{3,2,1,0:T(8,128)}, f32[2,16,16,1]{3,2,1,0:T(8,128)S(1)}, u32[]{:S(2)}, u32[]{:S(2)}) %collective-permute-start.5) | collective-permute-done | bytes 2080 | tf_op jit(solution)/shard_map/ppermute | solution.py:24
  43.2 0.7 copy-done.2
  44.0 6.0 %shard_map.95 = (f32[3,16,16,1024]{3,2,1,0:T(8,128)}, f32[2,1,16,1024]{3,2,1,0:T(8,128)}, f32[2,16,1,1024]{3,2,1,0:T(1,128)}, f32[2,16,16,1]{3,2,1,0:T(8,128)}) custom-call(f32[3,16,16,1024]{3,2,1,0:T(8,128)} %e_ref.3, f32[3,16,16,1024]{3,2,1,0:T(8,128)} %get-tuple-element.17.h_ref.hp_ref, f32[3,16,16,1024]{3,2,1,0:T(8,128)} %get-tuple-element.17.h_ref.hp_ref, ...), custom_call_target="tpu_custom_call" | custom-call | tf_op jit(solution)/shard_map/pallas_call | solution.py:196
  50.0 1.3 %collective-permute-start.6 = (f32[2,1,16,1024]{3,2,1,0:T(8,128)}, f32[2,1,16,1024]{3,2,1,0:T(8,128)S(1)}, u32[]{:S(2)}, u32[]{:S(2)}) collective-permute-start(f32[2,1,16,1024]{3,2,1,0:T(8,128)} %get-tuple-element.22), channel_id=1, source_target_pairs={{16,0},{32,16},{48,32},{64,48},{80,64},{96,80},{112,96},{17,1},{33... | collective-permute-start | bytes 393224 | tf_op jit(solution)/shard_map/ppermute | solution.py:19
  51.3 1.9 %collective-permute-start.7 = (f32[2,16,1,1024]{3,2,1,0:T(1,128)}, f32[2,16,1,1024]{3,2,1,0:T(1,128)S(1)}, u32[]{:S(2)}, u32[]{:S(2)}) collective-permute-start(f32[2,16,1,1024]{3,2,1,0:T(1,128)} %get-tuple-element.23), channel_id=1, source_target_pairs={{4,0},{8,4},{12,8},{5,1},{9,5},{13,9},{6,2},{10,6},{14,10},{7,3},{... | collective-permute-start | bytes 393224 | tf_op jit(solution)/shard_map/ppermute | solution.py:19
  53.2 1.3 %collective-permute-start.8 = (f32[2,16,16,1]{3,2,1,0:T(8,128)}, f32[2,16,16,1]{3,2,1,0:T(8,128)S(1)}, u32[]{:S(2)}, u32[]{:S(2)}) collective-permute-start(f32[2,16,16,1]{3,2,1,0:T(8,128)} %get-tuple-element.24), channel_id=1, source_target_pairs={{1,0},{2,1},{3,2},{5,4},{6,5},{7,6},{9,8},{10,9},{11,10},{13,12},{... | collective-permute-start | bytes 6152 | tf_op jit(solution)/shard_map/ppermute | solution.py:19
  54.5 6.4 %collective-permute-done.8.hz_ref = f32[2,16,16,1]{3,2,1,0:T(8,128)S(1)} collective-permute-done((f32[2,16,16,1]{3,2,1,0:T(8,128)}, f32[2,16,16,1]{3,2,1,0:T(8,128)S(1)}, u32[]{:S(2)}, u32[]{:S(2)}) %collective-permute-start.8) | collective-permute-done | bytes 2080 | tf_op jit(solution)/shard_map/ppermute | solution.py:19
  60.9 0.7 copy-done.1
  61.7 5.9 %shard_map.96 = (f32[3,16,16,1024]{3,2,1,0:T(8,128)}, f32[2,1,16,1024]{3,2,1,0:T(8,128)}, f32[2,16,1,1024]{3,2,1,0:T(1,128)}, f32[2,16,16,1]{3,2,1,0:T(8,128)}) custom-call(f32[3,16,16,1024]{3,2,1,0:T(8,128)} %get-tuple-element.21.e_ref.en_ref, f32[3,16,16,1024]{3,2,1,0:T(8,128)} %get-tuple-element.21.e_ref.en_ref, ...), custom_call_target="tpu_custom_call" | custom-call | tf_op jit(solution)/shard_map/pallas_call | solution.py:163
  67.5 4.8 %collective-permute-start.9 = (f32[2,1,16,1024]{3,2,1,0:T(8,128)}, f32[2,1,16,1024]{3,2,1,0:T(8,128)S(1)}, u32[]{:S(2)}, u32[]{:S(2)}) collective-permute-start(f32[2,1,16,1024]{3,2,1,0:T(8,128)} %get-tuple-element.26), channel_id=1, source_target_pairs={{0,16},{16,32},{32,48},{48,64},{64,80},{80,96},{96,112},{1,17},{17... | collective-permute-start | bytes 393224 | tf_op jit(solution)/shard_map/ppermute | solution.py:24
  72.3 7.4 %collective-permute-start.10 = (f32[2,16,1,1024]{3,2,1,0:T(1,128)}, f32[2,16,1,1024]{3,2,1,0:T(1,128)S(1)}, u32[]{:S(2)}, u32[]{:S(2)}) collective-permute-start(f32[2,16,1,1024]{3,2,1,0:T(1,128)} %get-tuple-element.27), channel_id=1, source_target_pairs={{0,4},{4,8},{8,12},{1,5},{5,9},{9,13},{2,6},{6,10},{10,14},{3,7},{... | collective-permute-start | bytes 393224 | tf_op jit(solution)/shard_map/ppermute | solution.py:24
  79.7 3.4 %collective-permute-start.11 = (f32[2,16,16,1]{3,2,1,0:T(8,128)}, f32[2,16,16,1]{3,2,1,0:T(8,128)S(1)}, u32[]{:S(2)}, u32[]{:S(2)}) collective-permute-start(f32[2,16,16,1]{3,2,1,0:T(8,128)} %get-tuple-element.28), channel_id=1, source_target_pairs={{0,1},{1,2},{2,3},{4,5},{5,6},{6,7},{8,9},{9,10},{10,11},{12,13},{... | collective-permute-start | bytes 6152 | tf_op jit(solution)/shard_map/ppermute | solution.py:24
  83.1 3.6 %collective-permute-done.11.hz_ref = f32[2,16,16,1]{3,2,1,0:T(8,128)S(1)} collective-permute-done((f32[2,16,16,1]{3,2,1,0:T(8,128)}, f32[2,16,16,1]{3,2,1,0:T(8,128)S(1)}, u32[]{:S(2)}, u32[]{:S(2)}) %collective-permute-start.11) | collective-permute-done | bytes 2080 | tf_op jit(solution)/shard_map/ppermute | solution.py:24
  86.7 0.7 copy-done
  87.5 7.2 %shard_map.97 = (f32[3,16,16,1024]{3,2,1,0:T(8,128)}, f32[16,16,1024]{2,1,0:T(8,128)}) custom-call(f32[3,16,16,1024]{3,2,1,0:T(8,128)} %get-tuple-element.21.e_ref.en_ref, f32[3,16,16,1024]{3,2,1,0:T(8,128)} %get-tuple-element.15.h_ref.hp_ref, f32[3,16,16,1024]{3,2,1,0:T(8,128)} %get-tuple-element.15.h_ref.hp_ref, f32[16,16,1024]{2,1,0:T(8,128)} %inv_ref.3, ...), custom_call_target="tpu_custom_call" | custom-call | tf_op jit(solution)/shard_map/pallas_call | solution.py:204
  94.6 7.6 %gather_fusion = f32[1024,1024]{1,0:T(8,128)} fusion(f32[256,1024]{1,0:T(8,128)} %bitcast.17, s32[1024]{0:T(1024)S(1)} %broadcast_clamp_fusion), kind=kCustom, calls=%fused_computation | custom fusion | bytes 8392704 | tf_op jit(solution)/shard_map/gather | solution.py:228
  102.2 2.9 %select_reduce_fusion = f32[1024]{0:T(1024)S(1)} fusion(f32[1024,1024]{1,0:T(8,128)} %gather_fusion, s32[1024]{0:T(1024)S(1)} %add_select_fusion), kind=kLoop, calls=%fused_computation.1 | loop fusion | flops 3144704 | bytes 4202496 | tf_op jit(solution)/shard_map/reduce_sum | solution.py:230
  105.1 1.1 convolution_bitcast_fusion
  106.3 19.8 %all_to_all.9 = f32[128,1,256]{2,1,0:T(1,128)S(1)} all-to-all(f32[128,1,256]{2,1,0:T(1,128)S(1)} %copy.10), channel_id=1, replica_groups=mesh['gx'=8,'gy'=4,'gz'=4] {'gx','gy','gz'}, dimensions={0} | all-to-all | bytes 262144 | tf_op jit(solution)/shard_map/all_to_all | solution.py:235
  126.1 0.7 reduce_sum.19
  (38 shorter events, 1.2 us)
Async XLA Ops:
  1.6 16.8 %collective-permute-start = (f32[2,1,16,1024]{3,2,1,0:T(8,128)S(1)}, f32[2,1,16,1024]{3,2,1,0:T(8,128)S(1)}, u32[]{:S(2)}, u32[]{:S(2)}) collective-permute-start(f32[2,1,16,1024]{3,2,1,0:T(8,128)S(1)} %slice.9), channel_id=1, source_target_pairs={{16,0},{32,16},{48,32},{64,48},{80,64},{96,80},{112,96},{17,1},{33... | collective-permute-start | bytes 393224 | tf_op jit(solution)/shard_map/ppermute | solution.py:19
  4.2 14.2 %collective-permute-start.1 = (f32[2,16,1,1024]{3,2,1,0:T(1,128)S(1)}, f32[2,16,1,1024]{3,2,1,0:T(1,128)S(1)}, u32[]{:S(2)}, u32[]{:S(2)}) collective-permute-start(f32[2,16,1,1024]{3,2,1,0:T(1,128)S(1)} %slice.10), channel_id=1, source_target_pairs={{4,0},{8,4},{12,8},{5,1},{9,5},{13,9},{6,2},{10,6},{14,10},{7,3},{... | collective-permute-start | bytes 393224 | tf_op jit(solution)/shard_map/ppermute | solution.py:19
  8.4 31.2 %copy-start.12 = (s32[1,1,1,1024]{3,2,1,0:T(1,128)S(1)}, s32[1,1,1,1024]{3,2,1,0:T(1,128)}, u32[]{:S(2)}) copy-start(s32[1,1,1,1024]{3,2,1,0:T(1,128)} %param.11) | copy-start | bytes 12292
  8.4 9.9 %collective-permute-start.2 = (f32[2,16,16,1]{3,2,1,0:T(8,128)S(1)}, f32[2,16,16,1]{3,2,1,0:T(8,128)S(1)}, u32[]{:S(2)}, u32[]{:S(2)}) collective-permute-start(f32[2,16,16,1]{3,2,1,0:T(8,128)S(1)} %slice.11), channel_id=1, source_target_pairs={{1,0},{2,1},{3,2},{5,4},{6,5},{7,6},{9,8},{10,9},{11,10},{13,12},{... | collective-permute-start | bytes 6152 | tf_op jit(solution)/shard_map/ppermute | solution.py:19
  18.3 0.7 copy-start.3
  18.4 0.7 copy-start.5
  19.1 0.7 copy-start.10
  25.6 17.6 %collective-permute-start.3 = (f32[2,1,16,1024]{3,2,1,0:T(8,128)}, f32[2,1,16,1024]{3,2,1,0:T(8,128)S(1)}, u32[]{:S(2)}, u32[]{:S(2)}) collective-permute-start(f32[2,1,16,1024]{3,2,1,0:T(8,128)} %get-tuple-element.18), channel_id=1, source_target_pairs={{0,16},{16,32},{32,48},{48,64},{64,80},{80,96},{96,112},{1,17},{17... | collective-permute-start | bytes 393224 | tf_op jit(solution)/shard_map/ppermute | solution.py:24
  29.9 13.3 %collective-permute-start.4 = (f32[2,16,1,1024]{3,2,1,0:T(1,128)}, f32[2,16,1,1024]{3,2,1,0:T(1,128)S(1)}, u32[]{:S(2)}, u32[]{:S(2)}) collective-permute-start(f32[2,16,1,1024]{3,2,1,0:T(1,128)} %get-tuple-element.19), channel_id=1, source_target_pairs={{0,4},{4,8},{8,12},{1,5},{5,9},{9,13},{2,6},{6,10},{10,14},{3,7},{... | collective-permute-start | bytes 393224 | tf_op jit(solution)/shard_map/ppermute | solution.py:24
  36.4 6.8 %collective-permute-start.5 = (f32[2,16,16,1]{3,2,1,0:T(8,128)}, f32[2,16,16,1]{3,2,1,0:T(8,128)S(1)}, u32[]{:S(2)}, u32[]{:S(2)}) collective-permute-start(f32[2,16,16,1]{3,2,1,0:T(8,128)} %get-tuple-element.20), channel_id=1, source_target_pairs={{0,1},{1,2},{2,3},{4,5},{5,6},{6,7},{8,9},{9,10},{10,11},{12,13},{... | collective-permute-start | bytes 6152 | tf_op jit(solution)/shard_map/ppermute | solution.py:24
  43.2 0.7 copy-start.2
  43.2 0.7 copy-start.6
  43.2 0.8 copy-start.9
  50.0 10.9 %collective-permute-start.6 = (f32[2,1,16,1024]{3,2,1,0:T(8,128)}, f32[2,1,16,1024]{3,2,1,0:T(8,128)S(1)}, u32[]{:S(2)}, u32[]{:S(2)}) collective-permute-start(f32[2,1,16,1024]{3,2,1,0:T(8,128)} %get-tuple-element.22), channel_id=1, source_target_pairs={{16,0},{32,16},{48,32},{64,48},{80,64},{96,80},{112,96},{17,1},{33... | collective-permute-start | bytes 393224 | tf_op jit(solution)/shard_map/ppermute | solution.py:19
  51.3 9.6 %collective-permute-start.7 = (f32[2,16,1,1024]{3,2,1,0:T(1,128)}, f32[2,16,1,1024]{3,2,1,0:T(1,128)S(1)}, u32[]{:S(2)}, u32[]{:S(2)}) collective-permute-start(f32[2,16,1,1024]{3,2,1,0:T(1,128)} %get-tuple-element.23), channel_id=1, source_target_pairs={{4,0},{8,4},{12,8},{5,1},{9,5},{13,9},{6,2},{10,6},{14,10},{7,3},{... | collective-permute-start | bytes 393224 | tf_op jit(solution)/shard_map/ppermute | solution.py:19
  53.2 7.7 %collective-permute-start.8 = (f32[2,16,16,1]{3,2,1,0:T(8,128)}, f32[2,16,16,1]{3,2,1,0:T(8,128)S(1)}, u32[]{:S(2)}, u32[]{:S(2)}) collective-permute-start(f32[2,16,16,1]{3,2,1,0:T(8,128)} %get-tuple-element.24), channel_id=1, source_target_pairs={{1,0},{2,1},{3,2},{5,4},{6,5},{7,6},{9,8},{10,9},{11,10},{13,12},{... | collective-permute-start | bytes 6152 | tf_op jit(solution)/shard_map/ppermute | solution.py:19
  60.9 0.7 copy-start.1
  60.9 0.7 copy-start.4
  60.9 0.8 copy-start.7
  67.5 19.2 %collective-permute-start.9 = (f32[2,1,16,1024]{3,2,1,0:T(8,128)}, f32[2,1,16,1024]{3,2,1,0:T(8,128)S(1)}, u32[]{:S(2)}, u32[]{:S(2)}) collective-permute-start(f32[2,1,16,1024]{3,2,1,0:T(8,128)} %get-tuple-element.26), channel_id=1, source_target_pairs={{0,16},{16,32},{32,48},{48,64},{64,80},{80,96},{96,112},{1,17},{17... | collective-permute-start | bytes 393224 | tf_op jit(solution)/shard_map/ppermute | solution.py:24
  72.3 14.4 %collective-permute-start.10 = (f32[2,16,1,1024]{3,2,1,0:T(1,128)}, f32[2,16,1,1024]{3,2,1,0:T(1,128)S(1)}, u32[]{:S(2)}, u32[]{:S(2)}) collective-permute-start(f32[2,16,1,1024]{3,2,1,0:T(1,128)} %get-tuple-element.27), channel_id=1, source_target_pairs={{0,4},{4,8},{8,12},{1,5},{5,9},{9,13},{2,6},{6,10},{10,14},{3,7},{... | collective-permute-start | bytes 393224 | tf_op jit(solution)/shard_map/ppermute | solution.py:24
  79.7 7.0 %collective-permute-start.11 = (f32[2,16,16,1]{3,2,1,0:T(8,128)}, f32[2,16,16,1]{3,2,1,0:T(8,128)S(1)}, u32[]{:S(2)}, u32[]{:S(2)}) collective-permute-start(f32[2,16,16,1]{3,2,1,0:T(8,128)} %get-tuple-element.28), channel_id=1, source_target_pairs={{0,1},{1,2},{2,3},{4,5},{5,6},{6,7},{8,9},{9,10},{10,11},{12,13},{... | collective-permute-start | bytes 6152 | tf_op jit(solution)/shard_map/ppermute | solution.py:24
  86.7 0.7 copy-start
  86.7 0.7 copy-start.8
  86.7 0.8 copy-start.11
  102.2 2.9 %copy-start.13 = (s32[1,1,1,1024]{3,2,1,0:T(1,128)S(1)}, s32[1,1,1,1024]{3,2,1,0:T(1,128)}, u32[]{:S(2)}) copy-start(s32[1,1,1,1024]{3,2,1,0:T(1,128)} %param.13) | copy-start | bytes 12292
  102.2 2.9 %copy-start.14 = (s32[1,1,1,1024,1]{3,4,2,1,0:T(1,128)S(1)}, s32[1,1,1,1024,1]{3,4,2,1,0:T(1,128)}, u32[]{:S(2)}) copy-start(s32[1,1,1,1024,1]{3,4,2,1,0:T(1,128)} %param.12) | copy-start | bytes 12292

commit v4 on v3

--- a/solution.py
+++ b/solution.py
@@ -159,7 +159,7 @@
     chunk = CHUNK
     faces_x = toward_lower(faces[0], "gx")
     faces_y = toward_lower(faces[1], "gy")
-    faces_z = toward_lower(faces[2], "gz")
+    faces_z = toward_lower(faces[2].reshape(2, nx * ny), "gz").reshape(2, nx, ny, 1)
     return pl.pallas_call(
         h_kernel,
         grid=(nx // chunk,),
@@ -181,7 +181,7 @@
     chunk = CHUNK
     faces_x = toward_upper(faces[0], "gx")
     faces_y = toward_upper(faces[1], "gy")
-    faces_z = toward_upper(faces[2], "gz")
+    faces_z = toward_upper(faces[2].reshape(2, nx * ny), "gz").reshape(2, nx, ny, 1)
     in_specs = [
         field_spec(nx, ny, nz, chunk),
         field_spec(nx, ny, nz, chunk),

time: 128 us -> 119 us (0.930)
  waiting for transfers between devices: 22.1 us -> 9.62 us
  other arithmetic: 3.62 us -> 6.89 us
  local copies, waits for them, and re-layouts: 14.6 us -> 17.7 us
  starting transfers between devices: 39.9 us -> 38.2 us
    ppermute x6, waiting for transfers between devices: 15 us -> 8.23 us  [toward_lower(): return lax.ppermute(x, axis, [(j, j - 1) for j in range(1, peers)])]
    ppermute x6, waiting for transfers between devices: 7.15 us -> 1.39 us  [toward_upper(): return lax.ppermute(x, axis, [(j, j + 1) for j in range(peers - 1)])]
    reshape x0 -> x8, local copies, waits for them, and re-layouts: none -> 3.97 us  [the longest x2 1.82 us: h_step(): toward_lower(faces[2].reshape(2, nx * ny), 'gz').reshape(2, nx, ny, 1)]
    pallas_call x0 -> x3, other arithmetic: none -> 3.27 us  [the longest x2 2.18 us: h_step(): pl.pallas_call(h_kernel, grid=(nx // chunk,), in_specs=[field_spec(nx, ny...]
    ppermute x6, starting transfers between devices: 29.5 us -> 27.9 us  [toward_upper(): return lax.ppermute(x, axis, [(j, j + 1) for j in range(peers - 1)])]
    unnamed x30 -> x22, local copies, waits for them, and re-layouts: 3.66 us -> 2.67 us
  transfers between devices with their start and end apart: 12 -> 12, of which waited for: 4 -> 6; matrix products, arithmetic and copies ran while one was open for 2% -> 8% of each run, Pallas kernels for 0% -> 0%
where the time goes in v4:
time: 119 us; the launch traced here: 118 us
  starting transfers between devices  38.2 us (32%)
  Pallas kernels  24.8 us (21%)
  blocking collectives  18.8 us (16%)
  local copies, waits for them, and re-layouts  17.7 us (15%)
  waiting for transfers between devices  9.62 us (8%)
  other arithmetic  6.89 us (6%)
    ppermute x6, starting transfers between devices, toward_upper(): return lax.ppermute(x, axis, [(j, j + 1) for j in range(peers - 1)])  27.9 us
    all_to_all x1, blocking collectives, body(): received = lax.all_to_all(per_owner, ('gx', 'gy', 'gz'), 0, 0, tiled=True)  18.8 us
    pallas_call x2, Pallas kernels, h_step(): pl.pallas_call(h_kernel, grid=(nx // chunk,), in_specs=[field_spec(nx, ny...  11.7 us
    ppermute x6, starting transfers between devices, toward_lower(): return lax.ppermute(x, axis, [(j, j - 1) for j in range(1, peers)])  10.3 us
    ppermute x6, waiting for transfers between devices, toward_lower(): return lax.ppermute(x, axis, [(j, j - 1) for j in range(1, peers)])  8.23 us
    gather x1, local copies, waits for them, and re-layouts, body(): rows = intersection.reshape(nx * ny, nz)[voxel_rows // nz]  7.6 us
    pallas_call x1, Pallas kernels, e_step(): pl.pallas_call(e_last_kernel, grid=(nx // chunk,), in_specs=in_specs + [f...  7.12 us
    pallas_call x1, Pallas kernels, e_step(): pl.pallas_call(e_kernel, grid=(nx // chunk,), in_specs=in_specs, out_spec...  6.03 us
  transfers between devices with their start and end apart: 12, of which 6 were waited for; matrix products, arithmetic and copies ran while one was open for 8% of the time, Pallas kernels for 0%

profile of v4, /device:TPU:1, one launch (start us, length us, event | category | flops | bytes accessed | tf_op | source)
XLA Modules:
  0.0 118.0 jit_solution(12536296111867314001)
XLA Ops:
  0.6 0.9 slice.9
  1.6 1.3 %collective-permute-start = (f32[2,1,16,1024]{3,2,1,0:T(8,128)S(1)}, f32[2,1,16,1024]{3,2,1,0:T(8,128)S(1)}, u32[]{:S(2)}, u32[]{:S(2)}) collective-permute-start(f32[2,1,16,1024]{3,2,1,0:T(8,128)S(1)} %slice.9), channel_id=1, source_target_pairs={{16,0},{32,16},{48,32},{64,48},{80,64},{96,80},{112,96},{17,1},{33... | collective-permute-start | bytes 393224 | tf_op jit(solution)/shard_map/ppermute | solution.py:19
  2.9 1.3 %slice.10 = f32[2,16,1,1024]{3,2,1,0:T(1,128)S(1)} slice(f32[3,16,16,1024]{3,2,1,0:T(8,128)} %e_ref.3), slice={[0:3:2], [0:16:1], [0:1:1], [0:1024:1]} | slice | bytes 262144 | tf_op jit(solution)/shard_map/slice | solution.py:154
  4.2 3.3 %collective-permute-start.1 = (f32[2,16,1,1024]{3,2,1,0:T(1,128)S(1)}, f32[2,16,1,1024]{3,2,1,0:T(1,128)S(1)}, u32[]{:S(2)}, u32[]{:S(2)}) collective-permute-start(f32[2,16,1,1024]{3,2,1,0:T(1,128)S(1)} %slice.10), channel_id=1, source_target_pairs={{4,0},{8,4},{12,8},{5,1},{9,5},{13,9},{6,2},{10,6},{14,10},{7,3},{... | collective-permute-start | bytes 393224 | tf_op jit(solution)/shard_map/ppermute | solution.py:19
  7.5 1.1 slice_reduce_fusion
  8.6 1.3 %collective-permute-start.2 = (f32[2,256]{1,0:T(2,128)S(1)}, f32[2,256]{1,0:T(2,128)S(1)}, u32[]{:S(2)}, u32[]{:S(2)}) collective-permute-start(f32[2,256]{1,0:T(2,128)S(1)} %reshape.143), channel_id=1, source_target_pairs={{1,0},{2,1},{3,2},{5,4},{6,5},{7,6},{9,8},{10,9},{11,10},{13,12},{... | collective-permute-start | bytes 6152 | tf_op jit(solution)/shard_map/ppermute | solution.py:19
  9.9 3.2 %collective-permute-done.2 = f32[2,256]{1,0:T(2,128)S(1)} collective-permute-done((f32[2,256]{1,0:T(2,128)S(1)}, f32[2,256]{1,0:T(2,128)S(1)}, u32[]{:S(2)}, u32[]{:S(2)}) %collective-permute-start.2) | collective-permute-done | bytes 2080 | tf_op jit(solution)/shard_map/ppermute | solution.py:19
  13.1 0.9 reshape.162.hz_ref
  14.0 1.2 %collective-permute-done.1.hy_ref = f32[2,16,1,1024]{3,2,1,0:T(1,128)S(1)} collective-permute-done((f32[2,16,1,1024]{3,2,1,0:T(1,128)S(1)}, f32[2,16,1,1024]{3,2,1,0:T(1,128)S(1)}, u32[]{:S(2)}, u32[]{:S(2)}) %collective-permute-start.1) | collective-permute-done | bytes 131104 | tf_op jit(solution)/shard_map/ppermute | solution.py:19
  15.9 5.8 %shard_map.94 = (f32[3,16,16,1024]{3,2,1,0:T(8,128)}, f32[2,1,16,1024]{3,2,1,0:T(8,128)}, f32[2,16,1,1024]{3,2,1,0:T(1,128)}, f32[2,16,16,1]{3,2,1,0:T(8,128)}) custom-call(f32[3,16,16,1024]{3,2,1,0:T(8,128)} %e_ref.3, f32[3,16,16,1024]{3,2,1,0:T(8,128)} %e_ref.3, f32[3,16,16,1024]{3,2,1,0:T(8,128)} %h_ref.1, f32[2,1,16,1024]{3,2,1,0:T(8,128)} %copy-done.4, ...), custom_call_target="tpu_custom_call" | custom-call | tf_op jit(solution)/shard_map/pallas_call | solution.py:163
  21.8 3.7 %collective-permute-start.3 = (f32[2,1,16,1024]{3,2,1,0:T(8,128)}, f32[2,1,16,1024]{3,2,1,0:T(8,128)S(1)}, u32[]{:S(2)}, u32[]{:S(2)}) collective-permute-start(f32[2,1,16,1024]{3,2,1,0:T(8,128)} %get-tuple-element.18), channel_id=1, source_target_pairs={{0,16},{16,32},{32,48},{48,64},{64,80},{80,96},{96,112},{1,17},{17... | collective-permute-start | bytes 393224 | tf_op jit(solution)/shard_map/ppermute | solution.py:24
  25.4 6.8 %collective-permute-start.4 = (f32[2,16,1,1024]{3,2,1,0:T(1,128)}, f32[2,16,1,1024]{3,2,1,0:T(1,128)S(1)}, u32[]{:S(2)}, u32[]{:S(2)}) collective-permute-start(f32[2,16,1,1024]{3,2,1,0:T(1,128)} %get-tuple-element.19), channel_id=1, source_target_pairs={{0,4},{4,8},{8,12},{1,5},{5,9},{9,13},{2,6},{6,10},{10,14},{3,7},{... | collective-permute-start | bytes 393224 | tf_op jit(solution)/shard_map/ppermute | solution.py:24
  32.2 1.1 reduce.2
  33.4 3.2 %collective-permute-start.5 = (f32[2,256]{1,0:T(2,128)S(1)}, f32[2,256]{1,0:T(2,128)S(1)}, u32[]{:S(2)}, u32[]{:S(2)}) collective-permute-start(f32[2,256]{1,0:T(2,128)S(1)} %reshape.145), channel_id=1, source_target_pairs={{0,1},{1,2},{2,3},{4,5},{5,6},{6,7},{8,9},{9,10},{10,11},{12,13},{... | collective-permute-start | bytes 6152 | tf_op jit(solution)/shard_map/ppermute | solution.py:24
  39.0 6.0 %shard_map.95 = (f32[3,16,16,1024]{3,2,1,0:T(8,128)}, f32[2,1,16,1024]{3,2,1,0:T(8,128)}, f32[2,16,1,1024]{3,2,1,0:T(1,128)}, f32[2,16,16,1]{3,2,1,0:T(8,128)}) custom-call(f32[3,16,16,1024]{3,2,1,0:T(8,128)} %e_ref.3, f32[3,16,16,1024]{3,2,1,0:T(8,128)} %get-tuple-element.17.h_ref.hp_ref, f32[3,16,16,1024]{3,2,1,0:T(8,128)} %get-tuple-element.17.h_ref.hp_ref, ...), custom_call_target="tpu_custom_call" | custom-call | tf_op jit(solution)/shard_map/pallas_call | solution.py:196
  45.0 1.3 %collective-permute-start.6 = (f32[2,1,16,1024]{3,2,1,0:T(8,128)}, f32[2,1,16,1024]{3,2,1,0:T(8,128)S(1)}, u32[]{:S(2)}, u32[]{:S(2)}) collective-permute-start(f32[2,1,16,1024]{3,2,1,0:T(8,128)} %get-tuple-element.22), channel_id=1, source_target_pairs={{16,0},{32,16},{48,32},{64,48},{80,64},{96,80},{112,96},{17,1},{33... | collective-permute-start | bytes 393224 | tf_op jit(solution)/shard_map/ppermute | solution.py:19
  46.3 1.9 %collective-permute-start.7 = (f32[2,16,1,1024]{3,2,1,0:T(1,128)}, f32[2,16,1,1024]{3,2,1,0:T(1,128)S(1)}, u32[]{:S(2)}, u32[]{:S(2)}) collective-permute-start(f32[2,16,1,1024]{3,2,1,0:T(1,128)} %get-tuple-element.23), channel_id=1, source_target_pairs={{4,0},{8,4},{12,8},{5,1},{9,5},{13,9},{6,2},{10,6},{14,10},{7,3},{... | collective-permute-start | bytes 393224 | tf_op jit(solution)/shard_map/ppermute | solution.py:19
  48.2 1.1 reduce.3
  49.4 1.3 %collective-permute-start.8 = (f32[2,256]{1,0:T(2,128)S(1)}, f32[2,256]{1,0:T(2,128)S(1)}, u32[]{:S(2)}, u32[]{:S(2)}) collective-permute-start(f32[2,256]{1,0:T(2,128)S(1)} %reshape.147), channel_id=1, source_target_pairs={{1,0},{2,1},{3,2},{5,4},{6,5},{7,6},{9,8},{10,9},{11,10},{13,12},{... | collective-permute-start | bytes 6152 | tf_op jit(solution)/shard_map/ppermute | solution.py:19
  50.7 3.3 %collective-permute-done.8 = f32[2,256]{1,0:T(2,128)S(1)} collective-permute-done((f32[2,256]{1,0:T(2,128)S(1)}, f32[2,256]{1,0:T(2,128)S(1)}, u32[]{:S(2)}, u32[]{:S(2)}) %collective-permute-start.8) | collective-permute-done | bytes 2080 | tf_op jit(solution)/shard_map/ppermute | solution.py:19
  54.0 0.9 reshape.164.hz_ref
  56.1 5.9 %shard_map.96 = (f32[3,16,16,1024]{3,2,1,0:T(8,128)}, f32[2,1,16,1024]{3,2,1,0:T(8,128)}, f32[2,16,1,1024]{3,2,1,0:T(1,128)}, f32[2,16,16,1]{3,2,1,0:T(8,128)}) custom-call(f32[3,16,16,1024]{3,2,1,0:T(8,128)} %get-tuple-element.21.e_ref.en_ref, f32[3,16,16,1024]{3,2,1,0:T(8,128)} %get-tuple-element.21.e_ref.en_ref, ...), custom_call_target="tpu_custom_call" | custom-call | tf_op jit(solution)/shard_map/pallas_call | solution.py:163
  61.9 3.7 %collective-permute-start.9 = (f32[2,1,16,1024]{3,2,1,0:T(8,128)}, f32[2,1,16,1024]{3,2,1,0:T(8,128)S(1)}, u32[]{:S(2)}, u32[]{:S(2)}) collective-permute-start(f32[2,1,16,1024]{3,2,1,0:T(8,128)} %get-tuple-element.26), channel_id=1, source_target_pairs={{0,16},{16,32},{32,48},{48,64},{64,80},{80,96},{96,112},{1,17},{17... | collective-permute-start | bytes 393224 | tf_op jit(solution)/shard_map/ppermute | solution.py:24
  65.6 6.9 %collective-permute-start.10 = (f32[2,16,1,1024]{3,2,1,0:T(1,128)}, f32[2,16,1,1024]{3,2,1,0:T(1,128)S(1)}, u32[]{:S(2)}, u32[]{:S(2)}) collective-permute-start(f32[2,16,1,1024]{3,2,1,0:T(1,128)} %get-tuple-element.27), channel_id=1, source_target_pairs={{0,4},{4,8},{8,12},{1,5},{5,9},{9,13},{2,6},{6,10},{10,14},{3,7},{... | collective-permute-start | bytes 393224 | tf_op jit(solution)/shard_map/ppermute | solution.py:24
  72.5 1.1 reduce.4
  73.7 3.6 %collective-permute-start.11 = (f32[2,256]{1,0:T(2,128)S(1)}, f32[2,256]{1,0:T(2,128)S(1)}, u32[]{:S(2)}, u32[]{:S(2)}) collective-permute-start(f32[2,256]{1,0:T(2,128)S(1)} %reshape.149), channel_id=1, source_target_pairs={{0,1},{1,2},{2,3},{4,5},{5,6},{6,7},{8,9},{9,10},{10,11},{12,13},{... | collective-permute-start | bytes 6152 | tf_op jit(solution)/shard_map/ppermute | solution.py:24
  78.0 0.9 reshape.165.hz_ref
  79.6 7.1 %shard_map.97 = (f32[3,16,16,1024]{3,2,1,0:T(8,128)}, f32[16,16,1024]{2,1,0:T(8,128)}) custom-call(f32[3,16,16,1024]{3,2,1,0:T(8,128)} %get-tuple-element.21.e_ref.en_ref, f32[3,16,16,1024]{3,2,1,0:T(8,128)} %get-tuple-element.15.h_ref.hp_ref, f32[3,16,16,1024]{3,2,1,0:T(8,128)} %get-tuple-element.15.h_ref.hp_ref, f32[16,16,1024]{2,1,0:T(8,128)} %inv_ref.3, ...), custom_call_target="tpu_custom_call" | custom-call | tf_op jit(solution)/shard_map/pallas_call | solution.py:204
  86.8 7.6 %gather_fusion = f32[1024,1024]{1,0:T(8,128)} fusion(f32[256,1024]{1,0:T(8,128)} %bitcast.17, s32[1024]{0:T(1024)S(1)} %broadcast_clamp_fusion), kind=kCustom, calls=%fused_computation | custom fusion | bytes 8392704 | tf_op jit(solution)/shard_map/gather | solution.py:228
  94.4 2.9 %select_reduce_fusion = f32[1024]{0:T(1024)S(1)} fusion(f32[1024,1024]{1,0:T(8,128)} %gather_fusion, s32[1024]{0:T(1024)S(1)} %add_select_fusion), kind=kLoop, calls=%fused_computation.1 | loop fusion | flops 3144704 | bytes 4202496 | tf_op jit(solution)/shard_map/reduce_sum | solution.py:230
  97.2 1.1 convolution_bitcast_fusion
  98.5 18.8 %all_to_all.9 = f32[128,1,256]{2,1,0:T(1,128)S(1)} all-to-all(f32[128,1,256]{2,1,0:T(1,128)S(1)} %copy.18), channel_id=1, replica_groups=mesh['gx'=8,'gy'=4,'gz'=4] {'gx','gy','gz'}, dimensions={0} | all-to-all | bytes 262144 | tf_op jit(solution)/shard_map/all_to_all | solution.py:235
  (41 shorter events, 6.7 us)
Async XLA Ops:
  1.6 12.5 %collective-permute-start = (f32[2,1,16,1024]{3,2,1,0:T(8,128)S(1)}, f32[2,1,16,1024]{3,2,1,0:T(8,128)S(1)}, u32[]{:S(2)}, u32[]{:S(2)}) collective-permute-start(f32[2,1,16,1024]{3,2,1,0:T(8,128)S(1)} %slice.9), channel_id=1, source_target_pairs={{16,0},{32,16},{48,32},{64,48},{80,64},{96,80},{112,96},{17,1},{33... | collective-permute-start | bytes 393224 | tf_op jit(solution)/shard_map/ppermute | solution.py:19
  4.2 11.1 %collective-permute-start.1 = (f32[2,16,1,1024]{3,2,1,0:T(1,128)S(1)}, f32[2,16,1,1024]{3,2,1,0:T(1,128)S(1)}, u32[]{:S(2)}, u32[]{:S(2)}) collective-permute-start(f32[2,16,1,1024]{3,2,1,0:T(1,128)S(1)} %slice.10), channel_id=1, source_target_pairs={{4,0},{8,4},{12,8},{5,1},{9,5},{13,9},{6,2},{10,6},{14,10},{7,3},{... | collective-permute-start | bytes 393224 | tf_op jit(solution)/shard_map/ppermute | solution.py:19
  8.6 4.5 %collective-permute-start.2 = (f32[2,256]{1,0:T(2,128)S(1)}, f32[2,256]{1,0:T(2,128)S(1)}, u32[]{:S(2)}, u32[]{:S(2)}) collective-permute-start(f32[2,256]{1,0:T(2,128)S(1)} %reshape.143), channel_id=1, source_target_pairs={{1,0},{2,1},{3,2},{5,4},{6,5},{7,6},{9,8},{10,9},{11,10},{13,12},{... | collective-permute-start | bytes 6152 | tf_op jit(solution)/shard_map/ppermute | solution.py:19
  14.0 22.6 %copy-start.8 = (s32[1,1,1,1024]{3,2,1,0:T(1,128)S(1)}, s32[1,1,1,1024]{3,2,1,0:T(1,128)}, u32[]{:S(2)}) copy-start(s32[1,1,1,1024]{3,2,1,0:T(1,128)} %param.11) | copy-start | bytes 12292
  14.0 1.3 %copy-start.4 = (f32[2,1,16,1024]{3,2,1,0:T(8,128)}, f32[2,1,16,1024]{3,2,1,0:T(8,128)S(1)}, u32[]{:S(2)}) copy-start(f32[2,1,16,1024]{3,2,1,0:T(8,128)S(1)} %collective-permute-done.hx_ref) | copy-start | bytes 393220
  15.3 0.6 copy-start.7
  21.8 16.5 %collective-permute-start.3 = (f32[2,1,16,1024]{3,2,1,0:T(8,128)}, f32[2,1,16,1024]{3,2,1,0:T(8,128)S(1)}, u32[]{:S(2)}, u32[]{:S(2)}) collective-permute-start(f32[2,1,16,1024]{3,2,1,0:T(8,128)} %get-tuple-element.18), channel_id=1, source_target_pairs={{0,16},{16,32},{32,48},{48,64},{64,80},{80,96},{96,112},{1,17},{17... | collective-permute-start | bytes 393224 | tf_op jit(solution)/shard_map/ppermute | solution.py:24
  25.4 12.8 %collective-permute-start.4 = (f32[2,16,1,1024]{3,2,1,0:T(1,128)}, f32[2,16,1,1024]{3,2,1,0:T(1,128)S(1)}, u32[]{:S(2)}, u32[]{:S(2)}) collective-permute-start(f32[2,16,1,1024]{3,2,1,0:T(1,128)} %get-tuple-element.19), channel_id=1, source_target_pairs={{0,4},{4,8},{8,12},{1,5},{5,9},{9,13},{2,6},{6,10},{10,14},{3,7},{... | collective-permute-start | bytes 393224 | tf_op jit(solution)/shard_map/ppermute | solution.py:24
  33.4 3.9 %collective-permute-start.5 = (f32[2,256]{1,0:T(2,128)S(1)}, f32[2,256]{1,0:T(2,128)S(1)}, u32[]{:S(2)}, u32[]{:S(2)}) collective-permute-start(f32[2,256]{1,0:T(2,128)S(1)} %reshape.145), channel_id=1, source_target_pairs={{0,1},{1,2},{2,3},{4,5},{5,6},{6,7},{8,9},{9,10},{10,11},{12,13},{... | collective-permute-start | bytes 6152 | tf_op jit(solution)/shard_map/ppermute | solution.py:24
  38.3 0.6 copy-start.1
  38.3 0.7 copy-start.5
  45.0 9.9 %collective-permute-start.6 = (f32[2,1,16,1024]{3,2,1,0:T(8,128)}, f32[2,1,16,1024]{3,2,1,0:T(8,128)S(1)}, u32[]{:S(2)}, u32[]{:S(2)}) collective-permute-start(f32[2,1,16,1024]{3,2,1,0:T(8,128)} %get-tuple-element.22), channel_id=1, source_target_pairs={{16,0},{32,16},{48,32},{64,48},{80,64},{96,80},{112,96},{17,1},{33... | collective-permute-start | bytes 393224 | tf_op jit(solution)/shard_map/ppermute | solution.py:19
  46.3 9.1 %collective-permute-start.7 = (f32[2,16,1,1024]{3,2,1,0:T(1,128)}, f32[2,16,1,1024]{3,2,1,0:T(1,128)S(1)}, u32[]{:S(2)}, u32[]{:S(2)}) collective-permute-start(f32[2,16,1,1024]{3,2,1,0:T(1,128)} %get-tuple-element.23), channel_id=1, source_target_pairs={{4,0},{8,4},{12,8},{5,1},{9,5},{13,9},{6,2},{10,6},{14,10},{7,3},{... | collective-permute-start | bytes 393224 | tf_op jit(solution)/shard_map/ppermute | solution.py:19
  49.4 4.6 %collective-permute-start.8 = (f32[2,256]{1,0:T(2,128)S(1)}, f32[2,256]{1,0:T(2,128)S(1)}, u32[]{:S(2)}, u32[]{:S(2)}) collective-permute-start(f32[2,256]{1,0:T(2,128)S(1)} %reshape.147), channel_id=1, source_target_pairs={{1,0},{2,1},{3,2},{5,4},{6,5},{7,6},{9,8},{10,9},{11,10},{13,12},{... | collective-permute-start | bytes 6152 | tf_op jit(solution)/shard_map/ppermute | solution.py:19
  54.9 0.6 copy-start
  55.4 0.6 copy-start.3
  61.9 17.0 %collective-permute-start.9 = (f32[2,1,16,1024]{3,2,1,0:T(8,128)}, f32[2,1,16,1024]{3,2,1,0:T(8,128)S(1)}, u32[]{:S(2)}, u32[]{:S(2)}) collective-permute-start(f32[2,1,16,1024]{3,2,1,0:T(8,128)} %get-tuple-element.26), channel_id=1, source_target_pairs={{0,16},{16,32},{32,48},{48,64},{64,80},{80,96},{96,112},{1,17},{17... | collective-permute-start | bytes 393224 | tf_op jit(solution)/shard_map/ppermute | solution.py:24
  65.6 13.4 %collective-permute-start.10 = (f32[2,16,1,1024]{3,2,1,0:T(1,128)}, f32[2,16,1,1024]{3,2,1,0:T(1,128)S(1)}, u32[]{:S(2)}, u32[]{:S(2)}) collective-permute-start(f32[2,16,1,1024]{3,2,1,0:T(1,128)} %get-tuple-element.27), channel_id=1, source_target_pairs={{0,4},{4,8},{8,12},{1,5},{5,9},{9,13},{2,6},{6,10},{10,14},{3,7},{... | collective-permute-start | bytes 393224 | tf_op jit(solution)/shard_map/ppermute | solution.py:24
  73.7 4.3 %collective-permute-start.11 = (f32[2,256]{1,0:T(2,128)S(1)}, f32[2,256]{1,0:T(2,128)S(1)}, u32[]{:S(2)}, u32[]{:S(2)}) collective-permute-start(f32[2,256]{1,0:T(2,128)S(1)} %reshape.149), channel_id=1, source_target_pairs={{0,1},{1,2},{2,3},{4,5},{5,6},{6,7},{8,9},{9,10},{10,11},{12,13},{... | collective-permute-start | bytes 6152 | tf_op jit(solution)/shard_map/ppermute | solution.py:24
  78.9 0.6 copy-start.2
  79.0 0.7 copy-start.6
  94.4 2.9 %copy-start.9 = (s32[1,1,1,1024]{3,2,1,0:T(1,128)S(1)}, s32[1,1,1,1024]{3,2,1,0:T(1,128)}, u32[]{:S(2)}) copy-start(s32[1,1,1,1024]{3,2,1,0:T(1,128)} %param.13) | copy-start | bytes 12292
  94.4 2.9 %copy-start.10 = (s32[1,1,1,1024,1]{3,4,2,1,0:T(1,128)S(1)}, s32[1,1,1,1024,1]{3,4,2,1,0:T(1,128)}, u32[]{:S(2)}) copy-start(s32[1,1,1,1024,1]{3,4,2,1,0:T(1,128)} %param.12) | copy-start | bytes 12292

commit v5 on v4

--- a/solution.py
+++ b/solution.py
@@ -122,12 +122,39 @@
     fz_ref[1] = out_ref[1, :, :, 0:1]
 
 
-def e_last_kernel(e_ref, h_ref, hp_ref, inv_ref, hx_ref, hy_ref, hz_ref, ef_ref, out_ref, inter_ref):
+def e_last_kernel(cell_ref, e_ref, h_ref, hp_ref, inv_ref, hx_ref, hy_ref, hz_ref, ef_ref, out_ref, picked_ref, inter_ref):
     new_x, new_y, new_z = e_update(e_ref, h_ref, hp_ref, inv_ref, hx_ref, hy_ref, hz_ref)
     out_ref[0] = new_x
     out_ref[1] = new_y
     out_ref[2] = new_z
-    inter_ref[...] = ef_ref[0] * new_x + ef_ref[1] * new_y + ef_ref[2] * new_z
+    b = new_x.shape[0]
+    step = pl.program_id(0)
+    inter_ref[pl.ds(step * b, b)] = ef_ref[0] * new_x + ef_ref[1] * new_y + ef_ref[2] * new_z
+    _, ny, nz = inter_ref.shape
+    lanes = picked_ref.shape[1]
+
+    @pl.when(step == pl.num_programs(0) - 1)
+    def _():
+        lane_at = lax.broadcasted_iota(jnp.int32, (8, lanes), 1)
+        sub_at = lax.broadcasted_iota(jnp.int32, (8, lanes), 0)
+
+        def pick(g, carry):
+            group = jnp.zeros((8, lanes), jnp.float32)
+            for j in range(8):
+                c = cell_ref[g * 8 + j]
+                x = c // (ny * nz)
+                y = (c // nz) % ny
+                z = c % nz
+                rows = pl.multiple_of((y // 8) * 8, 8)
+                start = pl.multiple_of((z // lanes) * lanes, lanes)
+                tile = inter_ref[x, pl.ds(rows, 8), pl.ds(start, lanes)]
+                hit = (sub_at == y % 8) & (lane_at == z % lanes)
+                row = jnp.sum(jnp.where(hit, tile, 0.0), axis=0, keepdims=True)
+                group = jnp.where(sub_at == j, row, group)
+            picked_ref[pl.ds(pl.multiple_of(g * 8, 8), 8), :] = group
+            return carry
+
+        lax.fori_loop(0, picked_ref.shape[0] // 8, pick, 0)
 
 
 def field_spec(nx, ny, nz, chunk):
@@ -176,7 +203,7 @@
     )(e, e, h, faces_x, faces_y, faces_z)
 
 
-def e_step(e, h, faces, inv, ef=None):
+def e_step(e, h, faces, inv, ef=None, cells=None):
     _, nx, ny, nz = e.shape
     chunk = CHUNK
     faces_x = toward_upper(faces[0], "gx")
@@ -201,33 +228,32 @@
             out_shape=[jax.ShapeDtypeStruct(e.shape, e.dtype)] + face_shapes(nx, ny, nz, e.dtype),
         )(*args)
         return outs[0], outs[1:]
+    count = cells.shape[0]
     return pl.pallas_call(
         e_last_kernel,
         grid=(nx // chunk,),
-        in_specs=in_specs + [field_spec(nx, ny, nz, chunk)],
-        out_specs=[field_spec(nx, ny, nz, chunk), pl.BlockSpec((chunk, ny, nz), lambda i: (i, 0, 0))],
-        out_shape=[jax.ShapeDtypeStruct(e.shape, e.dtype), jax.ShapeDtypeStruct(e.shape[1:], e.dtype)],
-    )(*args, ef)
+        in_specs=[pl.BlockSpec(memory_space=pltpu.SMEM)] + in_specs + [field_spec(nx, ny, nz, chunk)],
+        out_specs=[field_spec(nx, ny, nz, chunk), pl.BlockSpec((count, 128), lambda i: (0, 0))],
+        out_shape=[jax.ShapeDtypeStruct(e.shape, e.dtype), jax.ShapeDtypeStruct((count, 128), e.dtype)],
+        scratch_shapes=[pltpu.VMEM((nx, ny, nz), jnp.float32)],
+    )(cells, *args, ef)
 
 
 def body(e_forward, e_adjoint, h_adjoint, inv_perm, voxel_cell, voxel_owner, voxel_slot):
-    e, h = e_adjoint, h_adjoint
-    e_faces = lower_faces_of(e)
-    intersection = None
-    for repeat in range(STEPS):
-        h, *h_faces = h_step(e, h, e_faces)
-        if repeat == STEPS - 1:
-            e, intersection = e_step(e, h, h_faces, inv_perm, e_forward)
-        else:
-            e, e_faces = e_step(e, h, h_faces, inv_perm)
     count = voxel_cell.shape[-1]
     voxel_rows = voxel_cell.reshape(count)
     owners = voxel_owner.reshape(count)
     slot_ids = voxel_slot.reshape(count)
-    nx, ny, nz = intersection.shape
-    rows = intersection.reshape(nx * ny, nz)[voxel_rows // nz]
-    lanes = lax.broadcasted_iota(jnp.int32, rows.shape, 1)
-    terms = jnp.sum(jnp.where(lanes == (voxel_rows % nz)[:, None], rows, 0.0), axis=1)
+    e, h = e_adjoint, h_adjoint
+    e_faces = lower_faces_of(e)
+    picked = None
+    for repeat in range(STEPS):
+        h, *h_faces = h_step(e, h, e_faces)
+        if repeat == STEPS - 1:
+            e, picked = e_step(e, h, h_faces, inv_perm, e_forward, voxel_rows)
+        else:
+            e, e_faces = e_step(e, h, h_faces, inv_perm)
+    terms = jnp.sum(picked, axis=1)
     devices = lax.axis_size("gx") * lax.axis_size("gy") * lax.axis_size("gz")
     owner_hot = (owners[:, None] == lax.broadcasted_iota(jnp.int32, (count, devices), 1)).astype(jnp.float32)
     slot_hot = jnp.where(slot_ids[:, None] == lax.broadcasted_iota(jnp.int32, (count, P_DEV), 1), terms[:, None], 0.0)

time: 119 us -> 135 us (1.13)
  Pallas kernels: 24.8 us -> 49.9 us
  local copies, waits for them, and re-layouts: 17.7 us -> 10.1 us
  other arithmetic: 6.89 us -> 5.24 us
    pallas_call x1, Pallas kernels: 7.12 us -> 32.1 us  [e_step(): pl.pallas_call(e_last_kernel, grid=(nx // chunk,), in_specs=[pl.BlockSpec...]
    gather x1 -> x0, local copies, waits for them, and re-layouts: 7.6 us -> none  [body(): rows = intersection.reshape(nx * ny, nz)[voxel_rows // nz]]
    reduce_sum x1, other arithmetic: 2.86 us -> 1.25 us  [body(): terms = jnp.sum(picked, axis=1)]
    unnamed x22 -> x20, local copies, waits for them, and re-layouts: 2.67 us -> 2.7 us
  transfers between devices with their start and end apart: 12 -> 12, of which waited for: 6 -> 6; matrix products, arithmetic and copies ran while one was open for 8% -> 7% of each run, Pallas kernels for 0% -> 0%
where the time goes in v5:
time: 135 us; the launch traced here: 134 us
  Pallas kernels  49.9 us (37%)
  starting transfers between devices  38.2 us (28%)
  blocking collectives  18.8 us (14%)
  local copies, waits for them, and re-layouts  10.1 us (7%)
  waiting for transfers between devices  9.69 us (7%)
  other arithmetic  5.24 us (4%)
    pallas_call x1, Pallas kernels, e_step(): pl.pallas_call(e_last_kernel, grid=(nx // chunk,), in_specs=[pl.BlockSpec...  32.1 us
    ppermute x6, starting transfers between devices, toward_upper(): return lax.ppermute(x, axis, [(j, j + 1) for j in range(peers - 1)])  27.9 us
    all_to_all x1, blocking collectives, body(): received = lax.all_to_all(per_owner, ('gx', 'gy', 'gz'), 0, 0, tiled=True)  18.8 us
    pallas_call x2, Pallas kernels, h_step(): pl.pallas_call(h_kernel, grid=(nx // chunk,), in_specs=[field_spec(nx, ny...  11.7 us
    ppermute x6, starting transfers between devices, toward_lower(): return lax.ppermute(x, axis, [(j, j - 1) for j in range(1, peers)])  10.3 us
    ppermute x6, waiting for transfers between devices, toward_lower(): return lax.ppermute(x, axis, [(j, j - 1) for j in range(1, peers)])  8.24 us
    pallas_call x1, Pallas kernels, e_step(): pl.pallas_call(e_kernel, grid=(nx // chunk,), in_specs=in_specs, out_spec...  6.04 us
    slice x3, local copies, waits for them, and re-layouts, lower_faces_of(): return (e[1:3, 0:1], e[0::2, :, 0:1, :], e[0:2, :, :, 0:1])  3.31 us
  transfers between devices with their start and end apart: 12, of which 6 were waited for; matrix products, arithmetic and copies ran while one was open for 7% of the time, Pallas kernels for 0%

profile of v5, /device:TPU:1, one launch (start us, length us, event | category | flops | bytes accessed | tf_op | source)
XLA Modules:
  0.0 133.8 jit_solution(11855724403501354045)
XLA Ops:
  0.6 0.9 slice.9
  1.6 1.3 collective-permute-start
  2.9 1.3 slice.10
  4.2 3.3 %collective-permute-start.1 = (f32[2,16,1,1024]{3,2,1,0:T(1,128)S(1)}, f32[2,16,1,1024]{3,2,1,0:T(1,128)S(1)}, u32[]{:S(2)}, u32[]{:S(2)}) collective-permute-start(f32[2,16,1,1024]{3,2,1,0:T(1,128)S(1)} %slice.10), channel_id=1, source_target_pairs={{4,0},{8,4},{12,8},{5,1},{9,5},{13,9},{6,2},{10,6},{14,10},{7,3},{... | collective-permute-start | bytes 393224 | tf_op jit(solution)/shard_map/ppermute | solution.py:19
  7.5 1.1 slice_reduce_fusion
  8.6 1.3 collective-permute-start.2
  9.9 3.2 %collective-permute-done.2 = f32[2,256]{1,0:T(2,128)S(1)} collective-permute-done((f32[2,256]{1,0:T(2,128)S(1)}, f32[2,256]{1,0:T(2,128)S(1)}, u32[]{:S(2)}, u32[]{:S(2)}) %collective-permute-start.2) | collective-permute-done | bytes 2080 | tf_op jit(solution)/shard_map/ppermute | solution.py:19
  13.1 0.9 reshape.47.hz_ref
  14.0 1.3 collective-permute-done.1.hy_ref
  15.9 5.9 %shard_map.94 = (f32[3,16,16,1024]{3,2,1,0:T(8,128)}, f32[2,1,16,1024]{3,2,1,0:T(8,128)}, f32[2,16,1,1024]{3,2,1,0:T(1,128)}, f32[2,16,16,1]{3,2,1,0:T(8,128)}) custom-call(f32[3,16,16,1024]{3,2,1,0:T(8,128)} %e_ref.3, f32[3,16,16,1024]{3,2,1,0:T(8,128)} %e_ref.3, f32[3,16,16,1024]{3,2,1,0:T(8,128)} %h_ref.1, f32[2,1,16,1024]{3,2,1,0:T(8,128)} %copy-done.2, ...), custom_call_target="tpu_custom_call" | custom-call | tf_op jit(solution)/shard_map/pallas_call | solution.py:190
  21.8 3.7 %collective-permute-start.3 = (f32[2,1,16,1024]{3,2,1,0:T(8,128)}, f32[2,1,16,1024]{3,2,1,0:T(8,128)S(1)}, u32[]{:S(2)}, u32[]{:S(2)}) collective-permute-start(f32[2,1,16,1024]{3,2,1,0:T(8,128)} %get-tuple-element.18), channel_id=1, source_target_pairs={{0,16},{16,32},{32,48},{48,64},{64,80},{80,96},{96,112},{1,17},{17... | collective-permute-start | bytes 393224 | tf_op jit(solution)/shard_map/ppermute | solution.py:24
  25.5 6.8 %collective-permute-start.4 = (f32[2,16,1,1024]{3,2,1,0:T(1,128)}, f32[2,16,1,1024]{3,2,1,0:T(1,128)S(1)}, u32[]{:S(2)}, u32[]{:S(2)}) collective-permute-start(f32[2,16,1,1024]{3,2,1,0:T(1,128)} %get-tuple-element.19), channel_id=1, source_target_pairs={{0,4},{4,8},{8,12},{1,5},{5,9},{9,13},{2,6},{6,10},{10,14},{3,7},{... | collective-permute-start | bytes 393224 | tf_op jit(solution)/shard_map/ppermute | solution.py:24
  32.3 1.1 reduce.2
  33.4 3.2 %collective-permute-start.5 = (f32[2,256]{1,0:T(2,128)S(1)}, f32[2,256]{1,0:T(2,128)S(1)}, u32[]{:S(2)}, u32[]{:S(2)}) collective-permute-start(f32[2,256]{1,0:T(2,128)S(1)} %reshape.41), channel_id=1, source_target_pairs={{0,1},{1,2},{2,3},{4,5},{5,6},{6,7},{8,9},{9,10},{10,11},{12,13},{... | collective-permute-start | bytes 6152 | tf_op jit(solution)/shard_map/ppermute | solution.py:24
  37.4 0.9 reshape.48.hz_ref
  39.0 6.0 %shard_map.95 = (f32[3,16,16,1024]{3,2,1,0:T(8,128)}, f32[2,1,16,1024]{3,2,1,0:T(8,128)}, f32[2,16,1,1024]{3,2,1,0:T(1,128)}, f32[2,16,16,1]{3,2,1,0:T(8,128)}) custom-call(f32[3,16,16,1024]{3,2,1,0:T(8,128)} %e_ref.3, f32[3,16,16,1024]{3,2,1,0:T(8,128)} %get-tuple-element.17.h_ref.hp_ref, f32[3,16,16,1024]{3,2,1,0:T(8,128)} %get-tuple-element.17.h_ref.hp_ref, ...), custom_call_target="tpu_custom_call" | custom-call | tf_op jit(solution)/shard_map/pallas_call | solution.py:223
  45.0 1.3 collective-permute-start.6
  46.3 1.9 %collective-permute-start.7 = (f32[2,16,1,1024]{3,2,1,0:T(1,128)}, f32[2,16,1,1024]{3,2,1,0:T(1,128)S(1)}, u32[]{:S(2)}, u32[]{:S(2)}) collective-permute-start(f32[2,16,1,1024]{3,2,1,0:T(1,128)} %get-tuple-element.23), channel_id=1, source_target_pairs={{4,0},{8,4},{12,8},{5,1},{9,5},{13,9},{6,2},{10,6},{14,10},{7,3},{... | collective-permute-start | bytes 393224 | tf_op jit(solution)/shard_map/ppermute | solution.py:19
  48.2 1.1 reduce.3
  49.4 1.3 collective-permute-start.8
  50.7 3.3 %collective-permute-done.8 = f32[2,256]{1,0:T(2,128)S(1)} collective-permute-done((f32[2,256]{1,0:T(2,128)S(1)}, f32[2,256]{1,0:T(2,128)S(1)}, u32[]{:S(2)}, u32[]{:S(2)}) %collective-permute-start.8) | collective-permute-done | bytes 2080 | tf_op jit(solution)/shard_map/ppermute | solution.py:19
  54.0 0.9 reshape.49.hz_ref
  56.1 5.9 %shard_map.96 = (f32[3,16,16,1024]{3,2,1,0:T(8,128)}, f32[2,1,16,1024]{3,2,1,0:T(8,128)}, f32[2,16,1,1024]{3,2,1,0:T(1,128)}, f32[2,16,16,1]{3,2,1,0:T(8,128)}) custom-call(f32[3,16,16,1024]{3,2,1,0:T(8,128)} %get-tuple-element.21.e_ref.en_ref, f32[3,16,16,1024]{3,2,1,0:T(8,128)} %get-tuple-element.21.e_ref.en_ref, ...), custom_call_target="tpu_custom_call" | custom-call | tf_op jit(solution)/shard_map/pallas_call | solution.py:190
  62.0 3.7 %collective-permute-start.9 = (f32[2,1,16,1024]{3,2,1,0:T(8,128)}, f32[2,1,16,1024]{3,2,1,0:T(8,128)S(1)}, u32[]{:S(2)}, u32[]{:S(2)}) collective-permute-start(f32[2,1,16,1024]{3,2,1,0:T(8,128)} %get-tuple-element.26), channel_id=1, source_target_pairs={{0,16},{16,32},{32,48},{48,64},{64,80},{80,96},{96,112},{1,17},{17... | collective-permute-start | bytes 393224 | tf_op jit(solution)/shard_map/ppermute | solution.py:24
  65.7 6.9 %collective-permute-start.10 = (f32[2,16,1,1024]{3,2,1,0:T(1,128)}, f32[2,16,1,1024]{3,2,1,0:T(1,128)S(1)}, u32[]{:S(2)}, u32[]{:S(2)}) collective-permute-start(f32[2,16,1,1024]{3,2,1,0:T(1,128)} %get-tuple-element.27), channel_id=1, source_target_pairs={{0,4},{4,8},{8,12},{1,5},{5,9},{9,13},{2,6},{6,10},{10,14},{3,7},{... | collective-permute-start | bytes 393224 | tf_op jit(solution)/shard_map/ppermute | solution.py:24
  72.6 1.1 reduce.4
  73.8 3.6 %collective-permute-start.11 = (f32[2,256]{1,0:T(2,128)S(1)}, f32[2,256]{1,0:T(2,128)S(1)}, u32[]{:S(2)}, u32[]{:S(2)}) collective-permute-start(f32[2,256]{1,0:T(2,128)S(1)} %reshape.45), channel_id=1, source_target_pairs={{0,1},{1,2},{2,3},{4,5},{5,6},{6,7},{8,9},{9,10},{10,11},{12,13},{... | collective-permute-start | bytes 6152 | tf_op jit(solution)/shard_map/ppermute | solution.py:24
  78.1 0.9 reshape.50.hz_ref
  79.7 32.1 %shard_map.97 = (f32[3,16,16,1024]{3,2,1,0:T(8,128)}, f32[1024,128]{1,0:T(8,128)}) custom-call(s32[1024]{0:T(1024)} %bitcast.5, f32[3,16,16,1024]{3,2,1,0:T(8,128)} %get-tuple-element.21.e_ref.en_ref, f32[3,16,16,1024]{3,2,1,0:T(8,128)} %get-tuple-element.15.h_ref.hp_ref, f32[3,16,16,1024]{3,2,1,0:T(8,128)} %get-tuple-element.15.h_ref.hp_ref, ...), custom_call_target="tpu_custom_call" | custom-call | tf_op jit(solution)/shard_map/pallas_call | solution.py:232
  111.8 1.2 reduce_sum.18
  113.1 1.1 convolution_bitcast_fusion
  114.3 18.8 %all_to_all.9 = f32[128,1,256]{2,1,0:T(1,128)S(1)} all-to-all(f32[128,1,256]{2,1,0:T(1,128)S(1)} %copy.18), channel_id=1, replica_groups=mesh['gx'=8,'gy'=4,'gz'=4] {'gx','gy','gz'}, dimensions={0} | all-to-all | bytes 262144 | tf_op jit(solution)/shard_map/all_to_all | solution.py:261
  (35 shorter events, 5.9 us)
Async XLA Ops:
  1.6 12.5 %collective-permute-start = (f32[2,1,16,1024]{3,2,1,0:T(8,128)S(1)}, f32[2,1,16,1024]{3,2,1,0:T(8,128)S(1)}, u32[]{:S(2)}, u32[]{:S(2)}) collective-permute-start(f32[2,1,16,1024]{3,2,1,0:T(8,128)S(1)} %slice.9), channel_id=1, source_target_pairs={{16,0},{32,16},{48,32},{64,48},{80,64},{96,80},{112,96},{17,1},{33... | collective-permute-start | bytes 393224 | tf_op jit(solution)/shard_map/ppermute | solution.py:19
  4.2 11.1 %collective-permute-start.1 = (f32[2,16,1,1024]{3,2,1,0:T(1,128)S(1)}, f32[2,16,1,1024]{3,2,1,0:T(1,128)S(1)}, u32[]{:S(2)}, u32[]{:S(2)}) collective-permute-start(f32[2,16,1,1024]{3,2,1,0:T(1,128)S(1)} %slice.10), channel_id=1, source_target_pairs={{4,0},{8,4},{12,8},{5,1},{9,5},{13,9},{6,2},{10,6},{14,10},{7,3},{... | collective-permute-start | bytes 393224 | tf_op jit(solution)/shard_map/ppermute | solution.py:19
  8.6 4.5 %collective-permute-start.2 = (f32[2,256]{1,0:T(2,128)S(1)}, f32[2,256]{1,0:T(2,128)S(1)}, u32[]{:S(2)}, u32[]{:S(2)}) collective-permute-start(f32[2,256]{1,0:T(2,128)S(1)} %reshape.39), channel_id=1, source_target_pairs={{1,0},{2,1},{3,2},{5,4},{6,5},{7,6},{9,8},{10,9},{11,10},{13,12},{... | collective-permute-start | bytes 6152 | tf_op jit(solution)/shard_map/ppermute | solution.py:19
  14.0 1.3 copy-start.2
  15.3 0.7 copy-start.5
  21.8 16.5 %collective-permute-start.3 = (f32[2,1,16,1024]{3,2,1,0:T(8,128)}, f32[2,1,16,1024]{3,2,1,0:T(8,128)S(1)}, u32[]{:S(2)}, u32[]{:S(2)}) collective-permute-start(f32[2,1,16,1024]{3,2,1,0:T(8,128)} %get-tuple-element.18), channel_id=1, source_target_pairs={{0,16},{16,32},{32,48},{48,64},{64,80},{80,96},{96,112},{1,17},{17... | collective-permute-start | bytes 393224 | tf_op jit(solution)/shard_map/ppermute | solution.py:24
  25.5 12.8 %collective-permute-start.4 = (f32[2,16,1,1024]{3,2,1,0:T(1,128)}, f32[2,16,1,1024]{3,2,1,0:T(1,128)S(1)}, u32[]{:S(2)}, u32[]{:S(2)}) collective-permute-start(f32[2,16,1,1024]{3,2,1,0:T(1,128)} %get-tuple-element.19), channel_id=1, source_target_pairs={{0,4},{4,8},{8,12},{1,5},{5,9},{9,13},{2,6},{6,10},{10,14},{3,7},{... | collective-permute-start | bytes 393224 | tf_op jit(solution)/shard_map/ppermute | solution.py:24
  33.4 3.9 %collective-permute-start.5 = (f32[2,256]{1,0:T(2,128)S(1)}, f32[2,256]{1,0:T(2,128)S(1)}, u32[]{:S(2)}, u32[]{:S(2)}) collective-permute-start(f32[2,256]{1,0:T(2,128)S(1)} %reshape.41), channel_id=1, source_target_pairs={{0,1},{1,2},{2,3},{4,5},{5,6},{6,7},{8,9},{9,10},{10,11},{12,13},{... | collective-permute-start | bytes 6152 | tf_op jit(solution)/shard_map/ppermute | solution.py:24
  38.3 0.7 copy-start.1
  38.3 0.7 copy-start.4
  45.0 9.9 %collective-permute-start.6 = (f32[2,1,16,1024]{3,2,1,0:T(8,128)}, f32[2,1,16,1024]{3,2,1,0:T(8,128)S(1)}, u32[]{:S(2)}, u32[]{:S(2)}) collective-permute-start(f32[2,1,16,1024]{3,2,1,0:T(8,128)} %get-tuple-element.22), channel_id=1, source_target_pairs={{16,0},{32,16},{48,32},{64,48},{80,64},{96,80},{112,96},{17,1},{33... | collective-permute-start | bytes 393224 | tf_op jit(solution)/shard_map/ppermute | solution.py:19
  46.3 9.1 %collective-permute-start.7 = (f32[2,16,1,1024]{3,2,1,0:T(1,128)}, f32[2,16,1,1024]{3,2,1,0:T(1,128)S(1)}, u32[]{:S(2)}, u32[]{:S(2)}) collective-permute-start(f32[2,16,1,1024]{3,2,1,0:T(1,128)} %get-tuple-element.23), channel_id=1, source_target_pairs={{4,0},{8,4},{12,8},{5,1},{9,5},{13,9},{6,2},{10,6},{14,10},{7,3},{... | collective-permute-start | bytes 393224 | tf_op jit(solution)/shard_map/ppermute | solution.py:19
  49.4 4.6 %collective-permute-start.8 = (f32[2,256]{1,0:T(2,128)S(1)}, f32[2,256]{1,0:T(2,128)S(1)}, u32[]{:S(2)}, u32[]{:S(2)}) collective-permute-start(f32[2,256]{1,0:T(2,128)S(1)} %reshape.43), channel_id=1, source_target_pairs={{1,0},{2,1},{3,2},{5,4},{6,5},{7,6},{9,8},{10,9},{11,10},{13,12},{... | collective-permute-start | bytes 6152 | tf_op jit(solution)/shard_map/ppermute | solution.py:19
  54.9 0.6 copy-start
  55.5 0.6 copy-start.3
  62.0 17.0 %collective-permute-start.9 = (f32[2,1,16,1024]{3,2,1,0:T(8,128)}, f32[2,1,16,1024]{3,2,1,0:T(8,128)S(1)}, u32[]{:S(2)}, u32[]{:S(2)}) collective-permute-start(f32[2,1,16,1024]{3,2,1,0:T(8,128)} %get-tuple-element.26), channel_id=1, source_target_pairs={{0,16},{16,32},{32,48},{48,64},{64,80},{80,96},{96,112},{1,17},{17... | collective-permute-start | bytes 393224 | tf_op jit(solution)/shard_map/ppermute | solution.py:24
  65.7 13.4 %collective-permute-start.10 = (f32[2,16,1,1024]{3,2,1,0:T(1,128)}, f32[2,16,1,1024]{3,2,1,0:T(1,128)S(1)}, u32[]{:S(2)}, u32[]{:S(2)}) collective-permute-start(f32[2,16,1,1024]{3,2,1,0:T(1,128)} %get-tuple-element.27), channel_id=1, source_target_pairs={{0,4},{4,8},{8,12},{1,5},{5,9},{9,13},{2,6},{6,10},{10,14},{3,7},{... | collective-permute-start | bytes 393224 | tf_op jit(solution)/shard_map/ppermute | solution.py:24
  73.8 4.3 %collective-permute-start.11 = (f32[2,256]{1,0:T(2,128)S(1)}, f32[2,256]{1,0:T(2,128)S(1)}, u32[]{:S(2)}, u32[]{:S(2)}) collective-permute-start(f32[2,256]{1,0:T(2,128)S(1)} %reshape.45), channel_id=1, source_target_pairs={{0,1},{1,2},{2,3},{4,5},{5,6},{6,7},{8,9},{9,10},{10,11},{12,13},{... | collective-permute-start | bytes 6152 | tf_op jit(solution)/shard_map/ppermute | solution.py:24
  79.0 0.7 copy-start.6
  79.0 0.7 copy-start.7
  79.7 33.4 %copy-start.8 = (s32[1,1,1,1024]{3,2,1,0:T(1,128)S(1)}, s32[1,1,1,1024]{3,2,1,0:T(1,128)}, u32[]{:S(2)}) copy-start(s32[1,1,1,1024]{3,2,1,0:T(1,128)} %param.13) | copy-start | bytes 12292
  79.7 33.4 %copy-start.9 = (s32[1,1,1,1024,1]{3,4,2,1,0:T(1,128)S(1)}, s32[1,1,1,1024,1]{3,4,2,1,0:T(1,128)}, u32[]{:S(2)}) copy-start(s32[1,1,1,1024,1]{3,4,2,1,0:T(1,128)} %param.12) | copy-start | bytes 12292

commit v6 on v4

--- a/solution.py
+++ b/solution.py
@@ -122,12 +122,34 @@
     fz_ref[1] = out_ref[1, :, :, 0:1]
 
 
-def e_last_kernel(e_ref, h_ref, hp_ref, inv_ref, hx_ref, hy_ref, hz_ref, ef_ref, out_ref, inter_ref):
+def e_last_kernel(
+    e_ref, h_ref, hp_ref, inv_ref, hx_ref, hy_ref, hz_ref, ef_ref, zrow_ref, rrow_ref, out_ref, terms_ref, zhot_ref
+):
     new_x, new_y, new_z = e_update(e_ref, h_ref, hp_ref, inv_ref, hx_ref, hy_ref, hz_ref)
     out_ref[0] = new_x
     out_ref[1] = new_y
     out_ref[2] = new_z
-    inter_ref[...] = ef_ref[0] * new_x + ef_ref[1] * new_y + ef_ref[2] * new_z
+    step = pl.program_id(0)
+    b, ny, nz = new_x.shape
+    count = zhot_ref.shape[1]
+
+    @pl.when(step == 0)
+    def _():
+        zhot_ref[...] = (lax.broadcasted_iota(jnp.int32, (nz, count), 0) == zrow_ref[...]).astype(jnp.bfloat16)
+        terms_ref[...] = jnp.zeros_like(terms_ref)
+
+    inter = (ef_ref[0] * new_x + ef_ref[1] * new_y + ef_ref[2] * new_z).reshape(b * ny, nz)
+    hi = inter.astype(jnp.bfloat16)
+    rest = inter - hi.astype(jnp.float32)
+    mid = rest.astype(jnp.bfloat16)
+    lo = (rest - mid.astype(jnp.float32)).astype(jnp.bfloat16)
+    zhot = zhot_ref[...]
+    picked = (
+        jnp.dot(hi, zhot, preferred_element_type=jnp.float32)
+        + jnp.dot(mid, zhot, preferred_element_type=jnp.float32)
+    ) + jnp.dot(lo, zhot, preferred_element_type=jnp.float32)
+    row_at = step * (b * ny) + lax.broadcasted_iota(jnp.int32, picked.shape, 0)
+    terms_ref[...] += jnp.sum(jnp.where(row_at == rrow_ref[...], picked, 0.0), axis=0, keepdims=True)
 
 
 def field_spec(nx, ny, nz, chunk):
@@ -176,7 +198,7 @@
     )(e, e, h, faces_x, faces_y, faces_z)
 
 
-def e_step(e, h, faces, inv, ef=None):
+def e_step(e, h, faces, inv, ef=None, cells=None):
     _, nx, ny, nz = e.shape
     chunk = CHUNK
     faces_x = toward_upper(faces[0], "gx")
@@ -201,33 +223,39 @@
             out_shape=[jax.ShapeDtypeStruct(e.shape, e.dtype)] + face_shapes(nx, ny, nz, e.dtype),
         )(*args)
         return outs[0], outs[1:]
+    count = cells.shape[0]
+    zrow = (cells % nz).reshape(1, count)
+    rrow = (cells // nz).reshape(1, count)
     return pl.pallas_call(
         e_last_kernel,
         grid=(nx // chunk,),
-        in_specs=in_specs + [field_spec(nx, ny, nz, chunk)],
-        out_specs=[field_spec(nx, ny, nz, chunk), pl.BlockSpec((chunk, ny, nz), lambda i: (i, 0, 0))],
-        out_shape=[jax.ShapeDtypeStruct(e.shape, e.dtype), jax.ShapeDtypeStruct(e.shape[1:], e.dtype)],
-    )(*args, ef)
+        in_specs=in_specs
+        + [
+            field_spec(nx, ny, nz, chunk),
+            pl.BlockSpec((1, count), lambda i: (0, 0)),
+            pl.BlockSpec((1, count), lambda i: (0, 0)),
+        ],
+        out_specs=[field_spec(nx, ny, nz, chunk), pl.BlockSpec((1, count), lambda i: (0, 0))],
+        out_shape=[jax.ShapeDtypeStruct(e.shape, e.dtype), jax.ShapeDtypeStruct((1, count), jnp.float32)],
+        scratch_shapes=[pltpu.VMEM((nz, count), jnp.bfloat16)],
+    )(*args, ef, zrow, rrow)
 
 
 def body(e_forward, e_adjoint, h_adjoint, inv_perm, voxel_cell, voxel_owner, voxel_slot):
-    e, h = e_adjoint, h_adjoint
-    e_faces = lower_faces_of(e)
-    intersection = None
-    for repeat in range(STEPS):
-        h, *h_faces = h_step(e, h, e_faces)
-        if repeat == STEPS - 1:
-            e, intersection = e_step(e, h, h_faces, inv_perm, e_forward)
-        else:
-            e, e_faces = e_step(e, h, h_faces, inv_perm)
     count = voxel_cell.shape[-1]
     voxel_rows = voxel_cell.reshape(count)
     owners = voxel_owner.reshape(count)
     slot_ids = voxel_slot.reshape(count)
-    nx, ny, nz = intersection.shape
-    rows = intersection.reshape(nx * ny, nz)[voxel_rows // nz]
-    lanes = lax.broadcasted_iota(jnp.int32, rows.shape, 1)
-    terms = jnp.sum(jnp.where(lanes == (voxel_rows % nz)[:, None], rows, 0.0), axis=1)
+    e, h = e_adjoint, h_adjoint
+    e_faces = lower_faces_of(e)
+    terms = None
+    for repeat in range(STEPS):
+        h, *h_faces = h_step(e, h, e_faces)
+        if repeat == STEPS - 1:
+            e, terms = e_step(e, h, h_faces, inv_perm, e_forward, voxel_rows)
+        else:
+            e, e_faces = e_step(e, h, h_faces, inv_perm)
+    terms = terms.reshape(count)
     devices = lax.axis_size("gx") * lax.axis_size("gy") * lax.axis_size("gz")
     owner_hot = (owners[:, None] == lax.broadcasted_iota(jnp.int32, (count, devices), 1)).astype(jnp.float32)
     slot_hot = jnp.where(slot_ids[:, None] == lax.broadcasted_iota(jnp.int32, (count, P_DEV), 1), terms[:, None], 0.0)

time: 119 us -> 113 us (0.950)
  local copies, waits for them, and re-layouts: 17.7 us -> 10.1 us
  starting transfers between devices: 38.2 us -> 33.4 us
  Pallas kernels: 24.8 us -> 27.7 us
  waiting for transfers between devices: 9.62 us -> 12.2 us
  blocking collectives: 18.8 us -> 21.1 us
  other arithmetic: 6.89 us -> 5.2 us
    gather x1 -> x0, local copies, waits for them, and re-layouts: 7.6 us -> none  [body(): rows = intersection.reshape(nx * ny, nz)[voxel_rows // nz]]
    ppermute x6, starting transfers between devices: 27.9 us -> 23.1 us  [toward_upper(): return lax.ppermute(x, axis, [(j, j + 1) for j in range(peers - 1)])]
    reduce_sum x1 -> x0, other arithmetic: 2.86 us -> none  [body(): jnp.sum(jnp.where(lanes == (voxel_rows % nz)[:, None], rows, 0.0), axis=1)]
    pallas_call x1, Pallas kernels: 7.12 us -> 9.92 us  [e_step(): pl.pallas_call(e_last_kernel, grid=(nx // chunk,), in_specs=in_specs + [f...]
    all_to_all x1, blocking collectives: 18.8 us -> 21.1 us  [body(): received = lax.all_to_all(per_owner, ('gx', 'gy', 'gz'), 0, 0, tiled=True)]
    ppermute x6, waiting for transfers between devices: 8.23 us -> 10.1 us  [toward_lower(): return lax.ppermute(x, axis, [(j, j - 1) for j in range(1, peers)])]
where the time goes in v6:
time: 113 us; the launch traced here: 112 us
  starting transfers between devices  33.4 us (30%)
  Pallas kernels  27.7 us (25%)
  blocking collectives  21.1 us (19%)
  waiting for transfers between devices  12.2 us (11%)
  local copies, waits for them, and re-layouts  10.1 us (9%)
  other arithmetic  5.2 us (5%)
  matrix products  1.73 us (2%)
    ppermute x6, starting transfers between devices, toward_upper(): return lax.ppermute(x, axis, [(j, j + 1) for j in range(peers - 1)])  23.1 us
    all_to_all x1, blocking collectives, body(): received = lax.all_to_all(per_owner, ('gx', 'gy', 'gz'), 0, 0, tiled=True)  21.1 us
    pallas_call x2, Pallas kernels, h_step(): pl.pallas_call(h_kernel, grid=(nx // chunk,), in_specs=[field_spec(nx, ny...  11.7 us
    ppermute x6, starting transfers between devices, toward_lower(): return lax.ppermute(x, axis, [(j, j - 1) for j in range(1, peers)])  10.4 us
    ppermute x6, waiting for transfers between devices, toward_lower(): return lax.ppermute(x, axis, [(j, j - 1) for j in range(1, peers)])  10.1 us
    pallas_call x1, Pallas kernels, e_step(): pl.pallas_call(e_last_kernel, grid=(nx // chunk,), in_specs=in_specs + [f...  9.92 us
    pallas_call x1, Pallas kernels, e_step(): pl.pallas_call(e_kernel, grid=(nx // chunk,), in_specs=in_specs, out_spec...  6.03 us
    slice x3, local copies, waits for them, and re-layouts, lower_faces_of(): return (e[1:3, 0:1], e[0::2, :, 0:1, :], e[0:2, :, :, 0:1])  3.31 us
  transfers between devices with their start and end apart: 12, of which 6 were waited for; matrix products, arithmetic and copies ran while one was open for 8% of the time, Pallas kernels for 0%

profile of v6, /device:TPU:1, one launch (start us, length us, event | category | flops | bytes accessed | tf_op | source)
XLA Modules:
  0.0 112.2 jit_solution(13782629884358366002)
XLA Ops:
  0.6 0.9 slice.9
  1.6 1.3 %collective-permute-start = (f32[2,1,16,1024]{3,2,1,0:T(8,128)S(1)}, f32[2,1,16,1024]{3,2,1,0:T(8,128)S(1)}, u32[]{:S(2)}, u32[]{:S(2)}) collective-permute-start(f32[2,1,16,1024]{3,2,1,0:T(8,128)S(1)} %slice.9), channel_id=1, source_target_pairs={{16,0},{32,16},{48,32},{64,48},{80,64},{96,80},{112,96},{17,1},{33... | collective-permute-start | bytes 393224 | tf_op jit(solution)/shard_map/ppermute | solution.py:19
  2.9 1.3 %slice.10 = f32[2,16,1,1024]{3,2,1,0:T(1,128)S(1)} slice(f32[3,16,16,1024]{3,2,1,0:T(8,128)} %e_ref.3), slice={[0:3:2], [0:16:1], [0:1:1], [0:1024:1]} | slice | bytes 262144 | tf_op jit(solution)/shard_map/slice | solution.py:176
  4.2 3.3 %collective-permute-start.1 = (f32[2,16,1,1024]{3,2,1,0:T(1,128)S(1)}, f32[2,16,1,1024]{3,2,1,0:T(1,128)S(1)}, u32[]{:S(2)}, u32[]{:S(2)}) collective-permute-start(f32[2,16,1,1024]{3,2,1,0:T(1,128)S(1)} %slice.10), channel_id=1, source_target_pairs={{4,0},{8,4},{12,8},{5,1},{9,5},{13,9},{6,2},{10,6},{14,10},{7,3},{... | collective-permute-start | bytes 393224 | tf_op jit(solution)/shard_map/ppermute | solution.py:19
  7.5 1.1 slice_reduce_fusion
  8.6 1.3 %collective-permute-start.2 = (f32[2,256]{1,0:T(2,128)S(1)}, f32[2,256]{1,0:T(2,128)S(1)}, u32[]{:S(2)}, u32[]{:S(2)}) collective-permute-start(f32[2,256]{1,0:T(2,128)S(1)} %reshape.142), channel_id=1, source_target_pairs={{1,0},{2,1},{3,2},{5,4},{6,5},{7,6},{9,8},{10,9},{11,10},{13,12},{... | collective-permute-start | bytes 6152 | tf_op jit(solution)/shard_map/ppermute | solution.py:19
  9.9 3.2 %collective-permute-done.2 = f32[2,256]{1,0:T(2,128)S(1)} collective-permute-done((f32[2,256]{1,0:T(2,128)S(1)}, f32[2,256]{1,0:T(2,128)S(1)}, u32[]{:S(2)}, u32[]{:S(2)}) %collective-permute-start.2) | collective-permute-done | bytes 2080 | tf_op jit(solution)/shard_map/ppermute | solution.py:19
  13.1 0.9 reshape.151.hz_ref
  14.0 1.3 %collective-permute-done.1.hy_ref = f32[2,16,1,1024]{3,2,1,0:T(1,128)S(1)} collective-permute-done((f32[2,16,1,1024]{3,2,1,0:T(1,128)S(1)}, f32[2,16,1,1024]{3,2,1,0:T(1,128)S(1)}, u32[]{:S(2)}, u32[]{:S(2)}) %collective-permute-start.1) | collective-permute-done | bytes 131104 | tf_op jit(solution)/shard_map/ppermute | solution.py:19
  15.9 5.9 %shard_map.94 = (f32[3,16,16,1024]{3,2,1,0:T(8,128)}, f32[2,1,16,1024]{3,2,1,0:T(8,128)}, f32[2,16,1,1024]{3,2,1,0:T(1,128)}, f32[2,16,16,1]{3,2,1,0:T(8,128)}) custom-call(f32[3,16,16,1024]{3,2,1,0:T(8,128)} %e_ref.3, f32[3,16,16,1024]{3,2,1,0:T(8,128)} %e_ref.3, f32[3,16,16,1024]{3,2,1,0:T(8,128)} %h_ref.1, f32[2,1,16,1024]{3,2,1,0:T(8,128)} %copy-done.1, ...), custom_call_target="tpu_custom_call" | custom-call | tf_op jit(solution)/shard_map/pallas_call | solution.py:185
  21.8 3.7 %collective-permute-start.3 = (f32[2,1,16,1024]{3,2,1,0:T(8,128)}, f32[2,1,16,1024]{3,2,1,0:T(8,128)S(1)}, u32[]{:S(2)}, u32[]{:S(2)}) collective-permute-start(f32[2,1,16,1024]{3,2,1,0:T(8,128)} %get-tuple-element.18), channel_id=1, source_target_pairs={{0,16},{16,32},{32,48},{48,64},{64,80},{80,96},{96,112},{1,17},{17... | collective-permute-start | bytes 393224 | tf_op jit(solution)/shard_map/ppermute | solution.py:24
  25.4 6.8 %collective-permute-start.4 = (f32[2,16,1,1024]{3,2,1,0:T(1,128)}, f32[2,16,1,1024]{3,2,1,0:T(1,128)S(1)}, u32[]{:S(2)}, u32[]{:S(2)}) collective-permute-start(f32[2,16,1,1024]{3,2,1,0:T(1,128)} %get-tuple-element.19), channel_id=1, source_target_pairs={{0,4},{4,8},{8,12},{1,5},{5,9},{9,13},{2,6},{6,10},{10,14},{3,7},{... | collective-permute-start | bytes 393224 | tf_op jit(solution)/shard_map/ppermute | solution.py:24
  32.2 1.1 reduce.2
  33.4 3.2 %collective-permute-start.5 = (f32[2,256]{1,0:T(2,128)S(1)}, f32[2,256]{1,0:T(2,128)S(1)}, u32[]{:S(2)}, u32[]{:S(2)}) collective-permute-start(f32[2,256]{1,0:T(2,128)S(1)} %reshape.144), channel_id=1, source_target_pairs={{0,1},{1,2},{2,3},{4,5},{5,6},{6,7},{8,9},{9,10},{10,11},{12,13},{... | collective-permute-start | bytes 6152 | tf_op jit(solution)/shard_map/ppermute | solution.py:24
  39.0 6.0 %shard_map.95 = (f32[3,16,16,1024]{3,2,1,0:T(8,128)}, f32[2,1,16,1024]{3,2,1,0:T(8,128)}, f32[2,16,1,1024]{3,2,1,0:T(1,128)}, f32[2,16,16,1]{3,2,1,0:T(8,128)}) custom-call(f32[3,16,16,1024]{3,2,1,0:T(8,128)} %e_ref.3, f32[3,16,16,1024]{3,2,1,0:T(8,128)} %get-tuple-element.17.h_ref.hp_ref, f32[3,16,16,1024]{3,2,1,0:T(8,128)} %get-tuple-element.17.h_ref.hp_ref, ...), custom_call_target="tpu_custom_call" | custom-call | tf_op jit(solution)/shard_map/pallas_call | solution.py:218
  45.0 1.1 reduce.3
  46.2 1.3 %collective-permute-start.8 = (f32[2,256]{1,0:T(2,128)S(1)}, f32[2,256]{1,0:T(2,128)S(1)}, u32[]{:S(2)}, u32[]{:S(2)}) collective-permute-start(f32[2,256]{1,0:T(2,128)S(1)} %reshape.146), channel_id=1, source_target_pairs={{1,0},{2,1},{3,2},{5,4},{6,5},{7,6},{9,8},{10,9},{11,10},{13,12},{... | collective-permute-start | bytes 6152 | tf_op jit(solution)/shard_map/ppermute | solution.py:19
  47.5 1.3 %collective-permute-start.6 = (f32[2,1,16,1024]{3,2,1,0:T(8,128)}, f32[2,1,16,1024]{3,2,1,0:T(8,128)S(1)}, u32[]{:S(2)}, u32[]{:S(2)}) collective-permute-start(f32[2,1,16,1024]{3,2,1,0:T(8,128)} %get-tuple-element.22), channel_id=1, source_target_pairs={{16,0},{32,16},{48,32},{64,48},{80,64},{96,80},{112,96},{17,1},{33... | collective-permute-start | bytes 393224 | tf_op jit(solution)/shard_map/ppermute | solution.py:19
  48.8 1.9 %collective-permute-start.7 = (f32[2,16,1,1024]{3,2,1,0:T(1,128)}, f32[2,16,1,1024]{3,2,1,0:T(1,128)S(1)}, u32[]{:S(2)}, u32[]{:S(2)}) collective-permute-start(f32[2,16,1,1024]{3,2,1,0:T(1,128)} %get-tuple-element.23), channel_id=1, source_target_pairs={{4,0},{8,4},{12,8},{5,1},{9,5},{13,9},{6,2},{10,6},{14,10},{7,3},{... | collective-permute-start | bytes 393224 | tf_op jit(solution)/shard_map/ppermute | solution.py:19
  51.3 0.9 reshape.153.hz_ref
  52.2 1.3 %collective-permute-done.6.hx_ref = f32[2,1,16,1024]{3,2,1,0:T(8,128)S(1)} collective-permute-done((f32[2,1,16,1024]{3,2,1,0:T(8,128)}, f32[2,1,16,1024]{3,2,1,0:T(8,128)S(1)}, u32[]{:S(2)}, u32[]{:S(2)}) %collective-permute-start.6) | collective-permute-done | bytes 131104 | tf_op jit(solution)/shard_map/ppermute | solution.py:19
  53.6 4.3 %collective-permute-done.7.hy_ref = f32[2,16,1,1024]{3,2,1,0:T(1,128)S(1)} collective-permute-done((f32[2,16,1,1024]{3,2,1,0:T(1,128)}, f32[2,16,1,1024]{3,2,1,0:T(1,128)S(1)}, u32[]{:S(2)}, u32[]{:S(2)}) %collective-permute-start.7) | collective-permute-done | bytes 131104 | tf_op jit(solution)/shard_map/ppermute | solution.py:19
  58.6 5.9 %shard_map.96 = (f32[3,16,16,1024]{3,2,1,0:T(8,128)}, f32[2,1,16,1024]{3,2,1,0:T(8,128)}, f32[2,16,1,1024]{3,2,1,0:T(1,128)}, f32[2,16,16,1]{3,2,1,0:T(8,128)}) custom-call(f32[3,16,16,1024]{3,2,1,0:T(8,128)} %get-tuple-element.21.e_ref.en_ref, f32[3,16,16,1024]{3,2,1,0:T(8,128)} %get-tuple-element.21.e_ref.en_ref, ...), custom_call_target="tpu_custom_call" | custom-call | tf_op jit(solution)/shard_map/pallas_call | solution.py:185
  64.4 1.1 reduce.4
  65.6 4.5 %collective-permute-start.11 = (f32[2,256]{1,0:T(2,128)S(1)}, f32[2,256]{1,0:T(2,128)S(1)}, u32[]{:S(2)}, u32[]{:S(2)}) collective-permute-start(f32[2,256]{1,0:T(2,128)S(1)} %reshape.148), channel_id=1, source_target_pairs={{0,1},{1,2},{2,3},{4,5},{5,6},{6,7},{8,9},{9,10},{10,11},{12,13},{... | collective-permute-start | bytes 6152 | tf_op jit(solution)/shard_map/ppermute | solution.py:24
  70.1 2.1 %collective-permute-start.10 = (f32[2,16,1,1024]{3,2,1,0:T(1,128)}, f32[2,16,1,1024]{3,2,1,0:T(1,128)S(1)}, u32[]{:S(2)}, u32[]{:S(2)}) collective-permute-start(f32[2,16,1,1024]{3,2,1,0:T(1,128)} %get-tuple-element.27), channel_id=1, source_target_pairs={{0,4},{4,8},{8,12},{1,5},{5,9},{9,13},{2,6},{6,10},{10,14},{3,7},{... | collective-permute-start | bytes 393224 | tf_op jit(solution)/shard_map/ppermute | solution.py:24
  72.2 2.8 %collective-permute-start.9 = (f32[2,1,16,1024]{3,2,1,0:T(8,128)}, f32[2,1,16,1024]{3,2,1,0:T(8,128)S(1)}, u32[]{:S(2)}, u32[]{:S(2)}) collective-permute-start(f32[2,1,16,1024]{3,2,1,0:T(8,128)} %get-tuple-element.26), channel_id=1, source_target_pairs={{0,16},{16,32},{32,48},{48,64},{64,80},{80,96},{96,112},{1,17},{17... | collective-permute-start | bytes 393224 | tf_op jit(solution)/shard_map/ppermute | solution.py:24
  75.6 0.9 reshape.154.hz_ref
  76.6 1.4 %collective-permute-done.9.hx_ref = f32[2,1,16,1024]{3,2,1,0:T(8,128)S(1)} collective-permute-done((f32[2,1,16,1024]{3,2,1,0:T(8,128)}, f32[2,1,16,1024]{3,2,1,0:T(8,128)S(1)}, u32[]{:S(2)}, u32[]{:S(2)}) %collective-permute-start.9) | collective-permute-done | bytes 131104 | tf_op jit(solution)/shard_map/ppermute | solution.py:24
  78.6 9.9 %shard_map.97 = (f32[3,16,16,1024]{3,2,1,0:T(8,128)}, f32[1,1024]{1,0:T(1,128)}) custom-call(f32[3,16,16,1024]{3,2,1,0:T(8,128)} %get-tuple-element.21.e_ref.en_ref, f32[3,16,16,1024]{3,2,1,0:T(8,128)} %get-tuple-element.15.h_ref.hp_ref, f32[3,16,16,1024]{3,2,1,0:T(8,128)} %get-tuple-element.15.h_ref.hp_ref, f32[16,16,1024]{2,1,0:T(8,128)} %inv_ref.3, ...), custom_call_target="tpu_custom_call" | custom-call | tf_op jit(solution)/shard_map/pallas_call | solution.py:229
  88.5 1.7 %convolution_bitcast_fusion = f32[128,1,256]{2,0,1:T(8,128)S(1)} fusion(f32[1024]{0:T(1024)} %bitcast.19, s32[1024]{0:T(1024)S(1)} %bitcast.17, s32[1024]{0:T(1024)S(1)} %bitcast.18), kind=kOutput, calls=%fused_computation | convolution fusion | flops 403308544 | bytes 143360 | tf_op jit(solution)/shard_map/dot_general | solution.py:262
  90.4 21.1 %all_to_all.9 = f32[128,1,256]{2,1,0:T(1,128)S(1)} all-to-all(f32[128,1,256]{2,1,0:T(1,128)S(1)} %copy.18), channel_id=1, replica_groups=mesh['gx'=8,'gy'=4,'gz'=4] {'gx','gy','gz'}, dimensions={0} | all-to-all | bytes 262144 | tf_op jit(solution)/shard_map/all_to_all | solution.py:263
  (38 shorter events, 6.7 us)
Async XLA Ops:
  1.6 12.5 %collective-permute-start = (f32[2,1,16,1024]{3,2,1,0:T(8,128)S(1)}, f32[2,1,16,1024]{3,2,1,0:T(8,128)S(1)}, u32[]{:S(2)}, u32[]{:S(2)}) collective-permute-start(f32[2,1,16,1024]{3,2,1,0:T(8,128)S(1)} %slice.9), channel_id=1, source_target_pairs={{16,0},{32,16},{48,32},{64,48},{80,64},{96,80},{112,96},{17,1},{33... | collective-permute-start | bytes 393224 | tf_op jit(solution)/shard_map/ppermute | solution.py:19
  4.2 11.1 %collective-permute-start.1 = (f32[2,16,1,1024]{3,2,1,0:T(1,128)S(1)}, f32[2,16,1,1024]{3,2,1,0:T(1,128)S(1)}, u32[]{:S(2)}, u32[]{:S(2)}) collective-permute-start(f32[2,16,1,1024]{3,2,1,0:T(1,128)S(1)} %slice.10), channel_id=1, source_target_pairs={{4,0},{8,4},{12,8},{5,1},{9,5},{13,9},{6,2},{10,6},{14,10},{7,3},{... | collective-permute-start | bytes 393224 | tf_op jit(solution)/shard_map/ppermute | solution.py:19
  8.6 4.5 %collective-permute-start.2 = (f32[2,256]{1,0:T(2,128)S(1)}, f32[2,256]{1,0:T(2,128)S(1)}, u32[]{:S(2)}, u32[]{:S(2)}) collective-permute-start(f32[2,256]{1,0:T(2,128)S(1)} %reshape.142), channel_id=1, source_target_pairs={{1,0},{2,1},{3,2},{5,4},{6,5},{7,6},{9,8},{10,9},{11,10},{13,12},{... | collective-permute-start | bytes 6152 | tf_op jit(solution)/shard_map/ppermute | solution.py:19
  14.0 1.3 %copy-start.1 = (f32[2,1,16,1024]{3,2,1,0:T(8,128)}, f32[2,1,16,1024]{3,2,1,0:T(8,128)S(1)}, u32[]{:S(2)}) copy-start(f32[2,1,16,1024]{3,2,1,0:T(8,128)S(1)} %collective-permute-done.hx_ref) | copy-start | bytes 393220
  15.3 0.6 copy-start.4
  21.8 16.5 %collective-permute-start.3 = (f32[2,1,16,1024]{3,2,1,0:T(8,128)}, f32[2,1,16,1024]{3,2,1,0:T(8,128)S(1)}, u32[]{:S(2)}, u32[]{:S(2)}) collective-permute-start(f32[2,1,16,1024]{3,2,1,0:T(8,128)} %get-tuple-element.18), channel_id=1, source_target_pairs={{0,16},{16,32},{32,48},{48,64},{64,80},{80,96},{96,112},{1,17},{17... | collective-permute-start | bytes 393224 | tf_op jit(solution)/shard_map/ppermute | solution.py:24
  25.4 12.8 %collective-permute-start.4 = (f32[2,16,1,1024]{3,2,1,0:T(1,128)}, f32[2,16,1,1024]{3,2,1,0:T(1,128)S(1)}, u32[]{:S(2)}, u32[]{:S(2)}) collective-permute-start(f32[2,16,1,1024]{3,2,1,0:T(1,128)} %get-tuple-element.19), channel_id=1, source_target_pairs={{0,4},{4,8},{8,12},{1,5},{5,9},{9,13},{2,6},{6,10},{10,14},{3,7},{... | collective-permute-start | bytes 393224 | tf_op jit(solution)/shard_map/ppermute | solution.py:24
  33.4 3.9 %collective-permute-start.5 = (f32[2,256]{1,0:T(2,128)S(1)}, f32[2,256]{1,0:T(2,128)S(1)}, u32[]{:S(2)}, u32[]{:S(2)}) collective-permute-start(f32[2,256]{1,0:T(2,128)S(1)} %reshape.144), channel_id=1, source_target_pairs={{0,1},{1,2},{2,3},{4,5},{5,6},{6,7},{8,9},{9,10},{10,11},{12,13},{... | collective-permute-start | bytes 6152 | tf_op jit(solution)/shard_map/ppermute | solution.py:24
  38.3 0.6 copy-start
  38.3 0.7 copy-start.2
  39.0 11.7 %copy-start.8 = (s32[1,1,1,1024]{3,2,1,0:T(1,128)S(1)}, s32[1,1,1,1024]{3,2,1,0:T(1,128)}, u32[]{:S(2)}) copy-start(s32[1,1,1,1024]{3,2,1,0:T(1,128)} %param.11) | copy-start | bytes 12292
  46.2 5.1 %collective-permute-start.8 = (f32[2,256]{1,0:T(2,128)S(1)}, f32[2,256]{1,0:T(2,128)S(1)}, u32[]{:S(2)}, u32[]{:S(2)}) collective-permute-start(f32[2,256]{1,0:T(2,128)S(1)} %reshape.146), channel_id=1, source_target_pairs={{1,0},{2,1},{3,2},{5,4},{6,5},{7,6},{9,8},{10,9},{11,10},{13,12},{... | collective-permute-start | bytes 6152 | tf_op jit(solution)/shard_map/ppermute | solution.py:19
  47.5 6.1 %collective-permute-start.6 = (f32[2,1,16,1024]{3,2,1,0:T(8,128)}, f32[2,1,16,1024]{3,2,1,0:T(8,128)S(1)}, u32[]{:S(2)}, u32[]{:S(2)}) collective-permute-start(f32[2,1,16,1024]{3,2,1,0:T(8,128)} %get-tuple-element.22), channel_id=1, source_target_pairs={{16,0},{32,16},{48,32},{64,48},{80,64},{96,80},{112,96},{17,1},{33... | collective-permute-start | bytes 393224 | tf_op jit(solution)/shard_map/ppermute | solution.py:19
  48.8 9.1 %collective-permute-start.7 = (f32[2,16,1,1024]{3,2,1,0:T(1,128)}, f32[2,16,1,1024]{3,2,1,0:T(1,128)S(1)}, u32[]{:S(2)}, u32[]{:S(2)}) collective-permute-start(f32[2,16,1,1024]{3,2,1,0:T(1,128)} %get-tuple-element.23), channel_id=1, source_target_pairs={{4,0},{8,4},{12,8},{5,1},{9,5},{13,9},{6,2},{10,6},{14,10},{7,3},{... | collective-permute-start | bytes 393224 | tf_op jit(solution)/shard_map/ppermute | solution.py:19
  53.6 4.3 %copy-start.3 = (f32[2,1,16,1024]{3,2,1,0:T(8,128)}, f32[2,1,16,1024]{3,2,1,0:T(8,128)S(1)}, u32[]{:S(2)}) copy-start(f32[2,1,16,1024]{3,2,1,0:T(8,128)S(1)} %collective-permute-done.6.hx_ref) | copy-start | bytes 393220
  57.9 0.6 copy-start.6
  65.6 10.1 %collective-permute-start.11 = (f32[2,256]{1,0:T(2,128)S(1)}, f32[2,256]{1,0:T(2,128)S(1)}, u32[]{:S(2)}, u32[]{:S(2)}) collective-permute-start(f32[2,256]{1,0:T(2,128)S(1)} %reshape.148), channel_id=1, source_target_pairs={{0,1},{1,2},{2,3},{4,5},{5,6},{6,7},{8,9},{9,10},{10,11},{12,13},{... | collective-permute-start | bytes 6152 | tf_op jit(solution)/shard_map/ppermute | solution.py:24
  70.1 6.5 %collective-permute-start.10 = (f32[2,16,1,1024]{3,2,1,0:T(1,128)}, f32[2,16,1,1024]{3,2,1,0:T(1,128)S(1)}, u32[]{:S(2)}, u32[]{:S(2)}) collective-permute-start(f32[2,16,1,1024]{3,2,1,0:T(1,128)} %get-tuple-element.27), channel_id=1, source_target_pairs={{0,4},{4,8},{8,12},{1,5},{5,9},{9,13},{2,6},{6,10},{10,14},{3,7},{... | collective-permute-start | bytes 393224 | tf_op jit(solution)/shard_map/ppermute | solution.py:24
  72.2 5.7 %collective-permute-start.9 = (f32[2,1,16,1024]{3,2,1,0:T(8,128)}, f32[2,1,16,1024]{3,2,1,0:T(8,128)S(1)}, u32[]{:S(2)}, u32[]{:S(2)}) collective-permute-start(f32[2,1,16,1024]{3,2,1,0:T(8,128)} %get-tuple-element.26), channel_id=1, source_target_pairs={{0,16},{16,32},{32,48},{48,64},{64,80},{80,96},{96,112},{1,17},{17... | collective-permute-start | bytes 393224 | tf_op jit(solution)/shard_map/ppermute | solution.py:24
  76.5 1.4 %copy-start.5 = (f32[2,16,1,1024]{3,2,1,0:T(1,128)}, f32[2,16,1,1024]{3,2,1,0:T(1,128)S(1)}, u32[]{:S(2)}) copy-start(f32[2,16,1,1024]{3,2,1,0:T(1,128)S(1)} %collective-permute-done.10.hy_ref) | copy-start | bytes 393220
  77.9 0.7 copy-start.7
  78.6 9.9 %copy-start.9 = (s32[1,1,1,1024]{3,2,1,0:T(1,128)S(1)}, s32[1,1,1,1024]{3,2,1,0:T(1,128)}, u32[]{:S(2)}) copy-start(s32[1,1,1,1024]{3,2,1,0:T(1,128)} %param.13) | copy-start | bytes 12292
  78.6 9.9 %copy-start.10 = (s32[1,1,1,1024,1]{3,4,2,1,0:T(1,128)S(1)}, s32[1,1,1,1024,1]{3,4,2,1,0:T(1,128)}, u32[]{:S(2)}) copy-start(s32[1,1,1,1024,1]{3,4,2,1,0:T(1,128)} %param.12) | copy-start | bytes 12292

commit v7 on v6

--- a/solution.py
+++ b/solution.py
@@ -9,7 +9,7 @@
 
 STEPS = 2
 P_DEV = 256
-CHUNK = 4
+CHUNK = 8
 
 courant = 0.5
 

time: 113 us -> 108 us (0.956)
  Pallas kernels: 27.7 us -> 23.2 us
    pallas_call x1, Pallas kernels: 9.92 us -> 7.85 us  [e_step(): pl.pallas_call(e_last_kernel, grid=(nx // chunk,), in_specs=in_specs + [f...]
    pallas_call x2, Pallas kernels: 11.7 us -> 10 us  [h_step(): pl.pallas_call(h_kernel, grid=(nx // chunk,), in_specs=[field_spec(nx, ny...]
where the time goes in v7:
time: 108 us
  starting transfers between devices  33.4 us (31%)
  Pallas kernels  23.2 us (21%)
  blocking collectives  21.1 us (20%)
  waiting for transfers between devices  12.2 us (11%)
  local copies, waits for them, and re-layouts  10.1 us (9%)
  other arithmetic  5.2 us (5%)
  matrix products  1.73 us (2%)
    ppermute x6, starting transfers between devices, toward_upper(): return lax.ppermute(x, axis, [(j, j + 1) for j in range(peers - 1)])  23.1 us
    all_to_all x1, blocking collectives, body(): received = lax.all_to_all(per_owner, ('gx', 'gy', 'gz'), 0, 0, tiled=True)  21.1 us
    ppermute x6, starting transfers between devices, toward_lower(): return lax.ppermute(x, axis, [(j, j - 1) for j in range(1, peers)])  10.4 us
    ppermute x6, waiting for transfers between devices, toward_lower(): return lax.ppermute(x, axis, [(j, j - 1) for j in range(1, peers)])  10.1 us
    pallas_call x2, Pallas kernels, h_step(): pl.pallas_call(h_kernel, grid=(nx // chunk,), in_specs=[field_spec(nx, ny...  10 us
    pallas_call x1, Pallas kernels, e_step(): pl.pallas_call(e_last_kernel, grid=(nx // chunk,), in_specs=in_specs + [f...  7.85 us
    pallas_call x1, Pallas kernels, e_step(): pl.pallas_call(e_kernel, grid=(nx // chunk,), in_specs=in_specs, out_spec...  5.33 us
    slice x3, local copies, waits for them, and re-layouts, lower_faces_of(): return (e[1:3, 0:1], e[0::2, :, 0:1, :], e[0:2, :, :, 0:1])  3.31 us
  transfers between devices with their start and end apart: 12, of which 6 were waited for; matrix products, arithmetic and copies ran while one was open for 8% of the time, Pallas kernels for 0%

profile of v7, /device:TPU:1, one launch (start us, length us, event | category | flops | bytes accessed | tf_op | source)
XLA Modules:
  0.0 107.7 jit_solution(12502312806063667443)
XLA Ops:
  0.6 0.9 slice.9
  1.6 1.3 %collective-permute-start = (f32[2,1,16,1024]{3,2,1,0:T(8,128)S(1)}, f32[2,1,16,1024]{3,2,1,0:T(8,128)S(1)}, u32[]{:S(2)}, u32[]{:S(2)}) collective-permute-start(f32[2,1,16,1024]{3,2,1,0:T(8,128)S(1)} %slice.9), channel_id=1, source_target_pairs={{16,0},{32,16},{48,32},{64,48},{80,64},{96,80},{112,96},{17,1},{33... | collective-permute-start | bytes 393224 | tf_op jit(solution)/shard_map/ppermute | solution.py:19
  2.9 1.3 %slice.10 = f32[2,16,1,1024]{3,2,1,0:T(1,128)S(1)} slice(f32[3,16,16,1024]{3,2,1,0:T(8,128)} %e_ref.3), slice={[0:3:2], [0:16:1], [0:1:1], [0:1024:1]} | slice | bytes 262144 | tf_op jit(solution)/shard_map/slice | solution.py:176
  4.2 3.3 %collective-permute-start.1 = (f32[2,16,1,1024]{3,2,1,0:T(1,128)S(1)}, f32[2,16,1,1024]{3,2,1,0:T(1,128)S(1)}, u32[]{:S(2)}, u32[]{:S(2)}) collective-permute-start(f32[2,16,1,1024]{3,2,1,0:T(1,128)S(1)} %slice.10), channel_id=1, source_target_pairs={{4,0},{8,4},{12,8},{5,1},{9,5},{13,9},{6,2},{10,6},{14,10},{7,3},{... | collective-permute-start | bytes 393224 | tf_op jit(solution)/shard_map/ppermute | solution.py:19
  7.5 1.1 %slice_reduce_fusion = f32[2,16,16]{2,1,0:T(8,128)S(1)} fusion(f32[3,16,16,1024]{3,2,1,0:T(8,128)} %e_ref.3), kind=kLoop, calls=%fused_computation.8 | loop fusion | bytes 4096 | tf_op jit(solution)/shard_map/slice | solution.py:176
  8.6 1.3 %collective-permute-start.2 = (f32[2,256]{1,0:T(2,128)S(1)}, f32[2,256]{1,0:T(2,128)S(1)}, u32[]{:S(2)}, u32[]{:S(2)}) collective-permute-start(f32[2,256]{1,0:T(2,128)S(1)} %reshape.142), channel_id=1, source_target_pairs={{1,0},{2,1},{3,2},{5,4},{6,5},{7,6},{9,8},{10,9},{11,10},{13,12},{... | collective-permute-start | bytes 6152 | tf_op jit(solution)/shard_map/ppermute | solution.py:19
  9.9 3.2 %collective-permute-done.2 = f32[2,256]{1,0:T(2,128)S(1)} collective-permute-done((f32[2,256]{1,0:T(2,128)S(1)}, f32[2,256]{1,0:T(2,128)S(1)}, u32[]{:S(2)}, u32[]{:S(2)}) %collective-permute-start.2) | collective-permute-done | bytes 2080 | tf_op jit(solution)/shard_map/ppermute | solution.py:19
  13.1 0.9 reshape.151.hz_ref
  14.0 1.3 %collective-permute-done.1.hy_ref = f32[2,16,1,1024]{3,2,1,0:T(1,128)S(1)} collective-permute-done((f32[2,16,1,1024]{3,2,1,0:T(1,128)S(1)}, f32[2,16,1,1024]{3,2,1,0:T(1,128)S(1)}, u32[]{:S(2)}, u32[]{:S(2)}) %collective-permute-start.1) | collective-permute-done | bytes 131104 | tf_op jit(solution)/shard_map/ppermute | solution.py:19
  15.9 5.0 %shard_map.94 = (f32[3,16,16,1024]{3,2,1,0:T(8,128)}, f32[2,1,16,1024]{3,2,1,0:T(8,128)}, f32[2,16,1,1024]{3,2,1,0:T(1,128)}, f32[2,16,16,1]{3,2,1,0:T(8,128)}) custom-call(f32[3,16,16,1024]{3,2,1,0:T(8,128)} %e_ref.3, f32[3,16,16,1024]{3,2,1,0:T(8,128)} %e_ref.3, f32[3,16,16,1024]{3,2,1,0:T(8,128)} %h_ref.1, f32[2,1,16,1024]{3,2,1,0:T(8,128)} %copy-done.1, ...), custom_call_target="tpu_custom_call" | custom-call | tf_op jit(solution)/shard_map/pallas_call | solution.py:185
  20.9 3.7 %collective-permute-start.3 = (f32[2,1,16,1024]{3,2,1,0:T(8,128)}, f32[2,1,16,1024]{3,2,1,0:T(8,128)S(1)}, u32[]{:S(2)}, u32[]{:S(2)}) collective-permute-start(f32[2,1,16,1024]{3,2,1,0:T(8,128)} %get-tuple-element.18), channel_id=1, source_target_pairs={{0,16},{16,32},{32,48},{48,64},{64,80},{80,96},{96,112},{1,17},{17... | collective-permute-start | bytes 393224 | tf_op jit(solution)/shard_map/ppermute | solution.py:24
  24.6 6.8 %collective-permute-start.4 = (f32[2,16,1,1024]{3,2,1,0:T(1,128)}, f32[2,16,1,1024]{3,2,1,0:T(1,128)S(1)}, u32[]{:S(2)}, u32[]{:S(2)}) collective-permute-start(f32[2,16,1,1024]{3,2,1,0:T(1,128)} %get-tuple-element.19), channel_id=1, source_target_pairs={{0,4},{4,8},{8,12},{1,5},{5,9},{9,13},{2,6},{6,10},{10,14},{3,7},{... | collective-permute-start | bytes 393224 | tf_op jit(solution)/shard_map/ppermute | solution.py:24
  31.4 1.1 %reduce.2 = f32[2,16,16]{2,1,0:T(8,128)S(1)} reduce(f32[2,16,16,1]{3,2,1,0:T(8,128)} %get-tuple-element.20, f32[]{:T(128)} %constant.33), dimensions={3}, to_apply=%get-tuple-element.20.reduce_sub_computation | reduce | bytes 4100 | tf_op jit(solution)/shard_map/pallas_call | solution.py:185
  32.6 3.2 %collective-permute-start.5 = (f32[2,256]{1,0:T(2,128)S(1)}, f32[2,256]{1,0:T(2,128)S(1)}, u32[]{:S(2)}, u32[]{:S(2)}) collective-permute-start(f32[2,256]{1,0:T(2,128)S(1)} %reshape.144), channel_id=1, source_target_pairs={{0,1},{1,2},{2,3},{4,5},{5,6},{6,7},{8,9},{9,10},{10,11},{12,13},{... | collective-permute-start | bytes 6152 | tf_op jit(solution)/shard_map/ppermute | solution.py:24
  38.1 5.3 %shard_map.95 = (f32[3,16,16,1024]{3,2,1,0:T(8,128)}, f32[2,1,16,1024]{3,2,1,0:T(8,128)}, f32[2,16,1,1024]{3,2,1,0:T(1,128)}, f32[2,16,16,1]{3,2,1,0:T(8,128)}) custom-call(f32[3,16,16,1024]{3,2,1,0:T(8,128)} %e_ref.3, f32[3,16,16,1024]{3,2,1,0:T(8,128)} %get-tuple-element.17.h_ref.hp_ref, f32[3,16,16,1024]{3,2,1,0:T(8,128)} %get-tuple-element.17.h_ref.hp_ref, ...), custom_call_target="tpu_custom_call" | custom-call | tf_op jit(solution)/shard_map/pallas_call | solution.py:218
  43.4 1.1 %reduce.3 = f32[2,16,16]{2,1,0:T(8,128)S(1)} reduce(f32[2,16,16,1]{3,2,1,0:T(8,128)} %get-tuple-element.24, f32[]{:T(128)} %constant.33), dimensions={3}, to_apply=%get-tuple-element.24.reduce_sub_computation | reduce | bytes 4100 | tf_op jit(solution)/shard_map/pallas_call | solution.py:218
  44.6 1.3 %collective-permute-start.8 = (f32[2,256]{1,0:T(2,128)S(1)}, f32[2,256]{1,0:T(2,128)S(1)}, u32[]{:S(2)}, u32[]{:S(2)}) collective-permute-start(f32[2,256]{1,0:T(2,128)S(1)} %reshape.146), channel_id=1, source_target_pairs={{1,0},{2,1},{3,2},{5,4},{6,5},{7,6},{9,8},{10,9},{11,10},{13,12},{... | collective-permute-start | bytes 6152 | tf_op jit(solution)/shard_map/ppermute | solution.py:19
  45.9 1.3 %collective-permute-start.6 = (f32[2,1,16,1024]{3,2,1,0:T(8,128)}, f32[2,1,16,1024]{3,2,1,0:T(8,128)S(1)}, u32[]{:S(2)}, u32[]{:S(2)}) collective-permute-start(f32[2,1,16,1024]{3,2,1,0:T(8,128)} %get-tuple-element.22), channel_id=1, source_target_pairs={{16,0},{32,16},{48,32},{64,48},{80,64},{96,80},{112,96},{17,1},{33... | collective-permute-start | bytes 393224 | tf_op jit(solution)/shard_map/ppermute | solution.py:19
  47.2 1.9 %collective-permute-start.7 = (f32[2,16,1,1024]{3,2,1,0:T(1,128)}, f32[2,16,1,1024]{3,2,1,0:T(1,128)S(1)}, u32[]{:S(2)}, u32[]{:S(2)}) collective-permute-start(f32[2,16,1,1024]{3,2,1,0:T(1,128)} %get-tuple-element.23), channel_id=1, source_target_pairs={{4,0},{8,4},{12,8},{5,1},{9,5},{13,9},{6,2},{10,6},{14,10},{7,3},{... | collective-permute-start | bytes 393224 | tf_op jit(solution)/shard_map/ppermute | solution.py:19
  49.8 0.9 reshape.153.hz_ref
  50.7 1.3 %collective-permute-done.6.hx_ref = f32[2,1,16,1024]{3,2,1,0:T(8,128)S(1)} collective-permute-done((f32[2,1,16,1024]{3,2,1,0:T(8,128)}, f32[2,1,16,1024]{3,2,1,0:T(8,128)S(1)}, u32[]{:S(2)}, u32[]{:S(2)}) %collective-permute-start.6) | collective-permute-done | bytes 131104 | tf_op jit(solution)/shard_map/ppermute | solution.py:19
  52.0 4.3 %collective-permute-done.7.hy_ref = f32[2,16,1,1024]{3,2,1,0:T(1,128)S(1)} collective-permute-done((f32[2,16,1,1024]{3,2,1,0:T(1,128)}, f32[2,16,1,1024]{3,2,1,0:T(1,128)S(1)}, u32[]{:S(2)}, u32[]{:S(2)}) %collective-permute-start.7) | collective-permute-done | bytes 131104 | tf_op jit(solution)/shard_map/ppermute | solution.py:19
  57.0 5.0 %shard_map.96 = (f32[3,16,16,1024]{3,2,1,0:T(8,128)}, f32[2,1,16,1024]{3,2,1,0:T(8,128)}, f32[2,16,1,1024]{3,2,1,0:T(1,128)}, f32[2,16,16,1]{3,2,1,0:T(8,128)}) custom-call(f32[3,16,16,1024]{3,2,1,0:T(8,128)} %get-tuple-element.21.e_ref.en_ref, f32[3,16,16,1024]{3,2,1,0:T(8,128)} %get-tuple-element.21.e_ref.en_ref, ...), custom_call_target="tpu_custom_call" | custom-call | tf_op jit(solution)/shard_map/pallas_call | solution.py:185
  62.0 1.1 %reduce.4 = f32[2,16,16]{2,1,0:T(8,128)S(1)} reduce(f32[2,16,16,1]{3,2,1,0:T(8,128)} %get-tuple-element.28, f32[]{:T(128)} %constant.33), dimensions={3}, to_apply=%get-tuple-element.28.reduce_sub_computation | reduce | bytes 4100 | tf_op jit(solution)/shard_map/pallas_call | solution.py:185
  63.2 4.5 %collective-permute-start.11 = (f32[2,256]{1,0:T(2,128)S(1)}, f32[2,256]{1,0:T(2,128)S(1)}, u32[]{:S(2)}, u32[]{:S(2)}) collective-permute-start(f32[2,256]{1,0:T(2,128)S(1)} %reshape.148), channel_id=1, source_target_pairs={{0,1},{1,2},{2,3},{4,5},{5,6},{6,7},{8,9},{9,10},{10,11},{12,13},{... | collective-permute-start | bytes 6152 | tf_op jit(solution)/shard_map/ppermute | solution.py:24
  67.7 2.1 %collective-permute-start.10 = (f32[2,16,1,1024]{3,2,1,0:T(1,128)}, f32[2,16,1,1024]{3,2,1,0:T(1,128)S(1)}, u32[]{:S(2)}, u32[]{:S(2)}) collective-permute-start(f32[2,16,1,1024]{3,2,1,0:T(1,128)} %get-tuple-element.27), channel_id=1, source_target_pairs={{0,4},{4,8},{8,12},{1,5},{5,9},{9,13},{2,6},{6,10},{10,14},{3,7},{... | collective-permute-start | bytes 393224 | tf_op jit(solution)/shard_map/ppermute | solution.py:24
  69.8 2.8 %collective-permute-start.9 = (f32[2,1,16,1024]{3,2,1,0:T(8,128)}, f32[2,1,16,1024]{3,2,1,0:T(8,128)S(1)}, u32[]{:S(2)}, u32[]{:S(2)}) collective-permute-start(f32[2,1,16,1024]{3,2,1,0:T(8,128)} %get-tuple-element.26), channel_id=1, source_target_pairs={{0,16},{16,32},{32,48},{48,64},{64,80},{80,96},{96,112},{1,17},{17... | collective-permute-start | bytes 393224 | tf_op jit(solution)/shard_map/ppermute | solution.py:24
  73.2 0.9 reshape.154.hz_ref
  74.1 1.4 %collective-permute-done.9.hx_ref = f32[2,1,16,1024]{3,2,1,0:T(8,128)S(1)} collective-permute-done((f32[2,1,16,1024]{3,2,1,0:T(8,128)}, f32[2,1,16,1024]{3,2,1,0:T(8,128)S(1)}, u32[]{:S(2)}, u32[]{:S(2)}) %collective-permute-start.9) | collective-permute-done | bytes 131104 | tf_op jit(solution)/shard_map/ppermute | solution.py:24
  76.2 7.9 %shard_map.97 = (f32[3,16,16,1024]{3,2,1,0:T(8,128)}, f32[1,1024]{1,0:T(1,128)}) custom-call(f32[3,16,16,1024]{3,2,1,0:T(8,128)} %get-tuple-element.21.e_ref.en_ref, f32[3,16,16,1024]{3,2,1,0:T(8,128)} %get-tuple-element.15.h_ref.hp_ref, f32[3,16,16,1024]{3,2,1,0:T(8,128)} %get-tuple-element.15.h_ref.hp_ref, f32[16,16,1024]{2,1,0:T(8,128)} %inv_ref.3, ...), custom_call_target="tpu_custom_call" | custom-call | tf_op jit(solution)/shard_map/pallas_call | solution.py:229
  84.0 1.7 %convolution_bitcast_fusion = f32[128,1,256]{2,0,1:T(8,128)S(1)} fusion(f32[1024]{0:T(1024)} %bitcast.19, s32[1024]{0:T(1024)S(1)} %bitcast.17, s32[1024]{0:T(1024)S(1)} %bitcast.18), kind=kOutput, calls=%fused_computation | convolution fusion | flops 403308544 | bytes 143360 | tf_op jit(solution)/shard_map/dot_general | solution.py:262
  85.9 21.1 %all_to_all.9 = f32[128,1,256]{2,1,0:T(1,128)S(1)} all-to-all(f32[128,1,256]{2,1,0:T(1,128)S(1)} %copy.18), channel_id=1, replica_groups=mesh['gx'=8,'gy'=4,'gz'=4] {'gx','gy','gz'}, dimensions={0} | all-to-all | bytes 262144 | tf_op jit(solution)/shard_map/all_to_all | solution.py:263
  (38 shorter events, 6.7 us)
Async XLA Ops:
  1.6 12.5 %collective-permute-start = (f32[2,1,16,1024]{3,2,1,0:T(8,128)S(1)}, f32[2,1,16,1024]{3,2,1,0:T(8,128)S(1)}, u32[]{:S(2)}, u32[]{:S(2)}) collective-permute-start(f32[2,1,16,1024]{3,2,1,0:T(8,128)S(1)} %slice.9), channel_id=1, source_target_pairs={{16,0},{32,16},{48,32},{64,48},{80,64},{96,80},{112,96},{17,1},{33... | collective-permute-start | bytes 393224 | tf_op jit(solution)/shard_map/ppermute | solution.py:19
  4.2 11.1 %collective-permute-start.1 = (f32[2,16,1,1024]{3,2,1,0:T(1,128)S(1)}, f32[2,16,1,1024]{3,2,1,0:T(1,128)S(1)}, u32[]{:S(2)}, u32[]{:S(2)}) collective-permute-start(f32[2,16,1,1024]{3,2,1,0:T(1,128)S(1)} %slice.10), channel_id=1, source_target_pairs={{4,0},{8,4},{12,8},{5,1},{9,5},{13,9},{6,2},{10,6},{14,10},{7,3},{... | collective-permute-start | bytes 393224 | tf_op jit(solution)/shard_map/ppermute | solution.py:19
  8.6 4.5 %collective-permute-start.2 = (f32[2,256]{1,0:T(2,128)S(1)}, f32[2,256]{1,0:T(2,128)S(1)}, u32[]{:S(2)}, u32[]{:S(2)}) collective-permute-start(f32[2,256]{1,0:T(2,128)S(1)} %reshape.142), channel_id=1, source_target_pairs={{1,0},{2,1},{3,2},{5,4},{6,5},{7,6},{9,8},{10,9},{11,10},{13,12},{... | collective-permute-start | bytes 6152 | tf_op jit(solution)/shard_map/ppermute | solution.py:19
  14.0 1.3 %copy-start.1 = (f32[2,1,16,1024]{3,2,1,0:T(8,128)}, f32[2,1,16,1024]{3,2,1,0:T(8,128)S(1)}, u32[]{:S(2)}) copy-start(f32[2,1,16,1024]{3,2,1,0:T(8,128)S(1)} %collective-permute-done.hx_ref) | copy-start | bytes 393220
  15.3 0.6 copy-start.4
  20.9 16.5 %collective-permute-start.3 = (f32[2,1,16,1024]{3,2,1,0:T(8,128)}, f32[2,1,16,1024]{3,2,1,0:T(8,128)S(1)}, u32[]{:S(2)}, u32[]{:S(2)}) collective-permute-start(f32[2,1,16,1024]{3,2,1,0:T(8,128)} %get-tuple-element.18), channel_id=1, source_target_pairs={{0,16},{16,32},{32,48},{48,64},{64,80},{80,96},{96,112},{1,17},{17... | collective-permute-start | bytes 393224 | tf_op jit(solution)/shard_map/ppermute | solution.py:24
  24.6 12.8 %collective-permute-start.4 = (f32[2,16,1,1024]{3,2,1,0:T(1,128)}, f32[2,16,1,1024]{3,2,1,0:T(1,128)S(1)}, u32[]{:S(2)}, u32[]{:S(2)}) collective-permute-start(f32[2,16,1,1024]{3,2,1,0:T(1,128)} %get-tuple-element.19), channel_id=1, source_target_pairs={{0,4},{4,8},{8,12},{1,5},{5,9},{9,13},{2,6},{6,10},{10,14},{3,7},{... | collective-permute-start | bytes 393224 | tf_op jit(solution)/shard_map/ppermute | solution.py:24
  32.6 3.9 %collective-permute-start.5 = (f32[2,256]{1,0:T(2,128)S(1)}, f32[2,256]{1,0:T(2,128)S(1)}, u32[]{:S(2)}, u32[]{:S(2)}) collective-permute-start(f32[2,256]{1,0:T(2,128)S(1)} %reshape.144), channel_id=1, source_target_pairs={{0,1},{1,2},{2,3},{4,5},{5,6},{6,7},{8,9},{9,10},{10,11},{12,13},{... | collective-permute-start | bytes 6152 | tf_op jit(solution)/shard_map/ppermute | solution.py:24
  37.4 0.6 copy-start
  37.4 0.7 copy-start.2
  38.1 11.0 %copy-start.8 = (s32[1,1,1,1024]{3,2,1,0:T(1,128)S(1)}, s32[1,1,1,1024]{3,2,1,0:T(1,128)}, u32[]{:S(2)}) copy-start(s32[1,1,1,1024]{3,2,1,0:T(1,128)} %param.11) | copy-start | bytes 12292
  44.6 5.1 %collective-permute-start.8 = (f32[2,256]{1,0:T(2,128)S(1)}, f32[2,256]{1,0:T(2,128)S(1)}, u32[]{:S(2)}, u32[]{:S(2)}) collective-permute-start(f32[2,256]{1,0:T(2,128)S(1)} %reshape.146), channel_id=1, source_target_pairs={{1,0},{2,1},{3,2},{5,4},{6,5},{7,6},{9,8},{10,9},{11,10},{13,12},{... | collective-permute-start | bytes 6152 | tf_op jit(solution)/shard_map/ppermute | solution.py:19
  45.9 6.1 %collective-permute-start.6 = (f32[2,1,16,1024]{3,2,1,0:T(8,128)}, f32[2,1,16,1024]{3,2,1,0:T(8,128)S(1)}, u32[]{:S(2)}, u32[]{:S(2)}) collective-permute-start(f32[2,1,16,1024]{3,2,1,0:T(8,128)} %get-tuple-element.22), channel_id=1, source_target_pairs={{16,0},{32,16},{48,32},{64,48},{80,64},{96,80},{112,96},{17,1},{33... | collective-permute-start | bytes 393224 | tf_op jit(solution)/shard_map/ppermute | solution.py:19
  47.2 9.1 %collective-permute-start.7 = (f32[2,16,1,1024]{3,2,1,0:T(1,128)}, f32[2,16,1,1024]{3,2,1,0:T(1,128)S(1)}, u32[]{:S(2)}, u32[]{:S(2)}) collective-permute-start(f32[2,16,1,1024]{3,2,1,0:T(1,128)} %get-tuple-element.23), channel_id=1, source_target_pairs={{4,0},{8,4},{12,8},{5,1},{9,5},{13,9},{6,2},{10,6},{14,10},{7,3},{... | collective-permute-start | bytes 393224 | tf_op jit(solution)/shard_map/ppermute | solution.py:19
  52.0 4.3 %copy-start.3 = (f32[2,1,16,1024]{3,2,1,0:T(8,128)}, f32[2,1,16,1024]{3,2,1,0:T(8,128)S(1)}, u32[]{:S(2)}) copy-start(f32[2,1,16,1024]{3,2,1,0:T(8,128)S(1)} %collective-permute-done.6.hx_ref) | copy-start | bytes 393220
  56.4 0.6 copy-start.6
  63.2 10.1 %collective-permute-start.11 = (f32[2,256]{1,0:T(2,128)S(1)}, f32[2,256]{1,0:T(2,128)S(1)}, u32[]{:S(2)}, u32[]{:S(2)}) collective-permute-start(f32[2,256]{1,0:T(2,128)S(1)} %reshape.148), channel_id=1, source_target_pairs={{0,1},{1,2},{2,3},{4,5},{5,6},{6,7},{8,9},{9,10},{10,11},{12,13},{... | collective-permute-start | bytes 6152 | tf_op jit(solution)/shard_map/ppermute | solution.py:24
  67.7 6.5 %collective-permute-start.10 = (f32[2,16,1,1024]{3,2,1,0:T(1,128)}, f32[2,16,1,1024]{3,2,1,0:T(1,128)S(1)}, u32[]{:S(2)}, u32[]{:S(2)}) collective-permute-start(f32[2,16,1,1024]{3,2,1,0:T(1,128)} %get-tuple-element.27), channel_id=1, source_target_pairs={{0,4},{4,8},{8,12},{1,5},{5,9},{9,13},{2,6},{6,10},{10,14},{3,7},{... | collective-permute-start | bytes 393224 | tf_op jit(solution)/shard_map/ppermute | solution.py:24
  69.8 5.7 %collective-permute-start.9 = (f32[2,1,16,1024]{3,2,1,0:T(8,128)}, f32[2,1,16,1024]{3,2,1,0:T(8,128)S(1)}, u32[]{:S(2)}, u32[]{:S(2)}) collective-permute-start(f32[2,1,16,1024]{3,2,1,0:T(8,128)} %get-tuple-element.26), channel_id=1, source_target_pairs={{0,16},{16,32},{32,48},{48,64},{64,80},{80,96},{96,112},{1,17},{17... | collective-permute-start | bytes 393224 | tf_op jit(solution)/shard_map/ppermute | solution.py:24
  74.1 1.4 %copy-start.5 = (f32[2,16,1,1024]{3,2,1,0:T(1,128)}, f32[2,16,1,1024]{3,2,1,0:T(1,128)S(1)}, u32[]{:S(2)}) copy-start(f32[2,16,1,1024]{3,2,1,0:T(1,128)S(1)} %collective-permute-done.10.hy_ref) | copy-start | bytes 393220
  75.5 0.7 copy-start.7
  76.2 7.9 %copy-start.9 = (s32[1,1,1,1024]{3,2,1,0:T(1,128)S(1)}, s32[1,1,1,1024]{3,2,1,0:T(1,128)}, u32[]{:S(2)}) copy-start(s32[1,1,1,1024]{3,2,1,0:T(1,128)} %param.13) | copy-start | bytes 12292
  76.2 7.9 %copy-start.10 = (s32[1,1,1,1024,1]{3,4,2,1,0:T(1,128)S(1)}, s32[1,1,1,1024,1]{3,4,2,1,0:T(1,128)}, u32[]{:S(2)}) copy-start(s32[1,1,1,1024,1]{3,4,2,1,0:T(1,128)} %param.12) | copy-start | bytes 12292

commit v8 on v7

--- a/solution.py
+++ b/solution.py
@@ -46,6 +46,17 @@
     rolled = pltpu.roll(a, 1, 2)
     at = lax.broadcasted_iota(jnp.int32, a.shape, 2)
     return jnp.where(at == 0, col, rolled)
+
+
+def column_of(row, b, ny):
+    tile = jnp.broadcast_to(row, (128, b * ny))
+    return jnp.transpose(tile).reshape(b, ny, 128)[:, :, 0:1]
+
+
+def row_of(a, lanes):
+    b, ny, _ = a.shape
+    tile = jnp.transpose(a[:, :, lanes].reshape(b * ny, 128))
+    return tile
 
 
 def fwd_x(a, nxt):
@@ -67,14 +78,14 @@
     nxt_z = jnp.where(last, hx_ref[1], en_ref[2])
     ez_yp = fwd_y(ez, hy_ref[1])
     ex_yp = fwd_y(ex, hy_ref[0])
-    ey_zp = fwd_z(ey, hz_ref[1])
-    ex_zp = fwd_z(ex, hz_ref[0])
+    b, ny, nz = ex.shape
+    ey_zp = fwd_z(ey, column_of(hz_ref[1, 0], b, ny))
+    ex_zp = fwd_z(ex, column_of(hz_ref[0, 0], b, ny))
     ez_xp = fwd_x(ez, nxt_z)
     ey_xp = fwd_x(ey, nxt_y)
     out_ref[0] = h_ref[0] - courant * ((ez_yp - ez) - (ey_zp - ey))
     out_ref[1] = h_ref[1] - courant * ((ex_zp - ex) - (ez_xp - ez))
     out_ref[2] = h_ref[2] - courant * ((ey_xp - ey) - (ex_yp - ex))
-    b, ny, nz = ex.shape
 
     @pl.when(last)
     def _():
@@ -83,8 +94,9 @@
 
     fy_ref[0] = out_ref[0, :, ny - 1:ny, :]
     fy_ref[1] = out_ref[2, :, ny - 1:ny, :]
-    fz_ref[0] = out_ref[0, :, :, nz - 1:nz]
-    fz_ref[1] = out_ref[1, :, :, nz - 1:nz]
+    top = slice(nz - 128, nz)
+    fz_ref[0, 0] = row_of(out_ref[0], top)[127:128]
+    fz_ref[1, 0] = row_of(out_ref[1], top)[127:128]
 
 
 def e_update(e_ref, h_ref, hp_ref, inv_ref, hx_ref, hy_ref, hz_ref):
@@ -94,8 +106,9 @@
     prv_z = jnp.where(first, hx_ref[1], hp_ref[2])
     hz_ym = bwd_y(hz, hy_ref[1])
     hx_ym = bwd_y(hx, hy_ref[0])
-    hy_zm = bwd_z(hy, hz_ref[1])
-    hx_zm = bwd_z(hx, hz_ref[0])
+    b, ny, nz = hx.shape
+    hy_zm = bwd_z(hy, column_of(hz_ref[1, 0], b, ny))
+    hx_zm = bwd_z(hx, column_of(hz_ref[0, 0], b, ny))
     hz_xm = bwd_x(hz, prv_z)
     hy_xm = bwd_x(hy, prv_y)
     scale = courant * inv_ref[...]
@@ -118,8 +131,8 @@
 
     fy_ref[0] = out_ref[0, :, 0:1, :]
     fy_ref[1] = out_ref[2, :, 0:1, :]
-    fz_ref[0] = out_ref[0, :, :, 0:1]
-    fz_ref[1] = out_ref[1, :, :, 0:1]
+    fz_ref[0, 0] = row_of(out_ref[0], slice(0, 128))[0:1]
+    fz_ref[1, 0] = row_of(out_ref[1], slice(0, 128))[0:1]
 
 
 def e_last_kernel(
@@ -160,7 +173,7 @@
     return [
         pl.BlockSpec((2, 1, ny, nz), lambda i: (0, 0, 0, 0)),
         pl.BlockSpec((2, chunk, 1, nz), lambda i: (0, i, 0, 0)),
-        pl.BlockSpec((2, chunk, ny, 1), lambda i: (0, i, 0, 0)),
+        pl.BlockSpec((2, 1, 1, chunk * ny), lambda i: (0, i, 0, 0)),
     ]
 
 
@@ -168,12 +181,13 @@
     return [
         jax.ShapeDtypeStruct((2, 1, ny, nz), dtype),
         jax.ShapeDtypeStruct((2, nx, 1, nz), dtype),
-        jax.ShapeDtypeStruct((2, nx, ny, 1), dtype),
+        jax.ShapeDtypeStruct((2, nx // CHUNK, 1, CHUNK * ny), dtype),
     ]
 
 
 def lower_faces_of(e):
-    return e[1:3, 0:1], e[0::2, :, 0:1, :], e[0:2, :, :, 0:1]
+    _, nx, ny, _ = e.shape
+    return e[1:3, 0:1], e[0::2, :, 0:1, :], e[0:2, :, :, 0].reshape(2, nx // CHUNK, 1, CHUNK * ny)
 
 
 def h_step(e, h, faces):
@@ -181,7 +195,7 @@
     chunk = CHUNK
     faces_x = toward_lower(faces[0], "gx")
     faces_y = toward_lower(faces[1], "gy")
-    faces_z = toward_lower(faces[2].reshape(2, nx * ny), "gz").reshape(2, nx, ny, 1)
+    faces_z = toward_lower(faces[2], "gz")
     return pl.pallas_call(
         h_kernel,
         grid=(nx // chunk,),
@@ -191,7 +205,7 @@
             field_spec(nx, ny, nz, chunk),
             pl.BlockSpec((2, 1, ny, nz), lambda i: (0, 0, 0, 0)),
             pl.BlockSpec((2, chunk, 1, nz), lambda i: (0, i, 0, 0)),
-            pl.BlockSpec((2, chunk, ny, 1), lambda i: (0, i, 0, 0)),
+            pl.BlockSpec((2, 1, 1, chunk * ny), lambda i: (0, i, 0, 0)),
         ],
         out_specs=[field_spec(nx, ny, nz, chunk)] + face_specs(nx, ny, nz, chunk),
         out_shape=[jax.ShapeDtypeStruct(h.shape, h.dtype)] + face_shapes(nx, ny, nz, h.dtype),
@@ -203,7 +217,7 @@
     chunk = CHUNK
     faces_x = toward_upper(faces[0], "gx")
     faces_y = toward_upper(faces[1], "gy")
-    faces_z = toward_upper(faces[2].reshape(2, nx * ny), "gz").reshape(2, nx, ny, 1)
+    faces_z = toward_upper(faces[2], "gz")
     in_specs = [
         field_spec(nx, ny, nz, chunk),
         field_spec(nx, ny, nz, chunk),
@@ -211,7 +225,7 @@
         pl.BlockSpec((chunk, ny, nz), lambda i: (i, 0, 0)),
         pl.BlockSpec((2, 1, ny, nz), lambda i: (0, 0, 0, 0)),
         pl.BlockSpec((2, chunk, 1, nz), lambda i: (0, i, 0, 0)),
-        pl.BlockSpec((2, chunk, ny, 1), lambda i: (0, i, 0, 0)),
+        pl.BlockSpec((2, 1, 1, chunk * ny), lambda i: (0, i, 0, 0)),
     ]
     args = [e, h, h, inv, faces_x, faces_y, faces_z]
     if ef is None:

time: 108 us -> 100 us (0.926)
  local copies, waits for them, and re-layouts: 10.1 us -> 6.24 us
  other arithmetic: 5.2 us -> 1.92 us
  blocking collectives: 21.1 us -> 19.7 us
    reshape x8 -> x0, local copies, waits for them, and re-layouts: 3.97 us -> none  [the longest x2 1.82 us: h_step(): toward_lower(faces[2].reshape(2, nx * ny), 'gz').reshape(2, nx, ny, 1)]
    pallas_call x3 -> x0, other arithmetic: 3.27 us -> none  [the longest x2 2.18 us: h_step(): pl.pallas_call(h_kernel, grid=(nx // chunk,), in_specs=[field_spec(nx, ny...]
    all_to_all x1, blocking collectives: 21.1 us -> 19.7 us  [body(): received = lax.all_to_all(per_owner, ('gx', 'gy', 'gz'), 0, 0, tiled=True)]
    unnamed x22 -> x30, local copies, waits for them, and re-layouts: 2.65 us -> 2.71 us
  transfers between devices with their start and end apart: 12 -> 12, of which waited for: 6 -> 6; matrix products, arithmetic and copies ran while one was open for 8% -> 4% of each run, Pallas kernels for 0% -> 0%
where the time goes in v8:
time: 100 us; the launch traced here: 99.8 us
  starting transfers between devices  34.3 us (34%)
  Pallas kernels  23 us (23%)
  blocking collectives  19.7 us (20%)
  waiting for transfers between devices  12.1 us (12%)
  local copies, waits for them, and re-layouts  6.24 us (6%)
  other arithmetic  1.92 us (2%)
  matrix products  1.74 us (2%)
    ppermute x6, starting transfers between devices, toward_upper(): return lax.ppermute(x, axis, [(j, j + 1) for j in range(peers - 1)])  23.9 us
    all_to_all x1, blocking collectives, body(): received = lax.all_to_all(per_owner, ('gx', 'gy', 'gz'), 0, 0, tiled=True)  19.7 us
    ppermute x6, waiting for transfers between devices, toward_lower(): return lax.ppermute(x, axis, [(j, j - 1) for j in range(1, peers)])  10.9 us
    ppermute x6, starting transfers between devices, toward_lower(): return lax.ppermute(x, axis, [(j, j - 1) for j in range(1, peers)])  10.4 us
    pallas_call x2, Pallas kernels, h_step(): pl.pallas_call(h_kernel, grid=(nx // chunk,), in_specs=[field_spec(nx, ny...  9.84 us
    pallas_call x1, Pallas kernels, e_step(): pl.pallas_call(e_last_kernel, grid=(nx // chunk,), in_specs=in_specs + [f...  7.86 us
    pallas_call x1, Pallas kernels, e_step(): pl.pallas_call(e_kernel, grid=(nx // chunk,), in_specs=in_specs, out_spec...  5.26 us
    unnamed x30, local copies, waits for them, and re-layouts  2.71 us
  transfers between devices with their start and end apart: 12, of which 6 were waited for; matrix products, arithmetic and copies ran while one was open for 4% of the time, Pallas kernels for 0%

profile of v8, /device:TPU:1, one launch (start us, length us, event | category | flops | bytes accessed | tf_op | source)
XLA Modules:
  0.0 99.8 jit_solution(6955450112318669584)
XLA Ops:
  0.6 0.9 slice.9
  1.6 1.3 %collective-permute-start = (f32[2,1,16,1024]{3,2,1,0:T(8,128)S(1)}, f32[2,1,16,1024]{3,2,1,0:T(8,128)S(1)}, u32[]{:S(2)}, u32[]{:S(2)}) collective-permute-start(f32[2,1,16,1024]{3,2,1,0:T(8,128)S(1)} %slice.9), channel_id=1, source_target_pairs={{16,0},{32,16},{48,32},{64,48},{80,64},{96,80},{112,96},{17,1},{33... | collective-permute-start | bytes 393224 | tf_op jit(solution)/shard_map/ppermute | solution.py:19
  2.9 1.3 %slice.10 = f32[2,16,1,1024]{3,2,1,0:T(1,128)S(1)} slice(f32[3,16,16,1024]{3,2,1,0:T(8,128)} %e_ref.3), slice={[0:3:2], [0:16:1], [0:1:1], [0:1024:1]} | slice | bytes 262144 | tf_op jit(solution)/shard_map/slice | solution.py:190
  4.2 3.3 %collective-permute-start.1 = (f32[2,16,1,1024]{3,2,1,0:T(1,128)S(1)}, f32[2,16,1,1024]{3,2,1,0:T(1,128)S(1)}, u32[]{:S(2)}, u32[]{:S(2)}) collective-permute-start(f32[2,16,1,1024]{3,2,1,0:T(1,128)S(1)} %slice.10), channel_id=1, source_target_pairs={{4,0},{8,4},{12,8},{5,1},{9,5},{13,9},{6,2},{10,6},{14,10},{7,3},{... | collective-permute-start | bytes 393224 | tf_op jit(solution)/shard_map/ppermute | solution.py:19
  7.5 1.1 %slice_reduce_fusion = f32[2,16,16]{2,1,0:T(8,128)S(1)} fusion(f32[3,16,16,1024]{3,2,1,0:T(8,128)} %e_ref.3), kind=kLoop, calls=%fused_computation.8 | loop fusion | bytes 4096 | tf_op jit(solution)/shard_map/slice | solution.py:190
  8.6 1.3 %collective-permute-start.2 = (f32[2,2,1,128]{3,2,1,0:T(1,128)S(1)}, f32[2,2,1,128]{3,2,1,0:T(1,128)S(1)}, u32[]{:S(2)}, u32[]{:S(2)}) collective-permute-start(f32[2,2,1,128]{3,2,1,0:T(1,128)S(1)} %bitcast.18), channel_id=1, source_target_pairs={{1,0},{2,1},{3,2},{5,4},{6,5},{7,6},{9,8},{10,9},{11,10},{13,12},{... | collective-permute-start | bytes 6152 | tf_op jit(solution)/shard_map/ppermute | solution.py:19
  9.9 3.2 %collective-permute-done.2.hz_ref = f32[2,2,1,128]{3,2,1,0:T(1,128)S(1)} collective-permute-done((f32[2,2,1,128]{3,2,1,0:T(1,128)S(1)}, f32[2,2,1,128]{3,2,1,0:T(1,128)S(1)}, u32[]{:S(2)}, u32[]{:S(2)}) %collective-permute-start.2) | collective-permute-done | bytes 2080 | tf_op jit(solution)/shard_map/ppermute | solution.py:19
  13.1 2.2 %collective-permute-done.1.hy_ref = f32[2,16,1,1024]{3,2,1,0:T(1,128)S(1)} collective-permute-done((f32[2,16,1,1024]{3,2,1,0:T(1,128)S(1)}, f32[2,16,1,1024]{3,2,1,0:T(1,128)S(1)}, u32[]{:S(2)}, u32[]{:S(2)}) %collective-permute-start.1) | collective-permute-done | bytes 131104 | tf_op jit(solution)/shard_map/ppermute | solution.py:19
  15.3 0.6 copy-done.6
  15.9 4.9 %shard_map.94 = (f32[3,16,16,1024]{3,2,1,0:T(8,128)}, f32[2,1,16,1024]{3,2,1,0:T(8,128)}, f32[2,16,1,1024]{3,2,1,0:T(1,128)}, f32[2,2,1,128]{3,2,1,0:T(1,128)}) custom-call(f32[3,16,16,1024]{3,2,1,0:T(8,128)} %e_ref.3, f32[3,16,16,1024]{3,2,1,0:T(8,128)} %e_ref.3, f32[3,16,16,1024]{3,2,1,0:T(8,128)} %h_ref.1, f32[2,1,16,1024]{3,2,1,0:T(8,128)} %copy-done.1, ...), custom_call_target="tpu_custom_call" | custom-call | tf_op jit(solution)/shard_map/pallas_call | solution.py:199
  20.8 2.8 %collective-permute-start.3 = (f32[2,1,16,1024]{3,2,1,0:T(8,128)}, f32[2,1,16,1024]{3,2,1,0:T(8,128)S(1)}, u32[]{:S(2)}, u32[]{:S(2)}) collective-permute-start(f32[2,1,16,1024]{3,2,1,0:T(8,128)} %get-tuple-element.18), channel_id=1, source_target_pairs={{0,16},{16,32},{32,48},{48,64},{64,80},{80,96},{96,112},{1,17},{17... | collective-permute-start | bytes 393224 | tf_op jit(solution)/shard_map/ppermute | solution.py:24
  23.6 6.8 %collective-permute-start.4 = (f32[2,16,1,1024]{3,2,1,0:T(1,128)}, f32[2,16,1,1024]{3,2,1,0:T(1,128)S(1)}, u32[]{:S(2)}, u32[]{:S(2)}) collective-permute-start(f32[2,16,1,1024]{3,2,1,0:T(1,128)} %get-tuple-element.19), channel_id=1, source_target_pairs={{0,4},{4,8},{8,12},{1,5},{5,9},{9,13},{2,6},{6,10},{10,14},{3,7},{... | collective-permute-start | bytes 393224 | tf_op jit(solution)/shard_map/ppermute | solution.py:24
  30.4 3.2 %collective-permute-start.5 = (f32[2,2,1,128]{3,2,1,0:T(1,128)}, f32[2,2,1,128]{3,2,1,0:T(1,128)S(1)}, u32[]{:S(2)}, u32[]{:S(2)}) collective-permute-start(f32[2,2,1,128]{3,2,1,0:T(1,128)} %get-tuple-element.20), channel_id=1, source_target_pairs={{0,1},{1,2},{2,3},{4,5},{5,6},{6,7},{8,9},{9,10},{10,11},{12,13},{... | collective-permute-start | bytes 6152 | tf_op jit(solution)/shard_map/ppermute | solution.py:24
  33.6 0.9 collective-permute-done.5.hz_ref
  34.6 0.6 copy-done.10
  35.2 5.3 %shard_map.95 = (f32[3,16,16,1024]{3,2,1,0:T(8,128)}, f32[2,1,16,1024]{3,2,1,0:T(8,128)}, f32[2,16,1,1024]{3,2,1,0:T(1,128)}, f32[2,2,1,128]{3,2,1,0:T(1,128)}) custom-call(f32[3,16,16,1024]{3,2,1,0:T(8,128)} %e_ref.3, f32[3,16,16,1024]{3,2,1,0:T(8,128)} %get-tuple-element.17.h_ref.hp_ref, f32[3,16,16,1024]{3,2,1,0:T(8,128)} %get-tuple-element.17.h_ref.hp_ref, ...), custom_call_target="tpu_custom_call" | custom-call | tf_op jit(solution)/shard_map/pallas_call | solution.py:232
  40.5 1.3 %collective-permute-start.6 = (f32[2,1,16,1024]{3,2,1,0:T(8,128)}, f32[2,1,16,1024]{3,2,1,0:T(8,128)S(1)}, u32[]{:S(2)}, u32[]{:S(2)}) collective-permute-start(f32[2,1,16,1024]{3,2,1,0:T(8,128)} %get-tuple-element.22), channel_id=1, source_target_pairs={{16,0},{32,16},{48,32},{64,48},{80,64},{96,80},{112,96},{17,1},{33... | collective-permute-start | bytes 393224 | tf_op jit(solution)/shard_map/ppermute | solution.py:19
  41.8 1.9 %collective-permute-start.7 = (f32[2,16,1,1024]{3,2,1,0:T(1,128)}, f32[2,16,1,1024]{3,2,1,0:T(1,128)S(1)}, u32[]{:S(2)}, u32[]{:S(2)}) collective-permute-start(f32[2,16,1,1024]{3,2,1,0:T(1,128)} %get-tuple-element.23), channel_id=1, source_target_pairs={{4,0},{8,4},{12,8},{5,1},{9,5},{13,9},{6,2},{10,6},{14,10},{7,3},{... | collective-permute-start | bytes 393224 | tf_op jit(solution)/shard_map/ppermute | solution.py:19
  43.7 1.3 %collective-permute-start.8 = (f32[2,2,1,128]{3,2,1,0:T(1,128)}, f32[2,2,1,128]{3,2,1,0:T(1,128)S(1)}, u32[]{:S(2)}, u32[]{:S(2)}) collective-permute-start(f32[2,2,1,128]{3,2,1,0:T(1,128)} %get-tuple-element.24), channel_id=1, source_target_pairs={{1,0},{2,1},{3,2},{5,4},{6,5},{7,6},{9,8},{10,9},{11,10},{13,12},{... | collective-permute-start | bytes 6152 | tf_op jit(solution)/shard_map/ppermute | solution.py:19
  45.0 0.6 and_select_fusion
  45.7 2.9 %collective-permute-done.8.hz_ref = f32[2,2,1,128]{3,2,1,0:T(1,128)S(1)} collective-permute-done((f32[2,2,1,128]{3,2,1,0:T(1,128)}, f32[2,2,1,128]{3,2,1,0:T(1,128)S(1)}, u32[]{:S(2)}, u32[]{:S(2)}) %collective-permute-start.8) | collective-permute-done | bytes 2080 | tf_op jit(solution)/shard_map/ppermute | solution.py:19
  48.5 2.7 %collective-permute-done.7.hy_ref = f32[2,16,1,1024]{3,2,1,0:T(1,128)S(1)} collective-permute-done((f32[2,16,1,1024]{3,2,1,0:T(1,128)}, f32[2,16,1,1024]{3,2,1,0:T(1,128)S(1)}, u32[]{:S(2)}, u32[]{:S(2)}) %collective-permute-start.7) | collective-permute-done | bytes 131104 | tf_op jit(solution)/shard_map/ppermute | solution.py:19
  51.2 0.7 copy-done.3
  51.9 4.9 %shard_map.96 = (f32[3,16,16,1024]{3,2,1,0:T(8,128)}, f32[2,1,16,1024]{3,2,1,0:T(8,128)}, f32[2,16,1,1024]{3,2,1,0:T(1,128)}, f32[2,2,1,128]{3,2,1,0:T(1,128)}) custom-call(f32[3,16,16,1024]{3,2,1,0:T(8,128)} %get-tuple-element.21.e_ref.en_ref, f32[3,16,16,1024]{3,2,1,0:T(8,128)} %get-tuple-element.21.e_ref.en_ref, ...), custom_call_target="tpu_custom_call" | custom-call | tf_op jit(solution)/shard_map/pallas_call | solution.py:199
  56.8 3.4 %collective-permute-start.10 = (f32[2,16,1,1024]{3,2,1,0:T(1,128)}, f32[2,16,1,1024]{3,2,1,0:T(1,128)S(1)}, u32[]{:S(2)}, u32[]{:S(2)}) collective-permute-start(f32[2,16,1,1024]{3,2,1,0:T(1,128)} %get-tuple-element.27), channel_id=1, source_target_pairs={{0,4},{4,8},{8,12},{1,5},{5,9},{9,13},{2,6},{6,10},{10,14},{3,7},{... | collective-permute-start | bytes 393224 | tf_op jit(solution)/shard_map/ppermute | solution.py:24
  60.2 4.2 %collective-permute-start.9 = (f32[2,1,16,1024]{3,2,1,0:T(8,128)}, f32[2,1,16,1024]{3,2,1,0:T(8,128)S(1)}, u32[]{:S(2)}, u32[]{:S(2)}) collective-permute-start(f32[2,1,16,1024]{3,2,1,0:T(8,128)} %get-tuple-element.26), channel_id=1, source_target_pairs={{0,16},{16,32},{32,48},{48,64},{64,80},{80,96},{96,112},{1,17},{17... | collective-permute-start | bytes 393224 | tf_op jit(solution)/shard_map/ppermute | solution.py:24
  64.4 3.6 %collective-permute-start.11 = (f32[2,2,1,128]{3,2,1,0:T(1,128)}, f32[2,2,1,128]{3,2,1,0:T(1,128)S(1)}, u32[]{:S(2)}, u32[]{:S(2)}) collective-permute-start(f32[2,2,1,128]{3,2,1,0:T(1,128)} %get-tuple-element.28), channel_id=1, source_target_pairs={{0,1},{1,2},{2,3},{4,5},{5,6},{6,7},{8,9},{9,10},{10,11},{12,13},{... | collective-permute-start | bytes 6152 | tf_op jit(solution)/shard_map/ppermute | solution.py:24
  68.0 0.6 and_select_fusion.1.zrow_ref
  69.7 7.9 %shard_map.97 = (f32[3,16,16,1024]{3,2,1,0:T(8,128)}, f32[1,1024]{1,0:T(1,128)}) custom-call(f32[3,16,16,1024]{3,2,1,0:T(8,128)} %get-tuple-element.21.e_ref.en_ref, f32[3,16,16,1024]{3,2,1,0:T(8,128)} %get-tuple-element.15.h_ref.hp_ref, f32[3,16,16,1024]{3,2,1,0:T(8,128)} %get-tuple-element.15.h_ref.hp_ref, f32[16,16,1024]{2,1,0:T(8,128)} %inv_ref.3, ...), custom_call_target="tpu_custom_call" | custom-call | tf_op jit(solution)/shard_map/pallas_call | solution.py:243
  77.5 1.7 %convolution_bitcast_fusion = f32[128,1,256]{2,0,1:T(8,128)S(1)} fusion(f32[1024]{0:T(1024)} %bitcast.21, s32[1024]{0:T(1024)S(1)} %bitcast.19, s32[1024]{0:T(1024)S(1)} %bitcast.20), kind=kOutput, calls=%fused_computation | convolution fusion | flops 403308544 | bytes 143360 | tf_op jit(solution)/shard_map/dot_general | solution.py:276
  79.4 19.7 %all_to_all.9 = f32[128,1,256]{2,1,0:T(1,128)S(1)} all-to-all(f32[128,1,256]{2,1,0:T(1,128)S(1)} %copy.12), channel_id=1, replica_groups=mesh['gx'=8,'gy'=4,'gz'=4] {'gx','gy','gz'}, dimensions={0} | all-to-all | bytes 262144 | tf_op jit(solution)/shard_map/all_to_all | solution.py:277
  99.1 0.7 reduce_sum.9
  (36 shorter events, 1.4 us)
Async XLA Ops:
  1.6 11.5 %collective-permute-start = (f32[2,1,16,1024]{3,2,1,0:T(8,128)S(1)}, f32[2,1,16,1024]{3,2,1,0:T(8,128)S(1)}, u32[]{:S(2)}, u32[]{:S(2)}) collective-permute-start(f32[2,1,16,1024]{3,2,1,0:T(8,128)S(1)} %slice.9), channel_id=1, source_target_pairs={{16,0},{32,16},{48,32},{64,48},{80,64},{96,80},{112,96},{17,1},{33... | collective-permute-start | bytes 393224 | tf_op jit(solution)/shard_map/ppermute | solution.py:19
  4.2 11.1 %collective-permute-start.1 = (f32[2,16,1,1024]{3,2,1,0:T(1,128)S(1)}, f32[2,16,1,1024]{3,2,1,0:T(1,128)S(1)}, u32[]{:S(2)}, u32[]{:S(2)}) collective-permute-start(f32[2,16,1,1024]{3,2,1,0:T(1,128)S(1)} %slice.10), channel_id=1, source_target_pairs={{4,0},{8,4},{12,8},{5,1},{9,5},{13,9},{6,2},{10,6},{14,10},{7,3},{... | collective-permute-start | bytes 393224 | tf_op jit(solution)/shard_map/ppermute | solution.py:19
  8.6 4.5 %collective-permute-start.2 = (f32[2,2,1,128]{3,2,1,0:T(1,128)S(1)}, f32[2,2,1,128]{3,2,1,0:T(1,128)S(1)}, u32[]{:S(2)}, u32[]{:S(2)}) collective-permute-start(f32[2,2,1,128]{3,2,1,0:T(1,128)S(1)} %bitcast.18), channel_id=1, source_target_pairs={{1,0},{2,1},{3,2},{5,4},{6,5},{7,6},{9,8},{10,9},{11,10},{13,12},{... | collective-permute-start | bytes 6152 | tf_op jit(solution)/shard_map/ppermute | solution.py:19
  13.1 2.2 %copy-start.12 = (f32[2,2,1,128]{3,2,1,0:T(1,128)}, f32[2,2,1,128]{3,2,1,0:T(1,128)S(1)}, u32[]{:S(2)}) copy-start(f32[2,2,1,128]{3,2,1,0:T(1,128)S(1)} %collective-permute-done.2.hz_ref) | copy-start | bytes 6148
  13.1 2.2 %copy-start.1 = (f32[2,1,16,1024]{3,2,1,0:T(8,128)}, f32[2,1,16,1024]{3,2,1,0:T(8,128)S(1)}, u32[]{:S(2)}) copy-start(f32[2,1,16,1024]{3,2,1,0:T(8,128)S(1)} %collective-permute-done.hx_ref) | copy-start | bytes 393220
  15.3 0.6 copy-start.6
  20.8 13.7 %collective-permute-start.3 = (f32[2,1,16,1024]{3,2,1,0:T(8,128)}, f32[2,1,16,1024]{3,2,1,0:T(8,128)S(1)}, u32[]{:S(2)}, u32[]{:S(2)}) collective-permute-start(f32[2,1,16,1024]{3,2,1,0:T(8,128)} %get-tuple-element.18), channel_id=1, source_target_pairs={{0,16},{16,32},{32,48},{48,64},{64,80},{80,96},{96,112},{1,17},{17... | collective-permute-start | bytes 393224 | tf_op jit(solution)/shard_map/ppermute | solution.py:24
  23.6 10.9 %collective-permute-start.4 = (f32[2,16,1,1024]{3,2,1,0:T(1,128)}, f32[2,16,1,1024]{3,2,1,0:T(1,128)S(1)}, u32[]{:S(2)}, u32[]{:S(2)}) collective-permute-start(f32[2,16,1,1024]{3,2,1,0:T(1,128)} %get-tuple-element.19), channel_id=1, source_target_pairs={{0,4},{4,8},{8,12},{1,5},{5,9},{9,13},{2,6},{6,10},{10,14},{3,7},{... | collective-permute-start | bytes 393224 | tf_op jit(solution)/shard_map/ppermute | solution.py:24
  30.4 4.1 %collective-permute-start.5 = (f32[2,2,1,128]{3,2,1,0:T(1,128)}, f32[2,2,1,128]{3,2,1,0:T(1,128)S(1)}, u32[]{:S(2)}, u32[]{:S(2)}) collective-permute-start(f32[2,2,1,128]{3,2,1,0:T(1,128)} %get-tuple-element.20), channel_id=1, source_target_pairs={{0,1},{1,2},{2,3},{4,5},{5,6},{6,7},{8,9},{9,10},{10,11},{12,13},{... | collective-permute-start | bytes 6152 | tf_op jit(solution)/shard_map/ppermute | solution.py:24
  34.5 0.6 copy-start.10
  34.5 0.7 copy-start.4
  34.6 0.7 copy-start.7
  35.2 9.8 %copy-start.8 = (s32[1,1,1,1024]{3,2,1,0:T(1,128)S(1)}, s32[1,1,1,1024]{3,2,1,0:T(1,128)}, u32[]{:S(2)}) copy-start(s32[1,1,1,1024]{3,2,1,0:T(1,128)} %param.11) | copy-start | bytes 12292
  40.5 8.0 %collective-permute-start.6 = (f32[2,1,16,1024]{3,2,1,0:T(8,128)}, f32[2,1,16,1024]{3,2,1,0:T(8,128)S(1)}, u32[]{:S(2)}, u32[]{:S(2)}) collective-permute-start(f32[2,1,16,1024]{3,2,1,0:T(8,128)} %get-tuple-element.22), channel_id=1, source_target_pairs={{16,0},{32,16},{48,32},{64,48},{80,64},{96,80},{112,96},{17,1},{33... | collective-permute-start | bytes 393224 | tf_op jit(solution)/shard_map/ppermute | solution.py:19
  41.8 9.4 %collective-permute-start.7 = (f32[2,16,1,1024]{3,2,1,0:T(1,128)}, f32[2,16,1,1024]{3,2,1,0:T(1,128)S(1)}, u32[]{:S(2)}, u32[]{:S(2)}) collective-permute-start(f32[2,16,1,1024]{3,2,1,0:T(1,128)} %get-tuple-element.23), channel_id=1, source_target_pairs={{4,0},{8,4},{12,8},{5,1},{9,5},{13,9},{6,2},{10,6},{14,10},{7,3},{... | collective-permute-start | bytes 393224 | tf_op jit(solution)/shard_map/ppermute | solution.py:19
  43.7 4.8 %collective-permute-start.8 = (f32[2,2,1,128]{3,2,1,0:T(1,128)}, f32[2,2,1,128]{3,2,1,0:T(1,128)S(1)}, u32[]{:S(2)}, u32[]{:S(2)}) collective-permute-start(f32[2,2,1,128]{3,2,1,0:T(1,128)} %get-tuple-element.24), channel_id=1, source_target_pairs={{1,0},{2,1},{3,2},{5,4},{6,5},{7,6},{9,8},{10,9},{11,10},{13,12},{... | collective-permute-start | bytes 6152 | tf_op jit(solution)/shard_map/ppermute | solution.py:19
  48.5 2.7 %copy-start.11 = (f32[2,2,1,128]{3,2,1,0:T(1,128)}, f32[2,2,1,128]{3,2,1,0:T(1,128)S(1)}, u32[]{:S(2)}) copy-start(f32[2,2,1,128]{3,2,1,0:T(1,128)S(1)} %collective-permute-done.8.hz_ref) | copy-start | bytes 6148
  48.5 2.7 %copy-start = (f32[2,1,16,1024]{3,2,1,0:T(8,128)}, f32[2,1,16,1024]{3,2,1,0:T(8,128)S(1)}, u32[]{:S(2)}) copy-start(f32[2,1,16,1024]{3,2,1,0:T(8,128)S(1)} %collective-permute-done.6.hx_ref) | copy-start | bytes 393220
  51.2 0.7 copy-start.3
  56.8 12.1 %collective-permute-start.10 = (f32[2,16,1,1024]{3,2,1,0:T(1,128)}, f32[2,16,1,1024]{3,2,1,0:T(1,128)S(1)}, u32[]{:S(2)}, u32[]{:S(2)}) collective-permute-start(f32[2,16,1,1024]{3,2,1,0:T(1,128)} %get-tuple-element.27), channel_id=1, source_target_pairs={{0,4},{4,8},{8,12},{1,5},{5,9},{9,13},{2,6},{6,10},{10,14},{3,7},{... | collective-permute-start | bytes 393224 | tf_op jit(solution)/shard_map/ppermute | solution.py:24
  60.2 8.7 %collective-permute-start.9 = (f32[2,1,16,1024]{3,2,1,0:T(8,128)}, f32[2,1,16,1024]{3,2,1,0:T(8,128)S(1)}, u32[]{:S(2)}, u32[]{:S(2)}) collective-permute-start(f32[2,1,16,1024]{3,2,1,0:T(8,128)} %get-tuple-element.26), channel_id=1, source_target_pairs={{0,16},{16,32},{32,48},{48,64},{64,80},{80,96},{96,112},{1,17},{17... | collective-permute-start | bytes 393224 | tf_op jit(solution)/shard_map/ppermute | solution.py:24
  64.4 4.5 %collective-permute-start.11 = (f32[2,2,1,128]{3,2,1,0:T(1,128)}, f32[2,2,1,128]{3,2,1,0:T(1,128)S(1)}, u32[]{:S(2)}, u32[]{:S(2)}) collective-permute-start(f32[2,2,1,128]{3,2,1,0:T(1,128)} %get-tuple-element.28), channel_id=1, source_target_pairs={{0,1},{1,2},{2,3},{4,5},{5,6},{6,7},{8,9},{9,10},{10,11},{12,13},{... | collective-permute-start | bytes 6152 | tf_op jit(solution)/shard_map/ppermute | solution.py:24
  68.9 0.6 copy-start.9
  68.9 0.7 copy-start.2
  68.9 0.7 copy-start.5
  69.7 7.9 %copy-start.13 = (s32[1,1,1,1024]{3,2,1,0:T(1,128)S(1)}, s32[1,1,1,1024]{3,2,1,0:T(1,128)}, u32[]{:S(2)}) copy-start(s32[1,1,1,1024]{3,2,1,0:T(1,128)} %param.13) | copy-start | bytes 12292
  69.7 7.9 %copy-start.14 = (s32[1,1,1,1024,1]{3,4,2,1,0:T(1,128)S(1)}, s32[1,1,1,1024,1]{3,4,2,1,0:T(1,128)}, u32[]{:S(2)}) copy-start(s32[1,1,1,1024,1]{3,4,2,1,0:T(1,128)} %param.12) | copy-start | bytes 12292

commit v9 on v8

--- a/solution.py
+++ b/solution.py
@@ -185,9 +185,35 @@
     ]
 
 
+def faces_kernel(slab_ref, rows_ref, lanes_ref, fx_ref, fy_ref, fz_ref):
+    fx_ref[0] = slab_ref[1]
+    fx_ref[1] = slab_ref[2]
+    fy_ref[0] = rows_ref[0, :, 0:1, :]
+    fy_ref[1] = rows_ref[2, :, 0:1, :]
+    nx = lanes_ref.shape[1]
+    for i in range(nx // CHUNK):
+        part = slice(i * CHUNK, (i + 1) * CHUNK)
+        fz_ref[0, i] = row_of(lanes_ref[0, part], slice(0, 128))[0:1]
+        fz_ref[1, i] = row_of(lanes_ref[1, part], slice(0, 128))[0:1]
+
+
 def lower_faces_of(e):
-    _, nx, ny, _ = e.shape
-    return e[1:3, 0:1], e[0::2, :, 0:1, :], e[0:2, :, :, 0].reshape(2, nx // CHUNK, 1, CHUNK * ny)
+    _, nx, ny, nz = e.shape
+    return pl.pallas_call(
+        faces_kernel,
+        grid=(1,),
+        in_specs=[
+            pl.BlockSpec((3, 1, ny, nz), lambda i: (0, 0, 0, 0)),
+            pl.BlockSpec((3, nx, 8, nz), lambda i: (0, 0, 0, 0)),
+            pl.BlockSpec((3, nx, ny, 128), lambda i: (0, 0, 0, 0)),
+        ],
+        out_specs=[
+            pl.BlockSpec((2, 1, ny, nz), lambda i: (0, 0, 0, 0)),
+            pl.BlockSpec((2, nx, 1, nz), lambda i: (0, 0, 0, 0)),
+            pl.BlockSpec((2, nx // CHUNK, 1, CHUNK * ny), lambda i: (0, 0, 0, 0)),
+        ],
+        out_shape=face_shapes(nx, ny, nz, e.dtype),
+    )(e, e, e)
 
 
 def h_step(e, h, faces):

time: 100 us -> 99.4 us (level)
  local copies, waits for them, and re-layouts: 6.24 us -> 2.84 us
  waiting for transfers between devices: 12.1 us -> 14.8 us
  starting transfers between devices: 34.3 us -> 31.9 us
  Pallas kernels: 23 us -> 25.3 us
    slice x3 -> x0, local copies, waits for them, and re-layouts: 3.31 us -> none  [the longest x1 1.3 us: lower_faces_of(): e[0::2, :, 0:1, :]]
    ppermute x6, waiting for transfers between devices: 10.9 us -> 13.5 us  [toward_lower(): return lax.ppermute(x, axis, [(j, j - 1) for j in range(1, peers)])]
    ppermute x6, starting transfers between devices: 23.9 us -> 21.5 us  [toward_upper(): return lax.ppermute(x, axis, [(j, j + 1) for j in range(peers - 1)])]
    pallas_call x0 -> x1, Pallas kernels: none -> 2.33 us  [lower_faces_of(): pl.pallas_call(faces_kernel, grid=(1,), in_specs=[pl.BlockSpec((3, 1, ny,...]
  transfers between devices with their start and end apart: 12 -> 12, of which waited for: 6 -> 6; matrix products, arithmetic and copies ran while one was open for 4% -> 1% of each run, Pallas kernels for 0% -> 0%
where the time goes in v9:
time: 99.4 us; the launch traced here: 98.9 us
  starting transfers between devices  31.9 us (32%)
  Pallas kernels  25.3 us (25%)
  blocking collectives  19.7 us (20%)
  waiting for transfers between devices  14.8 us (15%)
  local copies, waits for them, and re-layouts  2.84 us (3%)
  other arithmetic  1.92 us (2%)
  matrix products  1.73 us (2%)
    ppermute x6, starting transfers between devices, toward_upper(): return lax.ppermute(x, axis, [(j, j + 1) for j in range(peers - 1)])  21.5 us
    all_to_all x1, blocking collectives, body(): received = lax.all_to_all(per_owner, ('gx', 'gy', 'gz'), 0, 0, tiled=True)  19.7 us
    ppermute x6, waiting for transfers between devices, toward_lower(): return lax.ppermute(x, axis, [(j, j - 1) for j in range(1, peers)])  13.5 us
    ppermute x6, starting transfers between devices, toward_lower(): return lax.ppermute(x, axis, [(j, j - 1) for j in range(1, peers)])  10.4 us
    pallas_call x2, Pallas kernels, h_step(): pl.pallas_call(h_kernel, grid=(nx // chunk,), in_specs=[field_spec(nx, ny...  9.84 us
    pallas_call x1, Pallas kernels, e_step(): pl.pallas_call(e_last_kernel, grid=(nx // chunk,), in_specs=in_specs + [f...  7.86 us
    pallas_call x1, Pallas kernels, e_step(): pl.pallas_call(e_kernel, grid=(nx // chunk,), in_specs=in_specs, out_spec...  5.25 us
    unnamed x30, local copies, waits for them, and re-layouts  2.71 us
  transfers between devices with their start and end apart: 12, of which 6 were waited for; matrix products, arithmetic and copies ran while one was open for 1% of the time, Pallas kernels for 0%

profile of v9, /device:TPU:1, one launch (start us, length us, event | category | flops | bytes accessed | tf_op | source)
XLA Modules:
  0.0 98.9 jit_solution(4985509481856306406)
XLA Ops:
  0.6 2.3 %shard_map.94 = (f32[2,1,16,1024]{3,2,1,0:T(8,128)}, f32[2,16,1,1024]{3,2,1,0:T(1,128)}, f32[2,2,1,128]{3,2,1,0:T(1,128)}) custom-call(f32[3,16,16,1024]{3,2,1,0:T(8,128)} %e_ref.3, f32[3,16,16,1024]{3,2,1,0:T(8,128)} %e_ref.3, f32[3,16,16,1024]{3,2,1,0:T(8,128)} %e_ref.3), custom_call_target="tpu_custom_call" | custom-call | tf_op jit(solution)/shard_map/pallas_call | solution.py:202
  3.0 1.3 %collective-permute-start = (f32[2,1,16,1024]{3,2,1,0:T(8,128)}, f32[2,1,16,1024]{3,2,1,0:T(8,128)S(1)}, u32[]{:S(2)}, u32[]{:S(2)}) collective-permute-start(f32[2,1,16,1024]{3,2,1,0:T(8,128)} %get-tuple-element.20), channel_id=1, source_target_pairs={{16,0},{32,16},{48,32},{64,48},{80,64},{96,80},{112,96},{17,1},{33... | collective-permute-start | bytes 393224 | tf_op jit(solution)/shard_map/ppermute | solution.py:19
  4.2 3.3 %collective-permute-start.1 = (f32[2,16,1,1024]{3,2,1,0:T(1,128)}, f32[2,16,1,1024]{3,2,1,0:T(1,128)S(1)}, u32[]{:S(2)}, u32[]{:S(2)}) collective-permute-start(f32[2,16,1,1024]{3,2,1,0:T(1,128)} %get-tuple-element.21), channel_id=1, source_target_pairs={{4,0},{8,4},{12,8},{5,1},{9,5},{13,9},{6,2},{10,6},{14,10},{7,3},{... | collective-permute-start | bytes 393224 | tf_op jit(solution)/shard_map/ppermute | solution.py:19
  7.5 1.3 %collective-permute-start.2 = (f32[2,2,1,128]{3,2,1,0:T(1,128)}, f32[2,2,1,128]{3,2,1,0:T(1,128)S(1)}, u32[]{:S(2)}, u32[]{:S(2)}) collective-permute-start(f32[2,2,1,128]{3,2,1,0:T(1,128)} %get-tuple-element.22), channel_id=1, source_target_pairs={{1,0},{2,1},{3,2},{5,4},{6,5},{7,6},{9,8},{10,9},{11,10},{13,12},{... | collective-permute-start | bytes 6152 | tf_op jit(solution)/shard_map/ppermute | solution.py:19
  8.8 3.4 %collective-permute-done.2.hz_ref = f32[2,2,1,128]{3,2,1,0:T(1,128)S(1)} collective-permute-done((f32[2,2,1,128]{3,2,1,0:T(1,128)}, f32[2,2,1,128]{3,2,1,0:T(1,128)S(1)}, u32[]{:S(2)}, u32[]{:S(2)}) %collective-permute-start.2) | collective-permute-done | bytes 2080 | tf_op jit(solution)/shard_map/ppermute | solution.py:19
  12.2 4.6 %collective-permute-done.1.hy_ref = f32[2,16,1,1024]{3,2,1,0:T(1,128)S(1)} collective-permute-done((f32[2,16,1,1024]{3,2,1,0:T(1,128)}, f32[2,16,1,1024]{3,2,1,0:T(1,128)S(1)}, u32[]{:S(2)}, u32[]{:S(2)}) %collective-permute-start.1) | collective-permute-done | bytes 131104 | tf_op jit(solution)/shard_map/ppermute | solution.py:19
  16.8 0.7 copy-done.6
  17.5 4.9 %shard_map.95 = (f32[3,16,16,1024]{3,2,1,0:T(8,128)}, f32[2,1,16,1024]{3,2,1,0:T(8,128)}, f32[2,16,1,1024]{3,2,1,0:T(1,128)}, f32[2,2,1,128]{3,2,1,0:T(1,128)}) custom-call(f32[3,16,16,1024]{3,2,1,0:T(8,128)} %e_ref.3, f32[3,16,16,1024]{3,2,1,0:T(8,128)} %e_ref.3, f32[3,16,16,1024]{3,2,1,0:T(8,128)} %h_ref.1, f32[2,1,16,1024]{3,2,1,0:T(8,128)} %copy-done.3, ...), custom_call_target="tpu_custom_call" | custom-call | tf_op jit(solution)/shard_map/pallas_call | solution.py:225
  22.4 1.3 %collective-permute-start.3 = (f32[2,1,16,1024]{3,2,1,0:T(8,128)}, f32[2,1,16,1024]{3,2,1,0:T(8,128)S(1)}, u32[]{:S(2)}, u32[]{:S(2)}) collective-permute-start(f32[2,1,16,1024]{3,2,1,0:T(8,128)} %get-tuple-element.24), channel_id=1, source_target_pairs={{0,16},{16,32},{32,48},{48,64},{64,80},{80,96},{96,112},{1,17},{17... | collective-permute-start | bytes 393224 | tf_op jit(solution)/shard_map/ppermute | solution.py:24
  23.7 5.9 %collective-permute-start.4 = (f32[2,16,1,1024]{3,2,1,0:T(1,128)}, f32[2,16,1,1024]{3,2,1,0:T(1,128)S(1)}, u32[]{:S(2)}, u32[]{:S(2)}) collective-permute-start(f32[2,16,1,1024]{3,2,1,0:T(1,128)} %get-tuple-element.25), channel_id=1, source_target_pairs={{0,4},{4,8},{8,12},{1,5},{5,9},{9,13},{2,6},{6,10},{10,14},{3,7},{... | collective-permute-start | bytes 393224 | tf_op jit(solution)/shard_map/ppermute | solution.py:24
  29.5 3.2 %collective-permute-start.5 = (f32[2,2,1,128]{3,2,1,0:T(1,128)}, f32[2,2,1,128]{3,2,1,0:T(1,128)S(1)}, u32[]{:S(2)}, u32[]{:S(2)}) collective-permute-start(f32[2,2,1,128]{3,2,1,0:T(1,128)} %get-tuple-element.26), channel_id=1, source_target_pairs={{0,1},{1,2},{2,3},{4,5},{5,6},{6,7},{8,9},{9,10},{10,11},{12,13},{... | collective-permute-start | bytes 6152 | tf_op jit(solution)/shard_map/ppermute | solution.py:24
  32.7 0.9 collective-permute-done.5.hz_ref
  33.7 0.6 copy-done.10
  34.4 5.2 %shard_map.96 = (f32[3,16,16,1024]{3,2,1,0:T(8,128)}, f32[2,1,16,1024]{3,2,1,0:T(8,128)}, f32[2,16,1,1024]{3,2,1,0:T(1,128)}, f32[2,2,1,128]{3,2,1,0:T(1,128)}) custom-call(f32[3,16,16,1024]{3,2,1,0:T(8,128)} %e_ref.3, f32[3,16,16,1024]{3,2,1,0:T(8,128)} %get-tuple-element.23.h_ref.hp_ref, f32[3,16,16,1024]{3,2,1,0:T(8,128)} %get-tuple-element.23.h_ref.hp_ref, ...), custom_call_target="tpu_custom_call" | custom-call | tf_op jit(solution)/shard_map/pallas_call | solution.py:258
  39.6 1.3 %collective-permute-start.6 = (f32[2,1,16,1024]{3,2,1,0:T(8,128)}, f32[2,1,16,1024]{3,2,1,0:T(8,128)S(1)}, u32[]{:S(2)}, u32[]{:S(2)}) collective-permute-start(f32[2,1,16,1024]{3,2,1,0:T(8,128)} %get-tuple-element.28), channel_id=1, source_target_pairs={{16,0},{32,16},{48,32},{64,48},{80,64},{96,80},{112,96},{17,1},{33... | collective-permute-start | bytes 393224 | tf_op jit(solution)/shard_map/ppermute | solution.py:19
  40.9 1.9 %collective-permute-start.7 = (f32[2,16,1,1024]{3,2,1,0:T(1,128)}, f32[2,16,1,1024]{3,2,1,0:T(1,128)S(1)}, u32[]{:S(2)}, u32[]{:S(2)}) collective-permute-start(f32[2,16,1,1024]{3,2,1,0:T(1,128)} %get-tuple-element.29), channel_id=1, source_target_pairs={{4,0},{8,4},{12,8},{5,1},{9,5},{13,9},{6,2},{10,6},{14,10},{7,3},{... | collective-permute-start | bytes 393224 | tf_op jit(solution)/shard_map/ppermute | solution.py:19
  42.8 1.3 %collective-permute-start.8 = (f32[2,2,1,128]{3,2,1,0:T(1,128)}, f32[2,2,1,128]{3,2,1,0:T(1,128)S(1)}, u32[]{:S(2)}, u32[]{:S(2)}) collective-permute-start(f32[2,2,1,128]{3,2,1,0:T(1,128)} %get-tuple-element.30), channel_id=1, source_target_pairs={{1,0},{2,1},{3,2},{5,4},{6,5},{7,6},{9,8},{10,9},{11,10},{13,12},{... | collective-permute-start | bytes 6152 | tf_op jit(solution)/shard_map/ppermute | solution.py:19
  44.1 0.6 and_select_fusion
  44.8 2.9 %collective-permute-done.8.hz_ref = f32[2,2,1,128]{3,2,1,0:T(1,128)S(1)} collective-permute-done((f32[2,2,1,128]{3,2,1,0:T(1,128)}, f32[2,2,1,128]{3,2,1,0:T(1,128)S(1)}, u32[]{:S(2)}, u32[]{:S(2)}) %collective-permute-start.8) | collective-permute-done | bytes 2080 | tf_op jit(solution)/shard_map/ppermute | solution.py:19
  47.6 2.7 %collective-permute-done.7.hy_ref = f32[2,16,1,1024]{3,2,1,0:T(1,128)S(1)} collective-permute-done((f32[2,16,1,1024]{3,2,1,0:T(1,128)}, f32[2,16,1,1024]{3,2,1,0:T(1,128)S(1)}, u32[]{:S(2)}, u32[]{:S(2)}) %collective-permute-start.7) | collective-permute-done | bytes 131104 | tf_op jit(solution)/shard_map/ppermute | solution.py:19
  50.3 0.7 copy-done.2
  51.0 4.9 %shard_map.97 = (f32[3,16,16,1024]{3,2,1,0:T(8,128)}, f32[2,1,16,1024]{3,2,1,0:T(8,128)}, f32[2,16,1,1024]{3,2,1,0:T(1,128)}, f32[2,2,1,128]{3,2,1,0:T(1,128)}) custom-call(f32[3,16,16,1024]{3,2,1,0:T(8,128)} %get-tuple-element.27.e_ref.en_ref, f32[3,16,16,1024]{3,2,1,0:T(8,128)} %get-tuple-element.27.e_ref.en_ref, ...), custom_call_target="tpu_custom_call" | custom-call | tf_op jit(solution)/shard_map/pallas_call | solution.py:225
  55.9 3.4 %collective-permute-start.10 = (f32[2,16,1,1024]{3,2,1,0:T(1,128)}, f32[2,16,1,1024]{3,2,1,0:T(1,128)S(1)}, u32[]{:S(2)}, u32[]{:S(2)}) collective-permute-start(f32[2,16,1,1024]{3,2,1,0:T(1,128)} %get-tuple-element.33), channel_id=1, source_target_pairs={{0,4},{4,8},{8,12},{1,5},{5,9},{9,13},{2,6},{6,10},{10,14},{3,7},{... | collective-permute-start | bytes 393224 | tf_op jit(solution)/shard_map/ppermute | solution.py:24
  59.3 4.2 %collective-permute-start.9 = (f32[2,1,16,1024]{3,2,1,0:T(8,128)}, f32[2,1,16,1024]{3,2,1,0:T(8,128)S(1)}, u32[]{:S(2)}, u32[]{:S(2)}) collective-permute-start(f32[2,1,16,1024]{3,2,1,0:T(8,128)} %get-tuple-element.32), channel_id=1, source_target_pairs={{0,16},{16,32},{32,48},{48,64},{64,80},{80,96},{96,112},{1,17},{17... | collective-permute-start | bytes 393224 | tf_op jit(solution)/shard_map/ppermute | solution.py:24
  63.5 3.6 %collective-permute-start.11 = (f32[2,2,1,128]{3,2,1,0:T(1,128)}, f32[2,2,1,128]{3,2,1,0:T(1,128)S(1)}, u32[]{:S(2)}, u32[]{:S(2)}) collective-permute-start(f32[2,2,1,128]{3,2,1,0:T(1,128)} %get-tuple-element.34), channel_id=1, source_target_pairs={{0,1},{1,2},{2,3},{4,5},{5,6},{6,7},{8,9},{9,10},{10,11},{12,13},{... | collective-permute-start | bytes 6152 | tf_op jit(solution)/shard_map/ppermute | solution.py:24
  67.1 0.6 and_select_fusion.1.zrow_ref
  67.7 0.3 collective-permute-done.11.hz_ref
  68.1 0.5 copy-done.9
  68.8 7.9 %shard_map.98 = (f32[3,16,16,1024]{3,2,1,0:T(8,128)}, f32[1,1024]{1,0:T(1,128)}) custom-call(f32[3,16,16,1024]{3,2,1,0:T(8,128)} %get-tuple-element.27.e_ref.en_ref, f32[3,16,16,1024]{3,2,1,0:T(8,128)} %get-tuple-element.18.h_ref.hp_ref, f32[3,16,16,1024]{3,2,1,0:T(8,128)} %get-tuple-element.18.h_ref.hp_ref, f32[16,16,1024]{2,1,0:T(8,128)} %inv_ref.3, ...), custom_call_target="tpu_custom_call" | custom-call | tf_op jit(solution)/shard_map/pallas_call | solution.py:269
  76.6 1.7 %convolution_bitcast_fusion = f32[128,1,256]{2,0,1:T(8,128)S(1)} fusion(f32[1024]{0:T(1024)} %bitcast.19, s32[1024]{0:T(1024)S(1)} %bitcast.17, s32[1024]{0:T(1024)S(1)} %bitcast.18), kind=kOutput, calls=%fused_computation | convolution fusion | flops 403308544 | bytes 143360 | tf_op jit(solution)/shard_map/dot_general | solution.py:302
  78.5 19.7 %all_to_all.9 = f32[128,1,256]{2,1,0:T(1,128)S(1)} all-to-all(f32[128,1,256]{2,1,0:T(1,128)S(1)} %copy.10), channel_id=1, replica_groups=mesh['gx'=8,'gy'=4,'gz'=4] {'gx','gy','gz'}, dimensions={0} | all-to-all | bytes 262144 | tf_op jit(solution)/shard_map/all_to_all | solution.py:303
  98.2 0.7 reduce_sum.9
  (33 shorter events, 0.5 us)
Async XLA Ops:
  3.0 9.3 %collective-permute-start = (f32[2,1,16,1024]{3,2,1,0:T(8,128)}, f32[2,1,16,1024]{3,2,1,0:T(8,128)S(1)}, u32[]{:S(2)}, u32[]{:S(2)}) collective-permute-start(f32[2,1,16,1024]{3,2,1,0:T(8,128)} %get-tuple-element.20), channel_id=1, source_target_pairs={{16,0},{32,16},{48,32},{64,48},{80,64},{96,80},{112,96},{17,1},{33... | collective-permute-start | bytes 393224 | tf_op jit(solution)/shard_map/ppermute | solution.py:19
  4.2 12.5 %collective-permute-start.1 = (f32[2,16,1,1024]{3,2,1,0:T(1,128)}, f32[2,16,1,1024]{3,2,1,0:T(1,128)S(1)}, u32[]{:S(2)}, u32[]{:S(2)}) collective-permute-start(f32[2,16,1,1024]{3,2,1,0:T(1,128)} %get-tuple-element.21), channel_id=1, source_target_pairs={{4,0},{8,4},{12,8},{5,1},{9,5},{13,9},{6,2},{10,6},{14,10},{7,3},{... | collective-permute-start | bytes 393224 | tf_op jit(solution)/shard_map/ppermute | solution.py:19
  7.5 4.7 %collective-permute-start.2 = (f32[2,2,1,128]{3,2,1,0:T(1,128)}, f32[2,2,1,128]{3,2,1,0:T(1,128)S(1)}, u32[]{:S(2)}, u32[]{:S(2)}) collective-permute-start(f32[2,2,1,128]{3,2,1,0:T(1,128)} %get-tuple-element.22), channel_id=1, source_target_pairs={{1,0},{2,1},{3,2},{5,4},{6,5},{7,6},{9,8},{10,9},{11,10},{13,12},{... | collective-permute-start | bytes 6152 | tf_op jit(solution)/shard_map/ppermute | solution.py:19
  12.2 4.6 %copy-start.12 = (f32[2,2,1,128]{3,2,1,0:T(1,128)}, f32[2,2,1,128]{3,2,1,0:T(1,128)S(1)}, u32[]{:S(2)}) copy-start(f32[2,2,1,128]{3,2,1,0:T(1,128)S(1)} %collective-permute-done.2.hz_ref) | copy-start | bytes 6148
  12.2 4.6 %copy-start.3 = (f32[2,1,16,1024]{3,2,1,0:T(8,128)}, f32[2,1,16,1024]{3,2,1,0:T(8,128)S(1)}, u32[]{:S(2)}) copy-start(f32[2,1,16,1024]{3,2,1,0:T(8,128)S(1)} %collective-permute-done.hx_ref) | copy-start | bytes 393220
  16.8 0.7 copy-start.6
  22.4 11.3 %collective-permute-start.3 = (f32[2,1,16,1024]{3,2,1,0:T(8,128)}, f32[2,1,16,1024]{3,2,1,0:T(8,128)S(1)}, u32[]{:S(2)}, u32[]{:S(2)}) collective-permute-start(f32[2,1,16,1024]{3,2,1,0:T(8,128)} %get-tuple-element.24), channel_id=1, source_target_pairs={{0,16},{16,32},{32,48},{48,64},{64,80},{80,96},{96,112},{1,17},{17... | collective-permute-start | bytes 393224 | tf_op jit(solution)/shard_map/ppermute | solution.py:24
  23.7 10.0 %collective-permute-start.4 = (f32[2,16,1,1024]{3,2,1,0:T(1,128)}, f32[2,16,1,1024]{3,2,1,0:T(1,128)S(1)}, u32[]{:S(2)}, u32[]{:S(2)}) collective-permute-start(f32[2,16,1,1024]{3,2,1,0:T(1,128)} %get-tuple-element.25), channel_id=1, source_target_pairs={{0,4},{4,8},{8,12},{1,5},{5,9},{9,13},{2,6},{6,10},{10,14},{3,7},{... | collective-permute-start | bytes 393224 | tf_op jit(solution)/shard_map/ppermute | solution.py:24
  29.5 4.1 %collective-permute-start.5 = (f32[2,2,1,128]{3,2,1,0:T(1,128)}, f32[2,2,1,128]{3,2,1,0:T(1,128)S(1)}, u32[]{:S(2)}, u32[]{:S(2)}) collective-permute-start(f32[2,2,1,128]{3,2,1,0:T(1,128)} %get-tuple-element.26), channel_id=1, source_target_pairs={{0,1},{1,2},{2,3},{4,5},{5,6},{6,7},{8,9},{9,10},{10,11},{12,13},{... | collective-permute-start | bytes 6152 | tf_op jit(solution)/shard_map/ppermute | solution.py:24
  33.7 0.6 copy-start.10
  33.7 0.7 copy-start.4
  33.7 0.7 copy-start.7
  34.4 9.8 %copy-start.8 = (s32[1,1,1,1024]{3,2,1,0:T(1,128)S(1)}, s32[1,1,1,1024]{3,2,1,0:T(1,128)}, u32[]{:S(2)}) copy-start(s32[1,1,1,1024]{3,2,1,0:T(1,128)} %param.11) | copy-start | bytes 12292
  39.6 8.0 %collective-permute-start.6 = (f32[2,1,16,1024]{3,2,1,0:T(8,128)}, f32[2,1,16,1024]{3,2,1,0:T(8,128)S(1)}, u32[]{:S(2)}, u32[]{:S(2)}) collective-permute-start(f32[2,1,16,1024]{3,2,1,0:T(8,128)} %get-tuple-element.28), channel_id=1, source_target_pairs={{16,0},{32,16},{48,32},{64,48},{80,64},{96,80},{112,96},{17,1},{33... | collective-permute-start | bytes 393224 | tf_op jit(solution)/shard_map/ppermute | solution.py:19
  40.9 9.4 %collective-permute-start.7 = (f32[2,16,1,1024]{3,2,1,0:T(1,128)}, f32[2,16,1,1024]{3,2,1,0:T(1,128)S(1)}, u32[]{:S(2)}, u32[]{:S(2)}) collective-permute-start(f32[2,16,1,1024]{3,2,1,0:T(1,128)} %get-tuple-element.29), channel_id=1, source_target_pairs={{4,0},{8,4},{12,8},{5,1},{9,5},{13,9},{6,2},{10,6},{14,10},{7,3},{... | collective-permute-start | bytes 393224 | tf_op jit(solution)/shard_map/ppermute | solution.py:19
  42.8 4.8 %collective-permute-start.8 = (f32[2,2,1,128]{3,2,1,0:T(1,128)}, f32[2,2,1,128]{3,2,1,0:T(1,128)S(1)}, u32[]{:S(2)}, u32[]{:S(2)}) collective-permute-start(f32[2,2,1,128]{3,2,1,0:T(1,128)} %get-tuple-element.30), channel_id=1, source_target_pairs={{1,0},{2,1},{3,2},{5,4},{6,5},{7,6},{9,8},{10,9},{11,10},{13,12},{... | collective-permute-start | bytes 6152 | tf_op jit(solution)/shard_map/ppermute | solution.py:19
  47.6 2.7 %copy-start.11 = (f32[2,2,1,128]{3,2,1,0:T(1,128)}, f32[2,2,1,128]{3,2,1,0:T(1,128)S(1)}, u32[]{:S(2)}) copy-start(f32[2,2,1,128]{3,2,1,0:T(1,128)S(1)} %collective-permute-done.8.hz_ref) | copy-start | bytes 6148
  47.6 2.7 %copy-start = (f32[2,1,16,1024]{3,2,1,0:T(8,128)}, f32[2,1,16,1024]{3,2,1,0:T(8,128)S(1)}, u32[]{:S(2)}) copy-start(f32[2,1,16,1024]{3,2,1,0:T(8,128)S(1)} %collective-permute-done.6.hx_ref) | copy-start | bytes 393220
  50.3 0.7 copy-start.2
  55.9 12.2 %collective-permute-start.10 = (f32[2,16,1,1024]{3,2,1,0:T(1,128)}, f32[2,16,1,1024]{3,2,1,0:T(1,128)S(1)}, u32[]{:S(2)}, u32[]{:S(2)}) collective-permute-start(f32[2,16,1,1024]{3,2,1,0:T(1,128)} %get-tuple-element.33), channel_id=1, source_target_pairs={{0,4},{4,8},{8,12},{1,5},{5,9},{9,13},{2,6},{6,10},{10,14},{3,7},{... | collective-permute-start | bytes 393224 | tf_op jit(solution)/shard_map/ppermute | solution.py:24
  59.3 8.7 %collective-permute-start.9 = (f32[2,1,16,1024]{3,2,1,0:T(8,128)}, f32[2,1,16,1024]{3,2,1,0:T(8,128)S(1)}, u32[]{:S(2)}, u32[]{:S(2)}) collective-permute-start(f32[2,1,16,1024]{3,2,1,0:T(8,128)} %get-tuple-element.32), channel_id=1, source_target_pairs={{0,16},{16,32},{32,48},{48,64},{64,80},{80,96},{96,112},{1,17},{17... | collective-permute-start | bytes 393224 | tf_op jit(solution)/shard_map/ppermute | solution.py:24
  63.5 4.5 %collective-permute-start.11 = (f32[2,2,1,128]{3,2,1,0:T(1,128)}, f32[2,2,1,128]{3,2,1,0:T(1,128)S(1)}, u32[]{:S(2)}, u32[]{:S(2)}) collective-permute-start(f32[2,2,1,128]{3,2,1,0:T(1,128)} %get-tuple-element.34), channel_id=1, source_target_pairs={{0,1},{1,2},{2,3},{4,5},{5,6},{6,7},{8,9},{9,10},{10,11},{12,13},{... | collective-permute-start | bytes 6152 | tf_op jit(solution)/shard_map/ppermute | solution.py:24
  68.1 0.5 copy-start.9
  68.1 0.6 copy-start.1
  68.1 0.7 copy-start.5
  68.8 7.9 %copy-start.13 = (s32[1,1,1,1024]{3,2,1,0:T(1,128)S(1)}, s32[1,1,1,1024]{3,2,1,0:T(1,128)}, u32[]{:S(2)}) copy-start(s32[1,1,1,1024]{3,2,1,0:T(1,128)} %param.13) | copy-start | bytes 12292
  68.8 7.9 %copy-start.14 = (s32[1,1,1,1024,1]{3,4,2,1,0:T(1,128)S(1)}, s32[1,1,1,1024,1]{3,4,2,1,0:T(1,128)}, u32[]{:S(2)}) copy-start(s32[1,1,1,1024,1]{3,4,2,1,0:T(1,128)} %param.12) | copy-start | bytes 12292

commit v10 on v9

--- a/solution.py
+++ b/solution.py
@@ -25,26 +25,26 @@
 
 
 def fwd_y(a, row):
-    rolled = pltpu.roll(a, a.shape[1] - 1, 1)
-    at = lax.broadcasted_iota(jnp.int32, a.shape, 1)
-    return jnp.where(at == a.shape[1] - 1, row, rolled)
+    rolled = pltpu.roll(a, a.shape[-2] - 1, a.ndim - 2)
+    at = lax.broadcasted_iota(jnp.int32, a.shape, a.ndim - 2)
+    return jnp.where(at == a.shape[-2] - 1, row, rolled)
 
 
 def fwd_z(a, col):
-    rolled = pltpu.roll(a, a.shape[2] - 1, 2)
-    at = lax.broadcasted_iota(jnp.int32, a.shape, 2)
-    return jnp.where(at == a.shape[2] - 1, col, rolled)
+    rolled = pltpu.roll(a, a.shape[-1] - 1, a.ndim - 1)
+    at = lax.broadcasted_iota(jnp.int32, a.shape, a.ndim - 1)
+    return jnp.where(at == a.shape[-1] - 1, col, rolled)
 
 
 def bwd_y(a, row):
-    rolled = pltpu.roll(a, 1, 1)
-    at = lax.broadcasted_iota(jnp.int32, a.shape, 1)
+    rolled = pltpu.roll(a, 1, a.ndim - 2)
+    at = lax.broadcasted_iota(jnp.int32, a.shape, a.ndim - 2)
     return jnp.where(at == 0, row, rolled)
 
 
 def bwd_z(a, col):
-    rolled = pltpu.roll(a, 1, 2)
-    at = lax.broadcasted_iota(jnp.int32, a.shape, 2)
+    rolled = pltpu.roll(a, 1, a.ndim - 1)
+    at = lax.broadcasted_iota(jnp.int32, a.shape, a.ndim - 1)
     return jnp.where(at == 0, col, rolled)
 
 
@@ -73,19 +73,22 @@
 
 def h_kernel(e_ref, en_ref, h_ref, hx_ref, hy_ref, hz_ref, out_ref, fx_ref, fy_ref, fz_ref):
     last = pl.program_id(0) == pl.num_programs(0) - 1
-    ex, ey, ez = e_ref[0], e_ref[1], e_ref[2]
+    _, b, ny, nz = e_ref.shape
     nxt_y = jnp.where(last, hx_ref[0], en_ref[1])
     nxt_z = jnp.where(last, hx_ref[1], en_ref[2])
-    ez_yp = fwd_y(ez, hy_ref[1])
-    ex_yp = fwd_y(ex, hy_ref[0])
-    b, ny, nz = ex.shape
-    ey_zp = fwd_z(ey, column_of(hz_ref[1, 0], b, ny))
-    ex_zp = fwd_z(ex, column_of(hz_ref[0, 0], b, ny))
-    ez_xp = fwd_x(ez, nxt_z)
-    ey_xp = fwd_x(ey, nxt_y)
-    out_ref[0] = h_ref[0] - courant * ((ez_yp - ez) - (ey_zp - ey))
-    out_ref[1] = h_ref[1] - courant * ((ex_zp - ex) - (ez_xp - ez))
-    out_ref[2] = h_ref[2] - courant * ((ey_xp - ey) - (ex_yp - ex))
+    col_x = column_of(hz_ref[0, 0], b, ny)
+    col_y = column_of(hz_ref[1, 0], b, ny)
+    for j in range(b):
+        ex, ey, ez = e_ref[0, j], e_ref[1, j], e_ref[2, j]
+        ey_xp = e_ref[1, j + 1] if j + 1 < b else nxt_y[0]
+        ez_xp = e_ref[2, j + 1] if j + 1 < b else nxt_z[0]
+        ez_yp = fwd_y(ez, hy_ref[1, j])
+        ex_yp = fwd_y(ex, hy_ref[0, j])
+        ey_zp = fwd_z(ey, col_y[j])
+        ex_zp = fwd_z(ex, col_x[j])
+        out_ref[0, j] = h_ref[0, j] - courant * ((ez_yp - ez) - (ey_zp - ey))
+        out_ref[1, j] = h_ref[1, j] - courant * ((ex_zp - ex) - (ez_xp - ez))
+        out_ref[2, j] = h_ref[2, j] - courant * ((ey_xp - ey) - (ex_yp - ex))
 
     @pl.when(last)
     def _():
@@ -99,30 +102,29 @@
     fz_ref[1, 0] = row_of(out_ref[1], top)[127:128]
 
 
-def e_update(e_ref, h_ref, hp_ref, inv_ref, hx_ref, hy_ref, hz_ref):
+def e_slabs(e_ref, h_ref, hp_ref, inv_ref, hx_ref, hy_ref, hz_ref, out_ref):
     first = pl.program_id(0) == 0
-    hx, hy, hz = h_ref[0], h_ref[1], h_ref[2]
+    _, b, ny, nz = h_ref.shape
     prv_y = jnp.where(first, hx_ref[0], hp_ref[1])
     prv_z = jnp.where(first, hx_ref[1], hp_ref[2])
-    hz_ym = bwd_y(hz, hy_ref[1])
-    hx_ym = bwd_y(hx, hy_ref[0])
-    b, ny, nz = hx.shape
-    hy_zm = bwd_z(hy, column_of(hz_ref[1, 0], b, ny))
-    hx_zm = bwd_z(hx, column_of(hz_ref[0, 0], b, ny))
-    hz_xm = bwd_x(hz, prv_z)
-    hy_xm = bwd_x(hy, prv_y)
-    scale = courant * inv_ref[...]
-    new_x = e_ref[0] + scale * ((hz - hz_ym) - (hy - hy_zm))
-    new_y = e_ref[1] + scale * ((hx - hx_zm) - (hz - hz_xm))
-    new_z = e_ref[2] + scale * ((hy - hy_xm) - (hx - hx_ym))
-    return new_x, new_y, new_z
+    col_x = column_of(hz_ref[0, 0], b, ny)
+    col_y = column_of(hz_ref[1, 0], b, ny)
+    for j in range(b):
+        hx, hy, hz = h_ref[0, j], h_ref[1, j], h_ref[2, j]
+        hz_xm = h_ref[2, j - 1] if j > 0 else prv_z[0]
+        hy_xm = h_ref[1, j - 1] if j > 0 else prv_y[0]
+        hz_ym = bwd_y(hz, hy_ref[1, j])
+        hx_ym = bwd_y(hx, hy_ref[0, j])
+        hy_zm = bwd_z(hy, col_y[j])
+        hx_zm = bwd_z(hx, col_x[j])
+        scale = courant * inv_ref[j]
+        out_ref[0, j] = e_ref[0, j] + scale * ((hz - hz_ym) - (hy - hy_zm))
+        out_ref[1, j] = e_ref[1, j] + scale * ((hx - hx_zm) - (hz - hz_xm))
+        out_ref[2, j] = e_ref[2, j] + scale * ((hy - hy_xm) - (hx - hx_ym))
 
 
 def e_kernel(e_ref, h_ref, hp_ref, inv_ref, hx_ref, hy_ref, hz_ref, out_ref, fx_ref, fy_ref, fz_ref):
-    new_x, new_y, new_z = e_update(e_ref, h_ref, hp_ref, inv_ref, hx_ref, hy_ref, hz_ref)
-    out_ref[0] = new_x
-    out_ref[1] = new_y
-    out_ref[2] = new_z
+    e_slabs(e_ref, h_ref, hp_ref, inv_ref, hx_ref, hy_ref, hz_ref, out_ref)
 
     @pl.when(pl.program_id(0) == 0)
     def _():
@@ -138,10 +140,8 @@
 def e_last_kernel(
     e_ref, h_ref, hp_ref, inv_ref, hx_ref, hy_ref, hz_ref, ef_ref, zrow_ref, rrow_ref, out_ref, terms_ref, zhot_ref
 ):
-    new_x, new_y, new_z = e_update(e_ref, h_ref, hp_ref, inv_ref, hx_ref, hy_ref, hz_ref)
-    out_ref[0] = new_x
-    out_ref[1] = new_y
-    out_ref[2] = new_z
+    e_slabs(e_ref, h_ref, hp_ref, inv_ref, hx_ref, hy_ref, hz_ref, out_ref)
+    new_x, new_y, new_z = out_ref[0], out_ref[1], out_ref[2]
     step = pl.program_id(0)
     b, ny, nz = new_x.shape
     count = zhot_ref.shape[1]

time: 99.4 us -> 98.8 us (level)
  no operation moved by 1% of the time
where the time goes in v10:
time: 98.8 us; the launch traced here: 98.4 us
  starting transfers between devices  31.9 us (32%)
  Pallas kernels  24.7 us (25%)
  blocking collectives  19.7 us (20%)
  waiting for transfers between devices  14.8 us (15%)
  local copies, waits for them, and re-layouts  2.84 us (3%)
  other arithmetic  1.92 us (2%)
  matrix products  1.73 us (2%)
    ppermute x6, starting transfers between devices, toward_upper(): return lax.ppermute(x, axis, [(j, j + 1) for j in range(peers - 1)])  21.5 us
    all_to_all x1, blocking collectives, body(): received = lax.all_to_all(per_owner, ('gx', 'gy', 'gz'), 0, 0, tiled=True)  19.7 us
    ppermute x6, waiting for transfers between devices, toward_lower(): return lax.ppermute(x, axis, [(j, j - 1) for j in range(1, peers)])  13.5 us
    ppermute x6, starting transfers between devices, toward_lower(): return lax.ppermute(x, axis, [(j, j - 1) for j in range(1, peers)])  10.4 us
    pallas_call x2, Pallas kernels, h_step(): pl.pallas_call(h_kernel, grid=(nx // chunk,), in_specs=[field_spec(nx, ny...  9.68 us
    pallas_call x1, Pallas kernels, e_step(): pl.pallas_call(e_last_kernel, grid=(nx // chunk,), in_specs=in_specs + [f...  7.6 us
    pallas_call x1, Pallas kernels, e_step(): pl.pallas_call(e_kernel, grid=(nx // chunk,), in_specs=in_specs, out_spec...  5.13 us
    unnamed x30, local copies, waits for them, and re-layouts  2.71 us
  transfers between devices with their start and end apart: 12, of which 6 were waited for; matrix products, arithmetic and copies ran while one was open for 1% of the time, Pallas kernels for 0%

profile of v10, /device:TPU:1, one launch (start us, length us, event | category | flops | bytes accessed | tf_op | source)
XLA Modules:
  0.0 98.4 jit_solution(10666284502517290497)
XLA Ops:
  0.6 2.3 %shard_map.94 = (f32[2,1,16,1024]{3,2,1,0:T(8,128)}, f32[2,16,1,1024]{3,2,1,0:T(1,128)}, f32[2,2,1,128]{3,2,1,0:T(1,128)}) custom-call(f32[3,16,16,1024]{3,2,1,0:T(8,128)} %e_ref.3, f32[3,16,16,1024]{3,2,1,0:T(8,128)} %e_ref.3, f32[3,16,16,1024]{3,2,1,0:T(8,128)} %e_ref.3), custom_call_target="tpu_custom_call" | custom-call | tf_op jit(solution)/shard_map/pallas_call | solution.py:202
  3.0 1.3 %collective-permute-start = (f32[2,1,16,1024]{3,2,1,0:T(8,128)}, f32[2,1,16,1024]{3,2,1,0:T(8,128)S(1)}, u32[]{:S(2)}, u32[]{:S(2)}) collective-permute-start(f32[2,1,16,1024]{3,2,1,0:T(8,128)} %get-tuple-element.20), channel_id=1, source_target_pairs={{16,0},{32,16},{48,32},{64,48},{80,64},{96,80},{112,96},{17,1},{33... | collective-permute-start | bytes 393224 | tf_op jit(solution)/shard_map/ppermute | solution.py:19
  4.2 3.3 %collective-permute-start.1 = (f32[2,16,1,1024]{3,2,1,0:T(1,128)}, f32[2,16,1,1024]{3,2,1,0:T(1,128)S(1)}, u32[]{:S(2)}, u32[]{:S(2)}) collective-permute-start(f32[2,16,1,1024]{3,2,1,0:T(1,128)} %get-tuple-element.21), channel_id=1, source_target_pairs={{4,0},{8,4},{12,8},{5,1},{9,5},{13,9},{6,2},{10,6},{14,10},{7,3},{... | collective-permute-start | bytes 393224 | tf_op jit(solution)/shard_map/ppermute | solution.py:19
  7.5 1.3 %collective-permute-start.2 = (f32[2,2,1,128]{3,2,1,0:T(1,128)}, f32[2,2,1,128]{3,2,1,0:T(1,128)S(1)}, u32[]{:S(2)}, u32[]{:S(2)}) collective-permute-start(f32[2,2,1,128]{3,2,1,0:T(1,128)} %get-tuple-element.22), channel_id=1, source_target_pairs={{1,0},{2,1},{3,2},{5,4},{6,5},{7,6},{9,8},{10,9},{11,10},{13,12},{... | collective-permute-start | bytes 6152 | tf_op jit(solution)/shard_map/ppermute | solution.py:19
  8.8 3.4 %collective-permute-done.2.hz_ref = f32[2,2,1,128]{3,2,1,0:T(1,128)S(1)} collective-permute-done((f32[2,2,1,128]{3,2,1,0:T(1,128)}, f32[2,2,1,128]{3,2,1,0:T(1,128)S(1)}, u32[]{:S(2)}, u32[]{:S(2)}) %collective-permute-start.2) | collective-permute-done | bytes 2080 | tf_op jit(solution)/shard_map/ppermute | solution.py:19
  12.2 4.6 %collective-permute-done.1.hy_ref = f32[2,16,1,1024]{3,2,1,0:T(1,128)S(1)} collective-permute-done((f32[2,16,1,1024]{3,2,1,0:T(1,128)}, f32[2,16,1,1024]{3,2,1,0:T(1,128)S(1)}, u32[]{:S(2)}, u32[]{:S(2)}) %collective-permute-start.1) | collective-permute-done | bytes 131104 | tf_op jit(solution)/shard_map/ppermute | solution.py:19
  16.8 0.7 copy-done.6
  17.5 4.8 %shard_map.95 = (f32[3,16,16,1024]{3,2,1,0:T(8,128)}, f32[2,1,16,1024]{3,2,1,0:T(8,128)}, f32[2,16,1,1024]{3,2,1,0:T(1,128)}, f32[2,2,1,128]{3,2,1,0:T(1,128)}) custom-call(f32[3,16,16,1024]{3,2,1,0:T(8,128)} %e_ref.3, f32[3,16,16,1024]{3,2,1,0:T(8,128)} %e_ref.3, f32[3,16,16,1024]{3,2,1,0:T(8,128)} %h_ref.1, f32[2,1,16,1024]{3,2,1,0:T(8,128)} %copy-done.3, ...), custom_call_target="tpu_custom_call" | custom-call | tf_op jit(solution)/shard_map/pallas_call | solution.py:225
  22.3 1.3 %collective-permute-start.3 = (f32[2,1,16,1024]{3,2,1,0:T(8,128)}, f32[2,1,16,1024]{3,2,1,0:T(8,128)S(1)}, u32[]{:S(2)}, u32[]{:S(2)}) collective-permute-start(f32[2,1,16,1024]{3,2,1,0:T(8,128)} %get-tuple-element.24), channel_id=1, source_target_pairs={{0,16},{16,32},{32,48},{48,64},{64,80},{80,96},{96,112},{1,17},{17... | collective-permute-start | bytes 393224 | tf_op jit(solution)/shard_map/ppermute | solution.py:24
  23.6 5.9 %collective-permute-start.4 = (f32[2,16,1,1024]{3,2,1,0:T(1,128)}, f32[2,16,1,1024]{3,2,1,0:T(1,128)S(1)}, u32[]{:S(2)}, u32[]{:S(2)}) collective-permute-start(f32[2,16,1,1024]{3,2,1,0:T(1,128)} %get-tuple-element.25), channel_id=1, source_target_pairs={{0,4},{4,8},{8,12},{1,5},{5,9},{9,13},{2,6},{6,10},{10,14},{3,7},{... | collective-permute-start | bytes 393224 | tf_op jit(solution)/shard_map/ppermute | solution.py:24
  29.5 3.2 %collective-permute-start.5 = (f32[2,2,1,128]{3,2,1,0:T(1,128)}, f32[2,2,1,128]{3,2,1,0:T(1,128)S(1)}, u32[]{:S(2)}, u32[]{:S(2)}) collective-permute-start(f32[2,2,1,128]{3,2,1,0:T(1,128)} %get-tuple-element.26), channel_id=1, source_target_pairs={{0,1},{1,2},{2,3},{4,5},{5,6},{6,7},{8,9},{9,10},{10,11},{12,13},{... | collective-permute-start | bytes 6152 | tf_op jit(solution)/shard_map/ppermute | solution.py:24
  32.7 0.9 collective-permute-done.5.hz_ref
  33.6 0.6 copy-done.10
  34.3 5.1 %shard_map.96 = (f32[3,16,16,1024]{3,2,1,0:T(8,128)}, f32[2,1,16,1024]{3,2,1,0:T(8,128)}, f32[2,16,1,1024]{3,2,1,0:T(1,128)}, f32[2,2,1,128]{3,2,1,0:T(1,128)}) custom-call(f32[3,16,16,1024]{3,2,1,0:T(8,128)} %e_ref.3, f32[3,16,16,1024]{3,2,1,0:T(8,128)} %get-tuple-element.23.h_ref.hp_ref, f32[3,16,16,1024]{3,2,1,0:T(8,128)} %get-tuple-element.23.h_ref.hp_ref, ...), custom_call_target="tpu_custom_call" | custom-call | tf_op jit(solution)/shard_map/pallas_call | solution.py:258
  39.4 1.3 %collective-permute-start.6 = (f32[2,1,16,1024]{3,2,1,0:T(8,128)}, f32[2,1,16,1024]{3,2,1,0:T(8,128)S(1)}, u32[]{:S(2)}, u32[]{:S(2)}) collective-permute-start(f32[2,1,16,1024]{3,2,1,0:T(8,128)} %get-tuple-element.28), channel_id=1, source_target_pairs={{16,0},{32,16},{48,32},{64,48},{80,64},{96,80},{112,96},{17,1},{33... | collective-permute-start | bytes 393224 | tf_op jit(solution)/shard_map/ppermute | solution.py:19
  40.7 1.9 %collective-permute-start.7 = (f32[2,16,1,1024]{3,2,1,0:T(1,128)}, f32[2,16,1,1024]{3,2,1,0:T(1,128)S(1)}, u32[]{:S(2)}, u32[]{:S(2)}) collective-permute-start(f32[2,16,1,1024]{3,2,1,0:T(1,128)} %get-tuple-element.29), channel_id=1, source_target_pairs={{4,0},{8,4},{12,8},{5,1},{9,5},{13,9},{6,2},{10,6},{14,10},{7,3},{... | collective-permute-start | bytes 393224 | tf_op jit(solution)/shard_map/ppermute | solution.py:19
  42.6 1.3 %collective-permute-start.8 = (f32[2,2,1,128]{3,2,1,0:T(1,128)}, f32[2,2,1,128]{3,2,1,0:T(1,128)S(1)}, u32[]{:S(2)}, u32[]{:S(2)}) collective-permute-start(f32[2,2,1,128]{3,2,1,0:T(1,128)} %get-tuple-element.30), channel_id=1, source_target_pairs={{1,0},{2,1},{3,2},{5,4},{6,5},{7,6},{9,8},{10,9},{11,10},{13,12},{... | collective-permute-start | bytes 6152 | tf_op jit(solution)/shard_map/ppermute | solution.py:19
  43.9 0.6 and_select_fusion
  44.6 2.9 %collective-permute-done.8.hz_ref = f32[2,2,1,128]{3,2,1,0:T(1,128)S(1)} collective-permute-done((f32[2,2,1,128]{3,2,1,0:T(1,128)}, f32[2,2,1,128]{3,2,1,0:T(1,128)S(1)}, u32[]{:S(2)}, u32[]{:S(2)}) %collective-permute-start.8) | collective-permute-done | bytes 2080 | tf_op jit(solution)/shard_map/ppermute | solution.py:19
  47.4 2.7 %collective-permute-done.7.hy_ref = f32[2,16,1,1024]{3,2,1,0:T(1,128)S(1)} collective-permute-done((f32[2,16,1,1024]{3,2,1,0:T(1,128)}, f32[2,16,1,1024]{3,2,1,0:T(1,128)S(1)}, u32[]{:S(2)}, u32[]{:S(2)}) %collective-permute-start.7) | collective-permute-done | bytes 131104 | tf_op jit(solution)/shard_map/ppermute | solution.py:19
  50.1 0.7 copy-done.2
  50.8 4.8 %shard_map.97 = (f32[3,16,16,1024]{3,2,1,0:T(8,128)}, f32[2,1,16,1024]{3,2,1,0:T(8,128)}, f32[2,16,1,1024]{3,2,1,0:T(1,128)}, f32[2,2,1,128]{3,2,1,0:T(1,128)}) custom-call(f32[3,16,16,1024]{3,2,1,0:T(8,128)} %get-tuple-element.27.e_ref.en_ref, f32[3,16,16,1024]{3,2,1,0:T(8,128)} %get-tuple-element.27.e_ref.en_ref, ...), custom_call_target="tpu_custom_call" | custom-call | tf_op jit(solution)/shard_map/pallas_call | solution.py:225
  55.6 3.4 %collective-permute-start.10 = (f32[2,16,1,1024]{3,2,1,0:T(1,128)}, f32[2,16,1,1024]{3,2,1,0:T(1,128)S(1)}, u32[]{:S(2)}, u32[]{:S(2)}) collective-permute-start(f32[2,16,1,1024]{3,2,1,0:T(1,128)} %get-tuple-element.33), channel_id=1, source_target_pairs={{0,4},{4,8},{8,12},{1,5},{5,9},{9,13},{2,6},{6,10},{10,14},{3,7},{... | collective-permute-start | bytes 393224 | tf_op jit(solution)/shard_map/ppermute | solution.py:24
  59.0 4.2 %collective-permute-start.9 = (f32[2,1,16,1024]{3,2,1,0:T(8,128)}, f32[2,1,16,1024]{3,2,1,0:T(8,128)S(1)}, u32[]{:S(2)}, u32[]{:S(2)}) collective-permute-start(f32[2,1,16,1024]{3,2,1,0:T(8,128)} %get-tuple-element.32), channel_id=1, source_target_pairs={{0,16},{16,32},{32,48},{48,64},{64,80},{80,96},{96,112},{1,17},{17... | collective-permute-start | bytes 393224 | tf_op jit(solution)/shard_map/ppermute | solution.py:24
  63.2 3.6 %collective-permute-start.11 = (f32[2,2,1,128]{3,2,1,0:T(1,128)}, f32[2,2,1,128]{3,2,1,0:T(1,128)S(1)}, u32[]{:S(2)}, u32[]{:S(2)}) collective-permute-start(f32[2,2,1,128]{3,2,1,0:T(1,128)} %get-tuple-element.34), channel_id=1, source_target_pairs={{0,1},{1,2},{2,3},{4,5},{5,6},{6,7},{8,9},{9,10},{10,11},{12,13},{... | collective-permute-start | bytes 6152 | tf_op jit(solution)/shard_map/ppermute | solution.py:24
  66.8 0.6 and_select_fusion.1.zrow_ref
  67.4 0.3 collective-permute-done.11.hz_ref
  67.8 0.5 copy-done.9
  68.5 7.6 %shard_map.98 = (f32[3,16,16,1024]{3,2,1,0:T(8,128)}, f32[1,1024]{1,0:T(1,128)}) custom-call(f32[3,16,16,1024]{3,2,1,0:T(8,128)} %get-tuple-element.27.e_ref.en_ref, f32[3,16,16,1024]{3,2,1,0:T(8,128)} %get-tuple-element.18.h_ref.hp_ref, f32[3,16,16,1024]{3,2,1,0:T(8,128)} %get-tuple-element.18.h_ref.hp_ref, f32[16,16,1024]{2,1,0:T(8,128)} %inv_ref.3, ...), custom_call_target="tpu_custom_call" | custom-call | tf_op jit(solution)/shard_map/pallas_call | solution.py:269
  76.1 1.7 %convolution_bitcast_fusion = f32[128,1,256]{2,0,1:T(8,128)S(1)} fusion(f32[1024]{0:T(1024)} %bitcast.19, s32[1024]{0:T(1024)S(1)} %bitcast.17, s32[1024]{0:T(1024)S(1)} %bitcast.18), kind=kOutput, calls=%fused_computation | convolution fusion | flops 403308544 | bytes 143360 | tf_op jit(solution)/shard_map/dot_general | solution.py:302
  78.0 19.7 %all_to_all.9 = f32[128,1,256]{2,1,0:T(1,128)S(1)} all-to-all(f32[128,1,256]{2,1,0:T(1,128)S(1)} %copy.10), channel_id=1, replica_groups=mesh['gx'=8,'gy'=4,'gz'=4] {'gx','gy','gz'}, dimensions={0} | all-to-all | bytes 262144 | tf_op jit(solution)/shard_map/all_to_all | solution.py:303
  97.7 0.7 reduce_sum.9
  (33 shorter events, 0.5 us)
Async XLA Ops:
  3.0 9.3 %collective-permute-start = (f32[2,1,16,1024]{3,2,1,0:T(8,128)}, f32[2,1,16,1024]{3,2,1,0:T(8,128)S(1)}, u32[]{:S(2)}, u32[]{:S(2)}) collective-permute-start(f32[2,1,16,1024]{3,2,1,0:T(8,128)} %get-tuple-element.20), channel_id=1, source_target_pairs={{16,0},{32,16},{48,32},{64,48},{80,64},{96,80},{112,96},{17,1},{33... | collective-permute-start | bytes 393224 | tf_op jit(solution)/shard_map/ppermute | solution.py:19
  4.2 12.5 %collective-permute-start.1 = (f32[2,16,1,1024]{3,2,1,0:T(1,128)}, f32[2,16,1,1024]{3,2,1,0:T(1,128)S(1)}, u32[]{:S(2)}, u32[]{:S(2)}) collective-permute-start(f32[2,16,1,1024]{3,2,1,0:T(1,128)} %get-tuple-element.21), channel_id=1, source_target_pairs={{4,0},{8,4},{12,8},{5,1},{9,5},{13,9},{6,2},{10,6},{14,10},{7,3},{... | collective-permute-start | bytes 393224 | tf_op jit(solution)/shard_map/ppermute | solution.py:19
  7.5 4.7 %collective-permute-start.2 = (f32[2,2,1,128]{3,2,1,0:T(1,128)}, f32[2,2,1,128]{3,2,1,0:T(1,128)S(1)}, u32[]{:S(2)}, u32[]{:S(2)}) collective-permute-start(f32[2,2,1,128]{3,2,1,0:T(1,128)} %get-tuple-element.22), channel_id=1, source_target_pairs={{1,0},{2,1},{3,2},{5,4},{6,5},{7,6},{9,8},{10,9},{11,10},{13,12},{... | collective-permute-start | bytes 6152 | tf_op jit(solution)/shard_map/ppermute | solution.py:19
  12.2 4.6 %copy-start.12 = (f32[2,2,1,128]{3,2,1,0:T(1,128)}, f32[2,2,1,128]{3,2,1,0:T(1,128)S(1)}, u32[]{:S(2)}) copy-start(f32[2,2,1,128]{3,2,1,0:T(1,128)S(1)} %collective-permute-done.2.hz_ref) | copy-start | bytes 6148
  12.2 4.6 %copy-start.3 = (f32[2,1,16,1024]{3,2,1,0:T(8,128)}, f32[2,1,16,1024]{3,2,1,0:T(8,128)S(1)}, u32[]{:S(2)}) copy-start(f32[2,1,16,1024]{3,2,1,0:T(8,128)S(1)} %collective-permute-done.hx_ref) | copy-start | bytes 393220
  16.8 0.7 copy-start.6
  22.3 11.3 %collective-permute-start.3 = (f32[2,1,16,1024]{3,2,1,0:T(8,128)}, f32[2,1,16,1024]{3,2,1,0:T(8,128)S(1)}, u32[]{:S(2)}, u32[]{:S(2)}) collective-permute-start(f32[2,1,16,1024]{3,2,1,0:T(8,128)} %get-tuple-element.24), channel_id=1, source_target_pairs={{0,16},{16,32},{32,48},{48,64},{64,80},{80,96},{96,112},{1,17},{17... | collective-permute-start | bytes 393224 | tf_op jit(solution)/shard_map/ppermute | solution.py:24
  23.6 10.0 %collective-permute-start.4 = (f32[2,16,1,1024]{3,2,1,0:T(1,128)}, f32[2,16,1,1024]{3,2,1,0:T(1,128)S(1)}, u32[]{:S(2)}, u32[]{:S(2)}) collective-permute-start(f32[2,16,1,1024]{3,2,1,0:T(1,128)} %get-tuple-element.25), channel_id=1, source_target_pairs={{0,4},{4,8},{8,12},{1,5},{5,9},{9,13},{2,6},{6,10},{10,14},{3,7},{... | collective-permute-start | bytes 393224 | tf_op jit(solution)/shard_map/ppermute | solution.py:24
  29.5 4.1 %collective-permute-start.5 = (f32[2,2,1,128]{3,2,1,0:T(1,128)}, f32[2,2,1,128]{3,2,1,0:T(1,128)S(1)}, u32[]{:S(2)}, u32[]{:S(2)}) collective-permute-start(f32[2,2,1,128]{3,2,1,0:T(1,128)} %get-tuple-element.26), channel_id=1, source_target_pairs={{0,1},{1,2},{2,3},{4,5},{5,6},{6,7},{8,9},{9,10},{10,11},{12,13},{... | collective-permute-start | bytes 6152 | tf_op jit(solution)/shard_map/ppermute | solution.py:24
  33.6 0.6 copy-start.10
  33.6 0.7 copy-start.4
  33.6 0.7 copy-start.7
  34.3 9.7 %copy-start.8 = (s32[1,1,1,1024]{3,2,1,0:T(1,128)S(1)}, s32[1,1,1,1024]{3,2,1,0:T(1,128)}, u32[]{:S(2)}) copy-start(s32[1,1,1,1024]{3,2,1,0:T(1,128)} %param.11) | copy-start | bytes 12292
  39.4 8.0 %collective-permute-start.6 = (f32[2,1,16,1024]{3,2,1,0:T(8,128)}, f32[2,1,16,1024]{3,2,1,0:T(8,128)S(1)}, u32[]{:S(2)}, u32[]{:S(2)}) collective-permute-start(f32[2,1,16,1024]{3,2,1,0:T(8,128)} %get-tuple-element.28), channel_id=1, source_target_pairs={{16,0},{32,16},{48,32},{64,48},{80,64},{96,80},{112,96},{17,1},{33... | collective-permute-start | bytes 393224 | tf_op jit(solution)/shard_map/ppermute | solution.py:19
  40.7 9.4 %collective-permute-start.7 = (f32[2,16,1,1024]{3,2,1,0:T(1,128)}, f32[2,16,1,1024]{3,2,1,0:T(1,128)S(1)}, u32[]{:S(2)}, u32[]{:S(2)}) collective-permute-start(f32[2,16,1,1024]{3,2,1,0:T(1,128)} %get-tuple-element.29), channel_id=1, source_target_pairs={{4,0},{8,4},{12,8},{5,1},{9,5},{13,9},{6,2},{10,6},{14,10},{7,3},{... | collective-permute-start | bytes 393224 | tf_op jit(solution)/shard_map/ppermute | solution.py:19
  42.6 4.8 %collective-permute-start.8 = (f32[2,2,1,128]{3,2,1,0:T(1,128)}, f32[2,2,1,128]{3,2,1,0:T(1,128)S(1)}, u32[]{:S(2)}, u32[]{:S(2)}) collective-permute-start(f32[2,2,1,128]{3,2,1,0:T(1,128)} %get-tuple-element.30), channel_id=1, source_target_pairs={{1,0},{2,1},{3,2},{5,4},{6,5},{7,6},{9,8},{10,9},{11,10},{13,12},{... | collective-permute-start | bytes 6152 | tf_op jit(solution)/shard_map/ppermute | solution.py:19
  47.4 2.7 %copy-start.11 = (f32[2,2,1,128]{3,2,1,0:T(1,128)}, f32[2,2,1,128]{3,2,1,0:T(1,128)S(1)}, u32[]{:S(2)}) copy-start(f32[2,2,1,128]{3,2,1,0:T(1,128)S(1)} %collective-permute-done.8.hz_ref) | copy-start | bytes 6148
  47.4 2.7 %copy-start = (f32[2,1,16,1024]{3,2,1,0:T(8,128)}, f32[2,1,16,1024]{3,2,1,0:T(8,128)S(1)}, u32[]{:S(2)}) copy-start(f32[2,1,16,1024]{3,2,1,0:T(8,128)S(1)} %collective-permute-done.6.hx_ref) | copy-start | bytes 393220
  50.1 0.7 copy-start.2
  55.6 12.2 %collective-permute-start.10 = (f32[2,16,1,1024]{3,2,1,0:T(1,128)}, f32[2,16,1,1024]{3,2,1,0:T(1,128)S(1)}, u32[]{:S(2)}, u32[]{:S(2)}) collective-permute-start(f32[2,16,1,1024]{3,2,1,0:T(1,128)} %get-tuple-element.33), channel_id=1, source_target_pairs={{0,4},{4,8},{8,12},{1,5},{5,9},{9,13},{2,6},{6,10},{10,14},{3,7},{... | collective-permute-start | bytes 393224 | tf_op jit(solution)/shard_map/ppermute | solution.py:24
  59.0 8.7 %collective-permute-start.9 = (f32[2,1,16,1024]{3,2,1,0:T(8,128)}, f32[2,1,16,1024]{3,2,1,0:T(8,128)S(1)}, u32[]{:S(2)}, u32[]{:S(2)}) collective-permute-start(f32[2,1,16,1024]{3,2,1,0:T(8,128)} %get-tuple-element.32), channel_id=1, source_target_pairs={{0,16},{16,32},{32,48},{48,64},{64,80},{80,96},{96,112},{1,17},{17... | collective-permute-start | bytes 393224 | tf_op jit(solution)/shard_map/ppermute | solution.py:24
  63.2 4.5 %collective-permute-start.11 = (f32[2,2,1,128]{3,2,1,0:T(1,128)}, f32[2,2,1,128]{3,2,1,0:T(1,128)S(1)}, u32[]{:S(2)}, u32[]{:S(2)}) collective-permute-start(f32[2,2,1,128]{3,2,1,0:T(1,128)} %get-tuple-element.34), channel_id=1, source_target_pairs={{0,1},{1,2},{2,3},{4,5},{5,6},{6,7},{8,9},{9,10},{10,11},{12,13},{... | collective-permute-start | bytes 6152 | tf_op jit(solution)/shard_map/ppermute | solution.py:24
  67.8 0.5 copy-start.9
  67.8 0.6 copy-start.1
  67.8 0.7 copy-start.5
  68.5 7.6 %copy-start.13 = (s32[1,1,1,1024]{3,2,1,0:T(1,128)S(1)}, s32[1,1,1,1024]{3,2,1,0:T(1,128)}, u32[]{:S(2)}) copy-start(s32[1,1,1,1024]{3,2,1,0:T(1,128)} %param.13) | copy-start | bytes 12292
  68.5 7.6 %copy-start.14 = (s32[1,1,1,1024,1]{3,4,2,1,0:T(1,128)S(1)}, s32[1,1,1,1024,1]{3,4,2,1,0:T(1,128)}, u32[]{:S(2)}) copy-start(s32[1,1,1,1024,1]{3,4,2,1,0:T(1,128)} %param.12) | copy-start | bytes 12292

commit v11 on v10

--- a/solution.py
+++ b/solution.py
@@ -137,8 +137,17 @@
     fz_ref[1, 0] = row_of(out_ref[1], slice(0, 128))[0:1]
 
 
+def split3(a):
+    hi = a.astype(jnp.bfloat16)
+    rest = a - hi.astype(jnp.float32)
+    mid = rest.astype(jnp.bfloat16)
+    lo = (rest - mid.astype(jnp.float32)).astype(jnp.bfloat16)
+    return hi, mid, lo
+
+
 def e_last_kernel(
-    e_ref, h_ref, hp_ref, inv_ref, hx_ref, hy_ref, hz_ref, ef_ref, zrow_ref, rrow_ref, out_ref, terms_ref, zhot_ref
+    e_ref, h_ref, hp_ref, inv_ref, hx_ref, hy_ref, hz_ref, ef_ref, zrow_ref, rrow_ref, orow_ref, srow_ref,
+    out_ref, owner_ref, terms_ref, zhot_ref
 ):
     e_slabs(e_ref, h_ref, hp_ref, inv_ref, hx_ref, hy_ref, hz_ref, out_ref)
     new_x, new_y, new_z = out_ref[0], out_ref[1], out_ref[2]
@@ -163,6 +172,20 @@
     ) + jnp.dot(lo, zhot, preferred_element_type=jnp.float32)
     row_at = step * (b * ny) + lax.broadcasted_iota(jnp.int32, picked.shape, 0)
     terms_ref[...] += jnp.sum(jnp.where(row_at == rrow_ref[...], picked, 0.0), axis=0, keepdims=True)
+
+    @pl.when(step == pl.num_programs(0) - 1)
+    def _():
+        owners, slots = owner_ref.shape
+        weighted = jnp.where(
+            lax.broadcasted_iota(jnp.int32, (owners, count), 0) == orow_ref[...], terms_ref[...], 0.0
+        )
+        slot_hot = (lax.broadcasted_iota(jnp.int32, (slots, count), 0) == srow_ref[...]).astype(jnp.bfloat16)
+        hi, mid, lo = split3(weighted)
+        nt = (((1,), (1,)), ((), ()))
+        owner_ref[...] = (
+            lax.dot_general(hi, slot_hot, nt, preferred_element_type=jnp.float32)
+            + lax.dot_general(mid, slot_hot, nt, preferred_element_type=jnp.float32)
+        ) + lax.dot_general(lo, slot_hot, nt, preferred_element_type=jnp.float32)
 
 
 def field_spec(nx, ny, nz, chunk):
@@ -238,7 +261,7 @@
     )(e, e, h, faces_x, faces_y, faces_z)
 
 
-def e_step(e, h, faces, inv, ef=None, cells=None):
+def e_step(e, h, faces, inv, ef=None, cells=None, owners=None, slots=None, devices=None):
     _, nx, ny, nz = e.shape
     chunk = CHUNK
     faces_x = toward_upper(faces[0], "gx")
@@ -274,11 +297,13 @@
             field_spec(nx, ny, nz, chunk),
             pl.BlockSpec((1, count), lambda i: (0, 0)),
             pl.BlockSpec((1, count), lambda i: (0, 0)),
+            pl.BlockSpec((1, count), lambda i: (0, 0)),
+            pl.BlockSpec((1, count), lambda i: (0, 0)),
         ],
-        out_specs=[field_spec(nx, ny, nz, chunk), pl.BlockSpec((1, count), lambda i: (0, 0))],
-        out_shape=[jax.ShapeDtypeStruct(e.shape, e.dtype), jax.ShapeDtypeStruct((1, count), jnp.float32)],
-        scratch_shapes=[pltpu.VMEM((nz, count), jnp.bfloat16)],
-    )(*args, ef, zrow, rrow)
+        out_specs=[field_spec(nx, ny, nz, chunk), pl.BlockSpec((devices, P_DEV), lambda i: (0, 0))],
+        out_shape=[jax.ShapeDtypeStruct(e.shape, e.dtype), jax.ShapeDtypeStruct((devices, P_DEV), jnp.float32)],
+        scratch_shapes=[pltpu.VMEM((1, count), jnp.float32), pltpu.VMEM((nz, count), jnp.bfloat16)],
+    )(*args, ef, zrow, rrow, owners.reshape(1, count), slots.reshape(1, count))
 
 
 def body(e_forward, e_adjoint, h_adjoint, inv_perm, voxel_cell, voxel_owner, voxel_slot):
@@ -286,20 +311,16 @@
     voxel_rows = voxel_cell.reshape(count)
     owners = voxel_owner.reshape(count)
     slot_ids = voxel_slot.reshape(count)
+    devices = lax.axis_size("gx") * lax.axis_size("gy") * lax.axis_size("gz")
     e, h = e_adjoint, h_adjoint
     e_faces = lower_faces_of(e)
-    terms = None
+    per_owner = None
     for repeat in range(STEPS):
         h, *h_faces = h_step(e, h, e_faces)
         if repeat == STEPS - 1:
-            e, terms = e_step(e, h, h_faces, inv_perm, e_forward, voxel_rows)
+            e, per_owner = e_step(e, h, h_faces, inv_perm, e_forward, voxel_rows, owners, slot_ids, devices)
         else:
             e, e_faces = e_step(e, h, h_faces, inv_perm)
-    terms = terms.reshape(count)
-    devices = lax.axis_size("gx") * lax.axis_size("gy") * lax.axis_size("gz")
-    owner_hot = (owners[:, None] == lax.broadcasted_iota(jnp.int32, (count, devices), 1)).astype(jnp.float32)
-    slot_hot = jnp.where(slot_ids[:, None] == lax.broadcasted_iota(jnp.int32, (count, P_DEV), 1), terms[:, None], 0.0)
-    per_owner = jnp.dot(owner_hot.T, slot_hot, precision=lax.Precision.HIGHEST, preferred_element_type=jnp.float32)
     received = lax.all_to_all(per_owner, ("gx", "gy", "gz"), 0, 0, tiled=True)
     gradient = received.sum(axis=0)
     return (e, h, gradient)

time: 98.8 us -> 98.7 us (level)
  matrix products: 1.73 us -> 0 us
    dot_general x1 -> x0, matrix products: 1.73 us -> none  [body(): jnp.dot(owner_hot.T, slot_hot, precision=lax.Precision.HIGHEST, preferred...]
    unnamed x30 -> x26, local copies, waits for them, and re-layouts: 2.71 us -> 2.71 us
where the time goes in v11:
time: 98.7 us; the launch traced here: 98.3 us
  starting transfers between devices  31.9 us (32%)
  Pallas kernels  25.5 us (26%)
  blocking collectives  19.7 us (20%)
  waiting for transfers between devices  14.8 us (15%)
  local copies, waits for them, and re-layouts  3.75 us (4%)
  other arithmetic  1.93 us (2%)
    ppermute x6, starting transfers between devices, toward_upper(): return lax.ppermute(x, axis, [(j, j + 1) for j in range(peers - 1)])  21.5 us
    all_to_all x1, blocking collectives, body(): received = lax.all_to_all(per_owner, ('gx', 'gy', 'gz'), 0, 0, tiled=True)  19.7 us
    ppermute x6, waiting for transfers between devices, toward_lower(): return lax.ppermute(x, axis, [(j, j - 1) for j in range(1, peers)])  13.5 us
    ppermute x6, starting transfers between devices, toward_lower(): return lax.ppermute(x, axis, [(j, j - 1) for j in range(1, peers)])  10.4 us
    pallas_call x2, Pallas kernels, h_step(): pl.pallas_call(h_kernel, grid=(nx // chunk,), in_specs=[field_spec(nx, ny...  9.67 us
    pallas_call x1, Pallas kernels, e_step(): pl.pallas_call(e_last_kernel, grid=(nx // chunk,), in_specs=in_specs + [f...  8.31 us
    pallas_call x1, Pallas kernels, e_step(): pl.pallas_call(e_kernel, grid=(nx // chunk,), in_specs=in_specs, out_spec...  5.17 us
    unnamed x26, local copies, waits for them, and re-layouts  2.71 us
  transfers between devices with their start and end apart: 12, of which 6 were waited for; matrix products, arithmetic and copies ran while one was open for 1% of the time, Pallas kernels for 0%

profile of v11, /device:TPU:1, one launch (start us, length us, event | category | flops | bytes accessed | tf_op | source)
XLA Modules:
  0.0 98.3 jit_solution(11438585410877711352)
XLA Ops:
  0.6 2.3 %shard_map.94 = (f32[2,1,16,1024]{3,2,1,0:T(8,128)}, f32[2,16,1,1024]{3,2,1,0:T(1,128)}, f32[2,2,1,128]{3,2,1,0:T(1,128)}) custom-call(f32[3,16,16,1024]{3,2,1,0:T(8,128)} %e_ref.3, f32[3,16,16,1024]{3,2,1,0:T(8,128)} %e_ref.3, f32[3,16,16,1024]{3,2,1,0:T(8,128)} %e_ref.3), custom_call_target="tpu_custom_call" | custom-call | tf_op jit(solution)/shard_map/pallas_call | solution.py:225
  3.0 1.3 %collective-permute-start = (f32[2,1,16,1024]{3,2,1,0:T(8,128)}, f32[2,1,16,1024]{3,2,1,0:T(8,128)S(1)}, u32[]{:S(2)}, u32[]{:S(2)}) collective-permute-start(f32[2,1,16,1024]{3,2,1,0:T(8,128)} %get-tuple-element.20), channel_id=1, source_target_pairs={{16,0},{32,16},{48,32},{64,48},{80,64},{96,80},{112,96},{17,1},{33... | collective-permute-start | bytes 393224 | tf_op jit(solution)/shard_map/ppermute | solution.py:19
  4.2 3.3 %collective-permute-start.1 = (f32[2,16,1,1024]{3,2,1,0:T(1,128)}, f32[2,16,1,1024]{3,2,1,0:T(1,128)S(1)}, u32[]{:S(2)}, u32[]{:S(2)}) collective-permute-start(f32[2,16,1,1024]{3,2,1,0:T(1,128)} %get-tuple-element.21), channel_id=1, source_target_pairs={{4,0},{8,4},{12,8},{5,1},{9,5},{13,9},{6,2},{10,6},{14,10},{7,3},{... | collective-permute-start | bytes 393224 | tf_op jit(solution)/shard_map/ppermute | solution.py:19
  7.5 1.3 %collective-permute-start.2 = (f32[2,2,1,128]{3,2,1,0:T(1,128)}, f32[2,2,1,128]{3,2,1,0:T(1,128)S(1)}, u32[]{:S(2)}, u32[]{:S(2)}) collective-permute-start(f32[2,2,1,128]{3,2,1,0:T(1,128)} %get-tuple-element.22), channel_id=1, source_target_pairs={{1,0},{2,1},{3,2},{5,4},{6,5},{7,6},{9,8},{10,9},{11,10},{13,12},{... | collective-permute-start | bytes 6152 | tf_op jit(solution)/shard_map/ppermute | solution.py:19
  8.8 3.4 %collective-permute-done.2.hz_ref = f32[2,2,1,128]{3,2,1,0:T(1,128)S(1)} collective-permute-done((f32[2,2,1,128]{3,2,1,0:T(1,128)}, f32[2,2,1,128]{3,2,1,0:T(1,128)S(1)}, u32[]{:S(2)}, u32[]{:S(2)}) %collective-permute-start.2) | collective-permute-done | bytes 2080 | tf_op jit(solution)/shard_map/ppermute | solution.py:19
  12.2 4.6 %collective-permute-done.1.hy_ref = f32[2,16,1,1024]{3,2,1,0:T(1,128)S(1)} collective-permute-done((f32[2,16,1,1024]{3,2,1,0:T(1,128)}, f32[2,16,1,1024]{3,2,1,0:T(1,128)S(1)}, u32[]{:S(2)}, u32[]{:S(2)}) %collective-permute-start.1) | collective-permute-done | bytes 131104 | tf_op jit(solution)/shard_map/ppermute | solution.py:19
  16.8 0.7 copy-done.6
  17.5 4.8 %shard_map.95 = (f32[3,16,16,1024]{3,2,1,0:T(8,128)}, f32[2,1,16,1024]{3,2,1,0:T(8,128)}, f32[2,16,1,1024]{3,2,1,0:T(1,128)}, f32[2,2,1,128]{3,2,1,0:T(1,128)}) custom-call(f32[3,16,16,1024]{3,2,1,0:T(8,128)} %e_ref.3, f32[3,16,16,1024]{3,2,1,0:T(8,128)} %e_ref.3, f32[3,16,16,1024]{3,2,1,0:T(8,128)} %h_ref.1, f32[2,1,16,1024]{3,2,1,0:T(8,128)} %copy-done.3, ...), custom_call_target="tpu_custom_call" | custom-call | tf_op jit(solution)/shard_map/pallas_call | solution.py:248
  22.3 1.3 %collective-permute-start.3 = (f32[2,1,16,1024]{3,2,1,0:T(8,128)}, f32[2,1,16,1024]{3,2,1,0:T(8,128)S(1)}, u32[]{:S(2)}, u32[]{:S(2)}) collective-permute-start(f32[2,1,16,1024]{3,2,1,0:T(8,128)} %get-tuple-element.24), channel_id=1, source_target_pairs={{0,16},{16,32},{32,48},{48,64},{64,80},{80,96},{96,112},{1,17},{17... | collective-permute-start | bytes 393224 | tf_op jit(solution)/shard_map/ppermute | solution.py:24
  23.6 5.9 %collective-permute-start.4 = (f32[2,16,1,1024]{3,2,1,0:T(1,128)}, f32[2,16,1,1024]{3,2,1,0:T(1,128)S(1)}, u32[]{:S(2)}, u32[]{:S(2)}) collective-permute-start(f32[2,16,1,1024]{3,2,1,0:T(1,128)} %get-tuple-element.25), channel_id=1, source_target_pairs={{0,4},{4,8},{8,12},{1,5},{5,9},{9,13},{2,6},{6,10},{10,14},{3,7},{... | collective-permute-start | bytes 393224 | tf_op jit(solution)/shard_map/ppermute | solution.py:24
  29.5 3.2 %collective-permute-start.5 = (f32[2,2,1,128]{3,2,1,0:T(1,128)}, f32[2,2,1,128]{3,2,1,0:T(1,128)S(1)}, u32[]{:S(2)}, u32[]{:S(2)}) collective-permute-start(f32[2,2,1,128]{3,2,1,0:T(1,128)} %get-tuple-element.26), channel_id=1, source_target_pairs={{0,1},{1,2},{2,3},{4,5},{5,6},{6,7},{8,9},{9,10},{10,11},{12,13},{... | collective-permute-start | bytes 6152 | tf_op jit(solution)/shard_map/ppermute | solution.py:24
  32.7 0.9 collective-permute-done.5.hz_ref
  33.6 0.6 copy-done.10
  34.3 5.2 %shard_map.96 = (f32[3,16,16,1024]{3,2,1,0:T(8,128)}, f32[2,1,16,1024]{3,2,1,0:T(8,128)}, f32[2,16,1,1024]{3,2,1,0:T(1,128)}, f32[2,2,1,128]{3,2,1,0:T(1,128)}) custom-call(f32[3,16,16,1024]{3,2,1,0:T(8,128)} %e_ref.3, f32[3,16,16,1024]{3,2,1,0:T(8,128)} %get-tuple-element.23.h_ref.hp_ref, f32[3,16,16,1024]{3,2,1,0:T(8,128)} %get-tuple-element.23.h_ref.hp_ref, ...), custom_call_target="tpu_custom_call" | custom-call | tf_op jit(solution)/shard_map/pallas_call | solution.py:281
  39.5 1.3 %collective-permute-start.6 = (f32[2,1,16,1024]{3,2,1,0:T(8,128)}, f32[2,1,16,1024]{3,2,1,0:T(8,128)S(1)}, u32[]{:S(2)}, u32[]{:S(2)}) collective-permute-start(f32[2,1,16,1024]{3,2,1,0:T(8,128)} %get-tuple-element.28), channel_id=1, source_target_pairs={{16,0},{32,16},{48,32},{64,48},{80,64},{96,80},{112,96},{17,1},{33... | collective-permute-start | bytes 393224 | tf_op jit(solution)/shard_map/ppermute | solution.py:19
  40.8 1.9 %collective-permute-start.7 = (f32[2,16,1,1024]{3,2,1,0:T(1,128)}, f32[2,16,1,1024]{3,2,1,0:T(1,128)S(1)}, u32[]{:S(2)}, u32[]{:S(2)}) collective-permute-start(f32[2,16,1,1024]{3,2,1,0:T(1,128)} %get-tuple-element.29), channel_id=1, source_target_pairs={{4,0},{8,4},{12,8},{5,1},{9,5},{13,9},{6,2},{10,6},{14,10},{7,3},{... | collective-permute-start | bytes 393224 | tf_op jit(solution)/shard_map/ppermute | solution.py:19
  42.7 1.3 %collective-permute-start.8 = (f32[2,2,1,128]{3,2,1,0:T(1,128)}, f32[2,2,1,128]{3,2,1,0:T(1,128)S(1)}, u32[]{:S(2)}, u32[]{:S(2)}) collective-permute-start(f32[2,2,1,128]{3,2,1,0:T(1,128)} %get-tuple-element.30), channel_id=1, source_target_pairs={{1,0},{2,1},{3,2},{5,4},{6,5},{7,6},{9,8},{10,9},{11,10},{13,12},{... | collective-permute-start | bytes 6152 | tf_op jit(solution)/shard_map/ppermute | solution.py:19
  44.0 0.6 and_select_fusion
  44.6 2.9 %collective-permute-done.8.hz_ref = f32[2,2,1,128]{3,2,1,0:T(1,128)S(1)} collective-permute-done((f32[2,2,1,128]{3,2,1,0:T(1,128)}, f32[2,2,1,128]{3,2,1,0:T(1,128)S(1)}, u32[]{:S(2)}, u32[]{:S(2)}) %collective-permute-start.8) | collective-permute-done | bytes 2080 | tf_op jit(solution)/shard_map/ppermute | solution.py:19
  47.5 2.7 %collective-permute-done.7.hy_ref = f32[2,16,1,1024]{3,2,1,0:T(1,128)S(1)} collective-permute-done((f32[2,16,1,1024]{3,2,1,0:T(1,128)}, f32[2,16,1,1024]{3,2,1,0:T(1,128)S(1)}, u32[]{:S(2)}, u32[]{:S(2)}) %collective-permute-start.7) | collective-permute-done | bytes 131104 | tf_op jit(solution)/shard_map/ppermute | solution.py:19
  50.2 0.7 copy-done.2
  50.8 4.8 %shard_map.97 = (f32[3,16,16,1024]{3,2,1,0:T(8,128)}, f32[2,1,16,1024]{3,2,1,0:T(8,128)}, f32[2,16,1,1024]{3,2,1,0:T(1,128)}, f32[2,2,1,128]{3,2,1,0:T(1,128)}) custom-call(f32[3,16,16,1024]{3,2,1,0:T(8,128)} %get-tuple-element.27.e_ref.en_ref, f32[3,16,16,1024]{3,2,1,0:T(8,128)} %get-tuple-element.27.e_ref.en_ref, ...), custom_call_target="tpu_custom_call" | custom-call | tf_op jit(solution)/shard_map/pallas_call | solution.py:248
  55.7 3.4 %collective-permute-start.10 = (f32[2,16,1,1024]{3,2,1,0:T(1,128)}, f32[2,16,1,1024]{3,2,1,0:T(1,128)S(1)}, u32[]{:S(2)}, u32[]{:S(2)}) collective-permute-start(f32[2,16,1,1024]{3,2,1,0:T(1,128)} %get-tuple-element.33), channel_id=1, source_target_pairs={{0,4},{4,8},{8,12},{1,5},{5,9},{9,13},{2,6},{6,10},{10,14},{3,7},{... | collective-permute-start | bytes 393224 | tf_op jit(solution)/shard_map/ppermute | solution.py:24
  59.1 4.2 %collective-permute-start.9 = (f32[2,1,16,1024]{3,2,1,0:T(8,128)}, f32[2,1,16,1024]{3,2,1,0:T(8,128)S(1)}, u32[]{:S(2)}, u32[]{:S(2)}) collective-permute-start(f32[2,1,16,1024]{3,2,1,0:T(8,128)} %get-tuple-element.32), channel_id=1, source_target_pairs={{0,16},{16,32},{32,48},{48,64},{64,80},{80,96},{96,112},{1,17},{17... | collective-permute-start | bytes 393224 | tf_op jit(solution)/shard_map/ppermute | solution.py:24
  63.3 3.6 %collective-permute-start.11 = (f32[2,2,1,128]{3,2,1,0:T(1,128)}, f32[2,2,1,128]{3,2,1,0:T(1,128)S(1)}, u32[]{:S(2)}, u32[]{:S(2)}) collective-permute-start(f32[2,2,1,128]{3,2,1,0:T(1,128)} %get-tuple-element.34), channel_id=1, source_target_pairs={{0,1},{1,2},{2,3},{4,5},{5,6},{6,7},{8,9},{9,10},{10,11},{12,13},{... | collective-permute-start | bytes 6152 | tf_op jit(solution)/shard_map/ppermute | solution.py:24
  66.9 0.6 and_select_fusion.1.zrow_ref
  67.5 0.3 collective-permute-done.11.hz_ref
  67.8 0.6 copy-done.9
  68.5 8.3 %shard_map.98 = (f32[3,16,16,1024]{3,2,1,0:T(8,128)}, f32[128,256]{1,0:T(8,128)}) custom-call(f32[3,16,16,1024]{3,2,1,0:T(8,128)} %get-tuple-element.27.e_ref.en_ref, f32[3,16,16,1024]{3,2,1,0:T(8,128)} %get-tuple-element.18.h_ref.hp_ref, f32[3,16,16,1024]{3,2,1,0:T(8,128)} %get-tuple-element.18.h_ref.hp_ref, f32[16,16,1024]{2,1,0:T(8,128)} %inv_ref.3, ...), custom_call_target="tpu_custom_call" | custom-call | tf_op jit(solution)/shard_map/pallas_call | solution.py:292
  76.8 1.0 %copy.10 = f32[128,1,256]{2,1,0:T(1,128)S(1)} copy(f32[128,1,256]{2,0,1:T(8,128)} %bitcast.15) | data formatting | bytes 262144 | tf_op jit(solution)/shard_map/all_to_all | solution.py:324
  77.9 19.7 %all_to_all.9 = f32[128,1,256]{2,1,0:T(1,128)S(1)} all-to-all(f32[128,1,256]{2,1,0:T(1,128)S(1)} %copy.10), channel_id=1, replica_groups=mesh['gx'=8,'gy'=4,'gz'=4] {'gx','gy','gz'}, dimensions={0} | all-to-all | bytes 262144 | tf_op jit(solution)/shard_map/all_to_all | solution.py:324
  97.6 0.7 reduce_sum.9
  (28 shorter events, 0.3 us)
Async XLA Ops:
  3.0 9.3 %collective-permute-start = (f32[2,1,16,1024]{3,2,1,0:T(8,128)}, f32[2,1,16,1024]{3,2,1,0:T(8,128)S(1)}, u32[]{:S(2)}, u32[]{:S(2)}) collective-permute-start(f32[2,1,16,1024]{3,2,1,0:T(8,128)} %get-tuple-element.20), channel_id=1, source_target_pairs={{16,0},{32,16},{48,32},{64,48},{80,64},{96,80},{112,96},{17,1},{33... | collective-permute-start | bytes 393224 | tf_op jit(solution)/shard_map/ppermute | solution.py:19
  4.2 12.5 %collective-permute-start.1 = (f32[2,16,1,1024]{3,2,1,0:T(1,128)}, f32[2,16,1,1024]{3,2,1,0:T(1,128)S(1)}, u32[]{:S(2)}, u32[]{:S(2)}) collective-permute-start(f32[2,16,1,1024]{3,2,1,0:T(1,128)} %get-tuple-element.21), channel_id=1, source_target_pairs={{4,0},{8,4},{12,8},{5,1},{9,5},{13,9},{6,2},{10,6},{14,10},{7,3},{... | collective-permute-start | bytes 393224 | tf_op jit(solution)/shard_map/ppermute | solution.py:19
  7.5 4.7 %collective-permute-start.2 = (f32[2,2,1,128]{3,2,1,0:T(1,128)}, f32[2,2,1,128]{3,2,1,0:T(1,128)S(1)}, u32[]{:S(2)}, u32[]{:S(2)}) collective-permute-start(f32[2,2,1,128]{3,2,1,0:T(1,128)} %get-tuple-element.22), channel_id=1, source_target_pairs={{1,0},{2,1},{3,2},{5,4},{6,5},{7,6},{9,8},{10,9},{11,10},{13,12},{... | collective-permute-start | bytes 6152 | tf_op jit(solution)/shard_map/ppermute | solution.py:19
  12.2 4.6 %copy-start.12 = (f32[2,2,1,128]{3,2,1,0:T(1,128)}, f32[2,2,1,128]{3,2,1,0:T(1,128)S(1)}, u32[]{:S(2)}) copy-start(f32[2,2,1,128]{3,2,1,0:T(1,128)S(1)} %collective-permute-done.2.hz_ref) | copy-start | bytes 6148
  12.2 4.6 %copy-start.3 = (f32[2,1,16,1024]{3,2,1,0:T(8,128)}, f32[2,1,16,1024]{3,2,1,0:T(8,128)S(1)}, u32[]{:S(2)}) copy-start(f32[2,1,16,1024]{3,2,1,0:T(8,128)S(1)} %collective-permute-done.hx_ref) | copy-start | bytes 393220
  16.8 0.7 copy-start.6
  22.3 11.3 %collective-permute-start.3 = (f32[2,1,16,1024]{3,2,1,0:T(8,128)}, f32[2,1,16,1024]{3,2,1,0:T(8,128)S(1)}, u32[]{:S(2)}, u32[]{:S(2)}) collective-permute-start(f32[2,1,16,1024]{3,2,1,0:T(8,128)} %get-tuple-element.24), channel_id=1, source_target_pairs={{0,16},{16,32},{32,48},{48,64},{64,80},{80,96},{96,112},{1,17},{17... | collective-permute-start | bytes 393224 | tf_op jit(solution)/shard_map/ppermute | solution.py:24
  23.6 10.0 %collective-permute-start.4 = (f32[2,16,1,1024]{3,2,1,0:T(1,128)}, f32[2,16,1,1024]{3,2,1,0:T(1,128)S(1)}, u32[]{:S(2)}, u32[]{:S(2)}) collective-permute-start(f32[2,16,1,1024]{3,2,1,0:T(1,128)} %get-tuple-element.25), channel_id=1, source_target_pairs={{0,4},{4,8},{8,12},{1,5},{5,9},{9,13},{2,6},{6,10},{10,14},{3,7},{... | collective-permute-start | bytes 393224 | tf_op jit(solution)/shard_map/ppermute | solution.py:24
  29.5 4.1 %collective-permute-start.5 = (f32[2,2,1,128]{3,2,1,0:T(1,128)}, f32[2,2,1,128]{3,2,1,0:T(1,128)S(1)}, u32[]{:S(2)}, u32[]{:S(2)}) collective-permute-start(f32[2,2,1,128]{3,2,1,0:T(1,128)} %get-tuple-element.26), channel_id=1, source_target_pairs={{0,1},{1,2},{2,3},{4,5},{5,6},{6,7},{8,9},{9,10},{10,11},{12,13},{... | collective-permute-start | bytes 6152 | tf_op jit(solution)/shard_map/ppermute | solution.py:24
  33.6 0.6 copy-start.10
  33.6 0.7 copy-start.4
  33.6 0.7 copy-start.7
  34.3 9.7 %copy-start.8 = (s32[1,1,1,1024]{3,2,1,0:T(1,128)S(1)}, s32[1,1,1,1024]{3,2,1,0:T(1,128)}, u32[]{:S(2)}) copy-start(s32[1,1,1,1024]{3,2,1,0:T(1,128)} %param.11) | copy-start | bytes 12292
  39.5 8.0 %collective-permute-start.6 = (f32[2,1,16,1024]{3,2,1,0:T(8,128)}, f32[2,1,16,1024]{3,2,1,0:T(8,128)S(1)}, u32[]{:S(2)}, u32[]{:S(2)}) collective-permute-start(f32[2,1,16,1024]{3,2,1,0:T(8,128)} %get-tuple-element.28), channel_id=1, source_target_pairs={{16,0},{32,16},{48,32},{64,48},{80,64},{96,80},{112,96},{17,1},{33... | collective-permute-start | bytes 393224 | tf_op jit(solution)/shard_map/ppermute | solution.py:19
  40.8 9.4 %collective-permute-start.7 = (f32[2,16,1,1024]{3,2,1,0:T(1,128)}, f32[2,16,1,1024]{3,2,1,0:T(1,128)S(1)}, u32[]{:S(2)}, u32[]{:S(2)}) collective-permute-start(f32[2,16,1,1024]{3,2,1,0:T(1,128)} %get-tuple-element.29), channel_id=1, source_target_pairs={{4,0},{8,4},{12,8},{5,1},{9,5},{13,9},{6,2},{10,6},{14,10},{7,3},{... | collective-permute-start | bytes 393224 | tf_op jit(solution)/shard_map/ppermute | solution.py:19
  42.7 4.8 %collective-permute-start.8 = (f32[2,2,1,128]{3,2,1,0:T(1,128)}, f32[2,2,1,128]{3,2,1,0:T(1,128)S(1)}, u32[]{:S(2)}, u32[]{:S(2)}) collective-permute-start(f32[2,2,1,128]{3,2,1,0:T(1,128)} %get-tuple-element.30), channel_id=1, source_target_pairs={{1,0},{2,1},{3,2},{5,4},{6,5},{7,6},{9,8},{10,9},{11,10},{13,12},{... | collective-permute-start | bytes 6152 | tf_op jit(solution)/shard_map/ppermute | solution.py:19
  47.5 2.7 %copy-start.11 = (f32[2,2,1,128]{3,2,1,0:T(1,128)}, f32[2,2,1,128]{3,2,1,0:T(1,128)S(1)}, u32[]{:S(2)}) copy-start(f32[2,2,1,128]{3,2,1,0:T(1,128)S(1)} %collective-permute-done.8.hz_ref) | copy-start | bytes 6148
  47.5 2.7 %copy-start = (f32[2,1,16,1024]{3,2,1,0:T(8,128)}, f32[2,1,16,1024]{3,2,1,0:T(8,128)S(1)}, u32[]{:S(2)}) copy-start(f32[2,1,16,1024]{3,2,1,0:T(8,128)S(1)} %collective-permute-done.6.hx_ref) | copy-start | bytes 393220
  50.2 0.7 copy-start.2
  55.7 12.1 %collective-permute-start.10 = (f32[2,16,1,1024]{3,2,1,0:T(1,128)}, f32[2,16,1,1024]{3,2,1,0:T(1,128)S(1)}, u32[]{:S(2)}, u32[]{:S(2)}) collective-permute-start(f32[2,16,1,1024]{3,2,1,0:T(1,128)} %get-tuple-element.33), channel_id=1, source_target_pairs={{0,4},{4,8},{8,12},{1,5},{5,9},{9,13},{2,6},{6,10},{10,14},{3,7},{... | collective-permute-start | bytes 393224 | tf_op jit(solution)/shard_map/ppermute | solution.py:24
  59.1 8.7 %collective-permute-start.9 = (f32[2,1,16,1024]{3,2,1,0:T(8,128)}, f32[2,1,16,1024]{3,2,1,0:T(8,128)S(1)}, u32[]{:S(2)}, u32[]{:S(2)}) collective-permute-start(f32[2,1,16,1024]{3,2,1,0:T(8,128)} %get-tuple-element.32), channel_id=1, source_target_pairs={{0,16},{16,32},{32,48},{48,64},{64,80},{80,96},{96,112},{1,17},{17... | collective-permute-start | bytes 393224 | tf_op jit(solution)/shard_map/ppermute | solution.py:24
  63.3 4.5 %collective-permute-start.11 = (f32[2,2,1,128]{3,2,1,0:T(1,128)}, f32[2,2,1,128]{3,2,1,0:T(1,128)S(1)}, u32[]{:S(2)}, u32[]{:S(2)}) collective-permute-start(f32[2,2,1,128]{3,2,1,0:T(1,128)} %get-tuple-element.34), channel_id=1, source_target_pairs={{0,1},{1,2},{2,3},{4,5},{5,6},{6,7},{8,9},{9,10},{10,11},{12,13},{... | collective-permute-start | bytes 6152 | tf_op jit(solution)/shard_map/ppermute | solution.py:24
  67.8 0.6 copy-start.9
  67.8 0.7 copy-start.1
  67.8 0.7 copy-start.5

commit v12 on v11

--- a/solution.py
+++ b/solution.py
@@ -162,30 +162,26 @@
 
     inter = (ef_ref[0] * new_x + ef_ref[1] * new_y + ef_ref[2] * new_z).reshape(b * ny, nz)
     hi = inter.astype(jnp.bfloat16)
-    rest = inter - hi.astype(jnp.float32)
-    mid = rest.astype(jnp.bfloat16)
-    lo = (rest - mid.astype(jnp.float32)).astype(jnp.bfloat16)
+    mid = (inter - hi.astype(jnp.float32)).astype(jnp.bfloat16)
     zhot = zhot_ref[...]
-    picked = (
-        jnp.dot(hi, zhot, preferred_element_type=jnp.float32)
-        + jnp.dot(mid, zhot, preferred_element_type=jnp.float32)
-    ) + jnp.dot(lo, zhot, preferred_element_type=jnp.float32)
+    picked = jnp.dot(hi, zhot, preferred_element_type=jnp.float32) + jnp.dot(mid, zhot, preferred_element_type=jnp.float32)
     row_at = step * (b * ny) + lax.broadcasted_iota(jnp.int32, picked.shape, 0)
     terms_ref[...] += jnp.sum(jnp.where(row_at == rrow_ref[...], picked, 0.0), axis=0, keepdims=True)
 
     @pl.when(step == pl.num_programs(0) - 1)
     def _():
-        owners, slots = owner_ref.shape
+        owners, _, slots = owner_ref.shape
         weighted = jnp.where(
             lax.broadcasted_iota(jnp.int32, (owners, count), 0) == orow_ref[...], terms_ref[...], 0.0
         )
         slot_hot = (lax.broadcasted_iota(jnp.int32, (slots, count), 0) == srow_ref[...]).astype(jnp.bfloat16)
         hi, mid, lo = split3(weighted)
         nt = (((1,), (1,)), ((), ()))
-        owner_ref[...] = (
+        summed = (
             lax.dot_general(hi, slot_hot, nt, preferred_element_type=jnp.float32)
             + lax.dot_general(mid, slot_hot, nt, preferred_element_type=jnp.float32)
         ) + lax.dot_general(lo, slot_hot, nt, preferred_element_type=jnp.float32)
+        owner_ref[...] = summed.reshape(owners, 1, slots)
 
 
 def field_spec(nx, ny, nz, chunk):
@@ -300,8 +296,8 @@
             pl.BlockSpec((1, count), lambda i: (0, 0)),
             pl.BlockSpec((1, count), lambda i: (0, 0)),
         ],
-        out_specs=[field_spec(nx, ny, nz, chunk), pl.BlockSpec((devices, P_DEV), lambda i: (0, 0))],
-        out_shape=[jax.ShapeDtypeStruct(e.shape, e.dtype), jax.ShapeDtypeStruct((devices, P_DEV), jnp.float32)],
+        out_specs=[field_spec(nx, ny, nz, chunk), pl.BlockSpec((devices, 1, P_DEV), lambda i: (0, 0, 0))],
+        out_shape=[jax.ShapeDtypeStruct(e.shape, e.dtype), jax.ShapeDtypeStruct((devices, 1, P_DEV), jnp.float32)],
         scratch_shapes=[pltpu.VMEM((1, count), jnp.float32), pltpu.VMEM((nz, count), jnp.bfloat16)],
     )(*args, ef, zrow, rrow, owners.reshape(1, count), slots.reshape(1, count))
 
@@ -322,7 +318,7 @@
         else:
             e, e_faces = e_step(e, h, h_faces, inv_perm)
     received = lax.all_to_all(per_owner, ("gx", "gy", "gz"), 0, 0, tiled=True)
-    gradient = received.sum(axis=0)
+    gradient = received.sum(axis=(0, 1))
     return (e, h, gradient)
 
 

time: 98.7 us -> 97.1 us (0.984)
  local copies, waits for them, and re-layouts: 3.75 us -> 2.71 us
    all_to_all x1 -> x0, local copies, waits for them, and re-layouts: 1.04 us -> none  [body(): received = lax.all_to_all(per_owner, ('gx', 'gy', 'gz'), 0, 0, tiled=True)]
where the time goes in v12:
time: 97.1 us; the launch traced here: 96.7 us
  starting transfers between devices  31.9 us (33%)
  Pallas kernels  25 us (26%)
  blocking collectives  19.6 us (20%)
  waiting for transfers between devices  14.8 us (15%)
  local copies, waits for them, and re-layouts  2.71 us (3%)
  other arithmetic  1.93 us (2%)
    ppermute x6, starting transfers between devices, toward_upper(): return lax.ppermute(x, axis, [(j, j + 1) for j in range(peers - 1)])  21.5 us
    all_to_all x1, blocking collectives, body(): received = lax.all_to_all(per_owner, ('gx', 'gy', 'gz'), 0, 0, tiled=True)  19.6 us
    ppermute x6, waiting for transfers between devices, toward_lower(): return lax.ppermute(x, axis, [(j, j - 1) for j in range(1, peers)])  13.5 us
    ppermute x6, starting transfers between devices, toward_lower(): return lax.ppermute(x, axis, [(j, j - 1) for j in range(1, peers)])  10.4 us
    pallas_call x2, Pallas kernels, h_step(): pl.pallas_call(h_kernel, grid=(nx // chunk,), in_specs=[field_spec(nx, ny...  9.67 us
    pallas_call x1, Pallas kernels, e_step(): pl.pallas_call(e_last_kernel, grid=(nx // chunk,), in_specs=in_specs + [f...  7.78 us
    pallas_call x1, Pallas kernels, e_step(): pl.pallas_call(e_kernel, grid=(nx // chunk,), in_specs=in_specs, out_spec...  5.17 us
    unnamed x26, local copies, waits for them, and re-layouts  2.71 us
  transfers between devices with their start and end apart: 12, of which 6 were waited for; matrix products, arithmetic and copies ran while one was open for 1% of the time, Pallas kernels for 0%

profile of v12, /device:TPU:1, one launch (start us, length us, event | category | flops | bytes accessed | tf_op | source)
XLA Modules:
  0.0 96.7 jit_solution(1262234247972747908)
XLA Ops:
  0.6 2.3 %shard_map.94 = (f32[2,1,16,1024]{3,2,1,0:T(8,128)}, f32[2,16,1,1024]{3,2,1,0:T(1,128)}, f32[2,2,1,128]{3,2,1,0:T(1,128)}) custom-call(f32[3,16,16,1024]{3,2,1,0:T(8,128)} %e_ref.3, f32[3,16,16,1024]{3,2,1,0:T(8,128)} %e_ref.3, f32[3,16,16,1024]{3,2,1,0:T(8,128)} %e_ref.3), custom_call_target="tpu_custom_call" | custom-call | tf_op jit(solution)/shard_map/pallas_call | solution.py:221
  3.0 1.3 %collective-permute-start = (f32[2,1,16,1024]{3,2,1,0:T(8,128)}, f32[2,1,16,1024]{3,2,1,0:T(8,128)S(1)}, u32[]{:S(2)}, u32[]{:S(2)}) collective-permute-start(f32[2,1,16,1024]{3,2,1,0:T(8,128)} %get-tuple-element.20), channel_id=1, source_target_pairs={{16,0},{32,16},{48,32},{64,48},{80,64},{96,80},{112,96},{17,1},{33... | collective-permute-start | bytes 393224 | tf_op jit(solution)/shard_map/ppermute | solution.py:19
  4.2 3.3 %collective-permute-start.1 = (f32[2,16,1,1024]{3,2,1,0:T(1,128)}, f32[2,16,1,1024]{3,2,1,0:T(1,128)S(1)}, u32[]{:S(2)}, u32[]{:S(2)}) collective-permute-start(f32[2,16,1,1024]{3,2,1,0:T(1,128)} %get-tuple-element.21), channel_id=1, source_target_pairs={{4,0},{8,4},{12,8},{5,1},{9,5},{13,9},{6,2},{10,6},{14,10},{7,3},{... | collective-permute-start | bytes 393224 | tf_op jit(solution)/shard_map/ppermute | solution.py:19
  7.5 1.3 %collective-permute-start.2 = (f32[2,2,1,128]{3,2,1,0:T(1,128)}, f32[2,2,1,128]{3,2,1,0:T(1,128)S(1)}, u32[]{:S(2)}, u32[]{:S(2)}) collective-permute-start(f32[2,2,1,128]{3,2,1,0:T(1,128)} %get-tuple-element.22), channel_id=1, source_target_pairs={{1,0},{2,1},{3,2},{5,4},{6,5},{7,6},{9,8},{10,9},{11,10},{13,12},{... | collective-permute-start | bytes 6152 | tf_op jit(solution)/shard_map/ppermute | solution.py:19
  8.8 3.4 %collective-permute-done.2.hz_ref = f32[2,2,1,128]{3,2,1,0:T(1,128)S(1)} collective-permute-done((f32[2,2,1,128]{3,2,1,0:T(1,128)}, f32[2,2,1,128]{3,2,1,0:T(1,128)S(1)}, u32[]{:S(2)}, u32[]{:S(2)}) %collective-permute-start.2) | collective-permute-done | bytes 2080 | tf_op jit(solution)/shard_map/ppermute | solution.py:19
  12.2 4.6 %collective-permute-done.1.hy_ref = f32[2,16,1,1024]{3,2,1,0:T(1,128)S(1)} collective-permute-done((f32[2,16,1,1024]{3,2,1,0:T(1,128)}, f32[2,16,1,1024]{3,2,1,0:T(1,128)S(1)}, u32[]{:S(2)}, u32[]{:S(2)}) %collective-permute-start.1) | collective-permute-done | bytes 131104 | tf_op jit(solution)/shard_map/ppermute | solution.py:19
  16.8 0.7 copy-done.6
  17.5 4.8 %shard_map.95 = (f32[3,16,16,1024]{3,2,1,0:T(8,128)}, f32[2,1,16,1024]{3,2,1,0:T(8,128)}, f32[2,16,1,1024]{3,2,1,0:T(1,128)}, f32[2,2,1,128]{3,2,1,0:T(1,128)}) custom-call(f32[3,16,16,1024]{3,2,1,0:T(8,128)} %e_ref.3, f32[3,16,16,1024]{3,2,1,0:T(8,128)} %e_ref.3, f32[3,16,16,1024]{3,2,1,0:T(8,128)} %h_ref.1, f32[2,1,16,1024]{3,2,1,0:T(8,128)} %copy-done.3, ...), custom_call_target="tpu_custom_call" | custom-call | tf_op jit(solution)/shard_map/pallas_call | solution.py:244
  22.3 1.3 %collective-permute-start.3 = (f32[2,1,16,1024]{3,2,1,0:T(8,128)}, f32[2,1,16,1024]{3,2,1,0:T(8,128)S(1)}, u32[]{:S(2)}, u32[]{:S(2)}) collective-permute-start(f32[2,1,16,1024]{3,2,1,0:T(8,128)} %get-tuple-element.24), channel_id=1, source_target_pairs={{0,16},{16,32},{32,48},{48,64},{64,80},{80,96},{96,112},{1,17},{17... | collective-permute-start | bytes 393224 | tf_op jit(solution)/shard_map/ppermute | solution.py:24
  23.6 5.9 %collective-permute-start.4 = (f32[2,16,1,1024]{3,2,1,0:T(1,128)}, f32[2,16,1,1024]{3,2,1,0:T(1,128)S(1)}, u32[]{:S(2)}, u32[]{:S(2)}) collective-permute-start(f32[2,16,1,1024]{3,2,1,0:T(1,128)} %get-tuple-element.25), channel_id=1, source_target_pairs={{0,4},{4,8},{8,12},{1,5},{5,9},{9,13},{2,6},{6,10},{10,14},{3,7},{... | collective-permute-start | bytes 393224 | tf_op jit(solution)/shard_map/ppermute | solution.py:24
  29.5 3.2 %collective-permute-start.5 = (f32[2,2,1,128]{3,2,1,0:T(1,128)}, f32[2,2,1,128]{3,2,1,0:T(1,128)S(1)}, u32[]{:S(2)}, u32[]{:S(2)}) collective-permute-start(f32[2,2,1,128]{3,2,1,0:T(1,128)} %get-tuple-element.26), channel_id=1, source_target_pairs={{0,1},{1,2},{2,3},{4,5},{5,6},{6,7},{8,9},{9,10},{10,11},{12,13},{... | collective-permute-start | bytes 6152 | tf_op jit(solution)/shard_map/ppermute | solution.py:24
  32.7 0.9 collective-permute-done.5.hz_ref
  33.6 0.6 copy-done.10
  34.3 5.2 %shard_map.96 = (f32[3,16,16,1024]{3,2,1,0:T(8,128)}, f32[2,1,16,1024]{3,2,1,0:T(8,128)}, f32[2,16,1,1024]{3,2,1,0:T(1,128)}, f32[2,2,1,128]{3,2,1,0:T(1,128)}) custom-call(f32[3,16,16,1024]{3,2,1,0:T(8,128)} %e_ref.3, f32[3,16,16,1024]{3,2,1,0:T(8,128)} %get-tuple-element.23.h_ref.hp_ref, f32[3,16,16,1024]{3,2,1,0:T(8,128)} %get-tuple-element.23.h_ref.hp_ref, ...), custom_call_target="tpu_custom_call" | custom-call | tf_op jit(solution)/shard_map/pallas_call | solution.py:277
  39.5 1.3 %collective-permute-start.6 = (f32[2,1,16,1024]{3,2,1,0:T(8,128)}, f32[2,1,16,1024]{3,2,1,0:T(8,128)S(1)}, u32[]{:S(2)}, u32[]{:S(2)}) collective-permute-start(f32[2,1,16,1024]{3,2,1,0:T(8,128)} %get-tuple-element.28), channel_id=1, source_target_pairs={{16,0},{32,16},{48,32},{64,48},{80,64},{96,80},{112,96},{17,1},{33... | collective-permute-start | bytes 393224 | tf_op jit(solution)/shard_map/ppermute | solution.py:19
  40.8 1.9 %collective-permute-start.7 = (f32[2,16,1,1024]{3,2,1,0:T(1,128)}, f32[2,16,1,1024]{3,2,1,0:T(1,128)S(1)}, u32[]{:S(2)}, u32[]{:S(2)}) collective-permute-start(f32[2,16,1,1024]{3,2,1,0:T(1,128)} %get-tuple-element.29), channel_id=1, source_target_pairs={{4,0},{8,4},{12,8},{5,1},{9,5},{13,9},{6,2},{10,6},{14,10},{7,3},{... | collective-permute-start | bytes 393224 | tf_op jit(solution)/shard_map/ppermute | solution.py:19
  42.7 1.3 %collective-permute-start.8 = (f32[2,2,1,128]{3,2,1,0:T(1,128)}, f32[2,2,1,128]{3,2,1,0:T(1,128)S(1)}, u32[]{:S(2)}, u32[]{:S(2)}) collective-permute-start(f32[2,2,1,128]{3,2,1,0:T(1,128)} %get-tuple-element.30), channel_id=1, source_target_pairs={{1,0},{2,1},{3,2},{5,4},{6,5},{7,6},{9,8},{10,9},{11,10},{13,12},{... | collective-permute-start | bytes 6152 | tf_op jit(solution)/shard_map/ppermute | solution.py:19
  44.0 0.6 and_select_fusion
  44.6 2.9 %collective-permute-done.8.hz_ref = f32[2,2,1,128]{3,2,1,0:T(1,128)S(1)} collective-permute-done((f32[2,2,1,128]{3,2,1,0:T(1,128)}, f32[2,2,1,128]{3,2,1,0:T(1,128)S(1)}, u32[]{:S(2)}, u32[]{:S(2)}) %collective-permute-start.8) | collective-permute-done | bytes 2080 | tf_op jit(solution)/shard_map/ppermute | solution.py:19
  47.5 2.7 %collective-permute-done.7.hy_ref = f32[2,16,1,1024]{3,2,1,0:T(1,128)S(1)} collective-permute-done((f32[2,16,1,1024]{3,2,1,0:T(1,128)}, f32[2,16,1,1024]{3,2,1,0:T(1,128)S(1)}, u32[]{:S(2)}, u32[]{:S(2)}) %collective-permute-start.7) | collective-permute-done | bytes 131104 | tf_op jit(solution)/shard_map/ppermute | solution.py:19
  50.2 0.7 copy-done.2
  50.8 4.8 %shard_map.97 = (f32[3,16,16,1024]{3,2,1,0:T(8,128)}, f32[2,1,16,1024]{3,2,1,0:T(8,128)}, f32[2,16,1,1024]{3,2,1,0:T(1,128)}, f32[2,2,1,128]{3,2,1,0:T(1,128)}) custom-call(f32[3,16,16,1024]{3,2,1,0:T(8,128)} %get-tuple-element.27.e_ref.en_ref, f32[3,16,16,1024]{3,2,1,0:T(8,128)} %get-tuple-element.27.e_ref.en_ref, ...), custom_call_target="tpu_custom_call" | custom-call | tf_op jit(solution)/shard_map/pallas_call | solution.py:244
  55.7 3.4 %collective-permute-start.10 = (f32[2,16,1,1024]{3,2,1,0:T(1,128)}, f32[2,16,1,1024]{3,2,1,0:T(1,128)S(1)}, u32[]{:S(2)}, u32[]{:S(2)}) collective-permute-start(f32[2,16,1,1024]{3,2,1,0:T(1,128)} %get-tuple-element.33), channel_id=1, source_target_pairs={{0,4},{4,8},{8,12},{1,5},{5,9},{9,13},{2,6},{6,10},{10,14},{3,7},{... | collective-permute-start | bytes 393224 | tf_op jit(solution)/shard_map/ppermute | solution.py:24
  59.1 4.2 %collective-permute-start.9 = (f32[2,1,16,1024]{3,2,1,0:T(8,128)}, f32[2,1,16,1024]{3,2,1,0:T(8,128)S(1)}, u32[]{:S(2)}, u32[]{:S(2)}) collective-permute-start(f32[2,1,16,1024]{3,2,1,0:T(8,128)} %get-tuple-element.32), channel_id=1, source_target_pairs={{0,16},{16,32},{32,48},{48,64},{64,80},{80,96},{96,112},{1,17},{17... | collective-permute-start | bytes 393224 | tf_op jit(solution)/shard_map/ppermute | solution.py:24
  63.3 3.6 %collective-permute-start.11 = (f32[2,2,1,128]{3,2,1,0:T(1,128)}, f32[2,2,1,128]{3,2,1,0:T(1,128)S(1)}, u32[]{:S(2)}, u32[]{:S(2)}) collective-permute-start(f32[2,2,1,128]{3,2,1,0:T(1,128)} %get-tuple-element.34), channel_id=1, source_target_pairs={{0,1},{1,2},{2,3},{4,5},{5,6},{6,7},{8,9},{9,10},{10,11},{12,13},{... | collective-permute-start | bytes 6152 | tf_op jit(solution)/shard_map/ppermute | solution.py:24
  66.9 0.6 and_select_fusion.1.zrow_ref
  67.5 0.3 collective-permute-done.11.hz_ref
  67.8 0.6 copy-done.9
  68.4 0.1 copy-done.1
  68.5 7.8 %shard_map.98 = (f32[3,16,16,1024]{3,2,1,0:T(8,128)}, f32[128,1,256]{2,1,0:T(1,128)}) custom-call(f32[3,16,16,1024]{3,2,1,0:T(8,128)} %get-tuple-element.27.e_ref.en_ref, f32[3,16,16,1024]{3,2,1,0:T(8,128)} %get-tuple-element.18.h_ref.hp_ref, f32[3,16,16,1024]{3,2,1,0:T(8,128)} %get-tuple-element.18.h_ref.hp_ref, f32[16,16,1024]{2,1,0:T(8,128)} %inv_ref.3, ...), custom_call_target="tpu_custom_call" | custom-call | tf_op jit(solution)/shard_map/pallas_call | solution.py:288
  76.3 19.6 %all_to_all.5 = f32[128,1,256]{2,1,0:T(1,128)S(1)} all-to-all(f32[128,1,256]{2,1,0:T(1,128)} %get-tuple-element.36), channel_id=1, replica_groups=mesh['gx'=8,'gy'=4,'gz'=4] {'gx','gy','gz'}, dimensions={0} | all-to-all | bytes 262144 | tf_op jit(solution)/shard_map/all_to_all | solution.py:320
  96.0 0.7 reduce_sum.9
  (27 shorter events, 0.2 us)
Async XLA Ops:
  3.0 9.3 %collective-permute-start = (f32[2,1,16,1024]{3,2,1,0:T(8,128)}, f32[2,1,16,1024]{3,2,1,0:T(8,128)S(1)}, u32[]{:S(2)}, u32[]{:S(2)}) collective-permute-start(f32[2,1,16,1024]{3,2,1,0:T(8,128)} %get-tuple-element.20), channel_id=1, source_target_pairs={{16,0},{32,16},{48,32},{64,48},{80,64},{96,80},{112,96},{17,1},{33... | collective-permute-start | bytes 393224 | tf_op jit(solution)/shard_map/ppermute | solution.py:19
  4.2 12.5 %collective-permute-start.1 = (f32[2,16,1,1024]{3,2,1,0:T(1,128)}, f32[2,16,1,1024]{3,2,1,0:T(1,128)S(1)}, u32[]{:S(2)}, u32[]{:S(2)}) collective-permute-start(f32[2,16,1,1024]{3,2,1,0:T(1,128)} %get-tuple-element.21), channel_id=1, source_target_pairs={{4,0},{8,4},{12,8},{5,1},{9,5},{13,9},{6,2},{10,6},{14,10},{7,3},{... | collective-permute-start | bytes 393224 | tf_op jit(solution)/shard_map/ppermute | solution.py:19
  7.5 4.7 %collective-permute-start.2 = (f32[2,2,1,128]{3,2,1,0:T(1,128)}, f32[2,2,1,128]{3,2,1,0:T(1,128)S(1)}, u32[]{:S(2)}, u32[]{:S(2)}) collective-permute-start(f32[2,2,1,128]{3,2,1,0:T(1,128)} %get-tuple-element.22), channel_id=1, source_target_pairs={{1,0},{2,1},{3,2},{5,4},{6,5},{7,6},{9,8},{10,9},{11,10},{13,12},{... | collective-permute-start | bytes 6152 | tf_op jit(solution)/shard_map/ppermute | solution.py:19
  12.2 4.6 %copy-start.12 = (f32[2,2,1,128]{3,2,1,0:T(1,128)}, f32[2,2,1,128]{3,2,1,0:T(1,128)S(1)}, u32[]{:S(2)}) copy-start(f32[2,2,1,128]{3,2,1,0:T(1,128)S(1)} %collective-permute-done.2.hz_ref) | copy-start | bytes 6148
  12.2 4.6 %copy-start.3 = (f32[2,1,16,1024]{3,2,1,0:T(8,128)}, f32[2,1,16,1024]{3,2,1,0:T(8,128)S(1)}, u32[]{:S(2)}) copy-start(f32[2,1,16,1024]{3,2,1,0:T(8,128)S(1)} %collective-permute-done.hx_ref) | copy-start | bytes 393220
  16.8 0.7 copy-start.6
  22.3 11.3 %collective-permute-start.3 = (f32[2,1,16,1024]{3,2,1,0:T(8,128)}, f32[2,1,16,1024]{3,2,1,0:T(8,128)S(1)}, u32[]{:S(2)}, u32[]{:S(2)}) collective-permute-start(f32[2,1,16,1024]{3,2,1,0:T(8,128)} %get-tuple-element.24), channel_id=1, source_target_pairs={{0,16},{16,32},{32,48},{48,64},{64,80},{80,96},{96,112},{1,17},{17... | collective-permute-start | bytes 393224 | tf_op jit(solution)/shard_map/ppermute | solution.py:24
  23.6 10.0 %collective-permute-start.4 = (f32[2,16,1,1024]{3,2,1,0:T(1,128)}, f32[2,16,1,1024]{3,2,1,0:T(1,128)S(1)}, u32[]{:S(2)}, u32[]{:S(2)}) collective-permute-start(f32[2,16,1,1024]{3,2,1,0:T(1,128)} %get-tuple-element.25), channel_id=1, source_target_pairs={{0,4},{4,8},{8,12},{1,5},{5,9},{9,13},{2,6},{6,10},{10,14},{3,7},{... | collective-permute-start | bytes 393224 | tf_op jit(solution)/shard_map/ppermute | solution.py:24
  29.5 4.1 %collective-permute-start.5 = (f32[2,2,1,128]{3,2,1,0:T(1,128)}, f32[2,2,1,128]{3,2,1,0:T(1,128)S(1)}, u32[]{:S(2)}, u32[]{:S(2)}) collective-permute-start(f32[2,2,1,128]{3,2,1,0:T(1,128)} %get-tuple-element.26), channel_id=1, source_target_pairs={{0,1},{1,2},{2,3},{4,5},{5,6},{6,7},{8,9},{9,10},{10,11},{12,13},{... | collective-permute-start | bytes 6152 | tf_op jit(solution)/shard_map/ppermute | solution.py:24
  33.6 0.6 copy-start.10
  33.6 0.7 copy-start.4
  33.6 0.7 copy-start.7
  34.3 9.7 %copy-start.8 = (s32[1,1,1,1024]{3,2,1,0:T(1,128)S(1)}, s32[1,1,1,1024]{3,2,1,0:T(1,128)}, u32[]{:S(2)}) copy-start(s32[1,1,1,1024]{3,2,1,0:T(1,128)} %param.11) | copy-start | bytes 12292
  39.5 8.0 %collective-permute-start.6 = (f32[2,1,16,1024]{3,2,1,0:T(8,128)}, f32[2,1,16,1024]{3,2,1,0:T(8,128)S(1)}, u32[]{:S(2)}, u32[]{:S(2)}) collective-permute-start(f32[2,1,16,1024]{3,2,1,0:T(8,128)} %get-tuple-element.28), channel_id=1, source_target_pairs={{16,0},{32,16},{48,32},{64,48},{80,64},{96,80},{112,96},{17,1},{33... | collective-permute-start | bytes 393224 | tf_op jit(solution)/shard_map/ppermute | solution.py:19
  40.8 9.4 %collective-permute-start.7 = (f32[2,16,1,1024]{3,2,1,0:T(1,128)}, f32[2,16,1,1024]{3,2,1,0:T(1,128)S(1)}, u32[]{:S(2)}, u32[]{:S(2)}) collective-permute-start(f32[2,16,1,1024]{3,2,1,0:T(1,128)} %get-tuple-element.29), channel_id=1, source_target_pairs={{4,0},{8,4},{12,8},{5,1},{9,5},{13,9},{6,2},{10,6},{14,10},{7,3},{... | collective-permute-start | bytes 393224 | tf_op jit(solution)/shard_map/ppermute | solution.py:19
  42.7 4.8 %collective-permute-start.8 = (f32[2,2,1,128]{3,2,1,0:T(1,128)}, f32[2,2,1,128]{3,2,1,0:T(1,128)S(1)}, u32[]{:S(2)}, u32[]{:S(2)}) collective-permute-start(f32[2,2,1,128]{3,2,1,0:T(1,128)} %get-tuple-element.30), channel_id=1, source_target_pairs={{1,0},{2,1},{3,2},{5,4},{6,5},{7,6},{9,8},{10,9},{11,10},{13,12},{... | collective-permute-start | bytes 6152 | tf_op jit(solution)/shard_map/ppermute | solution.py:19
  47.5 2.7 %copy-start.11 = (f32[2,2,1,128]{3,2,1,0:T(1,128)}, f32[2,2,1,128]{3,2,1,0:T(1,128)S(1)}, u32[]{:S(2)}) copy-start(f32[2,2,1,128]{3,2,1,0:T(1,128)S(1)} %collective-permute-done.8.hz_ref) | copy-start | bytes 6148
  47.5 2.7 %copy-start = (f32[2,1,16,1024]{3,2,1,0:T(8,128)}, f32[2,1,16,1024]{3,2,1,0:T(8,128)S(1)}, u32[]{:S(2)}) copy-start(f32[2,1,16,1024]{3,2,1,0:T(8,128)S(1)} %collective-permute-done.6.hx_ref) | copy-start | bytes 393220
  50.2 0.7 copy-start.2
  55.7 12.1 %collective-permute-start.10 = (f32[2,16,1,1024]{3,2,1,0:T(1,128)}, f32[2,16,1,1024]{3,2,1,0:T(1,128)S(1)}, u32[]{:S(2)}, u32[]{:S(2)}) collective-permute-start(f32[2,16,1,1024]{3,2,1,0:T(1,128)} %get-tuple-element.33), channel_id=1, source_target_pairs={{0,4},{4,8},{8,12},{1,5},{5,9},{9,13},{2,6},{6,10},{10,14},{3,7},{... | collective-permute-start | bytes 393224 | tf_op jit(solution)/shard_map/ppermute | solution.py:24
  59.1 8.7 %collective-permute-start.9 = (f32[2,1,16,1024]{3,2,1,0:T(8,128)}, f32[2,1,16,1024]{3,2,1,0:T(8,128)S(1)}, u32[]{:S(2)}, u32[]{:S(2)}) collective-permute-start(f32[2,1,16,1024]{3,2,1,0:T(8,128)} %get-tuple-element.32), channel_id=1, source_target_pairs={{0,16},{16,32},{32,48},{48,64},{64,80},{80,96},{96,112},{1,17},{17... | collective-permute-start | bytes 393224 | tf_op jit(solution)/shard_map/ppermute | solution.py:24
  63.3 4.5 %collective-permute-start.11 = (f32[2,2,1,128]{3,2,1,0:T(1,128)}, f32[2,2,1,128]{3,2,1,0:T(1,128)S(1)}, u32[]{:S(2)}, u32[]{:S(2)}) collective-permute-start(f32[2,2,1,128]{3,2,1,0:T(1,128)} %get-tuple-element.34), channel_id=1, source_target_pairs={{0,1},{1,2},{2,3},{4,5},{5,6},{6,7},{8,9},{9,10},{10,11},{12,13},{... | collective-permute-start | bytes 6152 | tf_op jit(solution)/shard_map/ppermute | solution.py:24
  67.8 0.6 copy-start.9
  67.8 0.7 copy-start.1
  67.8 0.7 copy-start.5

commit v13 on v12

--- a/solution.py
+++ b/solution.py
@@ -1,5 +1,3 @@
-import functools
-
 import jax
 import jax.numpy as jnp
 from jax import lax
@@ -7,6 +5,7 @@
 from jax.experimental.pallas import tpu as pltpu
 from jax.sharding import PartitionSpec as P
 
+
 STEPS = 2
 P_DEV = 256
 CHUNK = 8
@@ -57,18 +56,6 @@
     b, ny, _ = a.shape
     tile = jnp.transpose(a[:, :, lanes].reshape(b * ny, 128))
     return tile
-
-
-def fwd_x(a, nxt):
-    if a.shape[0] == 1:
-        return nxt
-    return jnp.concatenate([a[1:], nxt], axis=0)
-
-
-def bwd_x(a, prv):
-    if a.shape[0] == 1:
-        return prv
-    return jnp.concatenate([prv, a[:-1]], axis=0)
 
 
 def h_kernel(e_ref, en_ref, h_ref, hx_ref, hy_ref, hz_ref, out_ref, fx_ref, fy_ref, fz_ref):
@@ -104,7 +91,7 @@
 
 def e_slabs(e_ref, h_ref, hp_ref, inv_ref, hx_ref, hy_ref, hz_ref, out_ref):
     first = pl.program_id(0) == 0
-    _, b, ny, nz = h_ref.shape
+    _, b, ny, _ = h_ref.shape
     prv_y = jnp.where(first, hx_ref[0], hp_ref[1])
     prv_z = jnp.where(first, hx_ref[1], hp_ref[2])
     col_x = column_of(hz_ref[0, 0], b, ny)
@@ -184,11 +171,11 @@
         owner_ref[...] = summed.reshape(owners, 1, slots)
 
 
-def field_spec(nx, ny, nz, chunk):
+def field_spec(ny, nz, chunk):
     return pl.BlockSpec((3, chunk, ny, nz), lambda i: (0, i, 0, 0))
 
 
-def face_specs(nx, ny, nz, chunk):
+def face_specs(ny, nz, chunk):
     return [
         pl.BlockSpec((2, 1, ny, nz), lambda i: (0, 0, 0, 0)),
         pl.BlockSpec((2, chunk, 1, nz), lambda i: (0, i, 0, 0)),
@@ -238,21 +225,21 @@
 def h_step(e, h, faces):
     _, nx, ny, nz = e.shape
     chunk = CHUNK
+    faces_z = toward_lower(faces[2], "gz")
+    faces_y = toward_lower(faces[1], "gy")
     faces_x = toward_lower(faces[0], "gx")
-    faces_y = toward_lower(faces[1], "gy")
-    faces_z = toward_lower(faces[2], "gz")
     return pl.pallas_call(
         h_kernel,
         grid=(nx // chunk,),
         in_specs=[
-            field_spec(nx, ny, nz, chunk),
+            field_spec(ny, nz, chunk),
             pl.BlockSpec((3, 1, ny, nz), lambda i: (0, jnp.minimum((i + 1) * chunk, nx - 1), 0, 0)),
-            field_spec(nx, ny, nz, chunk),
+            field_spec(ny, nz, chunk),
             pl.BlockSpec((2, 1, ny, nz), lambda i: (0, 0, 0, 0)),
             pl.BlockSpec((2, chunk, 1, nz), lambda i: (0, i, 0, 0)),
             pl.BlockSpec((2, 1, 1, chunk * ny), lambda i: (0, i, 0, 0)),
         ],
-        out_specs=[field_spec(nx, ny, nz, chunk)] + face_specs(nx, ny, nz, chunk),
+        out_specs=[field_spec(ny, nz, chunk)] + face_specs(ny, nz, chunk),
         out_shape=[jax.ShapeDtypeStruct(h.shape, h.dtype)] + face_shapes(nx, ny, nz, h.dtype),
     )(e, e, h, faces_x, faces_y, faces_z)
 
@@ -260,12 +247,12 @@
 def e_step(e, h, faces, inv, ef=None, cells=None, owners=None, slots=None, devices=None):
     _, nx, ny, nz = e.shape
     chunk = CHUNK
+    faces_z = toward_upper(faces[2], "gz")
+    faces_y = toward_upper(faces[1], "gy")
     faces_x = toward_upper(faces[0], "gx")
-    faces_y = toward_upper(faces[1], "gy")
-    faces_z = toward_upper(faces[2], "gz")
     in_specs = [
-        field_spec(nx, ny, nz, chunk),
-        field_spec(nx, ny, nz, chunk),
+        field_spec(ny, nz, chunk),
+        field_spec(ny, nz, chunk),
         pl.BlockSpec((3, 1, ny, nz), lambda i: (0, jnp.maximum(i * chunk - 1, 0), 0, 0)),
         pl.BlockSpec((chunk, ny, nz), lambda i: (i, 0, 0)),
         pl.BlockSpec((2, 1, ny, nz), lambda i: (0, 0, 0, 0)),
@@ -278,7 +265,7 @@
             e_kernel,
             grid=(nx // chunk,),
             in_specs=in_specs,
-            out_specs=[field_spec(nx, ny, nz, chunk)] + face_specs(nx, ny, nz, chunk),
+            out_specs=[field_spec(ny, nz, chunk)] + face_specs(ny, nz, chunk),
             out_shape=[jax.ShapeDtypeStruct(e.shape, e.dtype)] + face_shapes(nx, ny, nz, e.dtype),
         )(*args)
         return outs[0], outs[1:]
@@ -290,13 +277,13 @@
         grid=(nx // chunk,),
         in_specs=in_specs
         + [
-            field_spec(nx, ny, nz, chunk),
+            field_spec(ny, nz, chunk),
             pl.BlockSpec((1, count), lambda i: (0, 0)),
             pl.BlockSpec((1, count), lambda i: (0, 0)),
             pl.BlockSpec((1, count), lambda i: (0, 0)),
             pl.BlockSpec((1, count), lambda i: (0, 0)),
         ],
-        out_specs=[field_spec(nx, ny, nz, chunk), pl.BlockSpec((devices, 1, P_DEV), lambda i: (0, 0, 0))],
+        out_specs=[field_spec(ny, nz, chunk), pl.BlockSpec((devices, 1, P_DEV), lambda i: (0, 0, 0))],
         out_shape=[jax.ShapeDtypeStruct(e.shape, e.dtype), jax.ShapeDtypeStruct((devices, 1, P_DEV), jnp.float32)],
         scratch_shapes=[pltpu.VMEM((1, count), jnp.float32), pltpu.VMEM((nz, count), jnp.bfloat16)],
     )(*args, ef, zrow, rrow, owners.reshape(1, count), slots.reshape(1, count))

time: 97.1 us -> 97.1 us (level)
  no operation moved by 1% of the time
where the time goes in v13:
time: 97.1 us; the launch traced here: 96.7 us
  starting transfers between devices  31.9 us (33%)
  Pallas kernels  25 us (26%)
  blocking collectives  19.6 us (20%)
  waiting for transfers between devices  14.8 us (15%)
  local copies, waits for them, and re-layouts  2.71 us (3%)
  other arithmetic  1.93 us (2%)
    ppermute x6, starting transfers between devices, toward_upper(): return lax.ppermute(x, axis, [(j, j + 1) for j in range(peers - 1)])  21.5 us
    all_to_all x1, blocking collectives, body(): received = lax.all_to_all(per_owner, ('gx', 'gy', 'gz'), 0, 0, tiled=True)  19.6 us
    ppermute x6, waiting for transfers between devices, toward_lower(): return lax.ppermute(x, axis, [(j, j - 1) for j in range(1, peers)])  13.5 us
    ppermute x6, starting transfers between devices, toward_lower(): return lax.ppermute(x, axis, [(j, j - 1) for j in range(1, peers)])  10.4 us
    pallas_call x2, Pallas kernels, h_step(): pl.pallas_call(h_kernel, grid=(nx // chunk,), in_specs=[field_spec(ny, nz...  9.67 us
    pallas_call x1, Pallas kernels, e_step(): pl.pallas_call(e_last_kernel, grid=(nx // chunk,), in_specs=in_specs + [f...  7.78 us
    pallas_call x1, Pallas kernels, e_step(): pl.pallas_call(e_kernel, grid=(nx // chunk,), in_specs=in_specs, out_spec...  5.17 us
    unnamed x26, local copies, waits for them, and re-layouts  2.71 us
  transfers between devices with their start and end apart: 12, of which 6 were waited for; matrix products, arithmetic and copies ran while one was open for 1% of the time, Pallas kernels for 0%

profile of v13, /device:TPU:1, one launch (start us, length us, event | category | flops | bytes accessed | tf_op | source)
XLA Modules:
  0.0 96.7 jit_solution(1262234247972747908)
XLA Ops:
  0.6 2.3 %shard_map.94 = (f32[2,1,16,1024]{3,2,1,0:T(8,128)}, f32[2,16,1,1024]{3,2,1,0:T(1,128)}, f32[2,2,1,128]{3,2,1,0:T(1,128)}) custom-call(f32[3,16,16,1024]{3,2,1,0:T(8,128)} %e_ref.3, f32[3,16,16,1024]{3,2,1,0:T(8,128)} %e_ref.3, f32[3,16,16,1024]{3,2,1,0:T(8,128)} %e_ref.3), custom_call_target="tpu_custom_call" | custom-call | tf_op jit(solution)/shard_map/pallas_call | solution.py:208
  3.0 1.3 %collective-permute-start = (f32[2,1,16,1024]{3,2,1,0:T(8,128)}, f32[2,1,16,1024]{3,2,1,0:T(8,128)S(1)}, u32[]{:S(2)}, u32[]{:S(2)}) collective-permute-start(f32[2,1,16,1024]{3,2,1,0:T(8,128)} %get-tuple-element.20), channel_id=1, source_target_pairs={{16,0},{32,16},{48,32},{64,48},{80,64},{96,80},{112,96},{17,1},{33... | collective-permute-start | bytes 393224 | tf_op jit(solution)/shard_map/ppermute | solution.py:18
  4.2 3.3 %collective-permute-start.1 = (f32[2,16,1,1024]{3,2,1,0:T(1,128)}, f32[2,16,1,1024]{3,2,1,0:T(1,128)S(1)}, u32[]{:S(2)}, u32[]{:S(2)}) collective-permute-start(f32[2,16,1,1024]{3,2,1,0:T(1,128)} %get-tuple-element.21), channel_id=1, source_target_pairs={{4,0},{8,4},{12,8},{5,1},{9,5},{13,9},{6,2},{10,6},{14,10},{7,3},{... | collective-permute-start | bytes 393224 | tf_op jit(solution)/shard_map/ppermute | solution.py:18
  7.5 1.3 %collective-permute-start.2 = (f32[2,2,1,128]{3,2,1,0:T(1,128)}, f32[2,2,1,128]{3,2,1,0:T(1,128)S(1)}, u32[]{:S(2)}, u32[]{:S(2)}) collective-permute-start(f32[2,2,1,128]{3,2,1,0:T(1,128)} %get-tuple-element.22), channel_id=1, source_target_pairs={{1,0},{2,1},{3,2},{5,4},{6,5},{7,6},{9,8},{10,9},{11,10},{13,12},{... | collective-permute-start | bytes 6152 | tf_op jit(solution)/shard_map/ppermute | solution.py:18
  8.8 3.4 %collective-permute-done.2.hz_ref = f32[2,2,1,128]{3,2,1,0:T(1,128)S(1)} collective-permute-done((f32[2,2,1,128]{3,2,1,0:T(1,128)}, f32[2,2,1,128]{3,2,1,0:T(1,128)S(1)}, u32[]{:S(2)}, u32[]{:S(2)}) %collective-permute-start.2) | collective-permute-done | bytes 2080 | tf_op jit(solution)/shard_map/ppermute | solution.py:18
  12.2 4.6 %collective-permute-done.1.hy_ref = f32[2,16,1,1024]{3,2,1,0:T(1,128)S(1)} collective-permute-done((f32[2,16,1,1024]{3,2,1,0:T(1,128)}, f32[2,16,1,1024]{3,2,1,0:T(1,128)S(1)}, u32[]{:S(2)}, u32[]{:S(2)}) %collective-permute-start.1) | collective-permute-done | bytes 131104 | tf_op jit(solution)/shard_map/ppermute | solution.py:18
  16.8 0.7 copy-done.6
  17.5 4.8 %shard_map.95 = (f32[3,16,16,1024]{3,2,1,0:T(8,128)}, f32[2,1,16,1024]{3,2,1,0:T(8,128)}, f32[2,16,1,1024]{3,2,1,0:T(1,128)}, f32[2,2,1,128]{3,2,1,0:T(1,128)}) custom-call(f32[3,16,16,1024]{3,2,1,0:T(8,128)} %e_ref.3, f32[3,16,16,1024]{3,2,1,0:T(8,128)} %e_ref.3, f32[3,16,16,1024]{3,2,1,0:T(8,128)} %h_ref.1, f32[2,1,16,1024]{3,2,1,0:T(8,128)} %copy-done.3, ...), custom_call_target="tpu_custom_call" | custom-call | tf_op jit(solution)/shard_map/pallas_call | solution.py:231
  22.3 1.3 %collective-permute-start.3 = (f32[2,1,16,1024]{3,2,1,0:T(8,128)}, f32[2,1,16,1024]{3,2,1,0:T(8,128)S(1)}, u32[]{:S(2)}, u32[]{:S(2)}) collective-permute-start(f32[2,1,16,1024]{3,2,1,0:T(8,128)} %get-tuple-element.24), channel_id=1, source_target_pairs={{0,16},{16,32},{32,48},{48,64},{64,80},{80,96},{96,112},{1,17},{17... | collective-permute-start | bytes 393224 | tf_op jit(solution)/shard_map/ppermute | solution.py:23
  23.6 5.9 %collective-permute-start.4 = (f32[2,16,1,1024]{3,2,1,0:T(1,128)}, f32[2,16,1,1024]{3,2,1,0:T(1,128)S(1)}, u32[]{:S(2)}, u32[]{:S(2)}) collective-permute-start(f32[2,16,1,1024]{3,2,1,0:T(1,128)} %get-tuple-element.25), channel_id=1, source_target_pairs={{0,4},{4,8},{8,12},{1,5},{5,9},{9,13},{2,6},{6,10},{10,14},{3,7},{... | collective-permute-start | bytes 393224 | tf_op jit(solution)/shard_map/ppermute | solution.py:23
  29.5 3.2 %collective-permute-start.5 = (f32[2,2,1,128]{3,2,1,0:T(1,128)}, f32[2,2,1,128]{3,2,1,0:T(1,128)S(1)}, u32[]{:S(2)}, u32[]{:S(2)}) collective-permute-start(f32[2,2,1,128]{3,2,1,0:T(1,128)} %get-tuple-element.26), channel_id=1, source_target_pairs={{0,1},{1,2},{2,3},{4,5},{5,6},{6,7},{8,9},{9,10},{10,11},{12,13},{... | collective-permute-start | bytes 6152 | tf_op jit(solution)/shard_map/ppermute | solution.py:23
  32.7 0.9 collective-permute-done.5.hz_ref
  33.6 0.6 copy-done.10
  34.3 5.2 %shard_map.96 = (f32[3,16,16,1024]{3,2,1,0:T(8,128)}, f32[2,1,16,1024]{3,2,1,0:T(8,128)}, f32[2,16,1,1024]{3,2,1,0:T(1,128)}, f32[2,2,1,128]{3,2,1,0:T(1,128)}) custom-call(f32[3,16,16,1024]{3,2,1,0:T(8,128)} %e_ref.3, f32[3,16,16,1024]{3,2,1,0:T(8,128)} %get-tuple-element.23.h_ref.hp_ref, f32[3,16,16,1024]{3,2,1,0:T(8,128)} %get-tuple-element.23.h_ref.hp_ref, ...), custom_call_target="tpu_custom_call" | custom-call | tf_op jit(solution)/shard_map/pallas_call | solution.py:264
  39.5 1.3 %collective-permute-start.6 = (f32[2,1,16,1024]{3,2,1,0:T(8,128)}, f32[2,1,16,1024]{3,2,1,0:T(8,128)S(1)}, u32[]{:S(2)}, u32[]{:S(2)}) collective-permute-start(f32[2,1,16,1024]{3,2,1,0:T(8,128)} %get-tuple-element.28), channel_id=1, source_target_pairs={{16,0},{32,16},{48,32},{64,48},{80,64},{96,80},{112,96},{17,1},{33... | collective-permute-start | bytes 393224 | tf_op jit(solution)/shard_map/ppermute | solution.py:18
  40.8 1.9 %collective-permute-start.7 = (f32[2,16,1,1024]{3,2,1,0:T(1,128)}, f32[2,16,1,1024]{3,2,1,0:T(1,128)S(1)}, u32[]{:S(2)}, u32[]{:S(2)}) collective-permute-start(f32[2,16,1,1024]{3,2,1,0:T(1,128)} %get-tuple-element.29), channel_id=1, source_target_pairs={{4,0},{8,4},{12,8},{5,1},{9,5},{13,9},{6,2},{10,6},{14,10},{7,3},{... | collective-permute-start | bytes 393224 | tf_op jit(solution)/shard_map/ppermute | solution.py:18
  42.7 1.3 %collective-permute-start.8 = (f32[2,2,1,128]{3,2,1,0:T(1,128)}, f32[2,2,1,128]{3,2,1,0:T(1,128)S(1)}, u32[]{:S(2)}, u32[]{:S(2)}) collective-permute-start(f32[2,2,1,128]{3,2,1,0:T(1,128)} %get-tuple-element.30), channel_id=1, source_target_pairs={{1,0},{2,1},{3,2},{5,4},{6,5},{7,6},{9,8},{10,9},{11,10},{13,12},{... | collective-permute-start | bytes 6152 | tf_op jit(solution)/shard_map/ppermute | solution.py:18
  44.0 0.6 and_select_fusion
  44.6 2.9 %collective-permute-done.8.hz_ref = f32[2,2,1,128]{3,2,1,0:T(1,128)S(1)} collective-permute-done((f32[2,2,1,128]{3,2,1,0:T(1,128)}, f32[2,2,1,128]{3,2,1,0:T(1,128)S(1)}, u32[]{:S(2)}, u32[]{:S(2)}) %collective-permute-start.8) | collective-permute-done | bytes 2080 | tf_op jit(solution)/shard_map/ppermute | solution.py:18
  47.5 2.7 %collective-permute-done.7.hy_ref = f32[2,16,1,1024]{3,2,1,0:T(1,128)S(1)} collective-permute-done((f32[2,16,1,1024]{3,2,1,0:T(1,128)}, f32[2,16,1,1024]{3,2,1,0:T(1,128)S(1)}, u32[]{:S(2)}, u32[]{:S(2)}) %collective-permute-start.7) | collective-permute-done | bytes 131104 | tf_op jit(solution)/shard_map/ppermute | solution.py:18
  50.2 0.7 copy-done.2
  50.8 4.8 %shard_map.97 = (f32[3,16,16,1024]{3,2,1,0:T(8,128)}, f32[2,1,16,1024]{3,2,1,0:T(8,128)}, f32[2,16,1,1024]{3,2,1,0:T(1,128)}, f32[2,2,1,128]{3,2,1,0:T(1,128)}) custom-call(f32[3,16,16,1024]{3,2,1,0:T(8,128)} %get-tuple-element.27.e_ref.en_ref, f32[3,16,16,1024]{3,2,1,0:T(8,128)} %get-tuple-element.27.e_ref.en_ref, ...), custom_call_target="tpu_custom_call" | custom-call | tf_op jit(solution)/shard_map/pallas_call | solution.py:231
  55.7 3.4 %collective-permute-start.10 = (f32[2,16,1,1024]{3,2,1,0:T(1,128)}, f32[2,16,1,1024]{3,2,1,0:T(1,128)S(1)}, u32[]{:S(2)}, u32[]{:S(2)}) collective-permute-start(f32[2,16,1,1024]{3,2,1,0:T(1,128)} %get-tuple-element.33), channel_id=1, source_target_pairs={{0,4},{4,8},{8,12},{1,5},{5,9},{9,13},{2,6},{6,10},{10,14},{3,7},{... | collective-permute-start | bytes 393224 | tf_op jit(solution)/shard_map/ppermute | solution.py:23
  59.1 4.2 %collective-permute-start.9 = (f32[2,1,16,1024]{3,2,1,0:T(8,128)}, f32[2,1,16,1024]{3,2,1,0:T(8,128)S(1)}, u32[]{:S(2)}, u32[]{:S(2)}) collective-permute-start(f32[2,1,16,1024]{3,2,1,0:T(8,128)} %get-tuple-element.32), channel_id=1, source_target_pairs={{0,16},{16,32},{32,48},{48,64},{64,80},{80,96},{96,112},{1,17},{17... | collective-permute-start | bytes 393224 | tf_op jit(solution)/shard_map/ppermute | solution.py:23
  63.3 3.6 %collective-permute-start.11 = (f32[2,2,1,128]{3,2,1,0:T(1,128)}, f32[2,2,1,128]{3,2,1,0:T(1,128)S(1)}, u32[]{:S(2)}, u32[]{:S(2)}) collective-permute-start(f32[2,2,1,128]{3,2,1,0:T(1,128)} %get-tuple-element.34), channel_id=1, source_target_pairs={{0,1},{1,2},{2,3},{4,5},{5,6},{6,7},{8,9},{9,10},{10,11},{12,13},{... | collective-permute-start | bytes 6152 | tf_op jit(solution)/shard_map/ppermute | solution.py:23
  66.9 0.6 and_select_fusion.1.zrow_ref
  67.5 0.3 collective-permute-done.11.hz_ref
  67.8 0.6 copy-done.9
  68.4 0.1 copy-done.1
  68.5 7.8 %shard_map.98 = (f32[3,16,16,1024]{3,2,1,0:T(8,128)}, f32[128,1,256]{2,1,0:T(1,128)}) custom-call(f32[3,16,16,1024]{3,2,1,0:T(8,128)} %get-tuple-element.27.e_ref.en_ref, f32[3,16,16,1024]{3,2,1,0:T(8,128)} %get-tuple-element.18.h_ref.hp_ref, f32[3,16,16,1024]{3,2,1,0:T(8,128)} %get-tuple-element.18.h_ref.hp_ref, f32[16,16,1024]{2,1,0:T(8,128)} %inv_ref.3, ...), custom_call_target="tpu_custom_call" | custom-call | tf_op jit(solution)/shard_map/pallas_call | solution.py:275
  76.3 19.6 %all_to_all.5 = f32[128,1,256]{2,1,0:T(1,128)S(1)} all-to-all(f32[128,1,256]{2,1,0:T(1,128)} %get-tuple-element.36), channel_id=1, replica_groups=mesh['gx'=8,'gy'=4,'gz'=4] {'gx','gy','gz'}, dimensions={0} | all-to-all | bytes 262144 | tf_op jit(solution)/shard_map/all_to_all | solution.py:307
  96.0 0.7 reduce_sum.9
  (27 shorter events, 0.2 us)
Async XLA Ops:
  3.0 9.3 %collective-permute-start = (f32[2,1,16,1024]{3,2,1,0:T(8,128)}, f32[2,1,16,1024]{3,2,1,0:T(8,128)S(1)}, u32[]{:S(2)}, u32[]{:S(2)}) collective-permute-start(f32[2,1,16,1024]{3,2,1,0:T(8,128)} %get-tuple-element.20), channel_id=1, source_target_pairs={{16,0},{32,16},{48,32},{64,48},{80,64},{96,80},{112,96},{17,1},{33... | collective-permute-start | bytes 393224 | tf_op jit(solution)/shard_map/ppermute | solution.py:18
  4.2 12.5 %collective-permute-start.1 = (f32[2,16,1,1024]{3,2,1,0:T(1,128)}, f32[2,16,1,1024]{3,2,1,0:T(1,128)S(1)}, u32[]{:S(2)}, u32[]{:S(2)}) collective-permute-start(f32[2,16,1,1024]{3,2,1,0:T(1,128)} %get-tuple-element.21), channel_id=1, source_target_pairs={{4,0},{8,4},{12,8},{5,1},{9,5},{13,9},{6,2},{10,6},{14,10},{7,3},{... | collective-permute-start | bytes 393224 | tf_op jit(solution)/shard_map/ppermute | solution.py:18
  7.5 4.7 %collective-permute-start.2 = (f32[2,2,1,128]{3,2,1,0:T(1,128)}, f32[2,2,1,128]{3,2,1,0:T(1,128)S(1)}, u32[]{:S(2)}, u32[]{:S(2)}) collective-permute-start(f32[2,2,1,128]{3,2,1,0:T(1,128)} %get-tuple-element.22), channel_id=1, source_target_pairs={{1,0},{2,1},{3,2},{5,4},{6,5},{7,6},{9,8},{10,9},{11,10},{13,12},{... | collective-permute-start | bytes 6152 | tf_op jit(solution)/shard_map/ppermute | solution.py:18
  12.2 4.6 %copy-start.12 = (f32[2,2,1,128]{3,2,1,0:T(1,128)}, f32[2,2,1,128]{3,2,1,0:T(1,128)S(1)}, u32[]{:S(2)}) copy-start(f32[2,2,1,128]{3,2,1,0:T(1,128)S(1)} %collective-permute-done.2.hz_ref) | copy-start | bytes 6148
  12.2 4.6 %copy-start.3 = (f32[2,1,16,1024]{3,2,1,0:T(8,128)}, f32[2,1,16,1024]{3,2,1,0:T(8,128)S(1)}, u32[]{:S(2)}) copy-start(f32[2,1,16,1024]{3,2,1,0:T(8,128)S(1)} %collective-permute-done.hx_ref) | copy-start | bytes 393220
  16.8 0.7 copy-start.6
  22.3 11.3 %collective-permute-start.3 = (f32[2,1,16,1024]{3,2,1,0:T(8,128)}, f32[2,1,16,1024]{3,2,1,0:T(8,128)S(1)}, u32[]{:S(2)}, u32[]{:S(2)}) collective-permute-start(f32[2,1,16,1024]{3,2,1,0:T(8,128)} %get-tuple-element.24), channel_id=1, source_target_pairs={{0,16},{16,32},{32,48},{48,64},{64,80},{80,96},{96,112},{1,17},{17... | collective-permute-start | bytes 393224 | tf_op jit(solution)/shard_map/ppermute | solution.py:23
  23.6 10.0 %collective-permute-start.4 = (f32[2,16,1,1024]{3,2,1,0:T(1,128)}, f32[2,16,1,1024]{3,2,1,0:T(1,128)S(1)}, u32[]{:S(2)}, u32[]{:S(2)}) collective-permute-start(f32[2,16,1,1024]{3,2,1,0:T(1,128)} %get-tuple-element.25), channel_id=1, source_target_pairs={{0,4},{4,8},{8,12},{1,5},{5,9},{9,13},{2,6},{6,10},{10,14},{3,7},{... | collective-permute-start | bytes 393224 | tf_op jit(solution)/shard_map/ppermute | solution.py:23
  29.5 4.1 %collective-permute-start.5 = (f32[2,2,1,128]{3,2,1,0:T(1,128)}, f32[2,2,1,128]{3,2,1,0:T(1,128)S(1)}, u32[]{:S(2)}, u32[]{:S(2)}) collective-permute-start(f32[2,2,1,128]{3,2,1,0:T(1,128)} %get-tuple-element.26), channel_id=1, source_target_pairs={{0,1},{1,2},{2,3},{4,5},{5,6},{6,7},{8,9},{9,10},{10,11},{12,13},{... | collective-permute-start | bytes 6152 | tf_op jit(solution)/shard_map/ppermute | solution.py:23
  33.6 0.6 copy-start.10
  33.6 0.7 copy-start.4
  33.6 0.7 copy-start.7
  34.3 9.7 %copy-start.8 = (s32[1,1,1,1024]{3,2,1,0:T(1,128)S(1)}, s32[1,1,1,1024]{3,2,1,0:T(1,128)}, u32[]{:S(2)}) copy-start(s32[1,1,1,1024]{3,2,1,0:T(1,128)} %param.11) | copy-start | bytes 12292
  39.5 8.0 %collective-permute-start.6 = (f32[2,1,16,1024]{3,2,1,0:T(8,128)}, f32[2,1,16,1024]{3,2,1,0:T(8,128)S(1)}, u32[]{:S(2)}, u32[]{:S(2)}) collective-permute-start(f32[2,1,16,1024]{3,2,1,0:T(8,128)} %get-tuple-element.28), channel_id=1, source_target_pairs={{16,0},{32,16},{48,32},{64,48},{80,64},{96,80},{112,96},{17,1},{33... | collective-permute-start | bytes 393224 | tf_op jit(solution)/shard_map/ppermute | solution.py:18
  40.8 9.4 %collective-permute-start.7 = (f32[2,16,1,1024]{3,2,1,0:T(1,128)}, f32[2,16,1,1024]{3,2,1,0:T(1,128)S(1)}, u32[]{:S(2)}, u32[]{:S(2)}) collective-permute-start(f32[2,16,1,1024]{3,2,1,0:T(1,128)} %get-tuple-element.29), channel_id=1, source_target_pairs={{4,0},{8,4},{12,8},{5,1},{9,5},{13,9},{6,2},{10,6},{14,10},{7,3},{... | collective-permute-start | bytes 393224 | tf_op jit(solution)/shard_map/ppermute | solution.py:18
  42.7 4.8 %collective-permute-start.8 = (f32[2,2,1,128]{3,2,1,0:T(1,128)}, f32[2,2,1,128]{3,2,1,0:T(1,128)S(1)}, u32[]{:S(2)}, u32[]{:S(2)}) collective-permute-start(f32[2,2,1,128]{3,2,1,0:T(1,128)} %get-tuple-element.30), channel_id=1, source_target_pairs={{1,0},{2,1},{3,2},{5,4},{6,5},{7,6},{9,8},{10,9},{11,10},{13,12},{... | collective-permute-start | bytes 6152 | tf_op jit(solution)/shard_map/ppermute | solution.py:18
  47.5 2.7 %copy-start.11 = (f32[2,2,1,128]{3,2,1,0:T(1,128)}, f32[2,2,1,128]{3,2,1,0:T(1,128)S(1)}, u32[]{:S(2)}) copy-start(f32[2,2,1,128]{3,2,1,0:T(1,128)S(1)} %collective-permute-done.8.hz_ref) | copy-start | bytes 6148
  47.5 2.7 %copy-start = (f32[2,1,16,1024]{3,2,1,0:T(8,128)}, f32[2,1,16,1024]{3,2,1,0:T(8,128)S(1)}, u32[]{:S(2)}) copy-start(f32[2,1,16,1024]{3,2,1,0:T(8,128)S(1)} %collective-permute-done.6.hx_ref) | copy-start | bytes 393220
  50.2 0.7 copy-start.2
  55.7 12.1 %collective-permute-start.10 = (f32[2,16,1,1024]{3,2,1,0:T(1,128)}, f32[2,16,1,1024]{3,2,1,0:T(1,128)S(1)}, u32[]{:S(2)}, u32[]{:S(2)}) collective-permute-start(f32[2,16,1,1024]{3,2,1,0:T(1,128)} %get-tuple-element.33), channel_id=1, source_target_pairs={{0,4},{4,8},{8,12},{1,5},{5,9},{9,13},{2,6},{6,10},{10,14},{3,7},{... | collective-permute-start | bytes 393224 | tf_op jit(solution)/shard_map/ppermute | solution.py:23
  59.1 8.7 %collective-permute-start.9 = (f32[2,1,16,1024]{3,2,1,0:T(8,128)}, f32[2,1,16,1024]{3,2,1,0:T(8,128)S(1)}, u32[]{:S(2)}, u32[]{:S(2)}) collective-permute-start(f32[2,1,16,1024]{3,2,1,0:T(8,128)} %get-tuple-element.32), channel_id=1, source_target_pairs={{0,16},{16,32},{32,48},{48,64},{64,80},{80,96},{96,112},{1,17},{17... | collective-permute-start | bytes 393224 | tf_op jit(solution)/shard_map/ppermute | solution.py:23
  63.3 4.5 %collective-permute-start.11 = (f32[2,2,1,128]{3,2,1,0:T(1,128)}, f32[2,2,1,128]{3,2,1,0:T(1,128)S(1)}, u32[]{:S(2)}, u32[]{:S(2)}) collective-permute-start(f32[2,2,1,128]{3,2,1,0:T(1,128)} %get-tuple-element.34), channel_id=1, source_target_pairs={{0,1},{1,2},{2,3},{4,5},{5,6},{6,7},{8,9},{9,10},{10,11},{12,13},{... | collective-permute-start | bytes 6152 | tf_op jit(solution)/shard_map/ppermute | solution.py:23
  67.8 0.6 copy-start.9
  67.8 0.7 copy-start.1
  67.8 0.7 copy-start.5

commit v14 on v13

--- a/solution.py
+++ b/solution.py
@@ -191,9 +191,7 @@
     ]
 
 
-def faces_kernel(slab_ref, rows_ref, lanes_ref, fx_ref, fy_ref, fz_ref):
-    fx_ref[0] = slab_ref[1]
-    fx_ref[1] = slab_ref[2]
+def faces_kernel(rows_ref, lanes_ref, fy_ref, fz_ref):
     fy_ref[0] = rows_ref[0, :, 0:1, :]
     fy_ref[1] = rows_ref[2, :, 0:1, :]
     nx = lanes_ref.shape[1]
@@ -205,29 +203,28 @@
 
 def lower_faces_of(e):
     _, nx, ny, nz = e.shape
-    return pl.pallas_call(
-        faces_kernel,
-        grid=(1,),
-        in_specs=[
-            pl.BlockSpec((3, 1, ny, nz), lambda i: (0, 0, 0, 0)),
-            pl.BlockSpec((3, nx, 8, nz), lambda i: (0, 0, 0, 0)),
-            pl.BlockSpec((3, nx, ny, 128), lambda i: (0, 0, 0, 0)),
-        ],
-        out_specs=[
-            pl.BlockSpec((2, 1, ny, nz), lambda i: (0, 0, 0, 0)),
-            pl.BlockSpec((2, nx, 1, nz), lambda i: (0, 0, 0, 0)),
-            pl.BlockSpec((2, nx // CHUNK, 1, CHUNK * ny), lambda i: (0, 0, 0, 0)),
-        ],
-        out_shape=face_shapes(nx, ny, nz, e.dtype),
-    )(e, e, e)
+    face_y, face_z = pl.pallas_call(
+    faces_kernel,
+    grid=(1,),
+    in_specs=[
+        pl.BlockSpec((3, nx, 8, nz), lambda i: (0, 0, 0, 0)),
+        pl.BlockSpec((2, nx, ny, 128), lambda i: (0, 0, 0, 0)),
+    ],
+    out_specs=[
+        pl.BlockSpec((2, nx, 1, nz), lambda i: (0, 0, 0, 0)),
+        pl.BlockSpec((2, nx // CHUNK, 1, CHUNK * ny), lambda i: (0, 0, 0, 0)),
+    ],
+    out_shape=face_shapes(nx, ny, nz, e.dtype)[1:],
+    )(e, e)
+    return e[1:3, 0:1], face_y, face_z
 
 
 def h_step(e, h, faces):
     _, nx, ny, nz = e.shape
     chunk = CHUNK
+    faces_x = toward_lower(faces[0], "gx")
+    faces_y = toward_lower(faces[1], "gy")
     faces_z = toward_lower(faces[2], "gz")
-    faces_y = toward_lower(faces[1], "gy")
-    faces_x = toward_lower(faces[0], "gx")
     return pl.pallas_call(
         h_kernel,
         grid=(nx // chunk,),
@@ -247,9 +244,9 @@
 def e_step(e, h, faces, inv, ef=None, cells=None, owners=None, slots=None, devices=None):
     _, nx, ny, nz = e.shape
     chunk = CHUNK
+    faces_x = toward_upper(faces[0], "gx")
+    faces_y = toward_upper(faces[1], "gy")
     faces_z = toward_upper(faces[2], "gz")
-    faces_y = toward_upper(faces[1], "gy")
-    faces_x = toward_upper(faces[0], "gx")
     in_specs = [
         field_spec(ny, nz, chunk),
         field_spec(ny, nz, chunk),
@@ -296,10 +293,12 @@
     slot_ids = voxel_slot.reshape(count)
     devices = lax.axis_size("gx") * lax.axis_size("gy") * lax.axis_size("gz")
     e, h = e_adjoint, h_adjoint
+    per_owner = None
     e_faces = lower_faces_of(e)
-    per_owner = None
+    h, *h_faces = h_step(e, h, e_faces)
     for repeat in range(STEPS):
-        h, *h_faces = h_step(e, h, e_faces)
+        if repeat > 0:
+            h, *h_faces = h_step(e, h, e_faces)
         if repeat == STEPS - 1:
             e, per_owner = e_step(e, h, h_faces, inv_perm, e_forward, voxel_rows, owners, slot_ids, devices)
         else:

time: 97.1 us -> 97.9 us (level)
  starting transfers between devices: 31.9 us -> 35.5 us
  waiting for transfers between devices: 14.8 us -> 11.2 us
    ppermute x6, starting transfers between devices: 21.5 us -> 25.1 us  [toward_upper(): return lax.ppermute(x, axis, [(j, j + 1) for j in range(peers - 1)])]
    ppermute x6, waiting for transfers between devices: 13.5 us -> 9.92 us  [toward_lower(): return lax.ppermute(x, axis, [(j, j - 1) for j in range(1, peers)])]
  transfers between devices with their start and end apart: 12 -> 12, of which waited for: 6 -> 6; matrix products, arithmetic and copies ran while one was open for 1% -> 2% of each run, Pallas kernels for 0% -> 0%
where the time goes in v14:
time: 97.9 us; the launch traced here: 97.4 us
  starting transfers between devices  35.5 us (36%)
  Pallas kernels  24.8 us (25%)
  blocking collectives  19.6 us (20%)
  waiting for transfers between devices  11.2 us (11%)
  local copies, waits for them, and re-layouts  3.63 us (4%)
  other arithmetic  1.93 us (2%)
    ppermute x6, starting transfers between devices, toward_upper(): return lax.ppermute(x, axis, [(j, j + 1) for j in range(peers - 1)])  25.1 us
    all_to_all x1, blocking collectives, body(): received = lax.all_to_all(per_owner, ('gx', 'gy', 'gz'), 0, 0, tiled=True)  19.6 us
    ppermute x6, starting transfers between devices, toward_lower(): return lax.ppermute(x, axis, [(j, j - 1) for j in range(1, peers)])  10.4 us
    ppermute x6, waiting for transfers between devices, toward_lower(): return lax.ppermute(x, axis, [(j, j - 1) for j in range(1, peers)])  9.92 us
    pallas_call x2, Pallas kernels, h_step(): pl.pallas_call(h_kernel, grid=(nx // chunk,), in_specs=[field_spec(ny, nz...  9.67 us
    pallas_call x1, Pallas kernels, e_step(): pl.pallas_call(e_last_kernel, grid=(nx // chunk,), in_specs=in_specs + [f...  7.79 us
    pallas_call x1, Pallas kernels, e_step(): pl.pallas_call(e_kernel, grid=(nx // chunk,), in_specs=in_specs, out_spec...  5.17 us
    unnamed x26, local copies, waits for them, and re-layouts  2.71 us
  transfers between devices with their start and end apart: 12, of which 6 were waited for; matrix products, arithmetic and copies ran while one was open for 2% of the time, Pallas kernels for 0%

profile of v14, /device:TPU:1, one launch (start us, length us, event | category | flops | bytes accessed | tf_op | source)
XLA Modules:
  0.0 97.4 jit_solution(16442902416623155494)
XLA Ops:
  0.6 2.1 %shard_map.94 = (f32[2,16,1,1024]{3,2,1,0:T(1,128)}, f32[2,2,1,128]{3,2,1,0:T(1,128)}) custom-call(f32[3,16,16,1024]{3,2,1,0:T(8,128)} %e_ref.3, f32[3,16,16,1024]{3,2,1,0:T(8,128)} %e_ref.3), custom_call_target="tpu_custom_call" | custom-call | tf_op jit(solution)/shard_map/pallas_call | solution.py:206
  2.8 3.3 %collective-permute-start.1 = (f32[2,16,1,1024]{3,2,1,0:T(1,128)}, f32[2,16,1,1024]{3,2,1,0:T(1,128)S(1)}, u32[]{:S(2)}, u32[]{:S(2)}) collective-permute-start(f32[2,16,1,1024]{3,2,1,0:T(1,128)} %get-tuple-element.19), channel_id=1, source_target_pairs={{4,0},{8,4},{12,8},{5,1},{9,5},{13,9},{6,2},{10,6},{14,10},{7,3},{... | collective-permute-start | bytes 393224 | tf_op jit(solution)/shard_map/ppermute | solution.py:18
  6.0 0.9 slice.3
  7.0 1.3 %collective-permute-start = (f32[2,1,16,1024]{3,2,1,0:T(8,128)S(1)}, f32[2,1,16,1024]{3,2,1,0:T(8,128)S(1)}, u32[]{:S(2)}, u32[]{:S(2)}) collective-permute-start(f32[2,1,16,1024]{3,2,1,0:T(8,128)S(1)} %slice.3), channel_id=1, source_target_pairs={{16,0},{32,16},{48,32},{64,48},{80,64},{96,80},{112,96},{17,1},{33... | collective-permute-start | bytes 393224 | tf_op jit(solution)/shard_map/ppermute | solution.py:18
  8.3 1.3 %collective-permute-start.2 = (f32[2,2,1,128]{3,2,1,0:T(1,128)}, f32[2,2,1,128]{3,2,1,0:T(1,128)S(1)}, u32[]{:S(2)}, u32[]{:S(2)}) collective-permute-start(f32[2,2,1,128]{3,2,1,0:T(1,128)} %get-tuple-element.20), channel_id=1, source_target_pairs={{1,0},{2,1},{3,2},{5,4},{6,5},{7,6},{9,8},{10,9},{11,10},{13,12},{... | collective-permute-start | bytes 6152 | tf_op jit(solution)/shard_map/ppermute | solution.py:18
  9.6 3.5 %collective-permute-done.2.hz_ref = f32[2,2,1,128]{3,2,1,0:T(1,128)S(1)} collective-permute-done((f32[2,2,1,128]{3,2,1,0:T(1,128)}, f32[2,2,1,128]{3,2,1,0:T(1,128)S(1)}, u32[]{:S(2)}, u32[]{:S(2)}) %collective-permute-start.2) | collective-permute-done | bytes 2080 | tf_op jit(solution)/shard_map/ppermute | solution.py:18
  13.1 0.8 collective-permute-done.hx_ref
  14.0 0.7 copy-done.6
  14.6 4.8 %shard_map.95 = (f32[3,16,16,1024]{3,2,1,0:T(8,128)}, f32[2,1,16,1024]{3,2,1,0:T(8,128)}, f32[2,16,1,1024]{3,2,1,0:T(1,128)}, f32[2,2,1,128]{3,2,1,0:T(1,128)}) custom-call(f32[3,16,16,1024]{3,2,1,0:T(8,128)} %e_ref.3, f32[3,16,16,1024]{3,2,1,0:T(8,128)} %e_ref.3, f32[3,16,16,1024]{3,2,1,0:T(8,128)} %h_ref.1, f32[2,1,16,1024]{3,2,1,0:T(8,128)} %copy-done.6, ...), custom_call_target="tpu_custom_call" | custom-call | tf_op jit(solution)/shard_map/pallas_call | solution.py:228
  19.4 4.7 %collective-permute-start.3 = (f32[2,1,16,1024]{3,2,1,0:T(8,128)}, f32[2,1,16,1024]{3,2,1,0:T(8,128)S(1)}, u32[]{:S(2)}, u32[]{:S(2)}) collective-permute-start(f32[2,1,16,1024]{3,2,1,0:T(8,128)} %get-tuple-element.22), channel_id=1, source_target_pairs={{0,16},{16,32},{32,48},{48,64},{64,80},{80,96},{96,112},{1,17},{17... | collective-permute-start | bytes 393224 | tf_op jit(solution)/shard_map/ppermute | solution.py:23
  24.1 6.1 %collective-permute-start.4 = (f32[2,16,1,1024]{3,2,1,0:T(1,128)}, f32[2,16,1,1024]{3,2,1,0:T(1,128)S(1)}, u32[]{:S(2)}, u32[]{:S(2)}) collective-permute-start(f32[2,16,1,1024]{3,2,1,0:T(1,128)} %get-tuple-element.23), channel_id=1, source_target_pairs={{0,4},{4,8},{8,12},{1,5},{5,9},{9,13},{2,6},{6,10},{10,14},{3,7},{... | collective-permute-start | bytes 393224 | tf_op jit(solution)/shard_map/ppermute | solution.py:23
  30.2 3.2 %collective-permute-start.5 = (f32[2,2,1,128]{3,2,1,0:T(1,128)}, f32[2,2,1,128]{3,2,1,0:T(1,128)S(1)}, u32[]{:S(2)}, u32[]{:S(2)}) collective-permute-start(f32[2,2,1,128]{3,2,1,0:T(1,128)} %get-tuple-element.24), channel_id=1, source_target_pairs={{0,1},{1,2},{2,3},{4,5},{5,6},{6,7},{8,9},{9,10},{10,11},{12,13},{... | collective-permute-start | bytes 6152 | tf_op jit(solution)/shard_map/ppermute | solution.py:23
  33.4 0.9 collective-permute-done.5.hz_ref
  34.4 0.6 copy-done.10
  35.1 5.2 %shard_map.96 = (f32[3,16,16,1024]{3,2,1,0:T(8,128)}, f32[2,1,16,1024]{3,2,1,0:T(8,128)}, f32[2,16,1,1024]{3,2,1,0:T(1,128)}, f32[2,2,1,128]{3,2,1,0:T(1,128)}) custom-call(f32[3,16,16,1024]{3,2,1,0:T(8,128)} %e_ref.3, f32[3,16,16,1024]{3,2,1,0:T(8,128)} %get-tuple-element.21.h_ref.hp_ref, f32[3,16,16,1024]{3,2,1,0:T(8,128)} %get-tuple-element.21.h_ref.hp_ref, ...), custom_call_target="tpu_custom_call" | custom-call | tf_op jit(solution)/shard_map/pallas_call | solution.py:261
  40.2 1.3 %collective-permute-start.6 = (f32[2,1,16,1024]{3,2,1,0:T(8,128)}, f32[2,1,16,1024]{3,2,1,0:T(8,128)S(1)}, u32[]{:S(2)}, u32[]{:S(2)}) collective-permute-start(f32[2,1,16,1024]{3,2,1,0:T(8,128)} %get-tuple-element.26), channel_id=1, source_target_pairs={{16,0},{32,16},{48,32},{64,48},{80,64},{96,80},{112,96},{17,1},{33... | collective-permute-start | bytes 393224 | tf_op jit(solution)/shard_map/ppermute | solution.py:18
  41.5 1.9 %collective-permute-start.7 = (f32[2,16,1,1024]{3,2,1,0:T(1,128)}, f32[2,16,1,1024]{3,2,1,0:T(1,128)S(1)}, u32[]{:S(2)}, u32[]{:S(2)}) collective-permute-start(f32[2,16,1,1024]{3,2,1,0:T(1,128)} %get-tuple-element.27), channel_id=1, source_target_pairs={{4,0},{8,4},{12,8},{5,1},{9,5},{13,9},{6,2},{10,6},{14,10},{7,3},{... | collective-permute-start | bytes 393224 | tf_op jit(solution)/shard_map/ppermute | solution.py:18
  43.5 1.3 %collective-permute-start.8 = (f32[2,2,1,128]{3,2,1,0:T(1,128)}, f32[2,2,1,128]{3,2,1,0:T(1,128)S(1)}, u32[]{:S(2)}, u32[]{:S(2)}) collective-permute-start(f32[2,2,1,128]{3,2,1,0:T(1,128)} %get-tuple-element.28), channel_id=1, source_target_pairs={{1,0},{2,1},{3,2},{5,4},{6,5},{7,6},{9,8},{10,9},{11,10},{13,12},{... | collective-permute-start | bytes 6152 | tf_op jit(solution)/shard_map/ppermute | solution.py:18
  44.8 0.6 and_select_fusion
  45.4 2.9 %collective-permute-done.8.hz_ref = f32[2,2,1,128]{3,2,1,0:T(1,128)S(1)} collective-permute-done((f32[2,2,1,128]{3,2,1,0:T(1,128)}, f32[2,2,1,128]{3,2,1,0:T(1,128)S(1)}, u32[]{:S(2)}, u32[]{:S(2)}) %collective-permute-start.8) | collective-permute-done | bytes 2080 | tf_op jit(solution)/shard_map/ppermute | solution.py:18
  48.3 2.7 %collective-permute-done.7.hy_ref = f32[2,16,1,1024]{3,2,1,0:T(1,128)S(1)} collective-permute-done((f32[2,16,1,1024]{3,2,1,0:T(1,128)}, f32[2,16,1,1024]{3,2,1,0:T(1,128)S(1)}, u32[]{:S(2)}, u32[]{:S(2)}) %collective-permute-start.7) | collective-permute-done | bytes 131104 | tf_op jit(solution)/shard_map/ppermute | solution.py:18
  50.9 0.7 copy-done.3
  51.6 4.8 %shard_map.97 = (f32[3,16,16,1024]{3,2,1,0:T(8,128)}, f32[2,1,16,1024]{3,2,1,0:T(8,128)}, f32[2,16,1,1024]{3,2,1,0:T(1,128)}, f32[2,2,1,128]{3,2,1,0:T(1,128)}) custom-call(f32[3,16,16,1024]{3,2,1,0:T(8,128)} %get-tuple-element.25.e_ref.en_ref, f32[3,16,16,1024]{3,2,1,0:T(8,128)} %get-tuple-element.25.e_ref.en_ref, ...), custom_call_target="tpu_custom_call" | custom-call | tf_op jit(solution)/shard_map/pallas_call | solution.py:228
  56.4 3.4 %collective-permute-start.10 = (f32[2,16,1,1024]{3,2,1,0:T(1,128)}, f32[2,16,1,1024]{3,2,1,0:T(1,128)S(1)}, u32[]{:S(2)}, u32[]{:S(2)}) collective-permute-start(f32[2,16,1,1024]{3,2,1,0:T(1,128)} %get-tuple-element.31), channel_id=1, source_target_pairs={{0,4},{4,8},{8,12},{1,5},{5,9},{9,13},{2,6},{6,10},{10,14},{3,7},{... | collective-permute-start | bytes 393224 | tf_op jit(solution)/shard_map/ppermute | solution.py:23
  59.9 4.1 %collective-permute-start.9 = (f32[2,1,16,1024]{3,2,1,0:T(8,128)}, f32[2,1,16,1024]{3,2,1,0:T(8,128)S(1)}, u32[]{:S(2)}, u32[]{:S(2)}) collective-permute-start(f32[2,1,16,1024]{3,2,1,0:T(8,128)} %get-tuple-element.30), channel_id=1, source_target_pairs={{0,16},{16,32},{32,48},{48,64},{64,80},{80,96},{96,112},{1,17},{17... | collective-permute-start | bytes 393224 | tf_op jit(solution)/shard_map/ppermute | solution.py:23
  64.0 3.6 %collective-permute-start.11 = (f32[2,2,1,128]{3,2,1,0:T(1,128)}, f32[2,2,1,128]{3,2,1,0:T(1,128)S(1)}, u32[]{:S(2)}, u32[]{:S(2)}) collective-permute-start(f32[2,2,1,128]{3,2,1,0:T(1,128)} %get-tuple-element.32), channel_id=1, source_target_pairs={{0,1},{1,2},{2,3},{4,5},{5,6},{6,7},{8,9},{9,10},{10,11},{12,13},{... | collective-permute-start | bytes 6152 | tf_op jit(solution)/shard_map/ppermute | solution.py:23
  67.6 0.6 and_select_fusion.1.zrow_ref
  68.2 0.3 collective-permute-done.11.hz_ref
  68.6 0.6 copy-done.9
  69.3 7.8 %shard_map.98 = (f32[3,16,16,1024]{3,2,1,0:T(8,128)}, f32[128,1,256]{2,1,0:T(1,128)}) custom-call(f32[3,16,16,1024]{3,2,1,0:T(8,128)} %get-tuple-element.25.e_ref.en_ref, f32[3,16,16,1024]{3,2,1,0:T(8,128)} %get-tuple-element.17.h_ref.hp_ref, f32[3,16,16,1024]{3,2,1,0:T(8,128)} %get-tuple-element.17.h_ref.hp_ref, f32[16,16,1024]{2,1,0:T(8,128)} %inv_ref.3, ...), custom_call_target="tpu_custom_call" | custom-call | tf_op jit(solution)/shard_map/pallas_call | solution.py:272
  77.0 19.6 %all_to_all.5 = f32[128,1,256]{2,1,0:T(1,128)S(1)} all-to-all(f32[128,1,256]{2,1,0:T(1,128)} %get-tuple-element.34), channel_id=1, replica_groups=mesh['gx'=8,'gy'=4,'gz'=4] {'gx','gy','gz'}, dimensions={0} | all-to-all | bytes 262144 | tf_op jit(solution)/shard_map/all_to_all | solution.py:306
  96.7 0.7 reduce_sum.9
  (28 shorter events, 0.3 us)
Async XLA Ops:
  2.8 10.3 %collective-permute-start.1 = (f32[2,16,1,1024]{3,2,1,0:T(1,128)}, f32[2,16,1,1024]{3,2,1,0:T(1,128)S(1)}, u32[]{:S(2)}, u32[]{:S(2)}) collective-permute-start(f32[2,16,1,1024]{3,2,1,0:T(1,128)} %get-tuple-element.19), channel_id=1, source_target_pairs={{4,0},{8,4},{12,8},{5,1},{9,5},{13,9},{6,2},{10,6},{14,10},{7,3},{... | collective-permute-start | bytes 393224 | tf_op jit(solution)/shard_map/ppermute | solution.py:18
  7.0 7.0 %collective-permute-start = (f32[2,1,16,1024]{3,2,1,0:T(8,128)S(1)}, f32[2,1,16,1024]{3,2,1,0:T(8,128)S(1)}, u32[]{:S(2)}, u32[]{:S(2)}) collective-permute-start(f32[2,1,16,1024]{3,2,1,0:T(8,128)S(1)} %slice.3), channel_id=1, source_target_pairs={{16,0},{32,16},{48,32},{64,48},{80,64},{96,80},{112,96},{17,1},{33... | collective-permute-start | bytes 393224 | tf_op jit(solution)/shard_map/ppermute | solution.py:18
  8.3 4.8 %collective-permute-start.2 = (f32[2,2,1,128]{3,2,1,0:T(1,128)}, f32[2,2,1,128]{3,2,1,0:T(1,128)S(1)}, u32[]{:S(2)}, u32[]{:S(2)}) collective-permute-start(f32[2,2,1,128]{3,2,1,0:T(1,128)} %get-tuple-element.20), channel_id=1, source_target_pairs={{1,0},{2,1},{3,2},{5,4},{6,5},{7,6},{9,8},{10,9},{11,10},{13,12},{... | collective-permute-start | bytes 6152 | tf_op jit(solution)/shard_map/ppermute | solution.py:18
  13.1 0.8 copy-start.12
  13.1 0.8 copy-start.2
  14.0 0.7 copy-start.6
  19.4 14.9 %collective-permute-start.3 = (f32[2,1,16,1024]{3,2,1,0:T(8,128)}, f32[2,1,16,1024]{3,2,1,0:T(8,128)S(1)}, u32[]{:S(2)}, u32[]{:S(2)}) collective-permute-start(f32[2,1,16,1024]{3,2,1,0:T(8,128)} %get-tuple-element.22), channel_id=1, source_target_pairs={{0,16},{16,32},{32,48},{48,64},{64,80},{80,96},{96,112},{1,17},{17... | collective-permute-start | bytes 393224 | tf_op jit(solution)/shard_map/ppermute | solution.py:23
  24.1 10.2 %collective-permute-start.4 = (f32[2,16,1,1024]{3,2,1,0:T(1,128)}, f32[2,16,1,1024]{3,2,1,0:T(1,128)S(1)}, u32[]{:S(2)}, u32[]{:S(2)}) collective-permute-start(f32[2,16,1,1024]{3,2,1,0:T(1,128)} %get-tuple-element.23), channel_id=1, source_target_pairs={{0,4},{4,8},{8,12},{1,5},{5,9},{9,13},{2,6},{6,10},{10,14},{3,7},{... | collective-permute-start | bytes 393224 | tf_op jit(solution)/shard_map/ppermute | solution.py:23
  30.2 4.1 %collective-permute-start.5 = (f32[2,2,1,128]{3,2,1,0:T(1,128)}, f32[2,2,1,128]{3,2,1,0:T(1,128)S(1)}, u32[]{:S(2)}, u32[]{:S(2)}) collective-permute-start(f32[2,2,1,128]{3,2,1,0:T(1,128)} %get-tuple-element.24), channel_id=1, source_target_pairs={{0,1},{1,2},{2,3},{4,5},{5,6},{6,7},{8,9},{9,10},{10,11},{12,13},{... | collective-permute-start | bytes 6152 | tf_op jit(solution)/shard_map/ppermute | solution.py:23
  34.4 0.6 copy-start.10
  34.4 0.7 copy-start.4
  34.4 0.7 copy-start.7
  35.1 9.7 %copy-start.8 = (s32[1,1,1,1024]{3,2,1,0:T(1,128)S(1)}, s32[1,1,1,1024]{3,2,1,0:T(1,128)}, u32[]{:S(2)}) copy-start(s32[1,1,1,1024]{3,2,1,0:T(1,128)} %param.11) | copy-start | bytes 12292
  40.2 8.0 %collective-permute-start.6 = (f32[2,1,16,1024]{3,2,1,0:T(8,128)}, f32[2,1,16,1024]{3,2,1,0:T(8,128)S(1)}, u32[]{:S(2)}, u32[]{:S(2)}) collective-permute-start(f32[2,1,16,1024]{3,2,1,0:T(8,128)} %get-tuple-element.26), channel_id=1, source_target_pairs={{16,0},{32,16},{48,32},{64,48},{80,64},{96,80},{112,96},{17,1},{33... | collective-permute-start | bytes 393224 | tf_op jit(solution)/shard_map/ppermute | solution.py:18
  41.5 9.4 %collective-permute-start.7 = (f32[2,16,1,1024]{3,2,1,0:T(1,128)}, f32[2,16,1,1024]{3,2,1,0:T(1,128)S(1)}, u32[]{:S(2)}, u32[]{:S(2)}) collective-permute-start(f32[2,16,1,1024]{3,2,1,0:T(1,128)} %get-tuple-element.27), channel_id=1, source_target_pairs={{4,0},{8,4},{12,8},{5,1},{9,5},{13,9},{6,2},{10,6},{14,10},{7,3},{... | collective-permute-start | bytes 393224 | tf_op jit(solution)/shard_map/ppermute | solution.py:18
  43.5 4.8 %collective-permute-start.8 = (f32[2,2,1,128]{3,2,1,0:T(1,128)}, f32[2,2,1,128]{3,2,1,0:T(1,128)S(1)}, u32[]{:S(2)}, u32[]{:S(2)}) collective-permute-start(f32[2,2,1,128]{3,2,1,0:T(1,128)} %get-tuple-element.28), channel_id=1, source_target_pairs={{1,0},{2,1},{3,2},{5,4},{6,5},{7,6},{9,8},{10,9},{11,10},{13,12},{... | collective-permute-start | bytes 6152 | tf_op jit(solution)/shard_map/ppermute | solution.py:18
  48.2 2.7 %copy-start.11 = (f32[2,2,1,128]{3,2,1,0:T(1,128)}, f32[2,2,1,128]{3,2,1,0:T(1,128)S(1)}, u32[]{:S(2)}) copy-start(f32[2,2,1,128]{3,2,1,0:T(1,128)S(1)} %collective-permute-done.8.hz_ref) | copy-start | bytes 6148
  48.2 2.7 %copy-start = (f32[2,1,16,1024]{3,2,1,0:T(8,128)}, f32[2,1,16,1024]{3,2,1,0:T(8,128)S(1)}, u32[]{:S(2)}) copy-start(f32[2,1,16,1024]{3,2,1,0:T(8,128)S(1)} %collective-permute-done.6.hx_ref) | copy-start | bytes 393220
  50.9 0.7 copy-start.3
  56.4 12.1 %collective-permute-start.10 = (f32[2,16,1,1024]{3,2,1,0:T(1,128)}, f32[2,16,1,1024]{3,2,1,0:T(1,128)S(1)}, u32[]{:S(2)}, u32[]{:S(2)}) collective-permute-start(f32[2,16,1,1024]{3,2,1,0:T(1,128)} %get-tuple-element.31), channel_id=1, source_target_pairs={{0,4},{4,8},{8,12},{1,5},{5,9},{9,13},{2,6},{6,10},{10,14},{3,7},{... | collective-permute-start | bytes 393224 | tf_op jit(solution)/shard_map/ppermute | solution.py:23
  59.9 8.7 %collective-permute-start.9 = (f32[2,1,16,1024]{3,2,1,0:T(8,128)}, f32[2,1,16,1024]{3,2,1,0:T(8,128)S(1)}, u32[]{:S(2)}, u32[]{:S(2)}) collective-permute-start(f32[2,1,16,1024]{3,2,1,0:T(8,128)} %get-tuple-element.30), channel_id=1, source_target_pairs={{0,16},{16,32},{32,48},{48,64},{64,80},{80,96},{96,112},{1,17},{17... | collective-permute-start | bytes 393224 | tf_op jit(solution)/shard_map/ppermute | solution.py:23
  64.0 4.5 %collective-permute-start.11 = (f32[2,2,1,128]{3,2,1,0:T(1,128)}, f32[2,2,1,128]{3,2,1,0:T(1,128)S(1)}, u32[]{:S(2)}, u32[]{:S(2)}) collective-permute-start(f32[2,2,1,128]{3,2,1,0:T(1,128)} %get-tuple-element.32), channel_id=1, source_target_pairs={{0,1},{1,2},{2,3},{4,5},{5,6},{6,7},{8,9},{9,10},{10,11},{12,13},{... | collective-permute-start | bytes 6152 | tf_op jit(solution)/shard_map/ppermute | solution.py:23
  68.5 0.6 copy-start.9
  68.5 0.7 copy-start.1
  68.6 0.7 copy-start.5

commit v15 on v12

--- a/solution.py
+++ b/solution.py
@@ -153,26 +153,31 @@
     new_x, new_y, new_z = out_ref[0], out_ref[1], out_ref[2]
     step = pl.program_id(0)
     b, ny, nz = new_x.shape
-    count = zhot_ref.shape[1]
+
+    count = zhot_ref.shape[0]
 
     @pl.when(step == 0)
     def _():
-        zhot_ref[...] = (lax.broadcasted_iota(jnp.int32, (nz, count), 0) == zrow_ref[...]).astype(jnp.bfloat16)
+        zhot_ref[...] = (lax.broadcasted_iota(jnp.int32, (count, nz), 1) == zrow_ref[...]).astype(jnp.bfloat16)
         terms_ref[...] = jnp.zeros_like(terms_ref)
 
     inter = (ef_ref[0] * new_x + ef_ref[1] * new_y + ef_ref[2] * new_z).reshape(b * ny, nz)
     hi = inter.astype(jnp.bfloat16)
     mid = (inter - hi.astype(jnp.float32)).astype(jnp.bfloat16)
     zhot = zhot_ref[...]
-    picked = jnp.dot(hi, zhot, preferred_element_type=jnp.float32) + jnp.dot(mid, zhot, preferred_element_type=jnp.float32)
-    row_at = step * (b * ny) + lax.broadcasted_iota(jnp.int32, picked.shape, 0)
-    terms_ref[...] += jnp.sum(jnp.where(row_at == rrow_ref[...], picked, 0.0), axis=0, keepdims=True)
+    nt = (((1,), (1,)), ((), ()))
+    picked = lax.dot_general(zhot, hi, nt, preferred_element_type=jnp.float32) + lax.dot_general(
+        zhot, mid, nt, preferred_element_type=jnp.float32
+    )
+    row_at = step * (b * ny) + lax.broadcasted_iota(jnp.int32, picked.shape, 1)
+    terms_ref[...] += jnp.sum(jnp.where(row_at == rrow_ref[...], picked, 0.0), axis=1, keepdims=True)
 
     @pl.when(step == pl.num_programs(0) - 1)
     def _():
         owners, _, slots = owner_ref.shape
+        terms_row = jnp.transpose(jnp.broadcast_to(terms_ref[...], (count, 128)))[0:1]
         weighted = jnp.where(
-            lax.broadcasted_iota(jnp.int32, (owners, count), 0) == orow_ref[...], terms_ref[...], 0.0
+            lax.broadcasted_iota(jnp.int32, (owners, count), 0) == orow_ref[...], terms_row, 0.0
         )
         slot_hot = (lax.broadcasted_iota(jnp.int32, (slots, count), 0) == srow_ref[...]).astype(jnp.bfloat16)
         hi, mid, lo = split3(weighted)
@@ -283,22 +288,22 @@
         )(*args)
         return outs[0], outs[1:]
     count = cells.shape[0]
-    zrow = (cells % nz).reshape(1, count)
-    rrow = (cells // nz).reshape(1, count)
+    zrow = (cells % nz).reshape(count, 1)
+    rrow = (cells // nz).reshape(count, 1)
     return pl.pallas_call(
         e_last_kernel,
         grid=(nx // chunk,),
         in_specs=in_specs
         + [
             field_spec(nx, ny, nz, chunk),
-            pl.BlockSpec((1, count), lambda i: (0, 0)),
-            pl.BlockSpec((1, count), lambda i: (0, 0)),
+            pl.BlockSpec((count, 1), lambda i: (0, 0)),
+            pl.BlockSpec((count, 1), lambda i: (0, 0)),
             pl.BlockSpec((1, count), lambda i: (0, 0)),
             pl.BlockSpec((1, count), lambda i: (0, 0)),
         ],
         out_specs=[field_spec(nx, ny, nz, chunk), pl.BlockSpec((devices, 1, P_DEV), lambda i: (0, 0, 0))],
         out_shape=[jax.ShapeDtypeStruct(e.shape, e.dtype), jax.ShapeDtypeStruct((devices, 1, P_DEV), jnp.float32)],
-        scratch_shapes=[pltpu.VMEM((1, count), jnp.float32), pltpu.VMEM((nz, count), jnp.bfloat16)],
+        scratch_shapes=[pltpu.VMEM((count, 1), jnp.float32), pltpu.VMEM((count, nz), jnp.bfloat16)],
     )(*args, ef, zrow, rrow, owners.reshape(1, count), slots.reshape(1, count))
 
 

time: 97.1 us -> 98.7 us (1.016)
  Pallas kernels: 25 us -> 26.5 us
    pallas_call x1, Pallas kernels: 7.78 us -> 9.32 us  [e_step(): pl.pallas_call(e_last_kernel, grid=(nx // chunk,), in_specs=in_specs + [f...]
  transfers between devices with their start and end apart: 12 -> 12, of which waited for: 6 -> 5; matrix products, arithmetic and copies ran while one was open for 1% -> 2% of each run, Pallas kernels for 0% -> 0%
where the time goes in v15:
time: 98.7 us; the launch traced here: 98.2 us
  starting transfers between devices  31.9 us (32%)
  Pallas kernels  26.5 us (27%)
  blocking collectives  19.1 us (19%)
  waiting for transfers between devices  14.8 us (15%)
  local copies, waits for them, and re-layouts  2.89 us (3%)
  other arithmetic  2.12 us (2%)
    ppermute x6, starting transfers between devices, toward_upper(): return lax.ppermute(x, axis, [(j, j + 1) for j in range(peers - 1)])  21.6 us
    all_to_all x1, blocking collectives, body(): received = lax.all_to_all(per_owner, ('gx', 'gy', 'gz'), 0, 0, tiled=True)  19.1 us
    ppermute x6, waiting for transfers between devices, toward_lower(): return lax.ppermute(x, axis, [(j, j - 1) for j in range(1, peers)])  13.9 us
    ppermute x6, starting transfers between devices, toward_lower(): return lax.ppermute(x, axis, [(j, j - 1) for j in range(1, peers)])  10.4 us
    pallas_call x2, Pallas kernels, h_step(): pl.pallas_call(h_kernel, grid=(nx // chunk,), in_specs=[field_spec(nx, ny...  9.66 us
    pallas_call x1, Pallas kernels, e_step(): pl.pallas_call(e_last_kernel, grid=(nx // chunk,), in_specs=in_specs + [f...  9.32 us
    pallas_call x1, Pallas kernels, e_step(): pl.pallas_call(e_kernel, grid=(nx // chunk,), in_specs=in_specs, out_spec...  5.17 us
    unnamed x26, local copies, waits for them, and re-layouts  2.67 us
  transfers between devices with their start and end apart: 12, of which 5 were waited for; matrix products, arithmetic and copies ran while one was open for 2% of the time, Pallas kernels for 0%

profile of v15, /device:TPU:1, one launch (start us, length us, event | category | flops | bytes accessed | tf_op | source)
XLA Modules:
  0.0 98.2 jit_solution(11872601242101197184)
XLA Ops:
  0.6 2.3 %shard_map.94 = (f32[2,1,16,1024]{3,2,1,0:T(8,128)}, f32[2,16,1,1024]{3,2,1,0:T(1,128)}, f32[2,2,1,128]{3,2,1,0:T(1,128)}) custom-call(f32[3,16,16,1024]{3,2,1,0:T(8,128)} %e_ref.3, f32[3,16,16,1024]{3,2,1,0:T(8,128)} %e_ref.3, f32[3,16,16,1024]{3,2,1,0:T(8,128)} %e_ref.3), custom_call_target="tpu_custom_call" | custom-call | tf_op jit(solution)/shard_map/pallas_call | solution.py:226
  3.0 1.3 %collective-permute-start = (f32[2,1,16,1024]{3,2,1,0:T(8,128)}, f32[2,1,16,1024]{3,2,1,0:T(8,128)S(1)}, u32[]{:S(2)}, u32[]{:S(2)}) collective-permute-start(f32[2,1,16,1024]{3,2,1,0:T(8,128)} %get-tuple-element.20), channel_id=1, source_target_pairs={{16,0},{32,16},{48,32},{64,48},{80,64},{96,80},{112,96},{17,1},{33... | collective-permute-start | bytes 393224 | tf_op jit(solution)/shard_map/ppermute | solution.py:19
  4.2 3.3 %collective-permute-start.1 = (f32[2,16,1,1024]{3,2,1,0:T(1,128)}, f32[2,16,1,1024]{3,2,1,0:T(1,128)S(1)}, u32[]{:S(2)}, u32[]{:S(2)}) collective-permute-start(f32[2,16,1,1024]{3,2,1,0:T(1,128)} %get-tuple-element.21), channel_id=1, source_target_pairs={{4,0},{8,4},{12,8},{5,1},{9,5},{13,9},{6,2},{10,6},{14,10},{7,3},{... | collective-permute-start | bytes 393224 | tf_op jit(solution)/shard_map/ppermute | solution.py:19
  7.5 1.3 %collective-permute-start.2 = (f32[2,2,1,128]{3,2,1,0:T(1,128)}, f32[2,2,1,128]{3,2,1,0:T(1,128)S(1)}, u32[]{:S(2)}, u32[]{:S(2)}) collective-permute-start(f32[2,2,1,128]{3,2,1,0:T(1,128)} %get-tuple-element.22), channel_id=1, source_target_pairs={{1,0},{2,1},{3,2},{5,4},{6,5},{7,6},{9,8},{10,9},{11,10},{13,12},{... | collective-permute-start | bytes 6152 | tf_op jit(solution)/shard_map/ppermute | solution.py:19
  8.8 3.4 %collective-permute-done.2.hz_ref = f32[2,2,1,128]{3,2,1,0:T(1,128)S(1)} collective-permute-done((f32[2,2,1,128]{3,2,1,0:T(1,128)}, f32[2,2,1,128]{3,2,1,0:T(1,128)S(1)}, u32[]{:S(2)}, u32[]{:S(2)}) %collective-permute-start.2) | collective-permute-done | bytes 2080 | tf_op jit(solution)/shard_map/ppermute | solution.py:19
  12.2 4.6 %collective-permute-done.1.hy_ref = f32[2,16,1,1024]{3,2,1,0:T(1,128)S(1)} collective-permute-done((f32[2,16,1,1024]{3,2,1,0:T(1,128)}, f32[2,16,1,1024]{3,2,1,0:T(1,128)S(1)}, u32[]{:S(2)}, u32[]{:S(2)}) %collective-permute-start.1) | collective-permute-done | bytes 131104 | tf_op jit(solution)/shard_map/ppermute | solution.py:19
  16.8 0.7 copy-done.6
  17.5 4.8 %shard_map.95 = (f32[3,16,16,1024]{3,2,1,0:T(8,128)}, f32[2,1,16,1024]{3,2,1,0:T(8,128)}, f32[2,16,1,1024]{3,2,1,0:T(1,128)}, f32[2,2,1,128]{3,2,1,0:T(1,128)}) custom-call(f32[3,16,16,1024]{3,2,1,0:T(8,128)} %e_ref.3, f32[3,16,16,1024]{3,2,1,0:T(8,128)} %e_ref.3, f32[3,16,16,1024]{3,2,1,0:T(8,128)} %h_ref.1, f32[2,1,16,1024]{3,2,1,0:T(8,128)} %copy-done.3, ...), custom_call_target="tpu_custom_call" | custom-call | tf_op jit(solution)/shard_map/pallas_call | solution.py:249
  22.3 1.3 %collective-permute-start.3 = (f32[2,1,16,1024]{3,2,1,0:T(8,128)}, f32[2,1,16,1024]{3,2,1,0:T(8,128)S(1)}, u32[]{:S(2)}, u32[]{:S(2)}) collective-permute-start(f32[2,1,16,1024]{3,2,1,0:T(8,128)} %get-tuple-element.24), channel_id=1, source_target_pairs={{0,16},{16,32},{32,48},{48,64},{64,80},{80,96},{96,112},{1,17},{17... | collective-permute-start | bytes 393224 | tf_op jit(solution)/shard_map/ppermute | solution.py:24
  23.6 5.9 %collective-permute-start.4 = (f32[2,16,1,1024]{3,2,1,0:T(1,128)}, f32[2,16,1,1024]{3,2,1,0:T(1,128)S(1)}, u32[]{:S(2)}, u32[]{:S(2)}) collective-permute-start(f32[2,16,1,1024]{3,2,1,0:T(1,128)} %get-tuple-element.25), channel_id=1, source_target_pairs={{0,4},{4,8},{8,12},{1,5},{5,9},{9,13},{2,6},{6,10},{10,14},{3,7},{... | collective-permute-start | bytes 393224 | tf_op jit(solution)/shard_map/ppermute | solution.py:24
  29.5 3.2 %collective-permute-start.5 = (f32[2,2,1,128]{3,2,1,0:T(1,128)}, f32[2,2,1,128]{3,2,1,0:T(1,128)S(1)}, u32[]{:S(2)}, u32[]{:S(2)}) collective-permute-start(f32[2,2,1,128]{3,2,1,0:T(1,128)} %get-tuple-element.26), channel_id=1, source_target_pairs={{0,1},{1,2},{2,3},{4,5},{5,6},{6,7},{8,9},{9,10},{10,11},{12,13},{... | collective-permute-start | bytes 6152 | tf_op jit(solution)/shard_map/ppermute | solution.py:24
  32.7 0.9 collective-permute-done.5.hz_ref
  33.6 0.6 copy-done.10
  34.2 0.1 copy-done.4
  34.3 5.2 %shard_map.96 = (f32[3,16,16,1024]{3,2,1,0:T(8,128)}, f32[2,1,16,1024]{3,2,1,0:T(8,128)}, f32[2,16,1,1024]{3,2,1,0:T(1,128)}, f32[2,2,1,128]{3,2,1,0:T(1,128)}) custom-call(f32[3,16,16,1024]{3,2,1,0:T(8,128)} %e_ref.3, f32[3,16,16,1024]{3,2,1,0:T(8,128)} %get-tuple-element.23.h_ref.hp_ref, f32[3,16,16,1024]{3,2,1,0:T(8,128)} %get-tuple-element.23.h_ref.hp_ref, ...), custom_call_target="tpu_custom_call" | custom-call | tf_op jit(solution)/shard_map/pallas_call | solution.py:282
  39.5 1.3 %collective-permute-start.6 = (f32[2,1,16,1024]{3,2,1,0:T(8,128)}, f32[2,1,16,1024]{3,2,1,0:T(8,128)S(1)}, u32[]{:S(2)}, u32[]{:S(2)}) collective-permute-start(f32[2,1,16,1024]{3,2,1,0:T(8,128)} %get-tuple-element.28), channel_id=1, source_target_pairs={{16,0},{32,16},{48,32},{64,48},{80,64},{96,80},{112,96},{17,1},{33... | collective-permute-start | bytes 393224 | tf_op jit(solution)/shard_map/ppermute | solution.py:19
  40.8 1.9 %collective-permute-start.7 = (f32[2,16,1,1024]{3,2,1,0:T(1,128)}, f32[2,16,1,1024]{3,2,1,0:T(1,128)S(1)}, u32[]{:S(2)}, u32[]{:S(2)}) collective-permute-start(f32[2,16,1,1024]{3,2,1,0:T(1,128)} %get-tuple-element.29), channel_id=1, source_target_pairs={{4,0},{8,4},{12,8},{5,1},{9,5},{13,9},{6,2},{10,6},{14,10},{7,3},{... | collective-permute-start | bytes 393224 | tf_op jit(solution)/shard_map/ppermute | solution.py:19
  42.7 1.3 %collective-permute-start.8 = (f32[2,2,1,128]{3,2,1,0:T(1,128)}, f32[2,2,1,128]{3,2,1,0:T(1,128)S(1)}, u32[]{:S(2)}, u32[]{:S(2)}) collective-permute-start(f32[2,2,1,128]{3,2,1,0:T(1,128)} %get-tuple-element.30), channel_id=1, source_target_pairs={{1,0},{2,1},{3,2},{5,4},{6,5},{7,6},{9,8},{10,9},{11,10},{13,12},{... | collective-permute-start | bytes 6152 | tf_op jit(solution)/shard_map/ppermute | solution.py:19
  44.0 0.2 copy.10
  44.2 3.2 %collective-permute-done.8.hz_ref = f32[2,2,1,128]{3,2,1,0:T(1,128)S(1)} collective-permute-done((f32[2,2,1,128]{3,2,1,0:T(1,128)}, f32[2,2,1,128]{3,2,1,0:T(1,128)S(1)}, u32[]{:S(2)}, u32[]{:S(2)}) %collective-permute-start.8) | collective-permute-done | bytes 2080 | tf_op jit(solution)/shard_map/ppermute | solution.py:19
  47.5 2.7 %collective-permute-done.7.hy_ref = f32[2,16,1,1024]{3,2,1,0:T(1,128)S(1)} collective-permute-done((f32[2,16,1,1024]{3,2,1,0:T(1,128)}, f32[2,16,1,1024]{3,2,1,0:T(1,128)S(1)}, u32[]{:S(2)}, u32[]{:S(2)}) %collective-permute-start.7) | collective-permute-done | bytes 131104 | tf_op jit(solution)/shard_map/ppermute | solution.py:19
  50.2 0.6 copy-done.5
  50.8 4.8 %shard_map.97 = (f32[3,16,16,1024]{3,2,1,0:T(8,128)}, f32[2,1,16,1024]{3,2,1,0:T(8,128)}, f32[2,16,1,1024]{3,2,1,0:T(1,128)}, f32[2,2,1,128]{3,2,1,0:T(1,128)}) custom-call(f32[3,16,16,1024]{3,2,1,0:T(8,128)} %get-tuple-element.27.e_ref.en_ref, f32[3,16,16,1024]{3,2,1,0:T(8,128)} %get-tuple-element.27.e_ref.en_ref, ...), custom_call_target="tpu_custom_call" | custom-call | tf_op jit(solution)/shard_map/pallas_call | solution.py:249
  55.6 3.4 %collective-permute-start.10 = (f32[2,16,1,1024]{3,2,1,0:T(1,128)}, f32[2,16,1,1024]{3,2,1,0:T(1,128)S(1)}, u32[]{:S(2)}, u32[]{:S(2)}) collective-permute-start(f32[2,16,1,1024]{3,2,1,0:T(1,128)} %get-tuple-element.33), channel_id=1, source_target_pairs={{0,4},{4,8},{8,12},{1,5},{5,9},{9,13},{2,6},{6,10},{10,14},{3,7},{... | collective-permute-start | bytes 393224 | tf_op jit(solution)/shard_map/ppermute | solution.py:24
  59.1 4.2 %collective-permute-start.9 = (f32[2,1,16,1024]{3,2,1,0:T(8,128)}, f32[2,1,16,1024]{3,2,1,0:T(8,128)S(1)}, u32[]{:S(2)}, u32[]{:S(2)}) collective-permute-start(f32[2,1,16,1024]{3,2,1,0:T(8,128)} %get-tuple-element.32), channel_id=1, source_target_pairs={{0,16},{16,32},{32,48},{48,64},{64,80},{80,96},{96,112},{1,17},{17... | collective-permute-start | bytes 393224 | tf_op jit(solution)/shard_map/ppermute | solution.py:24
  63.3 3.6 %collective-permute-start.11 = (f32[2,2,1,128]{3,2,1,0:T(1,128)}, f32[2,2,1,128]{3,2,1,0:T(1,128)S(1)}, u32[]{:S(2)}, u32[]{:S(2)}) collective-permute-start(f32[2,2,1,128]{3,2,1,0:T(1,128)} %get-tuple-element.34), channel_id=1, source_target_pairs={{0,1},{1,2},{2,3},{4,5},{5,6},{6,7},{8,9},{9,10},{10,11},{12,13},{... | collective-permute-start | bytes 6152 | tf_op jit(solution)/shard_map/ppermute | solution.py:24
  66.9 1.4 %add_select_fusion = (s32[1024,1]{1,0:T(8,128)}, s32[1024,1]{1,0:T(8,128)}) fusion(s32[1024,1]{1,0:T(8,128)S(1)} %copy.10), kind=kLoop, calls=%fused_computation | loop fusion | flops 19456 | bytes 12288 | tf_op jit(solution)/shard_map/jit(floor_divide)/jit(_where)/select_n | solution.py:292
  68.3 0.5 copy-done.9
  68.9 0.1 copy-done.2
  69.0 9.3 %shard_map.98 = (f32[3,16,16,1024]{3,2,1,0:T(8,128)}, f32[128,1,256]{2,1,0:T(1,128)}) custom-call(f32[3,16,16,1024]{3,2,1,0:T(8,128)} %get-tuple-element.27.e_ref.en_ref, f32[3,16,16,1024]{3,2,1,0:T(8,128)} %get-tuple-element.18.h_ref.hp_ref, f32[3,16,16,1024]{3,2,1,0:T(8,128)} %get-tuple-element.18.h_ref.hp_ref, f32[16,16,1024]{2,1,0:T(8,128)} %inv_ref.3, ...), custom_call_target="tpu_custom_call" | custom-call | tf_op jit(solution)/shard_map/pallas_call | solution.py:293
  78.3 19.1 %all_to_all.5 = f32[128,1,256]{2,1,0:T(1,128)S(1)} all-to-all(f32[128,1,256]{2,1,0:T(1,128)} %get-tuple-element.36), channel_id=1, replica_groups=mesh['gx'=8,'gy'=4,'gz'=4] {'gx','gy','gz'}, dimensions={0} | all-to-all | bytes 262144 | tf_op jit(solution)/shard_map/all_to_all | solution.py:325
  97.5 0.7 reduce_sum.9
  (27 shorter events, 0.1 us)
Async XLA Ops:
  3.0 9.3 %collective-permute-start = (f32[2,1,16,1024]{3,2,1,0:T(8,128)}, f32[2,1,16,1024]{3,2,1,0:T(8,128)S(1)}, u32[]{:S(2)}, u32[]{:S(2)}) collective-permute-start(f32[2,1,16,1024]{3,2,1,0:T(8,128)} %get-tuple-element.20), channel_id=1, source_target_pairs={{16,0},{32,16},{48,32},{64,48},{80,64},{96,80},{112,96},{17,1},{33... | collective-permute-start | bytes 393224 | tf_op jit(solution)/shard_map/ppermute | solution.py:19
  4.2 12.5 %collective-permute-start.1 = (f32[2,16,1,1024]{3,2,1,0:T(1,128)}, f32[2,16,1,1024]{3,2,1,0:T(1,128)S(1)}, u32[]{:S(2)}, u32[]{:S(2)}) collective-permute-start(f32[2,16,1,1024]{3,2,1,0:T(1,128)} %get-tuple-element.21), channel_id=1, source_target_pairs={{4,0},{8,4},{12,8},{5,1},{9,5},{13,9},{6,2},{10,6},{14,10},{7,3},{... | collective-permute-start | bytes 393224 | tf_op jit(solution)/shard_map/ppermute | solution.py:19
  7.5 4.7 %collective-permute-start.2 = (f32[2,2,1,128]{3,2,1,0:T(1,128)}, f32[2,2,1,128]{3,2,1,0:T(1,128)S(1)}, u32[]{:S(2)}, u32[]{:S(2)}) collective-permute-start(f32[2,2,1,128]{3,2,1,0:T(1,128)} %get-tuple-element.22), channel_id=1, source_target_pairs={{1,0},{2,1},{3,2},{5,4},{6,5},{7,6},{9,8},{10,9},{11,10},{13,12},{... | collective-permute-start | bytes 6152 | tf_op jit(solution)/shard_map/ppermute | solution.py:19
  12.2 4.6 %copy-start.12 = (f32[2,2,1,128]{3,2,1,0:T(1,128)}, f32[2,2,1,128]{3,2,1,0:T(1,128)S(1)}, u32[]{:S(2)}) copy-start(f32[2,2,1,128]{3,2,1,0:T(1,128)S(1)} %collective-permute-done.2.hz_ref) | copy-start | bytes 6148
  12.2 4.6 %copy-start.3 = (f32[2,1,16,1024]{3,2,1,0:T(8,128)}, f32[2,1,16,1024]{3,2,1,0:T(8,128)S(1)}, u32[]{:S(2)}) copy-start(f32[2,1,16,1024]{3,2,1,0:T(8,128)S(1)} %collective-permute-done.hx_ref) | copy-start | bytes 393220
  16.8 0.7 copy-start.6
  22.3 11.3 %collective-permute-start.3 = (f32[2,1,16,1024]{3,2,1,0:T(8,128)}, f32[2,1,16,1024]{3,2,1,0:T(8,128)S(1)}, u32[]{:S(2)}, u32[]{:S(2)}) collective-permute-start(f32[2,1,16,1024]{3,2,1,0:T(8,128)} %get-tuple-element.24), channel_id=1, source_target_pairs={{0,16},{16,32},{32,48},{48,64},{64,80},{80,96},{96,112},{1,17},{17... | collective-permute-start | bytes 393224 | tf_op jit(solution)/shard_map/ppermute | solution.py:24
  23.6 10.0 %collective-permute-start.4 = (f32[2,16,1,1024]{3,2,1,0:T(1,128)}, f32[2,16,1,1024]{3,2,1,0:T(1,128)S(1)}, u32[]{:S(2)}, u32[]{:S(2)}) collective-permute-start(f32[2,16,1,1024]{3,2,1,0:T(1,128)} %get-tuple-element.25), channel_id=1, source_target_pairs={{0,4},{4,8},{8,12},{1,5},{5,9},{9,13},{2,6},{6,10},{10,14},{3,7},{... | collective-permute-start | bytes 393224 | tf_op jit(solution)/shard_map/ppermute | solution.py:24
  29.5 4.1 %collective-permute-start.5 = (f32[2,2,1,128]{3,2,1,0:T(1,128)}, f32[2,2,1,128]{3,2,1,0:T(1,128)S(1)}, u32[]{:S(2)}, u32[]{:S(2)}) collective-permute-start(f32[2,2,1,128]{3,2,1,0:T(1,128)} %get-tuple-element.26), channel_id=1, source_target_pairs={{0,1},{1,2},{2,3},{4,5},{5,6},{6,7},{8,9},{9,10},{10,11},{12,13},{... | collective-permute-start | bytes 6152 | tf_op jit(solution)/shard_map/ppermute | solution.py:24
  33.6 0.6 copy-start.10
  33.6 0.7 copy-start.4
  33.6 0.7 copy-start.7
  34.3 9.7 %copy-start.8 = (s32[1,1,1,1024]{3,2,1,0:T(1,128)S(1)}, s32[1,1,1,1024]{3,2,1,0:T(1,128)}, u32[]{:S(2)}) copy-start(s32[1,1,1,1024]{3,2,1,0:T(1,128)} %param.11) | copy-start | bytes 12292
  39.5 8.0 %collective-permute-start.6 = (f32[2,1,16,1024]{3,2,1,0:T(8,128)}, f32[2,1,16,1024]{3,2,1,0:T(8,128)S(1)}, u32[]{:S(2)}, u32[]{:S(2)}) collective-permute-start(f32[2,1,16,1024]{3,2,1,0:T(8,128)} %get-tuple-element.28), channel_id=1, source_target_pairs={{16,0},{32,16},{48,32},{64,48},{80,64},{96,80},{112,96},{17,1},{33... | collective-permute-start | bytes 393224 | tf_op jit(solution)/shard_map/ppermute | solution.py:19
  40.8 9.4 %collective-permute-start.7 = (f32[2,16,1,1024]{3,2,1,0:T(1,128)}, f32[2,16,1,1024]{3,2,1,0:T(1,128)S(1)}, u32[]{:S(2)}, u32[]{:S(2)}) collective-permute-start(f32[2,16,1,1024]{3,2,1,0:T(1,128)} %get-tuple-element.29), channel_id=1, source_target_pairs={{4,0},{8,4},{12,8},{5,1},{9,5},{13,9},{6,2},{10,6},{14,10},{7,3},{... | collective-permute-start | bytes 393224 | tf_op jit(solution)/shard_map/ppermute | solution.py:19
  42.7 4.8 %collective-permute-start.8 = (f32[2,2,1,128]{3,2,1,0:T(1,128)}, f32[2,2,1,128]{3,2,1,0:T(1,128)S(1)}, u32[]{:S(2)}, u32[]{:S(2)}) collective-permute-start(f32[2,2,1,128]{3,2,1,0:T(1,128)} %get-tuple-element.30), channel_id=1, source_target_pairs={{1,0},{2,1},{3,2},{5,4},{6,5},{7,6},{9,8},{10,9},{11,10},{13,12},{... | collective-permute-start | bytes 6152 | tf_op jit(solution)/shard_map/ppermute | solution.py:19
  47.5 2.7 %copy-start.11 = (f32[2,2,1,128]{3,2,1,0:T(1,128)}, f32[2,2,1,128]{3,2,1,0:T(1,128)S(1)}, u32[]{:S(2)}) copy-start(f32[2,2,1,128]{3,2,1,0:T(1,128)S(1)} %collective-permute-done.8.hz_ref) | copy-start | bytes 6148
  47.5 2.7 %copy-start.1 = (f32[2,1,16,1024]{3,2,1,0:T(8,128)}, f32[2,1,16,1024]{3,2,1,0:T(8,128)S(1)}, u32[]{:S(2)}) copy-start(f32[2,1,16,1024]{3,2,1,0:T(8,128)S(1)} %collective-permute-done.6.hx_ref) | copy-start | bytes 393220
  50.2 0.6 copy-start.5
  55.6 12.6 %collective-permute-start.10 = (f32[2,16,1,1024]{3,2,1,0:T(1,128)}, f32[2,16,1,1024]{3,2,1,0:T(1,128)S(1)}, u32[]{:S(2)}, u32[]{:S(2)}) collective-permute-start(f32[2,16,1,1024]{3,2,1,0:T(1,128)} %get-tuple-element.33), channel_id=1, source_target_pairs={{0,4},{4,8},{8,12},{1,5},{5,9},{9,13},{2,6},{6,10},{10,14},{3,7},{... | collective-permute-start | bytes 393224 | tf_op jit(solution)/shard_map/ppermute | solution.py:24
  59.1 9.2 %collective-permute-start.9 = (f32[2,1,16,1024]{3,2,1,0:T(8,128)}, f32[2,1,16,1024]{3,2,1,0:T(8,128)S(1)}, u32[]{:S(2)}, u32[]{:S(2)}) collective-permute-start(f32[2,1,16,1024]{3,2,1,0:T(8,128)} %get-tuple-element.32), channel_id=1, source_target_pairs={{0,16},{16,32},{32,48},{48,64},{64,80},{80,96},{96,112},{1,17},{17... | collective-permute-start | bytes 393224 | tf_op jit(solution)/shard_map/ppermute | solution.py:24
  63.3 5.0 %collective-permute-start.11 = (f32[2,2,1,128]{3,2,1,0:T(1,128)}, f32[2,2,1,128]{3,2,1,0:T(1,128)S(1)}, u32[]{:S(2)}, u32[]{:S(2)}) collective-permute-start(f32[2,2,1,128]{3,2,1,0:T(1,128)} %get-tuple-element.34), channel_id=1, source_target_pairs={{0,1},{1,2},{2,3},{4,5},{5,6},{6,7},{8,9},{9,10},{10,11},{12,13},{... | collective-permute-start | bytes 6152 | tf_op jit(solution)/shard_map/ppermute | solution.py:24
  68.3 0.6 copy-start.9
  68.3 0.6 copy-start
  68.3 0.7 copy-start.2

commit v16 on v12

--- a/solution.py
+++ b/solution.py
@@ -204,11 +204,11 @@
     ]
 
 
-def faces_kernel(slab_ref, rows_ref, lanes_ref, fx_ref, fy_ref, fz_ref):
-    fx_ref[0] = slab_ref[1]
-    fx_ref[1] = slab_ref[2]
-    fy_ref[0] = rows_ref[0, :, 0:1, :]
-    fy_ref[1] = rows_ref[2, :, 0:1, :]
+def faces_kernel(slab_y_ref, slab_z_ref, rows_x_ref, rows_z_ref, lanes_ref, fx_ref, fy_ref, fz_ref):
+    fx_ref[0] = slab_y_ref[0]
+    fx_ref[1] = slab_z_ref[0]
+    fy_ref[0] = rows_x_ref[0, :, 0:1, :]
+    fy_ref[1] = rows_z_ref[0, :, 0:1, :]
     nx = lanes_ref.shape[1]
     for i in range(nx // CHUNK):
         part = slice(i * CHUNK, (i + 1) * CHUNK)
@@ -222,9 +222,11 @@
         faces_kernel,
         grid=(1,),
         in_specs=[
-            pl.BlockSpec((3, 1, ny, nz), lambda i: (0, 0, 0, 0)),
-            pl.BlockSpec((3, nx, 8, nz), lambda i: (0, 0, 0, 0)),
-            pl.BlockSpec((3, nx, ny, 128), lambda i: (0, 0, 0, 0)),
+            pl.BlockSpec((1, 1, ny, nz), lambda i: (1, 0, 0, 0)),
+            pl.BlockSpec((1, 1, ny, nz), lambda i: (2, 0, 0, 0)),
+            pl.BlockSpec((1, nx, 8, nz), lambda i: (0, 0, 0, 0)),
+            pl.BlockSpec((1, nx, 8, nz), lambda i: (2, 0, 0, 0)),
+            pl.BlockSpec((2, nx, ny, 128), lambda i: (0, 0, 0, 0)),
         ],
         out_specs=[
             pl.BlockSpec((2, 1, ny, nz), lambda i: (0, 0, 0, 0)),
@@ -232,7 +234,7 @@
             pl.BlockSpec((2, nx // CHUNK, 1, CHUNK * ny), lambda i: (0, 0, 0, 0)),
         ],
         out_shape=face_shapes(nx, ny, nz, e.dtype),
-    )(e, e, e)
+    )(e, e, e, e, e)
 
 
 def h_step(e, h, faces):

time: 97.1 us -> 96.9 us (level)
  no operation moved by 1% of the time
where the time goes in v16:
time: 96.9 us; the launch traced here: 96.4 us
  starting transfers between devices  31.9 us (33%)
  Pallas kernels  24.7 us (25%)
  blocking collectives  19.6 us (20%)
  waiting for transfers between devices  14.8 us (15%)
  local copies, waits for them, and re-layouts  2.71 us (3%)
  other arithmetic  1.93 us (2%)
    ppermute x6, starting transfers between devices, toward_upper(): return lax.ppermute(x, axis, [(j, j + 1) for j in range(peers - 1)])  21.5 us
    all_to_all x1, blocking collectives, body(): received = lax.all_to_all(per_owner, ('gx', 'gy', 'gz'), 0, 0, tiled=True)  19.6 us
    ppermute x6, waiting for transfers between devices, toward_lower(): return lax.ppermute(x, axis, [(j, j - 1) for j in range(1, peers)])  13.5 us
    ppermute x6, starting transfers between devices, toward_lower(): return lax.ppermute(x, axis, [(j, j - 1) for j in range(1, peers)])  10.4 us
    pallas_call x2, Pallas kernels, h_step(): pl.pallas_call(h_kernel, grid=(nx // chunk,), in_specs=[field_spec(nx, ny...  9.67 us
    pallas_call x1, Pallas kernels, e_step(): pl.pallas_call(e_last_kernel, grid=(nx // chunk,), in_specs=in_specs + [f...  7.78 us
    pallas_call x1, Pallas kernels, e_step(): pl.pallas_call(e_kernel, grid=(nx // chunk,), in_specs=in_specs, out_spec...  5.17 us
    unnamed x26, local copies, waits for them, and re-layouts  2.71 us
  transfers between devices with their start and end apart: 12, of which 6 were waited for; matrix products, arithmetic and copies ran while one was open for 1% of the time, Pallas kernels for 0%

profile of v16, /device:TPU:1, one launch (start us, length us, event | category | flops | bytes accessed | tf_op | source)
XLA Modules:
  0.0 96.4 jit_solution(1759399971807936764)
XLA Ops:
  0.6 2.1 %shard_map.94 = (f32[2,1,16,1024]{3,2,1,0:T(8,128)}, f32[2,16,1,1024]{3,2,1,0:T(1,128)}, f32[2,2,1,128]{3,2,1,0:T(1,128)}) custom-call(f32[3,16,16,1024]{3,2,1,0:T(8,128)} %e_ref.3, f32[3,16,16,1024]{3,2,1,0:T(8,128)} %e_ref.3, f32[3,16,16,1024]{3,2,1,0:T(8,128)} %e_ref.3, f32[3,16,16,1024]{3,2,1,0:T(8,128)} %e_ref.3, f32[3,16,16,1024]{3,2,1,0:T(8,128)} %e_ref.3), custom_call_target="tpu_custom_call" | custom-call | tf_op jit(solution)/shard_map/pallas_call | solution.py:221
  2.7 1.3 %collective-permute-start = (f32[2,1,16,1024]{3,2,1,0:T(8,128)}, f32[2,1,16,1024]{3,2,1,0:T(8,128)S(1)}, u32[]{:S(2)}, u32[]{:S(2)}) collective-permute-start(f32[2,1,16,1024]{3,2,1,0:T(8,128)} %get-tuple-element.20), channel_id=1, source_target_pairs={{16,0},{32,16},{48,32},{64,48},{80,64},{96,80},{112,96},{17,1},{33... | collective-permute-start | bytes 393224 | tf_op jit(solution)/shard_map/ppermute | solution.py:19
  4.0 3.3 %collective-permute-start.1 = (f32[2,16,1,1024]{3,2,1,0:T(1,128)}, f32[2,16,1,1024]{3,2,1,0:T(1,128)S(1)}, u32[]{:S(2)}, u32[]{:S(2)}) collective-permute-start(f32[2,16,1,1024]{3,2,1,0:T(1,128)} %get-tuple-element.21), channel_id=1, source_target_pairs={{4,0},{8,4},{12,8},{5,1},{9,5},{13,9},{6,2},{10,6},{14,10},{7,3},{... | collective-permute-start | bytes 393224 | tf_op jit(solution)/shard_map/ppermute | solution.py:19
  7.3 1.3 %collective-permute-start.2 = (f32[2,2,1,128]{3,2,1,0:T(1,128)}, f32[2,2,1,128]{3,2,1,0:T(1,128)S(1)}, u32[]{:S(2)}, u32[]{:S(2)}) collective-permute-start(f32[2,2,1,128]{3,2,1,0:T(1,128)} %get-tuple-element.22), channel_id=1, source_target_pairs={{1,0},{2,1},{3,2},{5,4},{6,5},{7,6},{9,8},{10,9},{11,10},{13,12},{... | collective-permute-start | bytes 6152 | tf_op jit(solution)/shard_map/ppermute | solution.py:19
  8.6 3.4 %collective-permute-done.2.hz_ref = f32[2,2,1,128]{3,2,1,0:T(1,128)S(1)} collective-permute-done((f32[2,2,1,128]{3,2,1,0:T(1,128)}, f32[2,2,1,128]{3,2,1,0:T(1,128)S(1)}, u32[]{:S(2)}, u32[]{:S(2)}) %collective-permute-start.2) | collective-permute-done | bytes 2080 | tf_op jit(solution)/shard_map/ppermute | solution.py:19
  12.0 4.6 %collective-permute-done.1.hy_ref = f32[2,16,1,1024]{3,2,1,0:T(1,128)S(1)} collective-permute-done((f32[2,16,1,1024]{3,2,1,0:T(1,128)}, f32[2,16,1,1024]{3,2,1,0:T(1,128)S(1)}, u32[]{:S(2)}, u32[]{:S(2)}) %collective-permute-start.1) | collective-permute-done | bytes 131104 | tf_op jit(solution)/shard_map/ppermute | solution.py:19
  16.5 0.7 copy-done.6
  17.2 4.8 %shard_map.95 = (f32[3,16,16,1024]{3,2,1,0:T(8,128)}, f32[2,1,16,1024]{3,2,1,0:T(8,128)}, f32[2,16,1,1024]{3,2,1,0:T(1,128)}, f32[2,2,1,128]{3,2,1,0:T(1,128)}) custom-call(f32[3,16,16,1024]{3,2,1,0:T(8,128)} %e_ref.3, f32[3,16,16,1024]{3,2,1,0:T(8,128)} %e_ref.3, f32[3,16,16,1024]{3,2,1,0:T(8,128)} %h_ref.1, f32[2,1,16,1024]{3,2,1,0:T(8,128)} %copy-done.3, ...), custom_call_target="tpu_custom_call" | custom-call | tf_op jit(solution)/shard_map/pallas_call | solution.py:246
  22.0 1.3 %collective-permute-start.3 = (f32[2,1,16,1024]{3,2,1,0:T(8,128)}, f32[2,1,16,1024]{3,2,1,0:T(8,128)S(1)}, u32[]{:S(2)}, u32[]{:S(2)}) collective-permute-start(f32[2,1,16,1024]{3,2,1,0:T(8,128)} %get-tuple-element.24), channel_id=1, source_target_pairs={{0,16},{16,32},{32,48},{48,64},{64,80},{80,96},{96,112},{1,17},{17... | collective-permute-start | bytes 393224 | tf_op jit(solution)/shard_map/ppermute | solution.py:24
  23.3 5.9 %collective-permute-start.4 = (f32[2,16,1,1024]{3,2,1,0:T(1,128)}, f32[2,16,1,1024]{3,2,1,0:T(1,128)S(1)}, u32[]{:S(2)}, u32[]{:S(2)}) collective-permute-start(f32[2,16,1,1024]{3,2,1,0:T(1,128)} %get-tuple-element.25), channel_id=1, source_target_pairs={{0,4},{4,8},{8,12},{1,5},{5,9},{9,13},{2,6},{6,10},{10,14},{3,7},{... | collective-permute-start | bytes 393224 | tf_op jit(solution)/shard_map/ppermute | solution.py:24
  29.2 3.2 %collective-permute-start.5 = (f32[2,2,1,128]{3,2,1,0:T(1,128)}, f32[2,2,1,128]{3,2,1,0:T(1,128)S(1)}, u32[]{:S(2)}, u32[]{:S(2)}) collective-permute-start(f32[2,2,1,128]{3,2,1,0:T(1,128)} %get-tuple-element.26), channel_id=1, source_target_pairs={{0,1},{1,2},{2,3},{4,5},{5,6},{6,7},{8,9},{9,10},{10,11},{12,13},{... | collective-permute-start | bytes 6152 | tf_op jit(solution)/shard_map/ppermute | solution.py:24
  32.4 0.9 collective-permute-done.5.hz_ref
  33.4 0.6 copy-done.10
  34.0 5.2 %shard_map.96 = (f32[3,16,16,1024]{3,2,1,0:T(8,128)}, f32[2,1,16,1024]{3,2,1,0:T(8,128)}, f32[2,16,1,1024]{3,2,1,0:T(1,128)}, f32[2,2,1,128]{3,2,1,0:T(1,128)}) custom-call(f32[3,16,16,1024]{3,2,1,0:T(8,128)} %e_ref.3, f32[3,16,16,1024]{3,2,1,0:T(8,128)} %get-tuple-element.23.h_ref.hp_ref, f32[3,16,16,1024]{3,2,1,0:T(8,128)} %get-tuple-element.23.h_ref.hp_ref, ...), custom_call_target="tpu_custom_call" | custom-call | tf_op jit(solution)/shard_map/pallas_call | solution.py:279
  39.2 1.3 %collective-permute-start.6 = (f32[2,1,16,1024]{3,2,1,0:T(8,128)}, f32[2,1,16,1024]{3,2,1,0:T(8,128)S(1)}, u32[]{:S(2)}, u32[]{:S(2)}) collective-permute-start(f32[2,1,16,1024]{3,2,1,0:T(8,128)} %get-tuple-element.28), channel_id=1, source_target_pairs={{16,0},{32,16},{48,32},{64,48},{80,64},{96,80},{112,96},{17,1},{33... | collective-permute-start | bytes 393224 | tf_op jit(solution)/shard_map/ppermute | solution.py:19
  40.5 1.9 %collective-permute-start.7 = (f32[2,16,1,1024]{3,2,1,0:T(1,128)}, f32[2,16,1,1024]{3,2,1,0:T(1,128)S(1)}, u32[]{:S(2)}, u32[]{:S(2)}) collective-permute-start(f32[2,16,1,1024]{3,2,1,0:T(1,128)} %get-tuple-element.29), channel_id=1, source_target_pairs={{4,0},{8,4},{12,8},{5,1},{9,5},{13,9},{6,2},{10,6},{14,10},{7,3},{... | collective-permute-start | bytes 393224 | tf_op jit(solution)/shard_map/ppermute | solution.py:19
  42.4 1.3 %collective-permute-start.8 = (f32[2,2,1,128]{3,2,1,0:T(1,128)}, f32[2,2,1,128]{3,2,1,0:T(1,128)S(1)}, u32[]{:S(2)}, u32[]{:S(2)}) collective-permute-start(f32[2,2,1,128]{3,2,1,0:T(1,128)} %get-tuple-element.30), channel_id=1, source_target_pairs={{1,0},{2,1},{3,2},{5,4},{6,5},{7,6},{9,8},{10,9},{11,10},{13,12},{... | collective-permute-start | bytes 6152 | tf_op jit(solution)/shard_map/ppermute | solution.py:19
  43.8 0.6 and_select_fusion
  44.4 2.9 %collective-permute-done.8.hz_ref = f32[2,2,1,128]{3,2,1,0:T(1,128)S(1)} collective-permute-done((f32[2,2,1,128]{3,2,1,0:T(1,128)}, f32[2,2,1,128]{3,2,1,0:T(1,128)S(1)}, u32[]{:S(2)}, u32[]{:S(2)}) %collective-permute-start.8) | collective-permute-done | bytes 2080 | tf_op jit(solution)/shard_map/ppermute | solution.py:19
  47.2 2.7 %collective-permute-done.7.hy_ref = f32[2,16,1,1024]{3,2,1,0:T(1,128)S(1)} collective-permute-done((f32[2,16,1,1024]{3,2,1,0:T(1,128)}, f32[2,16,1,1024]{3,2,1,0:T(1,128)S(1)}, u32[]{:S(2)}, u32[]{:S(2)}) %collective-permute-start.7) | collective-permute-done | bytes 131104 | tf_op jit(solution)/shard_map/ppermute | solution.py:19
  49.9 0.7 copy-done.2
  50.6 4.8 %shard_map.97 = (f32[3,16,16,1024]{3,2,1,0:T(8,128)}, f32[2,1,16,1024]{3,2,1,0:T(8,128)}, f32[2,16,1,1024]{3,2,1,0:T(1,128)}, f32[2,2,1,128]{3,2,1,0:T(1,128)}) custom-call(f32[3,16,16,1024]{3,2,1,0:T(8,128)} %get-tuple-element.27.e_ref.en_ref, f32[3,16,16,1024]{3,2,1,0:T(8,128)} %get-tuple-element.27.e_ref.en_ref, ...), custom_call_target="tpu_custom_call" | custom-call | tf_op jit(solution)/shard_map/pallas_call | solution.py:246
  55.4 3.4 %collective-permute-start.10 = (f32[2,16,1,1024]{3,2,1,0:T(1,128)}, f32[2,16,1,1024]{3,2,1,0:T(1,128)S(1)}, u32[]{:S(2)}, u32[]{:S(2)}) collective-permute-start(f32[2,16,1,1024]{3,2,1,0:T(1,128)} %get-tuple-element.33), channel_id=1, source_target_pairs={{0,4},{4,8},{8,12},{1,5},{5,9},{9,13},{2,6},{6,10},{10,14},{3,7},{... | collective-permute-start | bytes 393224 | tf_op jit(solution)/shard_map/ppermute | solution.py:24
  58.8 4.2 %collective-permute-start.9 = (f32[2,1,16,1024]{3,2,1,0:T(8,128)}, f32[2,1,16,1024]{3,2,1,0:T(8,128)S(1)}, u32[]{:S(2)}, u32[]{:S(2)}) collective-permute-start(f32[2,1,16,1024]{3,2,1,0:T(8,128)} %get-tuple-element.32), channel_id=1, source_target_pairs={{0,16},{16,32},{32,48},{48,64},{64,80},{80,96},{96,112},{1,17},{17... | collective-permute-start | bytes 393224 | tf_op jit(solution)/shard_map/ppermute | solution.py:24
  63.0 3.6 %collective-permute-start.11 = (f32[2,2,1,128]{3,2,1,0:T(1,128)}, f32[2,2,1,128]{3,2,1,0:T(1,128)S(1)}, u32[]{:S(2)}, u32[]{:S(2)}) collective-permute-start(f32[2,2,1,128]{3,2,1,0:T(1,128)} %get-tuple-element.34), channel_id=1, source_target_pairs={{0,1},{1,2},{2,3},{4,5},{5,6},{6,7},{8,9},{9,10},{10,11},{12,13},{... | collective-permute-start | bytes 6152 | tf_op jit(solution)/shard_map/ppermute | solution.py:24
  66.6 0.6 and_select_fusion.1.zrow_ref
  67.2 0.3 collective-permute-done.11.hz_ref
  67.6 0.6 copy-done.9
  68.1 0.1 copy-done.1
  68.3 7.8 %shard_map.98 = (f32[3,16,16,1024]{3,2,1,0:T(8,128)}, f32[128,1,256]{2,1,0:T(1,128)}) custom-call(f32[3,16,16,1024]{3,2,1,0:T(8,128)} %get-tuple-element.27.e_ref.en_ref, f32[3,16,16,1024]{3,2,1,0:T(8,128)} %get-tuple-element.18.h_ref.hp_ref, f32[3,16,16,1024]{3,2,1,0:T(8,128)} %get-tuple-element.18.h_ref.hp_ref, f32[16,16,1024]{2,1,0:T(8,128)} %inv_ref.3, ...), custom_call_target="tpu_custom_call" | custom-call | tf_op jit(solution)/shard_map/pallas_call | solution.py:290
  76.1 19.6 %all_to_all.5 = f32[128,1,256]{2,1,0:T(1,128)S(1)} all-to-all(f32[128,1,256]{2,1,0:T(1,128)} %get-tuple-element.36), channel_id=1, replica_groups=mesh['gx'=8,'gy'=4,'gz'=4] {'gx','gy','gz'}, dimensions={0} | all-to-all | bytes 262144 | tf_op jit(solution)/shard_map/all_to_all | solution.py:322
  95.7 0.7 reduce_sum.9
  (27 shorter events, 0.2 us)
Async XLA Ops:
  2.7 9.3 %collective-permute-start = (f32[2,1,16,1024]{3,2,1,0:T(8,128)}, f32[2,1,16,1024]{3,2,1,0:T(8,128)S(1)}, u32[]{:S(2)}, u32[]{:S(2)}) collective-permute-start(f32[2,1,16,1024]{3,2,1,0:T(8,128)} %get-tuple-element.20), channel_id=1, source_target_pairs={{16,0},{32,16},{48,32},{64,48},{80,64},{96,80},{112,96},{17,1},{33... | collective-permute-start | bytes 393224 | tf_op jit(solution)/shard_map/ppermute | solution.py:19
  4.0 12.5 %collective-permute-start.1 = (f32[2,16,1,1024]{3,2,1,0:T(1,128)}, f32[2,16,1,1024]{3,2,1,0:T(1,128)S(1)}, u32[]{:S(2)}, u32[]{:S(2)}) collective-permute-start(f32[2,16,1,1024]{3,2,1,0:T(1,128)} %get-tuple-element.21), channel_id=1, source_target_pairs={{4,0},{8,4},{12,8},{5,1},{9,5},{13,9},{6,2},{10,6},{14,10},{7,3},{... | collective-permute-start | bytes 393224 | tf_op jit(solution)/shard_map/ppermute | solution.py:19
  7.3 4.7 %collective-permute-start.2 = (f32[2,2,1,128]{3,2,1,0:T(1,128)}, f32[2,2,1,128]{3,2,1,0:T(1,128)S(1)}, u32[]{:S(2)}, u32[]{:S(2)}) collective-permute-start(f32[2,2,1,128]{3,2,1,0:T(1,128)} %get-tuple-element.22), channel_id=1, source_target_pairs={{1,0},{2,1},{3,2},{5,4},{6,5},{7,6},{9,8},{10,9},{11,10},{13,12},{... | collective-permute-start | bytes 6152 | tf_op jit(solution)/shard_map/ppermute | solution.py:19
  12.0 4.6 %copy-start.12 = (f32[2,2,1,128]{3,2,1,0:T(1,128)}, f32[2,2,1,128]{3,2,1,0:T(1,128)S(1)}, u32[]{:S(2)}) copy-start(f32[2,2,1,128]{3,2,1,0:T(1,128)S(1)} %collective-permute-done.2.hz_ref) | copy-start | bytes 6148
  12.0 4.6 %copy-start.3 = (f32[2,1,16,1024]{3,2,1,0:T(8,128)}, f32[2,1,16,1024]{3,2,1,0:T(8,128)S(1)}, u32[]{:S(2)}) copy-start(f32[2,1,16,1024]{3,2,1,0:T(8,128)S(1)} %collective-permute-done.hx_ref) | copy-start | bytes 393220
  16.5 0.7 copy-start.6
  22.0 11.3 %collective-permute-start.3 = (f32[2,1,16,1024]{3,2,1,0:T(8,128)}, f32[2,1,16,1024]{3,2,1,0:T(8,128)S(1)}, u32[]{:S(2)}, u32[]{:S(2)}) collective-permute-start(f32[2,1,16,1024]{3,2,1,0:T(8,128)} %get-tuple-element.24), channel_id=1, source_target_pairs={{0,16},{16,32},{32,48},{48,64},{64,80},{80,96},{96,112},{1,17},{17... | collective-permute-start | bytes 393224 | tf_op jit(solution)/shard_map/ppermute | solution.py:24
  23.3 10.0 %collective-permute-start.4 = (f32[2,16,1,1024]{3,2,1,0:T(1,128)}, f32[2,16,1,1024]{3,2,1,0:T(1,128)S(1)}, u32[]{:S(2)}, u32[]{:S(2)}) collective-permute-start(f32[2,16,1,1024]{3,2,1,0:T(1,128)} %get-tuple-element.25), channel_id=1, source_target_pairs={{0,4},{4,8},{8,12},{1,5},{5,9},{9,13},{2,6},{6,10},{10,14},{3,7},{... | collective-permute-start | bytes 393224 | tf_op jit(solution)/shard_map/ppermute | solution.py:24
  29.2 4.1 %collective-permute-start.5 = (f32[2,2,1,128]{3,2,1,0:T(1,128)}, f32[2,2,1,128]{3,2,1,0:T(1,128)S(1)}, u32[]{:S(2)}, u32[]{:S(2)}) collective-permute-start(f32[2,2,1,128]{3,2,1,0:T(1,128)} %get-tuple-element.26), channel_id=1, source_target_pairs={{0,1},{1,2},{2,3},{4,5},{5,6},{6,7},{8,9},{9,10},{10,11},{12,13},{... | collective-permute-start | bytes 6152 | tf_op jit(solution)/shard_map/ppermute | solution.py:24
  33.4 0.6 copy-start.10
  33.4 0.7 copy-start.4
  33.4 0.7 copy-start.7
  34.0 9.7 %copy-start.8 = (s32[1,1,1,1024]{3,2,1,0:T(1,128)S(1)}, s32[1,1,1,1024]{3,2,1,0:T(1,128)}, u32[]{:S(2)}) copy-start(s32[1,1,1,1024]{3,2,1,0:T(1,128)} %param.11) | copy-start | bytes 12292
  39.2 8.0 %collective-permute-start.6 = (f32[2,1,16,1024]{3,2,1,0:T(8,128)}, f32[2,1,16,1024]{3,2,1,0:T(8,128)S(1)}, u32[]{:S(2)}, u32[]{:S(2)}) collective-permute-start(f32[2,1,16,1024]{3,2,1,0:T(8,128)} %get-tuple-element.28), channel_id=1, source_target_pairs={{16,0},{32,16},{48,32},{64,48},{80,64},{96,80},{112,96},{17,1},{33... | collective-permute-start | bytes 393224 | tf_op jit(solution)/shard_map/ppermute | solution.py:19
  40.5 9.4 %collective-permute-start.7 = (f32[2,16,1,1024]{3,2,1,0:T(1,128)}, f32[2,16,1,1024]{3,2,1,0:T(1,128)S(1)}, u32[]{:S(2)}, u32[]{:S(2)}) collective-permute-start(f32[2,16,1,1024]{3,2,1,0:T(1,128)} %get-tuple-element.29), channel_id=1, source_target_pairs={{4,0},{8,4},{12,8},{5,1},{9,5},{13,9},{6,2},{10,6},{14,10},{7,3},{... | collective-permute-start | bytes 393224 | tf_op jit(solution)/shard_map/ppermute | solution.py:19
  42.4 4.8 %collective-permute-start.8 = (f32[2,2,1,128]{3,2,1,0:T(1,128)}, f32[2,2,1,128]{3,2,1,0:T(1,128)S(1)}, u32[]{:S(2)}, u32[]{:S(2)}) collective-permute-start(f32[2,2,1,128]{3,2,1,0:T(1,128)} %get-tuple-element.30), channel_id=1, source_target_pairs={{1,0},{2,1},{3,2},{5,4},{6,5},{7,6},{9,8},{10,9},{11,10},{13,12},{... | collective-permute-start | bytes 6152 | tf_op jit(solution)/shard_map/ppermute | solution.py:19
  47.2 2.7 %copy-start.11 = (f32[2,2,1,128]{3,2,1,0:T(1,128)}, f32[2,2,1,128]{3,2,1,0:T(1,128)S(1)}, u32[]{:S(2)}) copy-start(f32[2,2,1,128]{3,2,1,0:T(1,128)S(1)} %collective-permute-done.8.hz_ref) | copy-start | bytes 6148
  47.2 2.7 %copy-start = (f32[2,1,16,1024]{3,2,1,0:T(8,128)}, f32[2,1,16,1024]{3,2,1,0:T(8,128)S(1)}, u32[]{:S(2)}) copy-start(f32[2,1,16,1024]{3,2,1,0:T(8,128)S(1)} %collective-permute-done.6.hx_ref) | copy-start | bytes 393220
  49.9 0.7 copy-start.2
  55.4 12.1 %collective-permute-start.10 = (f32[2,16,1,1024]{3,2,1,0:T(1,128)}, f32[2,16,1,1024]{3,2,1,0:T(1,128)S(1)}, u32[]{:S(2)}, u32[]{:S(2)}) collective-permute-start(f32[2,16,1,1024]{3,2,1,0:T(1,128)} %get-tuple-element.33), channel_id=1, source_target_pairs={{0,4},{4,8},{8,12},{1,5},{5,9},{9,13},{2,6},{6,10},{10,14},{3,7},{... | collective-permute-start | bytes 393224 | tf_op jit(solution)/shard_map/ppermute | solution.py:24
  58.8 8.7 %collective-permute-start.9 = (f32[2,1,16,1024]{3,2,1,0:T(8,128)}, f32[2,1,16,1024]{3,2,1,0:T(8,128)S(1)}, u32[]{:S(2)}, u32[]{:S(2)}) collective-permute-start(f32[2,1,16,1024]{3,2,1,0:T(8,128)} %get-tuple-element.32), channel_id=1, source_target_pairs={{0,16},{16,32},{32,48},{48,64},{64,80},{80,96},{96,112},{1,17},{17... | collective-permute-start | bytes 393224 | tf_op jit(solution)/shard_map/ppermute | solution.py:24
  63.0 4.5 %collective-permute-start.11 = (f32[2,2,1,128]{3,2,1,0:T(1,128)}, f32[2,2,1,128]{3,2,1,0:T(1,128)S(1)}, u32[]{:S(2)}, u32[]{:S(2)}) collective-permute-start(f32[2,2,1,128]{3,2,1,0:T(1,128)} %get-tuple-element.34), channel_id=1, source_target_pairs={{0,1},{1,2},{2,3},{4,5},{5,6},{6,7},{8,9},{9,10},{10,11},{12,13},{... | collective-permute-start | bytes 6152 | tf_op jit(solution)/shard_map/ppermute | solution.py:24
  67.6 0.6 copy-start.9
  67.6 0.7 copy-start.1
  67.6 0.7 copy-start.5

commit v17 on v12

--- a/solution.py
+++ b/solution.py
@@ -175,12 +175,12 @@
             lax.broadcasted_iota(jnp.int32, (owners, count), 0) == orow_ref[...], terms_ref[...], 0.0
         )
         slot_hot = (lax.broadcasted_iota(jnp.int32, (slots, count), 0) == srow_ref[...]).astype(jnp.bfloat16)
-        hi, mid, lo = split3(weighted)
+        hi = weighted.astype(jnp.bfloat16)
+        mid = (weighted - hi.astype(jnp.float32)).astype(jnp.bfloat16)
         nt = (((1,), (1,)), ((), ()))
-        summed = (
-            lax.dot_general(hi, slot_hot, nt, preferred_element_type=jnp.float32)
-            + lax.dot_general(mid, slot_hot, nt, preferred_element_type=jnp.float32)
-        ) + lax.dot_general(lo, slot_hot, nt, preferred_element_type=jnp.float32)
+        summed = lax.dot_general(hi, slot_hot, nt, preferred_element_type=jnp.float32) + lax.dot_general(
+            mid, slot_hot, nt, preferred_element_type=jnp.float32
+        )
         owner_ref[...] = summed.reshape(owners, 1, slots)
 
 

time: 97.1 us -> 96.9 us (level)
  no operation moved by 1% of the time
where the time goes in v17:
time: 96.9 us; the launch traced here: 96.5 us
  starting transfers between devices  31.9 us (33%)
  Pallas kernels  24.7 us (25%)
  blocking collectives  19.6 us (20%)
  waiting for transfers between devices  14.8 us (15%)
  local copies, waits for them, and re-layouts  2.71 us (3%)
  other arithmetic  1.93 us (2%)
    ppermute x6, starting transfers between devices, toward_upper(): return lax.ppermute(x, axis, [(j, j + 1) for j in range(peers - 1)])  21.5 us
    all_to_all x1, blocking collectives, body(): received = lax.all_to_all(per_owner, ('gx', 'gy', 'gz'), 0, 0, tiled=True)  19.6 us
    ppermute x6, waiting for transfers between devices, toward_lower(): return lax.ppermute(x, axis, [(j, j - 1) for j in range(1, peers)])  13.5 us
    ppermute x6, starting transfers between devices, toward_lower(): return lax.ppermute(x, axis, [(j, j - 1) for j in range(1, peers)])  10.4 us
    pallas_call x2, Pallas kernels, h_step(): pl.pallas_call(h_kernel, grid=(nx // chunk,), in_specs=[field_spec(nx, ny...  9.67 us
    pallas_call x1, Pallas kernels, e_step(): pl.pallas_call(e_last_kernel, grid=(nx // chunk,), in_specs=in_specs + [f...  7.57 us
    pallas_call x1, Pallas kernels, e_step(): pl.pallas_call(e_kernel, grid=(nx // chunk,), in_specs=in_specs, out_spec...  5.17 us
    unnamed x26, local copies, waits for them, and re-layouts  2.71 us
  transfers between devices with their start and end apart: 12, of which 6 were waited for; matrix products, arithmetic and copies ran while one was open for 1% of the time, Pallas kernels for 0%

profile of v17, /device:TPU:1, one launch (start us, length us, event | category | flops | bytes accessed | tf_op | source)
XLA Modules:
  0.0 96.5 jit_solution(1850481738466168192)
XLA Ops:
  0.6 2.3 %shard_map.94 = (f32[2,1,16,1024]{3,2,1,0:T(8,128)}, f32[2,16,1,1024]{3,2,1,0:T(1,128)}, f32[2,2,1,128]{3,2,1,0:T(1,128)}) custom-call(f32[3,16,16,1024]{3,2,1,0:T(8,128)} %e_ref.3, f32[3,16,16,1024]{3,2,1,0:T(8,128)} %e_ref.3, f32[3,16,16,1024]{3,2,1,0:T(8,128)} %e_ref.3), custom_call_target="tpu_custom_call" | custom-call | tf_op jit(solution)/shard_map/pallas_call | solution.py:221
  3.0 1.3 %collective-permute-start = (f32[2,1,16,1024]{3,2,1,0:T(8,128)}, f32[2,1,16,1024]{3,2,1,0:T(8,128)S(1)}, u32[]{:S(2)}, u32[]{:S(2)}) collective-permute-start(f32[2,1,16,1024]{3,2,1,0:T(8,128)} %get-tuple-element.20), channel_id=1, source_target_pairs={{16,0},{32,16},{48,32},{64,48},{80,64},{96,80},{112,96},{17,1},{33... | collective-permute-start | bytes 393224 | tf_op jit(solution)/shard_map/ppermute | solution.py:19
  4.2 3.3 %collective-permute-start.1 = (f32[2,16,1,1024]{3,2,1,0:T(1,128)}, f32[2,16,1,1024]{3,2,1,0:T(1,128)S(1)}, u32[]{:S(2)}, u32[]{:S(2)}) collective-permute-start(f32[2,16,1,1024]{3,2,1,0:T(1,128)} %get-tuple-element.21), channel_id=1, source_target_pairs={{4,0},{8,4},{12,8},{5,1},{9,5},{13,9},{6,2},{10,6},{14,10},{7,3},{... | collective-permute-start | bytes 393224 | tf_op jit(solution)/shard_map/ppermute | solution.py:19
  7.5 1.3 %collective-permute-start.2 = (f32[2,2,1,128]{3,2,1,0:T(1,128)}, f32[2,2,1,128]{3,2,1,0:T(1,128)S(1)}, u32[]{:S(2)}, u32[]{:S(2)}) collective-permute-start(f32[2,2,1,128]{3,2,1,0:T(1,128)} %get-tuple-element.22), channel_id=1, source_target_pairs={{1,0},{2,1},{3,2},{5,4},{6,5},{7,6},{9,8},{10,9},{11,10},{13,12},{... | collective-permute-start | bytes 6152 | tf_op jit(solution)/shard_map/ppermute | solution.py:19
  8.8 3.4 %collective-permute-done.2.hz_ref = f32[2,2,1,128]{3,2,1,0:T(1,128)S(1)} collective-permute-done((f32[2,2,1,128]{3,2,1,0:T(1,128)}, f32[2,2,1,128]{3,2,1,0:T(1,128)S(1)}, u32[]{:S(2)}, u32[]{:S(2)}) %collective-permute-start.2) | collective-permute-done | bytes 2080 | tf_op jit(solution)/shard_map/ppermute | solution.py:19
  12.2 4.6 %collective-permute-done.1.hy_ref = f32[2,16,1,1024]{3,2,1,0:T(1,128)S(1)} collective-permute-done((f32[2,16,1,1024]{3,2,1,0:T(1,128)}, f32[2,16,1,1024]{3,2,1,0:T(1,128)S(1)}, u32[]{:S(2)}, u32[]{:S(2)}) %collective-permute-start.1) | collective-permute-done | bytes 131104 | tf_op jit(solution)/shard_map/ppermute | solution.py:19
  16.8 0.7 copy-done.6
  17.5 4.8 %shard_map.95 = (f32[3,16,16,1024]{3,2,1,0:T(8,128)}, f32[2,1,16,1024]{3,2,1,0:T(8,128)}, f32[2,16,1,1024]{3,2,1,0:T(1,128)}, f32[2,2,1,128]{3,2,1,0:T(1,128)}) custom-call(f32[3,16,16,1024]{3,2,1,0:T(8,128)} %e_ref.3, f32[3,16,16,1024]{3,2,1,0:T(8,128)} %e_ref.3, f32[3,16,16,1024]{3,2,1,0:T(8,128)} %h_ref.1, f32[2,1,16,1024]{3,2,1,0:T(8,128)} %copy-done.3, ...), custom_call_target="tpu_custom_call" | custom-call | tf_op jit(solution)/shard_map/pallas_call | solution.py:244
  22.3 1.3 %collective-permute-start.3 = (f32[2,1,16,1024]{3,2,1,0:T(8,128)}, f32[2,1,16,1024]{3,2,1,0:T(8,128)S(1)}, u32[]{:S(2)}, u32[]{:S(2)}) collective-permute-start(f32[2,1,16,1024]{3,2,1,0:T(8,128)} %get-tuple-element.24), channel_id=1, source_target_pairs={{0,16},{16,32},{32,48},{48,64},{64,80},{80,96},{96,112},{1,17},{17... | collective-permute-start | bytes 393224 | tf_op jit(solution)/shard_map/ppermute | solution.py:24
  23.6 5.9 %collective-permute-start.4 = (f32[2,16,1,1024]{3,2,1,0:T(1,128)}, f32[2,16,1,1024]{3,2,1,0:T(1,128)S(1)}, u32[]{:S(2)}, u32[]{:S(2)}) collective-permute-start(f32[2,16,1,1024]{3,2,1,0:T(1,128)} %get-tuple-element.25), channel_id=1, source_target_pairs={{0,4},{4,8},{8,12},{1,5},{5,9},{9,13},{2,6},{6,10},{10,14},{3,7},{... | collective-permute-start | bytes 393224 | tf_op jit(solution)/shard_map/ppermute | solution.py:24
  29.5 3.2 %collective-permute-start.5 = (f32[2,2,1,128]{3,2,1,0:T(1,128)}, f32[2,2,1,128]{3,2,1,0:T(1,128)S(1)}, u32[]{:S(2)}, u32[]{:S(2)}) collective-permute-start(f32[2,2,1,128]{3,2,1,0:T(1,128)} %get-tuple-element.26), channel_id=1, source_target_pairs={{0,1},{1,2},{2,3},{4,5},{5,6},{6,7},{8,9},{9,10},{10,11},{12,13},{... | collective-permute-start | bytes 6152 | tf_op jit(solution)/shard_map/ppermute | solution.py:24
  32.7 0.9 collective-permute-done.5.hz_ref
  33.6 0.6 copy-done.10
  34.3 5.2 %shard_map.96 = (f32[3,16,16,1024]{3,2,1,0:T(8,128)}, f32[2,1,16,1024]{3,2,1,0:T(8,128)}, f32[2,16,1,1024]{3,2,1,0:T(1,128)}, f32[2,2,1,128]{3,2,1,0:T(1,128)}) custom-call(f32[3,16,16,1024]{3,2,1,0:T(8,128)} %e_ref.3, f32[3,16,16,1024]{3,2,1,0:T(8,128)} %get-tuple-element.23.h_ref.hp_ref, f32[3,16,16,1024]{3,2,1,0:T(8,128)} %get-tuple-element.23.h_ref.hp_ref, ...), custom_call_target="tpu_custom_call" | custom-call | tf_op jit(solution)/shard_map/pallas_call | solution.py:277
  39.5 1.3 %collective-permute-start.6 = (f32[2,1,16,1024]{3,2,1,0:T(8,128)}, f32[2,1,16,1024]{3,2,1,0:T(8,128)S(1)}, u32[]{:S(2)}, u32[]{:S(2)}) collective-permute-start(f32[2,1,16,1024]{3,2,1,0:T(8,128)} %get-tuple-element.28), channel_id=1, source_target_pairs={{16,0},{32,16},{48,32},{64,48},{80,64},{96,80},{112,96},{17,1},{33... | collective-permute-start | bytes 393224 | tf_op jit(solution)/shard_map/ppermute | solution.py:19
  40.8 1.9 %collective-permute-start.7 = (f32[2,16,1,1024]{3,2,1,0:T(1,128)}, f32[2,16,1,1024]{3,2,1,0:T(1,128)S(1)}, u32[]{:S(2)}, u32[]{:S(2)}) collective-permute-start(f32[2,16,1,1024]{3,2,1,0:T(1,128)} %get-tuple-element.29), channel_id=1, source_target_pairs={{4,0},{8,4},{12,8},{5,1},{9,5},{13,9},{6,2},{10,6},{14,10},{7,3},{... | collective-permute-start | bytes 393224 | tf_op jit(solution)/shard_map/ppermute | solution.py:19
  42.7 1.3 %collective-permute-start.8 = (f32[2,2,1,128]{3,2,1,0:T(1,128)}, f32[2,2,1,128]{3,2,1,0:T(1,128)S(1)}, u32[]{:S(2)}, u32[]{:S(2)}) collective-permute-start(f32[2,2,1,128]{3,2,1,0:T(1,128)} %get-tuple-element.30), channel_id=1, source_target_pairs={{1,0},{2,1},{3,2},{5,4},{6,5},{7,6},{9,8},{10,9},{11,10},{13,12},{... | collective-permute-start | bytes 6152 | tf_op jit(solution)/shard_map/ppermute | solution.py:19
  44.0 0.6 and_select_fusion
  44.6 2.9 %collective-permute-done.8.hz_ref = f32[2,2,1,128]{3,2,1,0:T(1,128)S(1)} collective-permute-done((f32[2,2,1,128]{3,2,1,0:T(1,128)}, f32[2,2,1,128]{3,2,1,0:T(1,128)S(1)}, u32[]{:S(2)}, u32[]{:S(2)}) %collective-permute-start.8) | collective-permute-done | bytes 2080 | tf_op jit(solution)/shard_map/ppermute | solution.py:19
  47.5 2.7 %collective-permute-done.7.hy_ref = f32[2,16,1,1024]{3,2,1,0:T(1,128)S(1)} collective-permute-done((f32[2,16,1,1024]{3,2,1,0:T(1,128)}, f32[2,16,1,1024]{3,2,1,0:T(1,128)S(1)}, u32[]{:S(2)}, u32[]{:S(2)}) %collective-permute-start.7) | collective-permute-done | bytes 131104 | tf_op jit(solution)/shard_map/ppermute | solution.py:19
  50.2 0.7 copy-done.2
  50.8 4.8 %shard_map.97 = (f32[3,16,16,1024]{3,2,1,0:T(8,128)}, f32[2,1,16,1024]{3,2,1,0:T(8,128)}, f32[2,16,1,1024]{3,2,1,0:T(1,128)}, f32[2,2,1,128]{3,2,1,0:T(1,128)}) custom-call(f32[3,16,16,1024]{3,2,1,0:T(8,128)} %get-tuple-element.27.e_ref.en_ref, f32[3,16,16,1024]{3,2,1,0:T(8,128)} %get-tuple-element.27.e_ref.en_ref, ...), custom_call_target="tpu_custom_call" | custom-call | tf_op jit(solution)/shard_map/pallas_call | solution.py:244
  55.7 3.4 %collective-permute-start.10 = (f32[2,16,1,1024]{3,2,1,0:T(1,128)}, f32[2,16,1,1024]{3,2,1,0:T(1,128)S(1)}, u32[]{:S(2)}, u32[]{:S(2)}) collective-permute-start(f32[2,16,1,1024]{3,2,1,0:T(1,128)} %get-tuple-element.33), channel_id=1, source_target_pairs={{0,4},{4,8},{8,12},{1,5},{5,9},{9,13},{2,6},{6,10},{10,14},{3,7},{... | collective-permute-start | bytes 393224 | tf_op jit(solution)/shard_map/ppermute | solution.py:24
  59.1 4.2 %collective-permute-start.9 = (f32[2,1,16,1024]{3,2,1,0:T(8,128)}, f32[2,1,16,1024]{3,2,1,0:T(8,128)S(1)}, u32[]{:S(2)}, u32[]{:S(2)}) collective-permute-start(f32[2,1,16,1024]{3,2,1,0:T(8,128)} %get-tuple-element.32), channel_id=1, source_target_pairs={{0,16},{16,32},{32,48},{48,64},{64,80},{80,96},{96,112},{1,17},{17... | collective-permute-start | bytes 393224 | tf_op jit(solution)/shard_map/ppermute | solution.py:24
  63.3 3.6 %collective-permute-start.11 = (f32[2,2,1,128]{3,2,1,0:T(1,128)}, f32[2,2,1,128]{3,2,1,0:T(1,128)S(1)}, u32[]{:S(2)}, u32[]{:S(2)}) collective-permute-start(f32[2,2,1,128]{3,2,1,0:T(1,128)} %get-tuple-element.34), channel_id=1, source_target_pairs={{0,1},{1,2},{2,3},{4,5},{5,6},{6,7},{8,9},{9,10},{10,11},{12,13},{... | collective-permute-start | bytes 6152 | tf_op jit(solution)/shard_map/ppermute | solution.py:24
  66.9 0.6 and_select_fusion.1.zrow_ref
  67.5 0.3 collective-permute-done.11.hz_ref
  67.8 0.6 copy-done.9
  68.4 0.1 copy-done.1
  68.5 7.6 %shard_map.98 = (f32[3,16,16,1024]{3,2,1,0:T(8,128)}, f32[128,1,256]{2,1,0:T(1,128)}) custom-call(f32[3,16,16,1024]{3,2,1,0:T(8,128)} %get-tuple-element.27.e_ref.en_ref, f32[3,16,16,1024]{3,2,1,0:T(8,128)} %get-tuple-element.18.h_ref.hp_ref, f32[3,16,16,1024]{3,2,1,0:T(8,128)} %get-tuple-element.18.h_ref.hp_ref, f32[16,16,1024]{2,1,0:T(8,128)} %inv_ref.3, ...), custom_call_target="tpu_custom_call" | custom-call | tf_op jit(solution)/shard_map/pallas_call | solution.py:288
  76.1 19.6 %all_to_all.5 = f32[128,1,256]{2,1,0:T(1,128)S(1)} all-to-all(f32[128,1,256]{2,1,0:T(1,128)} %get-tuple-element.36), channel_id=1, replica_groups=mesh['gx'=8,'gy'=4,'gz'=4] {'gx','gy','gz'}, dimensions={0} | all-to-all | bytes 262144 | tf_op jit(solution)/shard_map/all_to_all | solution.py:320
  95.7 0.7 reduce_sum.9
  (27 shorter events, 0.2 us)
Async XLA Ops:
  3.0 9.3 %collective-permute-start = (f32[2,1,16,1024]{3,2,1,0:T(8,128)}, f32[2,1,16,1024]{3,2,1,0:T(8,128)S(1)}, u32[]{:S(2)}, u32[]{:S(2)}) collective-permute-start(f32[2,1,16,1024]{3,2,1,0:T(8,128)} %get-tuple-element.20), channel_id=1, source_target_pairs={{16,0},{32,16},{48,32},{64,48},{80,64},{96,80},{112,96},{17,1},{33... | collective-permute-start | bytes 393224 | tf_op jit(solution)/shard_map/ppermute | solution.py:19
  4.2 12.5 %collective-permute-start.1 = (f32[2,16,1,1024]{3,2,1,0:T(1,128)}, f32[2,16,1,1024]{3,2,1,0:T(1,128)S(1)}, u32[]{:S(2)}, u32[]{:S(2)}) collective-permute-start(f32[2,16,1,1024]{3,2,1,0:T(1,128)} %get-tuple-element.21), channel_id=1, source_target_pairs={{4,0},{8,4},{12,8},{5,1},{9,5},{13,9},{6,2},{10,6},{14,10},{7,3},{... | collective-permute-start | bytes 393224 | tf_op jit(solution)/shard_map/ppermute | solution.py:19
  7.5 4.7 %collective-permute-start.2 = (f32[2,2,1,128]{3,2,1,0:T(1,128)}, f32[2,2,1,128]{3,2,1,0:T(1,128)S(1)}, u32[]{:S(2)}, u32[]{:S(2)}) collective-permute-start(f32[2,2,1,128]{3,2,1,0:T(1,128)} %get-tuple-element.22), channel_id=1, source_target_pairs={{1,0},{2,1},{3,2},{5,4},{6,5},{7,6},{9,8},{10,9},{11,10},{13,12},{... | collective-permute-start | bytes 6152 | tf_op jit(solution)/shard_map/ppermute | solution.py:19
  12.2 4.6 %copy-start.12 = (f32[2,2,1,128]{3,2,1,0:T(1,128)}, f32[2,2,1,128]{3,2,1,0:T(1,128)S(1)}, u32[]{:S(2)}) copy-start(f32[2,2,1,128]{3,2,1,0:T(1,128)S(1)} %collective-permute-done.2.hz_ref) | copy-start | bytes 6148
  12.2 4.6 %copy-start.3 = (f32[2,1,16,1024]{3,2,1,0:T(8,128)}, f32[2,1,16,1024]{3,2,1,0:T(8,128)S(1)}, u32[]{:S(2)}) copy-start(f32[2,1,16,1024]{3,2,1,0:T(8,128)S(1)} %collective-permute-done.hx_ref) | copy-start | bytes 393220
  16.8 0.7 copy-start.6
  22.3 11.3 %collective-permute-start.3 = (f32[2,1,16,1024]{3,2,1,0:T(8,128)}, f32[2,1,16,1024]{3,2,1,0:T(8,128)S(1)}, u32[]{:S(2)}, u32[]{:S(2)}) collective-permute-start(f32[2,1,16,1024]{3,2,1,0:T(8,128)} %get-tuple-element.24), channel_id=1, source_target_pairs={{0,16},{16,32},{32,48},{48,64},{64,80},{80,96},{96,112},{1,17},{17... | collective-permute-start | bytes 393224 | tf_op jit(solution)/shard_map/ppermute | solution.py:24
  23.6 10.0 %collective-permute-start.4 = (f32[2,16,1,1024]{3,2,1,0:T(1,128)}, f32[2,16,1,1024]{3,2,1,0:T(1,128)S(1)}, u32[]{:S(2)}, u32[]{:S(2)}) collective-permute-start(f32[2,16,1,1024]{3,2,1,0:T(1,128)} %get-tuple-element.25), channel_id=1, source_target_pairs={{0,4},{4,8},{8,12},{1,5},{5,9},{9,13},{2,6},{6,10},{10,14},{3,7},{... | collective-permute-start | bytes 393224 | tf_op jit(solution)/shard_map/ppermute | solution.py:24
  29.5 4.1 %collective-permute-start.5 = (f32[2,2,1,128]{3,2,1,0:T(1,128)}, f32[2,2,1,128]{3,2,1,0:T(1,128)S(1)}, u32[]{:S(2)}, u32[]{:S(2)}) collective-permute-start(f32[2,2,1,128]{3,2,1,0:T(1,128)} %get-tuple-element.26), channel_id=1, source_target_pairs={{0,1},{1,2},{2,3},{4,5},{5,6},{6,7},{8,9},{9,10},{10,11},{12,13},{... | collective-permute-start | bytes 6152 | tf_op jit(solution)/shard_map/ppermute | solution.py:24
  33.6 0.6 copy-start.10
  33.6 0.7 copy-start.4
  33.6 0.7 copy-start.7
  34.3 9.7 %copy-start.8 = (s32[1,1,1,1024]{3,2,1,0:T(1,128)S(1)}, s32[1,1,1,1024]{3,2,1,0:T(1,128)}, u32[]{:S(2)}) copy-start(s32[1,1,1,1024]{3,2,1,0:T(1,128)} %param.11) | copy-start | bytes 12292
  39.5 8.0 %collective-permute-start.6 = (f32[2,1,16,1024]{3,2,1,0:T(8,128)}, f32[2,1,16,1024]{3,2,1,0:T(8,128)S(1)}, u32[]{:S(2)}, u32[]{:S(2)}) collective-permute-start(f32[2,1,16,1024]{3,2,1,0:T(8,128)} %get-tuple-element.28), channel_id=1, source_target_pairs={{16,0},{32,16},{48,32},{64,48},{80,64},{96,80},{112,96},{17,1},{33... | collective-permute-start | bytes 393224 | tf_op jit(solution)/shard_map/ppermute | solution.py:19
  40.8 9.4 %collective-permute-start.7 = (f32[2,16,1,1024]{3,2,1,0:T(1,128)}, f32[2,16,1,1024]{3,2,1,0:T(1,128)S(1)}, u32[]{:S(2)}, u32[]{:S(2)}) collective-permute-start(f32[2,16,1,1024]{3,2,1,0:T(1,128)} %get-tuple-element.29), channel_id=1, source_target_pairs={{4,0},{8,4},{12,8},{5,1},{9,5},{13,9},{6,2},{10,6},{14,10},{7,3},{... | collective-permute-start | bytes 393224 | tf_op jit(solution)/shard_map/ppermute | solution.py:19
  42.7 4.8 %collective-permute-start.8 = (f32[2,2,1,128]{3,2,1,0:T(1,128)}, f32[2,2,1,128]{3,2,1,0:T(1,128)S(1)}, u32[]{:S(2)}, u32[]{:S(2)}) collective-permute-start(f32[2,2,1,128]{3,2,1,0:T(1,128)} %get-tuple-element.30), channel_id=1, source_target_pairs={{1,0},{2,1},{3,2},{5,4},{6,5},{7,6},{9,8},{10,9},{11,10},{13,12},{... | collective-permute-start | bytes 6152 | tf_op jit(solution)/shard_map/ppermute | solution.py:19
  47.5 2.7 %copy-start.11 = (f32[2,2,1,128]{3,2,1,0:T(1,128)}, f32[2,2,1,128]{3,2,1,0:T(1,128)S(1)}, u32[]{:S(2)}) copy-start(f32[2,2,1,128]{3,2,1,0:T(1,128)S(1)} %collective-permute-done.8.hz_ref) | copy-start | bytes 6148
  47.5 2.7 %copy-start = (f32[2,1,16,1024]{3,2,1,0:T(8,128)}, f32[2,1,16,1024]{3,2,1,0:T(8,128)S(1)}, u32[]{:S(2)}) copy-start(f32[2,1,16,1024]{3,2,1,0:T(8,128)S(1)} %collective-permute-done.6.hx_ref) | copy-start | bytes 393220
  50.2 0.7 copy-start.2
  55.7 12.1 %collective-permute-start.10 = (f32[2,16,1,1024]{3,2,1,0:T(1,128)}, f32[2,16,1,1024]{3,2,1,0:T(1,128)S(1)}, u32[]{:S(2)}, u32[]{:S(2)}) collective-permute-start(f32[2,16,1,1024]{3,2,1,0:T(1,128)} %get-tuple-element.33), channel_id=1, source_target_pairs={{0,4},{4,8},{8,12},{1,5},{5,9},{9,13},{2,6},{6,10},{10,14},{3,7},{... | collective-permute-start | bytes 393224 | tf_op jit(solution)/shard_map/ppermute | solution.py:24
  59.1 8.7 %collective-permute-start.9 = (f32[2,1,16,1024]{3,2,1,0:T(8,128)}, f32[2,1,16,1024]{3,2,1,0:T(8,128)S(1)}, u32[]{:S(2)}, u32[]{:S(2)}) collective-permute-start(f32[2,1,16,1024]{3,2,1,0:T(8,128)} %get-tuple-element.32), channel_id=1, source_target_pairs={{0,16},{16,32},{32,48},{48,64},{64,80},{80,96},{96,112},{1,17},{17... | collective-permute-start | bytes 393224 | tf_op jit(solution)/shard_map/ppermute | solution.py:24
  63.3 4.5 %collective-permute-start.11 = (f32[2,2,1,128]{3,2,1,0:T(1,128)}, f32[2,2,1,128]{3,2,1,0:T(1,128)S(1)}, u32[]{:S(2)}, u32[]{:S(2)}) collective-permute-start(f32[2,2,1,128]{3,2,1,0:T(1,128)} %get-tuple-element.34), channel_id=1, source_target_pairs={{0,1},{1,2},{2,3},{4,5},{5,6},{6,7},{8,9},{9,10},{10,11},{12,13},{... | collective-permute-start | bytes 6152 | tf_op jit(solution)/shard_map/ppermute | solution.py:24
  67.8 0.6 copy-start.9
  67.8 0.7 copy-start.1
  67.8 0.7 copy-start.5
